TPU v7x, 128 devices: a whole 4x4x4 slice. The times are simulated.
128 devices in a mesh: grid: 32 (over y, x, core), layer: 4 (over z).
Axes of the slice: x: 4, y: 4, z: 4, core: 2. Of those that a mesh axis runs over, the one named last changes fastest.
Arguments:
- h_blocks: bfloat16 [1024, 8, 128, 128], P('grid', 'layer'), may hold values from -0.09375 to 0.09375
- block_cols: int32 [1024, 8], P('grid', 'layer'), may hold values from 0 to 1023, as said below
- t_now: bfloat16 [131072, 1536], P(('grid', 'layer')), may hold values from -6 to 6
- t_prev: bfloat16 [131072, 1536], P(('grid', 'layer')), may hold values from -6 to 6
Outputs:
- next_term: bfloat16 [131072, 1536], P(('grid', 'layer'))
- after_term: bfloat16 [131072, 1536], P(('grid', 'layer'))
Inputs may be any that keep to these rules, and one draw needn't show every extreme that they name: block_cols[i, 0] = i. With g = i // 32, every block column lies among the block rows g * 32 - 2 to g * 32 + 33 counted cyclically modulo 1024, and both ends of that range are named in every block row.
All inputs are finite; a program needn't handle non-finite values.
Results may differ from a plain program's by a relative error of at most 0.019.
Values may be sent and summed in bfloat16 or wider, within the bound.
No kernel may reach another device: no remote copies, remote signals or barrier semaphores. Data moves between devices by JAX's collectives and lax.ppermute only.
A program may use at most 192 MiB of HBM per device.

v0:
```python
import jax
import jax.numpy as jnp
from jax import lax
from jax.sharding import PartitionSpec as P

KB = 8
HB = 2


def padded(array, sides, width):
    for axis, dim in sides:
        size, length = (lax.axis_size(axis), array.shape[dim])
        up = [(i, (i + 1) % size) for i in range(size)]
        down = [(j, i) for i, j in up]
        last = lax.slice_in_dim(array, length - width, length, axis=dim)
        leading = lax.slice_in_dim(array, 0, width, axis=dim)
        before = lax.ppermute(last, axis, up)
        after = lax.ppermute(leading, axis, down)
        array = jnp.concatenate([before, array, after], axis=dim)
    return array


def layer_parts(h_part, rel_part, panel):
    block_size = h_part.shape[2]
    group_rows = h_part.shape[0]
    width = panel.shape[1]
    wide = padded(panel, (("grid", 0),), HB * block_size)
    blocks = wide.reshape(wide.shape[0] // block_size, block_size, width)
    picked = blocks[rel_part]
    per_layer = KB // lax.axis_size("layer")
    groups = h_part.shape[1] // per_layer
    h_split = h_part.reshape(group_rows, groups, per_layer, block_size, block_size)
    p_split = picked.reshape(group_rows, groups, per_layer, block_size, width)
    return jnp.einsum("rqsij,rqsjc->qric", h_split, p_split, preferred_element_type=jnp.float32)


def shards(h_blocks, block_cols, t_now, t_prev):
    group_rows = h_blocks.shape[0]
    block_size = h_blocks.shape[2]
    total_blocks = group_rows * lax.axis_size("grid")
    first_block = lax.axis_index("grid") * group_rows
    relative = (block_cols - first_block + HB + total_blocks) % total_blocks

    def recur(current, previous):
        panel = lax.all_gather(current, "layer", axis=0, tiled=True)
        parts = layer_parts(h_blocks, relative, panel)
        flat = parts[0].reshape(group_rows * block_size, panel.shape[1])
        summed = lax.psum_scatter(
            flat.astype(jnp.bfloat16), "layer", scatter_dimension=0, tiled=True
        ).astype(jnp.float32)
        return (2.0 * summed - previous.astype(jnp.float32)).astype(jnp.bfloat16)

    next_term = recur(t_now, t_prev)
    after_term = recur(next_term, t_now)
    return (next_term, after_term)


def solution(mesh):
    in_specs = (
        P("grid", "layer", None, None),
        P("grid", "layer"),
        P(("grid", "layer"), None),
        P(("grid", "layer"), None),
    )
    out_specs = (P(("grid", "layer"), None), P(("grid", "layer"), None))
    return jax.shard_map(shards, mesh=mesh, in_specs=in_specs, out_specs=out_specs, check_vma=False)
```

profile of v0, /device:TPU:0, one launch (start us, length us, event | category | flops | bytes accessed | tf_op | source)
XLA Modules:
  0.0 626.2 jit_solution(10292019900121889898)
XLA Ops:
  7.2 0.0 copy-start
  7.2 0.0 all-gather.3.cloned.1.call-start
  7.2 0.7 all-gather.3.cloned.1.call-update
  7.9 0.0 reduce-scatter.3.cloned.1.call-start
  8.0 122.8 %all-gather.3.cloned.1.call-done = bf16[4096,1536]{1,0:T(8,128)(2,1)} async-done(((bf16[1024,1536]{1,0:T(8,128)(2,1)}), bf16[4096,1536]{1,0:T(8,128)(2,1)}) %all-gather.3.cloned.1.call-update) | async-done | bytes 12582928 | tf_op jit(solution)/shard_map/all_gather | solution.py:45
  130.8 2.6 fusion.2
  133.4 5.1 collective-permute-start.1
  138.5 0.7 compare_select_fusion
  139.1 0.1 copy.7
  139.2 0.1 reshape.32
  139.4 9.0 %collective-permute-done = bf16[256,1536]{1,0:T(8,128)(2,1)S(1)} collective-permute-done((bf16[256,1536]{1,0:T(8,128)(2,1)}, bf16[256,1536]{1,0:T(8,128)(2,1)S(1)}, u32[]{:S(2)}, u32[]{:S(2)}) %collective-permute-start) | collective-permute-done | bytes 786464 | tf_op jit(solution)/shard_map/ppermute | solution.py:17
  148.3 16.6 %pad_maximum_fusion = bf16[4608,1536]{1,0:T(8,128)(2,1)} fusion(bf16[256,1536]{1,0:T(8,128)(2,1)} %collective-permute-done.1, bf16[4096,1536]{1,0:T(8,128)(2,1)} %all-gather.3.cloned.1.call-done, bf16[256,1536]{1,0:T(8,128)(2,1)S(1)} %collective-permute-done), kind=kLoop, calls=%fused_computation.4 | loop fusion | flops 42467328 | bytes 28311552 | tf_op jit(solution)/shard_map/concatenate | solution.py:19
  165.0 15.5 %gather_fusion = bf16[64,128,1536]{2,1,0:T(8,128)(2,1)} fusion(bf16[36,128,1536]{2,1,0:T(8,128)(2,1)} %bitcast.23, s32[1024]{0:T(1024)S(1)} %pad_clamp_fusion), kind=kCustom, calls=%fused_computation | custom fusion | bytes 50331904 | tf_op jit(solution)/shard_map/gather | solution.py:29
  180.5 14.5 %bitcast_convert_fusion.1 = bf16[32,1536,128]{1,2,0:T(8,128)(2,1)} fusion(bf16[32,2,128,128]{3,2,1,0:T(8,128)(2,1)S(1)} %copy-done, bf16[32,2,128,1536]{3,2,1,0:T(8,128)(2,1)} %bitcast.21), kind=kOutput, calls=%fused_computation.3 | convolution fusion | flops 3227516928 | bytes 39845888 | tf_op jit(solution)/shard_map/rqsij,rqsjc->qric/dot_general | solution.py:34
  194.9 0.0 reduce-scatter.3.cloned.1.call-update
  195.0 0.0 all-gather.5.cloned.1.call-start
  195.0 115.6 %reduce-scatter.3.cloned.1.call-done = bf16[1024,1536]{1,0:T(8,128)(2,1)} async-done(((bf16[4096,1536]{1,0:T(8,128)(2,1)}), bf16[1024,1536]{1,0:T(8,128)(2,1)}) %reduce-scatter.3.cloned.1.call-update) | async-done | bytes 3145744 | tf_op jit(solution)/shard_map/reduce_scatter | solution.py:48
  310.6 5.5 subtract_convert_fusion.1
  316.0 0.0 all-gather.5.cloned.1.call-update
  316.1 0.0 reduce-scatter.5.cloned.1.call-start
  316.1 118.3 %all-gather.5.cloned.1.call-done = bf16[4096,1536]{1,0:T(8,128)(2,1)} async-done(((bf16[1024,1536]{1,0:T(8,128)(2,1)}), bf16[4096,1536]{1,0:T(8,128)(2,1)}) %all-gather.5.cloned.1.call-update) | async-done | bytes 12582928 | tf_op jit(solution)/shard_map/all_gather | solution.py:45
  434.4 1.5 fusion.1
  435.9 0.1 collective-permute-start.2
  436.0 5.1 collective-permute-start.3
  441.0 9.7 %collective-permute-done.2 = bf16[256,1536]{1,0:T(8,128)(2,1)S(1)} collective-permute-done((bf16[256,1536]{1,0:T(8,128)(2,1)S(1)}, bf16[256,1536]{1,0:T(8,128)(2,1)S(1)}, u32[]{:S(2)}, u32[]{:S(2)}) %collective-permute-start.2) | collective-permute-done | bytes 786464 | tf_op jit(solution)/shard_map/ppermute | solution.py:17
  450.7 0.0 collective-permute-done.3
  450.7 18.0 %pad_maximum_fusion.1 = bf16[4608,1536]{1,0:T(8,128)(2,1)} fusion(bf16[256,1536]{1,0:T(8,128)(2,1)S(1)} %collective-permute-done.3, bf16[4096,1536]{1,0:T(8,128)(2,1)} %all-gather.5.cloned.1.call-done, bf16[256,1536]{1,0:T(8,128)(2,1)S(1)} %collective-permute-done.2), kind=kLoop, calls=%fused_computation.5 | loop fusion | flops 42467328 | bytes 28311552 | tf_op jit(solution)/shard_map/concatenate | solution.py:19
  468.7 15.5 %gather_fusion.1 = bf16[64,128,1536]{2,1,0:T(8,128)(2,1)} fusion(bf16[36,128,1536]{2,1,0:T(8,128)(2,1)} %bitcast.22, s32[1024]{0:T(1024)S(1)} %pad_clamp_fusion), kind=kCustom, calls=%fused_computation.1 | custom fusion | bytes 50331904 | tf_op jit(solution)/shard_map/gather | solution.py:29
  484.2 14.4 %bitcast_convert_fusion = bf16[32,1536,128]{1,2,0:T(8,128)(2,1)} fusion(bf16[32,2,128,128]{3,2,1,0:T(8,128)(2,1)S(1)} %copy-done, bf16[32,2,128,1536]{3,2,1,0:T(8,128)(2,1)} %bitcast.20), kind=kOutput, calls=%fused_computation.2 | convolution fusion | flops 3227516928 | bytes 39845888 | tf_op jit(solution)/shard_map/rqsij,rqsjc->qric/dot_general | solution.py:34
  498.6 0.0 reduce-scatter.5.cloned.1.call-update
  498.6 115.5 %reduce-scatter.5.cloned.1.call-done = bf16[1024,1536]{1,0:T(8,128)(2,1)} async-done(((bf16[4096,1536]{1,0:T(8,128)(2,1)}), bf16[1024,1536]{1,0:T(8,128)(2,1)}) %reduce-scatter.5.cloned.1.call-update) | async-done | bytes 3145744 | tf_op jit(solution)/shard_map/reduce_scatter | solution.py:48
  614.2 5.5 subtract_convert_fusion
  (4 shorter events, 0.0 us)
Async XLA Ops:
  7.2 173.3 %copy-start = (bf16[32,2,128,128]{3,2,1,0:T(8,128)(2,1)S(1)}, bf16[32,2,128,128]{3,2,1,0:T(8,128)(2,1)}, u32[]{:S(2)}) copy-start(bf16[32,2,128,128]{3,2,1,0:T(8,128)(2,1)} %param.4) | copy-start | bytes 6291460
  7.2 123.6 %all-gather.3.cloned.1.call-start = ((), (), s32[]{:S(2)}) async-start(), calls=%async_computation.2 | async-start | bytes 15728640 | tf_op jit(solution)/shard_map/all_gather | solution.py:45
  7.9 302.7 %reduce-scatter.3.cloned.1.call-start = ((), (), s32[]{:S(2)}) async-start(), calls=%async_computation.3 | async-start | bytes 15728640 | tf_op jit(solution)/shard_map/reduce_scatter | solution.py:48
  133.4 14.9 %collective-permute-start = (bf16[256,1536]{1,0:T(8,128)(2,1)}, bf16[256,1536]{1,0:T(8,128)(2,1)S(1)}, u32[]{:S(2)}, u32[]{:S(2)}) collective-permute-start(bf16[256,1536]{1,0:T(8,128)(2,1)} %get-tuple-element.4), channel_id=1, source_target_pairs={{0,4},{4,8},{8,12},{12,16},{16,20},{20,24},{24,28},{28,32},{32,36}... | collective-permute-start | bytes 2359304 | tf_op jit(solution)/shard_map/ppermute | solution.py:17
  133.4 14.9 %collective-permute-start.1 = (bf16[256,1536]{1,0:T(8,128)(2,1)}, bf16[256,1536]{1,0:T(8,128)(2,1)}, u32[]{:S(2)}, u32[]{:S(2)}) collective-permute-start(bf16[256,1536]{1,0:T(8,128)(2,1)} %get-tuple-element.5), channel_id=1, source_target_pairs={{4,0},{8,4},{12,8},{16,12},{20,16},{24,20},{28,24},{32,28},{36,32}... | collective-permute-start | bytes 2359304 | tf_op jit(solution)/shard_map/ppermute | solution.py:18
  195.0 239.5 %all-gather.5.cloned.1.call-start = ((), (), s32[]{:S(2)}) async-start(), calls=%async_computation.4 | async-start | bytes 15728640 | tf_op jit(solution)/shard_map/all_gather | solution.py:45
  316.1 298.1 %reduce-scatter.5.cloned.1.call-start = ((), (), s32[]{:S(2)}) async-start(), calls=%async_computation.5 | async-start | bytes 15728640 | tf_op jit(solution)/shard_map/reduce_scatter | solution.py:48
  435.9 14.8 %collective-permute-start.2 = (bf16[256,1536]{1,0:T(8,128)(2,1)S(1)}, bf16[256,1536]{1,0:T(8,128)(2,1)S(1)}, u32[]{:S(2)}, u32[]{:S(2)}) collective-permute-start(bf16[256,1536]{1,0:T(8,128)(2,1)S(1)} %get-tuple-element.2), channel_id=1, source_target_pairs={{0,4},{4,8},{8,12},{12,16},{16,20},{20,24},{24,28},{28,32},{32,36}... | collective-permute-start | bytes 2359304 | tf_op jit(solution)/shard_map/ppermute | solution.py:17
  436.0 14.7 %collective-permute-start.3 = (bf16[256,1536]{1,0:T(8,128)(2,1)S(1)}, bf16[256,1536]{1,0:T(8,128)(2,1)S(1)}, u32[]{:S(2)}, u32[]{:S(2)}) collective-permute-start(bf16[256,1536]{1,0:T(8,128)(2,1)S(1)} %get-tuple-element.3), channel_id=1, source_target_pairs={{4,0},{8,4},{12,8},{16,12},{20,16},{24,20},{28,24},{32,28},{36,32}... | collective-permute-start | bytes 2359304 | tf_op jit(solution)/shard_map/ppermute | solution.py:18
Sparse Core Ops, SparseCore 0:
  9.6 121.0 all-gather.2
  195.1 115.4 reduce-scatter.2
  316.2 118.1 all-gather.4
  498.7 115.3 reduce-scatter.4
where the time goes:
time: 627 us; the launch traced here: 626 us
  waiting for transfers between devices  492 us (78%)
  other arithmetic  46.2 us (7%)
  local copies, waits for them, and re-layouts  35.2 us (6%)
  matrix products  28.9 us (5%)
  between operations  13.8 us (2%)
  starting transfers between devices  10.4 us (2%)
    all_gather x2, waiting for transfers between devices, recur(): panel = lax.all_gather(current, 'layer', axis=0, tiled=True)  241 us
    reduce_scatter x2, waiting for transfers between devices, recur(): lax.psum_scatter(flat.astype(jnp.bfloat16), 'layer', scatter_dimension=0,...  231 us
    concatenate x2, other arithmetic, padded(): array = jnp.concatenate([before, array, after], axis=dim)  34.6 us
    gather x2, local copies, waits for them, and re-layouts, layer_parts(): picked = blocks[rel_part]  31 us
    dot_general x2, matrix products, layer_parts(): jnp.einsum('rqsij,rqsjc->qric', h_split, p_split, preferred_element_type=...  28.9 us
    ppermute x2, waiting for transfers between devices, padded(): before = lax.ppermute(last, axis, up)  18.6 us
  transfers between devices with their start and end apart: 8, of which 6 were waited for; matrix products, arithmetic and copies ran while one was open for 0% of the time, Pallas kernels for 0%

commit v1 on v0

v1 whole, which is shorter than its diff:
```python
import jax
import jax.numpy as jnp
from jax import lax
from jax.sharding import PartitionSpec as P

KB = 8
HB = 2
NCH = 4


def padded(array, width):
    size, length = (lax.axis_size("grid"), array.shape[0])
    up = [(i, (i + 1) % size) for i in range(size)]
    down = [(j, i) for i, j in up]
    before = lax.ppermute(array[length - width:], "grid", up)
    after = lax.ppermute(array[:width], "grid", down)
    return jnp.concatenate([before, array, after], axis=0)


def own_rows(h_own, rel_own, chunk):
    block_size = h_own.shape[2]
    panel = lax.all_gather(chunk, "layer", axis=0, tiled=True)
    wide = padded(panel, HB * block_size)
    blocks = wide.reshape(wide.shape[0] // block_size, block_size, chunk.shape[1])
    picked = blocks[rel_own]
    acc = jnp.einsum("rsij,rsjc->ric", h_own, picked, preferred_element_type=jnp.float32)
    return acc.reshape(chunk.shape[0], chunk.shape[1])


def shards(h_blocks, block_cols, t_now, t_prev):
    group_rows = h_blocks.shape[0]
    total_blocks = group_rows * lax.axis_size("grid")
    first_block = lax.axis_index("grid") * group_rows
    relative = (block_cols - first_block + HB + total_blocks) % total_blocks
    h_own = lax.all_to_all(h_blocks, "layer", 0, 1, tiled=True)
    rel_own = lax.all_to_all(relative, "layer", 0, 1, tiled=True)
    width = t_now.shape[1]
    step = width // NCH

    def recur(current, previous):
        outs = []
        for c in range(NCH):
            acc = own_rows(h_own, rel_own, current[c])
            outs.append((2.0 * acc - previous[c].astype(jnp.float32)).astype(jnp.bfloat16))
        return outs

    now_chunks = [t_now[:, c * step:(c + 1) * step] for c in range(NCH)]
    prev_chunks = [t_prev[:, c * step:(c + 1) * step] for c in range(NCH)]
    next_chunks = recur(now_chunks, prev_chunks)
    after_chunks = recur(next_chunks, now_chunks)
    return (jnp.concatenate(next_chunks, axis=1), jnp.concatenate(after_chunks, axis=1))


def solution(mesh):
    in_specs = (
        P("grid", "layer", None, None),
        P("grid", "layer"),
        P(("grid", "layer"), None),
        P(("grid", "layer"), None),
    )
    out_specs = (P(("grid", "layer"), None), P(("grid", "layer"), None))
    return jax.shard_map(shards, mesh=mesh, in_specs=in_specs, out_specs=out_specs, check_vma=False)
```

time: 627 us -> 542 us (0.86)
  waiting for transfers between devices: 492 us -> 298 us
  local copies, waits for them, and re-layouts: 35.2 us -> 70.3 us
  starting transfers between devices: 10.4 us -> 42.9 us
  other arithmetic: 46.2 us -> 61.2 us
  blocking collectives: 0 us -> 10.5 us
  matrix products: 28.9 us -> 37.7 us
    reduce_scatter x2 -> x0, waiting for transfers between devices: 231 us -> none  [recur(): lax.psum_scatter(flat.astype(jnp.bfloat16), 'layer', scatter_dimension=0,...]
    all_to_all x0 -> x1, waiting for transfers between devices: none -> 48.1 us  [shards(): h_own = lax.all_to_all(h_blocks, 'layer', 0, 1, tiled=True)]
    ppermute x4 -> x16, starting transfers between devices: 10.2 us -> 39 us  [the longest x8 38.8 us: padded(): after = lax.ppermute(array[:width], 'grid', down)]
    concatenate x2 -> x10, other arithmetic: 34.6 us -> 58.2 us  [the longest x8 53.4 us: padded(): return jnp.concatenate([before, array, after], axis=0)]
    ppermute x4 -> x16, waiting for transfers between devices: 18.7 us -> 0.04 us  [the longest x8 0.02 us: padded(): after = lax.ppermute(array[:width], 'grid', down)]
    gather x2 -> x8, local copies, waits for them, and re-layouts: 31 us -> 48.5 us  [own_rows(): picked = blocks[rel_own]]
    slice x2 -> x9, local copies, waits for them, and re-layouts: 4.08 us -> 16.6 us  [the longest x8 13 us: padded(): before = lax.ppermute(array[length - width:], 'grid', up)]
    all_to_all x0 -> x1, blocking collectives: none -> 10.5 us  [shards(): rel_own = lax.all_to_all(relative, 'layer', 0, 1, tiled=True)]
  transfers between devices with their start and end apart: 8 -> 25, of which waited for: 6 -> 8; matrix products, arithmetic and copies ran while one was open for 0% -> 23% of each run, Pallas kernels for 0% -> 0%
where the time goes in v1:
time: 542 us; the launch traced here: 536 us
  waiting for transfers between devices  298 us (55%)
  local copies, waits for them, and re-layouts  70.3 us (13%)
  other arithmetic  61.2 us (11%)
  starting transfers between devices  42.9 us (8%)
  matrix products  37.7 us (7%)
  between operations  14.6 us (3%)
  blocking collectives  10.5 us (2%)
    all_gather x8, waiting for transfers between devices, own_rows(): panel = lax.all_gather(chunk, 'layer', axis=0, tiled=True)  246 us
    concatenate x8, other arithmetic, padded(): return jnp.concatenate([before, array, after], axis=0)  53.4 us
    gather x8, local copies, waits for them, and re-layouts, own_rows(): picked = blocks[rel_own]  48.5 us
    all_to_all x1, waiting for transfers between devices, shards(): h_own = lax.all_to_all(h_blocks, 'layer', 0, 1, tiled=True)  48.1 us
    ppermute x8, starting transfers between devices, padded(): after = lax.ppermute(array[:width], 'grid', down)  38.8 us
    dot_general x8, matrix products, own_rows(): jnp.einsum('rsij,rsjc->ric', h_own, picked, preferred_element_type=jnp.fl...  37.7 us
    slice x8, local copies, waits for them, and re-layouts, padded(): before = lax.ppermute(array[length - width:], 'grid', up)  13 us
  transfers between devices with their start and end apart: 25, of which 8 were waited for; matrix products, arithmetic and copies ran while one was open for 23% of the time, Pallas kernels for 0%

profile of v1, /device:TPU:0, one launch (start us, length us, event | category | flops | bytes accessed | tf_op | source)
XLA Modules:
  0.0 535.6 jit_solution(12677658248927611347)
XLA Ops:
  13.1 10.5 %all_to_all.37 = s32[4,8,2]{1,2,0:T(2,128)S(1)} all-to-all(s32[4,8,2]{1,2,0:T(2,128)S(1)} %copy.9), channel_id=1, replica_groups=mesh['grid'=32,'layer'=4] {'layer'}, dimensions={0} | all-to-all | bytes 512 | tf_op jit(solution)/shard_map/all_to_all | solution.py:36
  27.4 48.1 %all-to-all-done.1 = bf16[32,2,128,128]{3,2,1,0:T(8,128)(2,1)S(1)} async-done(((bf16[32,2,128,128]{3,2,1,0:T(8,128)(2,1)}), bf16[32,2,128,128]{3,2,1,0:T(8,128)(2,1)S(1)}, u32[]{:S(2)}, u32[]{:S(2)}) %all-to-all-start.1) | async-done | bytes 2097184 | tf_op jit(solution)/shard_map/all_to_all | solution.py:35
  84.8 32.1 %all-gather.13.cloned.1.call-done = bf16[4096,384]{1,0:T(8,128)(2,1)} async-done(((bf16[1024,384]{1,0:T(8,128)(2,1)}), bf16[4096,384]{1,0:T(8,128)(2,1)}) %all-gather.13.cloned.1.call-update) | async-done | bytes 3145744 | tf_op jit(solution)/shard_map/all_gather | solution.py:22
  118.8 5.1 collective-permute-start.5
  123.8 34.6 %all-gather.11.cloned.1.call-done = bf16[4096,384]{1,0:T(8,128)(2,1)} async-done(((bf16[1024,384]{1,0:T(8,128)(2,1)}), bf16[4096,384]{1,0:T(8,128)(2,1)}) %all-gather.11.cloned.1.call-update) | async-done | bytes 3145744 | tf_op jit(solution)/shard_map/all_gather | solution.py:22
  160.2 40.0 %all-gather.9.cloned.1.call-done = bf16[4096,384]{1,0:T(8,128)(2,1)} async-done(((bf16[1024,384]{1,0:T(8,128)(2,1)}), bf16[4096,384]{1,0:T(8,128)(2,1)}) %all-gather.9.cloned.1.call-update) | async-done | bytes 3145744 | tf_op jit(solution)/shard_map/all_gather | solution.py:22
  206.2 7.1 %pad_maximum_fusion.3 = bf16[4608,384]{1,0:T(8,128)(2,1)} fusion(bf16[256,384]{1,0:T(8,128)(2,1)S(1)} %collective-permute-done.7, bf16[4096,384]{1,0:T(8,128)(2,1)} %all-gather.15.cloned.1.call-done, bf16[256,384]{1,0:T(8,128)(2,1)S(1)} %collective-permute-done.6), kind=kLoop, calls=%fused_computation.11 | loop fusion | flops 10616832 | bytes 7077888 | tf_op jit(solution)/shard_map/concatenate | solution.py:17
  213.3 6.1 %gather_fusion.3 = bf16[64,128,384]{2,1,0:T(8,128)(2,1)} fusion(bf16[36,128,384]{2,1,0:T(8,128)(2,1)} %bitcast.132, s32[1024]{0:T(1024)S(1)} %pad_clamp_fusion), kind=kCustom, calls=%fused_computation.3 | custom fusion | bytes 12583168 | tf_op jit(solution)/shard_map/gather | solution.py:25
  219.4 5.2 collective-permute-start.1
  224.6 7.0 %pad_maximum_fusion.2 = bf16[4608,384]{1,0:T(8,128)(2,1)} fusion(bf16[256,384]{1,0:T(8,128)(2,1)S(1)} %collective-permute-done.5, bf16[4096,384]{1,0:T(8,128)(2,1)} %all-gather.13.cloned.1.call-done, bf16[256,384]{1,0:T(8,128)(2,1)S(1)} %collective-permute-done.4), kind=kLoop, calls=%fused_computation.10 | loop fusion | flops 10616832 | bytes 7077888 | tf_op jit(solution)/shard_map/concatenate | solution.py:17
  231.7 6.1 %gather_fusion.2 = bf16[64,128,384]{2,1,0:T(8,128)(2,1)} fusion(bf16[36,128,384]{2,1,0:T(8,128)(2,1)} %bitcast.133, s32[1024]{0:T(1024)S(1)} %pad_clamp_fusion), kind=kCustom, calls=%fused_computation.2 | custom fusion | bytes 12583168 | tf_op jit(solution)/shard_map/gather | solution.py:25
  237.8 5.3 bitcast_multiply_fusion.4
  245.6 6.3 %pad_maximum_fusion.1 = bf16[4608,384]{1,0:T(8,128)(2,1)} fusion(bf16[256,384]{1,0:T(8,128)(2,1)S(1)} %collective-permute-done.3, bf16[4096,384]{1,0:T(8,128)(2,1)S(1)} %copy-done.11, bf16[256,384]{1,0:T(8,128)(2,1)S(1)} %collective-permute-done.2), kind=kLoop, calls=%fused_computation.9 | loop fusion | flops 10616832 | bytes 7077888 | tf_op jit(solution)/shard_map/concatenate | solution.py:17
  251.9 6.1 %gather_fusion.1 = bf16[64,128,384]{2,1,0:T(8,128)(2,1)} fusion(bf16[36,128,384]{2,1,0:T(8,128)(2,1)} %bitcast.134, s32[1024]{0:T(1024)S(1)} %pad_clamp_fusion), kind=kCustom, calls=%fused_computation.1 | custom fusion | bytes 12583168 | tf_op jit(solution)/shard_map/gather | solution.py:25
  258.0 5.3 bitcast_multiply_fusion.6
  263.3 6.7 %pad_maximum_fusion = bf16[4608,384]{1,0:T(8,128)(2,1)} fusion(bf16[256,384]{1,0:T(8,128)(2,1)S(1)} %collective-permute-done.1, bf16[4096,384]{1,0:T(8,128)(2,1)S(1)} %copy-done.10, bf16[256,384]{1,0:T(8,128)(2,1)S(1)} %collective-permute-done), kind=kLoop, calls=%fused_computation.8 | loop fusion | flops 10616832 | bytes 7077888 | tf_op jit(solution)/shard_map/concatenate | solution.py:17
  270.0 6.1 %gather_fusion = bf16[64,128,384]{2,1,0:T(8,128)(2,1)} fusion(bf16[36,128,384]{2,1,0:T(8,128)(2,1)} %bitcast.135, s32[1024]{0:T(1024)S(1)} %pad_clamp_fusion), kind=kCustom, calls=%fused_computation | custom fusion | bytes 12583168 | tf_op jit(solution)/shard_map/gather | solution.py:25
  288.5 29.9 %all-gather.23.cloned.1.call-done = bf16[4096,384]{1,0:T(8,128)(2,1)} async-done(((bf16[1024,384]{1,0:T(8,128)(2,1)}), bf16[4096,384]{1,0:T(8,128)(2,1)}) %all-gather.23.cloned.1.call-update) | async-done | bytes 3145744 | tf_op jit(solution)/shard_map/all_gather | solution.py:22
  324.6 35.1 %all-gather.21.cloned.1.call-done = bf16[4096,384]{1,0:T(8,128)(2,1)} async-done(((bf16[1024,384]{1,0:T(8,128)(2,1)}), bf16[4096,384]{1,0:T(8,128)(2,1)}) %all-gather.21.cloned.1.call-update) | async-done | bytes 3145744 | tf_op jit(solution)/shard_map/all_gather | solution.py:22
  366.6 34.6 %all-gather.19.cloned.1.call-done = bf16[4096,384]{1,0:T(8,128)(2,1)} async-done(((bf16[1024,384]{1,0:T(8,128)(2,1)}), bf16[4096,384]{1,0:T(8,128)(2,1)}) %all-gather.19.cloned.1.call-update) | async-done | bytes 3145744 | tf_op jit(solution)/shard_map/all_gather | solution.py:22
  403.0 40.2 %all-gather.17.cloned.1.call-done = bf16[4096,384]{1,0:T(8,128)(2,1)} async-done(((bf16[1024,384]{1,0:T(8,128)(2,1)}), bf16[4096,384]{1,0:T(8,128)(2,1)}) %all-gather.17.cloned.1.call-update) | async-done | bytes 3145744 | tf_op jit(solution)/shard_map/all_gather | solution.py:22
  449.1 7.1 %pad_maximum_fusion.7 = bf16[4608,384]{1,0:T(8,128)(2,1)} fusion(bf16[256,384]{1,0:T(8,128)(2,1)S(1)} %collective-permute-done.15, bf16[4096,384]{1,0:T(8,128)(2,1)} %all-gather.23.cloned.1.call-done, bf16[256,384]{1,0:T(8,128)(2,1)S(1)} %collective-permute-done.14), kind=kLoop, calls=%fused_computation.15 | loop fusion | flops 10616832 | bytes 7077888 | tf_op jit(solution)/shard_map/concatenate | solution.py:17
  456.2 6.1 %gather_fusion.7 = bf16[64,128,384]{2,1,0:T(8,128)(2,1)} fusion(bf16[36,128,384]{2,1,0:T(8,128)(2,1)} %bitcast.136, s32[1024]{0:T(1024)S(1)} %pad_clamp_fusion), kind=kCustom, calls=%fused_computation.7 | custom fusion | bytes 12583168 | tf_op jit(solution)/shard_map/gather | solution.py:25
  462.2 5.4 %bitcast_multiply_fusion = f32[8,384,128]{1,2,0:T(8,128)} fusion(bf16[8,8,128,128]{3,2,1,0:T(8,128)(2,1)S(1)} %bitcast.119, bf16[8,8,128,384]{3,2,1,0:T(8,128)(2,1)} %bitcast.128), kind=kOutput, calls=%fused_computation.34 | convolution fusion | flops 805699584 | bytes 9961472 | tf_op jit(solution)/shard_map/rsij,rsjc->ric/dot_general | solution.py:26
  472.7 6.4 %pad_maximum_fusion.6 = bf16[4608,384]{1,0:T(8,128)(2,1)} fusion(bf16[256,384]{1,0:T(8,128)(2,1)S(1)} %collective-permute-done.13, bf16[4096,384]{1,0:T(8,128)(2,1)S(1)} %copy-done.14, bf16[256,384]{1,0:T(8,128)(2,1)S(1)} %collective-permute-done.12), kind=kLoop, calls=%fused_computation.14 | loop fusion | flops 10616832 | bytes 7077888 | tf_op jit(solution)/shard_map/concatenate | solution.py:17
  479.1 6.1 %gather_fusion.6 = bf16[64,128,384]{2,1,0:T(8,128)(2,1)} fusion(bf16[36,128,384]{2,1,0:T(8,128)(2,1)} %bitcast.137, s32[1024]{0:T(1024)S(1)} %pad_clamp_fusion), kind=kCustom, calls=%fused_computation.6 | custom fusion | bytes 12583168 | tf_op jit(solution)/shard_map/gather | solution.py:25
  485.2 5.4 %bitcast_multiply_fusion.1 = f32[8,384,128]{1,2,0:T(8,128)} fusion(bf16[8,8,128,128]{3,2,1,0:T(8,128)(2,1)S(1)} %bitcast.120, bf16[8,8,128,384]{3,2,1,0:T(8,128)(2,1)} %bitcast.129), kind=kOutput, calls=%fused_computation.35 | convolution fusion | flops 805699584 | bytes 9961472 | tf_op jit(solution)/shard_map/rsij,rsjc->ric/dot_general | solution.py:26
  490.6 6.3 %pad_maximum_fusion.5 = bf16[4608,384]{1,0:T(8,128)(2,1)} fusion(bf16[256,384]{1,0:T(8,128)(2,1)S(1)} %collective-permute-done.11, bf16[4096,384]{1,0:T(8,128)(2,1)S(1)} %copy-done.13, bf16[256,384]{1,0:T(8,128)(2,1)S(1)} %collective-permute-done.10), kind=kLoop, calls=%fused_computation.13 | loop fusion | flops 10616832 | bytes 7077888 | tf_op jit(solution)/shard_map/concatenate | solution.py:17
  496.9 6.1 %gather_fusion.5 = bf16[64,128,384]{2,1,0:T(8,128)(2,1)} fusion(bf16[36,128,384]{2,1,0:T(8,128)(2,1)} %bitcast.138, s32[1024]{0:T(1024)S(1)} %pad_clamp_fusion), kind=kCustom, calls=%fused_computation.5 | custom fusion | bytes 12583168 | tf_op jit(solution)/shard_map/gather | solution.py:25
  502.9 5.3 bitcast_multiply_fusion.2
  508.3 6.5 %pad_maximum_fusion.4 = bf16[4608,384]{1,0:T(8,128)(2,1)} fusion(bf16[256,384]{1,0:T(8,128)(2,1)S(1)} %collective-permute-done.9, bf16[4096,384]{1,0:T(8,128)(2,1)S(1)} %copy-done.12, bf16[256,384]{1,0:T(8,128)(2,1)S(1)} %collective-permute-done.8), kind=kLoop, calls=%fused_computation.12 | loop fusion | flops 10616832 | bytes 7077888 | tf_op jit(solution)/shard_map/concatenate | solution.py:17
  514.8 6.1 %gather_fusion.4 = bf16[64,128,384]{2,1,0:T(8,128)(2,1)} fusion(bf16[36,128,384]{2,1,0:T(8,128)(2,1)} %bitcast.131, s32[1024]{0:T(1024)S(1)} %pad_clamp_fusion), kind=kCustom, calls=%fused_computation.4 | custom fusion | bytes 12583168 | tf_op jit(solution)/shard_map/gather | solution.py:25
  (110 shorter events, 76.9 us)
Async XLA Ops:
  7.2 5.8 %copy-start.18 = (s32[32,2]{0,1:T(2,128)S(1)}, s32[32,2]{0,1:T(2,128)}, u32[]{:S(2)}) copy-start(s32[32,2]{0,1:T(2,128)} %param.5) | copy-start | bytes 772
  7.2 71.4 %all-gather.15.cloned.1.call-start = ((), (), s32[]{:S(2)}) async-start(), calls=%async_computation.5 | async-start | bytes 3932160 | tf_op jit(solution)/shard_map/all_gather | solution.py:22
  10.9 106.1 %all-gather.13.cloned.1.call-start = ((), (), s32[]{:S(2)}) async-start(), calls=%async_computation.4 | async-start | bytes 3932160 | tf_op jit(solution)/shard_map/all_gather | solution.py:22
  11.6 146.8 %all-gather.11.cloned.1.call-start = ((), (), s32[]{:S(2)}) async-start(), calls=%async_computation.3 | async-start | bytes 3932160 | tf_op jit(solution)/shard_map/all_gather | solution.py:22
  12.4 187.9 %all-gather.9.cloned.1.call-start = ((), (), s32[]{:S(2)}) async-start(), calls=%async_computation.2 | async-start | bytes 3932160 | tf_op jit(solution)/shard_map/all_gather | solution.py:22
  23.6 52.0 %all-to-all-start.1 = ((bf16[32,2,128,128]{3,2,1,0:T(8,128)(2,1)}), bf16[32,2,128,128]{3,2,1,0:T(8,128)(2,1)S(1)}, u32[]{:S(2)}, u32[]{:S(2)}) async-start(bf16[32,2,128,128]{3,2,1,0:T(8,128)(2,1)} %param.4), calls=%async_computation.1 | async-start | bytes 4194304 | tf_op jit(solution)/shard_map/all_to_all | solution.py:35
  27.2 291.3 %all-gather.23.cloned.1.call-start = ((), (), s32[]{:S(2)}) async-start(), calls=%async_computation.9 | async-start | bytes 3932160 | tf_op jit(solution)/shard_map/all_gather | solution.py:22
  79.7 122.4 %collective-permute-start.6 = (bf16[256,384]{1,0:T(8,128)(2,1)S(1)}, bf16[256,384]{1,0:T(8,128)(2,1)S(1)}, u32[]{:S(2)}, u32[]{:S(2)}) collective-permute-start(bf16[256,384]{1,0:T(8,128)(2,1)S(1)} %get-tuple-element.28), channel_id=1, source_target_pairs={{0,4},{4,8},{8,12},{12,16},{16,20},{20,24},{24,28},{28,32},{32,36}... | collective-permute-start | bytes 589832 | tf_op jit(solution)/shard_map/ppermute | solution.py:15
  79.8 126.4 %collective-permute-start.7 = (bf16[256,384]{1,0:T(8,128)(2,1)S(1)}, bf16[256,384]{1,0:T(8,128)(2,1)S(1)}, u32[]{:S(2)}, u32[]{:S(2)}) collective-permute-start(bf16[256,384]{1,0:T(8,128)(2,1)S(1)} %get-tuple-element.29), channel_id=1, source_target_pairs={{4,0},{8,4},{12,8},{16,12},{20,16},{24,20},{28,24},{32,28},{36,32}... | collective-permute-start | bytes 589832 | tf_op jit(solution)/shard_map/ppermute | solution.py:16
  118.8 100.6 %collective-permute-start.4 = (bf16[256,384]{1,0:T(8,128)(2,1)}, bf16[256,384]{1,0:T(8,128)(2,1)S(1)}, u32[]{:S(2)}, u32[]{:S(2)}) collective-permute-start(bf16[256,384]{1,0:T(8,128)(2,1)} %get-tuple-element.26), channel_id=1, source_target_pairs={{0,4},{4,8},{8,12},{12,16},{16,20},{20,24},{24,28},{28,32},{32,36}... | collective-permute-start | bytes 589832 | tf_op jit(solution)/shard_map/ppermute | solution.py:15
  118.8 105.9 %collective-permute-start.5 = (bf16[256,384]{1,0:T(8,128)(2,1)}, bf16[256,384]{1,0:T(8,128)(2,1)S(1)}, u32[]{:S(2)}, u32[]{:S(2)}) collective-permute-start(bf16[256,384]{1,0:T(8,128)(2,1)} %get-tuple-element.27), channel_id=1, source_target_pairs={{4,0},{8,4},{12,8},{16,12},{20,16},{24,20},{28,24},{32,28},{36,32}... | collective-permute-start | bytes 589832 | tf_op jit(solution)/shard_map/ppermute | solution.py:16
  160.2 85.4 %collective-permute-start.2 = (bf16[256,384]{1,0:T(8,128)(2,1)}, bf16[256,384]{1,0:T(8,128)(2,1)S(1)}, u32[]{:S(2)}, u32[]{:S(2)}) collective-permute-start(bf16[256,384]{1,0:T(8,128)(2,1)} %get-tuple-element.24), channel_id=1, source_target_pairs={{0,4},{4,8},{8,12},{12,16},{16,20},{20,24},{24,28},{28,32},{32,36}... | collective-permute-start | bytes 589832 | tf_op jit(solution)/shard_map/ppermute | solution.py:15
  202.1 43.6 %collective-permute-start.3 = (bf16[256,384]{1,0:T(8,128)(2,1)}, bf16[256,384]{1,0:T(8,128)(2,1)S(1)}, u32[]{:S(2)}, u32[]{:S(2)}) collective-permute-start(bf16[256,384]{1,0:T(8,128)(2,1)} %get-tuple-element.25), channel_id=1, source_target_pairs={{4,0},{8,4},{12,8},{16,12},{20,16},{24,20},{28,24},{32,28},{36,32}... | collective-permute-start | bytes 589832 | tf_op jit(solution)/shard_map/ppermute | solution.py:16
  206.2 57.1 %collective-permute-start = (bf16[256,384]{1,0:T(8,128)(2,1)}, bf16[256,384]{1,0:T(8,128)(2,1)S(1)}, u32[]{:S(2)}, u32[]{:S(2)}) collective-permute-start(bf16[256,384]{1,0:T(8,128)(2,1)} %get-tuple-element.18), channel_id=1, source_target_pairs={{0,4},{4,8},{8,12},{12,16},{16,20},{20,24},{24,28},{28,32},{32,36}... | collective-permute-start | bytes 589832 | tf_op jit(solution)/shard_map/ppermute | solution.py:15
  213.3 6.1 %copy-start.16 = (bf16[256,384]{1,0:T(8,128)(2,1)S(1)}, bf16[256,384]{1,0:T(8,128)(2,1)}, u32[]{:S(2)}) copy-start(bf16[256,384]{1,0:T(8,128)(2,1)} %get-tuple-element.19) | copy-start | bytes 589828
  219.4 43.9 %collective-permute-start.1 = (bf16[256,384]{1,0:T(8,128)(2,1)S(1)}, bf16[256,384]{1,0:T(8,128)(2,1)S(1)}, u32[]{:S(2)}, u32[]{:S(2)}) collective-permute-start(bf16[256,384]{1,0:T(8,128)(2,1)S(1)} %copy-done.16), channel_id=1, source_target_pairs={{4,0},{8,4},{12,8},{16,12},{20,16},{24,20},{28,24},{32,28},{36,32}... | collective-permute-start | bytes 589832 | tf_op jit(solution)/shard_map/ppermute | solution.py:16
  258.0 5.4 copy-start.10
  283.4 76.3 %all-gather.21.cloned.1.call-start = ((), (), s32[]{:S(2)}) async-start(), calls=%async_computation.8 | async-start | bytes 3932160 | tf_op jit(solution)/shard_map/all_gather | solution.py:22
  284.0 117.2 %all-gather.19.cloned.1.call-start = ((), (), s32[]{:S(2)}) async-start(), calls=%async_computation.7 | async-start | bytes 3932160 | tf_op jit(solution)/shard_map/all_gather | solution.py:22
  284.7 158.4 %all-gather.17.cloned.1.call-start = ((), (), s32[]{:S(2)}) async-start(), calls=%async_computation.6 | async-start | bytes 3932160 | tf_op jit(solution)/shard_map/all_gather | solution.py:22
  319.5 125.5 %collective-permute-start.14 = (bf16[256,384]{1,0:T(8,128)(2,1)S(1)}, bf16[256,384]{1,0:T(8,128)(2,1)S(1)}, u32[]{:S(2)}, u32[]{:S(2)}) collective-permute-start(bf16[256,384]{1,0:T(8,128)(2,1)S(1)} %get-tuple-element.12), channel_id=1, source_target_pairs={{0,4},{4,8},{8,12},{12,16},{16,20},{20,24},{24,28},{28,32},{32,36}... | collective-permute-start | bytes 589832 | tf_op jit(solution)/shard_map/ppermute | solution.py:15
  319.6 129.5 %collective-permute-start.15 = (bf16[256,384]{1,0:T(8,128)(2,1)S(1)}, bf16[256,384]{1,0:T(8,128)(2,1)S(1)}, u32[]{:S(2)}, u32[]{:S(2)}) collective-permute-start(bf16[256,384]{1,0:T(8,128)(2,1)S(1)} %get-tuple-element.13), channel_id=1, source_target_pairs={{4,0},{8,4},{12,8},{16,12},{20,16},{24,20},{28,24},{32,28},{36,32}... | collective-permute-start | bytes 589832 | tf_op jit(solution)/shard_map/ppermute | solution.py:16
  361.5 106.1 %collective-permute-start.12 = (bf16[256,384]{1,0:T(8,128)(2,1)}, bf16[256,384]{1,0:T(8,128)(2,1)S(1)}, u32[]{:S(2)}, u32[]{:S(2)}) collective-permute-start(bf16[256,384]{1,0:T(8,128)(2,1)} %get-tuple-element.10), channel_id=1, source_target_pairs={{0,4},{4,8},{8,12},{12,16},{16,20},{20,24},{24,28},{28,32},{32,36}... | collective-permute-start | bytes 589832 | tf_op jit(solution)/shard_map/ppermute | solution.py:15
  361.5 111.1 %collective-permute-start.13 = (bf16[256,384]{1,0:T(8,128)(2,1)}, bf16[256,384]{1,0:T(8,128)(2,1)S(1)}, u32[]{:S(2)}, u32[]{:S(2)}) collective-permute-start(bf16[256,384]{1,0:T(8,128)(2,1)} %get-tuple-element.11), channel_id=1, source_target_pairs={{4,0},{8,4},{12,8},{16,12},{20,16},{24,20},{28,24},{32,28},{36,32}... | collective-permute-start | bytes 589832 | tf_op jit(solution)/shard_map/ppermute | solution.py:16
  403.0 87.6 %collective-permute-start.10 = (bf16[256,384]{1,0:T(8,128)(2,1)}, bf16[256,384]{1,0:T(8,128)(2,1)S(1)}, u32[]{:S(2)}, u32[]{:S(2)}) collective-permute-start(bf16[256,384]{1,0:T(8,128)(2,1)} %get-tuple-element.8), channel_id=1, source_target_pairs={{0,4},{4,8},{8,12},{12,16},{16,20},{20,24},{24,28},{28,32},{32,36}... | collective-permute-start | bytes 589832 | tf_op jit(solution)/shard_map/ppermute | solution.py:15
  445.0 45.6 %collective-permute-start.11 = (bf16[256,384]{1,0:T(8,128)(2,1)}, bf16[256,384]{1,0:T(8,128)(2,1)S(1)}, u32[]{:S(2)}, u32[]{:S(2)}) collective-permute-start(bf16[256,384]{1,0:T(8,128)(2,1)} %get-tuple-element.9), channel_id=1, source_target_pairs={{4,0},{8,4},{12,8},{16,12},{20,16},{24,20},{28,24},{32,28},{36,32}... | collective-permute-start | bytes 589832 | tf_op jit(solution)/shard_map/ppermute | solution.py:16
  449.1 59.2 %collective-permute-start.8 = (bf16[256,384]{1,0:T(8,128)(2,1)}, bf16[256,384]{1,0:T(8,128)(2,1)S(1)}, u32[]{:S(2)}, u32[]{:S(2)}) collective-permute-start(bf16[256,384]{1,0:T(8,128)(2,1)} %get-tuple-element.6), channel_id=1, source_target_pairs={{0,4},{4,8},{8,12},{12,16},{16,20},{20,24},{24,28},{28,32},{32,36}... | collective-permute-start | bytes 589832 | tf_op jit(solution)/shard_map/ppermute | solution.py:15
  462.2 5.4 %copy-start.17 = (bf16[256,384]{1,0:T(8,128)(2,1)S(1)}, bf16[256,384]{1,0:T(8,128)(2,1)}, u32[]{:S(2)}) copy-start(bf16[256,384]{1,0:T(8,128)(2,1)} %get-tuple-element.7) | copy-start | bytes 589828
  462.2 10.4 %copy-start.14 = (bf16[4096,384]{1,0:T(8,128)(2,1)S(1)}, bf16[4096,384]{1,0:T(8,128)(2,1)}, u32[]{:S(2)}) copy-start(bf16[4096,384]{1,0:T(8,128)(2,1)} %all-gather.21.cloned.1.call-done) | copy-start | bytes 9437188
  467.6 40.7 %collective-permute-start.9 = (bf16[256,384]{1,0:T(8,128)(2,1)S(1)}, bf16[256,384]{1,0:T(8,128)(2,1)S(1)}, u32[]{:S(2)}, u32[]{:S(2)}) collective-permute-start(bf16[256,384]{1,0:T(8,128)(2,1)S(1)} %copy-done.17), channel_id=1, source_target_pairs={{4,0},{8,4},{12,8},{16,12},{20,16},{24,20},{28,24},{32,28},{36,32}... | collective-permute-start | bytes 589832 | tf_op jit(solution)/shard_map/ppermute | solution.py:16
  485.2 5.4 %copy-start.13 = (bf16[4096,384]{1,0:T(8,128)(2,1)S(1)}, bf16[4096,384]{1,0:T(8,128)(2,1)}, u32[]{:S(2)}) copy-start(bf16[4096,384]{1,0:T(8,128)(2,1)} %all-gather.19.cloned.1.call-done) | copy-start | bytes 9437188
  502.9 5.4 copy-start.12
  (12 other events, 47.2 us)
Sparse Core Ops, SparseCore 0:
  11.0 64.1 all-gather.14
  76.8 40.1 all-gather.12
  118.6 39.7 all-gather.10
  160.5 39.7 all-gather.8
  283.5 34.8 all-gather.22
  320.0 39.7 all-gather.20
  361.4 39.7 all-gather.18
  403.4 39.7 all-gather.16

commit v2 on v1

v2 whole, which is shorter than its diff:
```python
import jax
import jax.numpy as jnp
from jax import lax
from jax.sharding import PartitionSpec as P

KB = 8
HB = 2
NCH = 2


def shift(size, k):
    return [(i, (i + k) % size) for i in range(size)]


def exchange(own, lidx, block_size):
    nl = lax.axis_size("layer")
    ng = lax.axis_size("grid")
    half = own.shape[0] // 2
    from_prev = lax.ppermute(own, "layer", shift(nl, 1))
    from_next = lax.ppermute(own, "layer", shift(nl, nl - 1))
    far_a = lax.ppermute(from_prev[:half], "layer", shift(nl, 1))
    far_b = lax.ppermute(from_next[half:], "layer", shift(nl, nl - 1))
    panel = jnp.concatenate([own, from_next, far_a, far_b, from_prev], axis=0)
    rows = own.shape[0]
    width = HB * block_size
    last_at = ((nl - 1 - lidx) % nl) * rows + rows - width
    first_at = ((0 - lidx) % nl) * rows
    last = lax.dynamic_slice_in_dim(panel, last_at, width, axis=0)
    first = lax.dynamic_slice_in_dim(panel, first_at, width, axis=0)
    lo = lax.ppermute(last, "grid", shift(ng, 1))
    hi = lax.ppermute(first, "grid", shift(ng, ng - 1))
    return jnp.concatenate([panel, lo, hi], axis=0)


def own_rows(h_own, pos_own, chunk, lidx):
    block_size = h_own.shape[2]
    wide = exchange(chunk, lidx, block_size)
    blocks = wide.reshape(wide.shape[0] // block_size, block_size, chunk.shape[1])
    picked = blocks[pos_own]
    acc = jnp.einsum("rsij,rsjc->ric", h_own, picked, preferred_element_type=jnp.float32)
    return acc.reshape(chunk.shape[0], chunk.shape[1])


def shards(h_blocks, block_cols, t_now, t_prev):
    group_rows, block_size = h_blocks.shape[0], h_blocks.shape[2]
    nl = lax.axis_size("layer")
    total_blocks = group_rows * lax.axis_size("grid")
    per_dev = group_rows // nl
    lidx = lax.axis_index("layer")
    first_block = lax.axis_index("grid") * group_rows
    rel = (block_cols - first_block + HB + total_blocks) % total_blocks

    h_split = h_blocks.reshape(nl, per_dev, *h_blocks.shape[1:])
    p_split = rel.reshape(nl, per_dev, rel.shape[1])
    h_parts = [lax.dynamic_index_in_dim(h_split, lidx, 0, keepdims=False)]
    p_parts = [lax.dynamic_index_in_dim(p_split, lidx, 0, keepdims=False)]
    for k in range(1, nl):
        dest = (lidx + k) % nl
        h_parts.append(lax.ppermute(lax.dynamic_index_in_dim(h_split, dest, 0, keepdims=False), "layer", shift(nl, k)))
        p_parts.append(lax.ppermute(lax.dynamic_index_in_dim(p_split, dest, 0, keepdims=False), "layer", shift(nl, k)))
    h_own = jnp.concatenate(h_parts, axis=1)
    rel_own = jnp.concatenate(p_parts, axis=1)
    inner = rel_own - HB
    owner = inner // per_dev
    pos_own = ((owner - lidx) % nl) * per_dev + inner % per_dev
    pos_own = jnp.where(rel_own < HB, nl * per_dev + rel_own, pos_own)
    pos_own = jnp.where(rel_own >= HB + group_rows, rel_own, pos_own)

    width = t_now.shape[1]
    step = width // NCH

    def recur(current, previous):
        outs = []
        for c in range(NCH):
            acc = own_rows(h_own, pos_own, current[c], lidx)
            outs.append((2.0 * acc - previous[c].astype(jnp.float32)).astype(jnp.bfloat16))
        return outs

    now_chunks = [t_now[:, c * step:(c + 1) * step] for c in range(NCH)]
    prev_chunks = [t_prev[:, c * step:(c + 1) * step] for c in range(NCH)]
    next_chunks = recur(now_chunks, prev_chunks)
    after_chunks = recur(next_chunks, now_chunks)
    return (jnp.concatenate(next_chunks, axis=1), jnp.concatenate(after_chunks, axis=1))


def solution(mesh):
    in_specs = (
        P("grid", "layer", None, None),
        P("grid", "layer"),
        P(("grid", "layer"), None),
        P(("grid", "layer"), None),
    )
    out_specs = (P(("grid", "layer"), None), P(("grid", "layer"), None))
    return jax.shard_map(shards, mesh=mesh, in_specs=in_specs, out_specs=out_specs, check_vma=False)
```

time: 542 us -> 317 us (0.58); the launches traced: 536 us -> 317 us
  waiting for transfers between devices: 298 us -> 143 us
  other arithmetic: 61.2 us -> 5.23 us
  local copies, waits for them, and re-layouts: 70.3 us -> 90.9 us
  matrix products: 37.7 us -> 21.8 us
  between operations: 14.6 us -> 0.91 us
  starting transfers between devices: 42.9 us -> 54.7 us
  blocking collectives: 10.5 us -> 0 us
    all_gather x8 -> x0, waiting for transfers between devices: 246 us -> none  [own_rows(): panel = lax.all_gather(chunk, 'layer', axis=0, tiled=True)]
    ppermute x16 -> x30, waiting for transfers between devices: 0.04 us -> 143 us  [the longest x4 116 us: exchange(): from_prev = lax.ppermute(own, 'layer', shift(nl, 1))]
    concatenate x8 -> x0, other arithmetic: 53.4 us -> none  [padded(): return jnp.concatenate([before, array, after], axis=0)]
    all_to_all x1 -> x0, waiting for transfers between devices: 48.1 us -> none  [shards(): h_own = lax.all_to_all(h_blocks, 'layer', 0, 1, tiled=True)]
    unnamed x38 -> x36, local copies, waits for them, and re-layouts: 3.13 us -> 32.7 us
    dot_general x8 -> x4, matrix products: 37.7 us -> 21.8 us  [own_rows(): jnp.einsum('rsij,rsjc->ric', h_own, picked, preferred_element_type=jnp.fl...]
    ppermute x16 -> x30, starting transfers between devices: 39 us -> 54.7 us  [the longest x4 20 us: exchange(): hi = lax.ppermute(first, 'grid', shift(ng, ng - 1))]
    slice x9 -> x8, local copies, waits for them, and re-layouts: 16.6 us -> 4.53 us  [the longest x4 3.36 us: exchange(): far_b = lax.ppermute(from_next[half:], 'layer', shift(nl, nl - 1))]
  transfers between devices with their start and end apart: 25 -> 30, of which waited for: 8 -> 8; matrix products, arithmetic and copies ran while one was open for 23% -> 23% of each run, Pallas kernels for 0% -> 0%
where the time goes in v2:
time: 317 us
  waiting for transfers between devices  143 us (45%)
  local copies, waits for them, and re-layouts  90.9 us (29%)
  starting transfers between devices  54.7 us (17%)
  matrix products  21.8 us (7%)
  other arithmetic  5.23 us (2%)
    ppermute x4, waiting for transfers between devices, exchange(): from_prev = lax.ppermute(own, 'layer', shift(nl, 1))  116 us
    gather x4, local copies, waits for them, and re-layouts, own_rows(): picked = blocks[pos_own]  41 us
    unnamed x36, local copies, waits for them, and re-layouts  32.7 us
    ppermute x4, waiting for transfers between devices, exchange(): far_a = lax.ppermute(from_prev[:half], 'layer', shift(nl, 1))  27.3 us
    dot_general x4, matrix products, own_rows(): jnp.einsum('rsij,rsjc->ric', h_own, picked, preferred_element_type=jnp.fl...  21.8 us
    ppermute x4, starting transfers between devices, exchange(): hi = lax.ppermute(first, 'grid', shift(ng, ng - 1))  20 us
    ppermute x4, starting transfers between devices, exchange(): far_b = lax.ppermute(from_next[half:], 'layer', shift(nl, nl - 1))  13.3 us
    ppermute x4, starting transfers between devices, exchange(): from_next = lax.ppermute(own, 'layer', shift(nl, nl - 1))  10.8 us
  transfers between devices with their start and end apart: 30, of which 8 were waited for; matrix products, arithmetic and copies ran while one was open for 23% of the time, Pallas kernels for 0%

profile of v2, /device:TPU:0, one launch (start us, length us, event | category | flops | bytes accessed | tf_op | source)
XLA Modules:
  0.0 316.8 jit_solution(3050882811410994678)
XLA Ops:
  0.6 5.8 %constant_dynamic-update-slice_fusion.4 = (bf16[4096,768]{1,0:T(8,128)(2,1)}, bf16[4608,768]{1,0:T(8,128)(2,1)}, bf16[4096,768]{1,0:T(8,128)(2,1)}, bf16[4608,76...) fusion(bf16[1024,1536]{1,0:T(8,128)(2,1)} %param.6), kind=kLoop, calls=%fused_computation.27 | loop fusion | bytes 12582912
  10.6 3.2 %collective-permute-start.3 = (bf16[1024,768]{1,0:T(8,128)(2,1)}, bf16[1024,768]{1,0:T(8,128)(2,1)}, u32[]{:S(2)}, u32[]{:S(2)}) collective-permute-start(bf16[1024,768]{1,0:T(8,128)(2,1)} %get-tuple-element.19), channel_id=1, source_target_pairs={{0,3},{1,0},{2,1},{3,2},{4,7},{5,4},{6,5},{7,6},{8,11},{9,8},{10,9... | collective-permute-start | bytes 4718600 | tf_op jit(solution)/shard_map/ppermute | solution.py:20
  13.9 32.2 %collective-permute-done.13 = bf16[1024,768]{1,0:T(8,128)(2,1)S(1)} collective-permute-done((bf16[1024,768]{1,0:T(8,128)(2,1)}, bf16[1024,768]{1,0:T(8,128)(2,1)S(1)}, u32[]{:S(2)}, u32[]{:S(2)}) %collective-permute-start.13) | collective-permute-done | bytes 1572896 | tf_op jit(solution)/shard_map/ppermute | solution.py:19
  49.3 3.2 %collective-permute-start.15 = (bf16[512,768]{1,0:T(8,128)(2,1)}, bf16[512,768]{1,0:T(8,128)(2,1)}, u32[]{:S(2)}, u32[]{:S(2)}) collective-permute-start(bf16[512,768]{1,0:T(8,128)(2,1)} %slice.59), channel_id=1, source_target_pairs={{0,3},{1,0},{2,1},{3,2},{4,7},{5,4},{6,5},{7,6},{8,11},{9,8},{10,9... | collective-permute-start | bytes 2359304 | tf_op jit(solution)/shard_map/ppermute | solution.py:22
  53.2 3.1 dynamic-slice_bitcast_fusion.3
  56.3 23.5 %collective-permute-done.4 = bf16[1024,768]{1,0:T(8,128)(2,1)S(1)} collective-permute-done((bf16[1024,768]{1,0:T(8,128)(2,1)}, bf16[1024,768]{1,0:T(8,128)(2,1)S(1)}, u32[]{:S(2)}, u32[]{:S(2)}) %collective-permute-start.4) | collective-permute-done | bytes 1572896 | tf_op jit(solution)/shard_map/ppermute | solution.py:19
  81.1 3.3 %collective-permute-start.6 = (bf16[512,768]{1,0:T(8,128)(2,1)S(1)}, bf16[512,768]{1,0:T(8,128)(2,1)S(1)}, u32[]{:S(2)}, u32[]{:S(2)}) collective-permute-start(bf16[512,768]{1,0:T(8,128)(2,1)S(1)} %slice.57), channel_id=1, source_target_pairs={{0,3},{1,0},{2,1},{3,2},{4,7},{5,4},{6,5},{7,6},{8,11},{9,8},{10,9... | collective-permute-start | bytes 2359304 | tf_op jit(solution)/shard_map/ppermute | solution.py:22
  84.4 2.8 constant_dynamic-update-slice_fusion.15
  87.2 3.2 %constant_dynamic-update-slice_fusion.3 = (bf16[4096,768]{1,0:T(8,128)(2,1)}, bf16[4608,768]{1,0:T(8,128)(2,1)}) fusion(bf16[4096,768]{1,0:T(8,128)(2,1)} %get-tuple-element.14, bf16[1024,768]{1,0:T(8,128)(2,1)} %collective-permute-done.3, bf16[4608,768]{1,0:T(8,128)(2,1)} %get-tuple-element.15), kind=kLoop, calls=%fused_computation.26 | loop fusion | bytes 4718592
  90.4 6.3 %collective-permute-done.14 = bf16[512,768]{1,0:T(8,128)(2,1)} collective-permute-done((bf16[512,768]{1,0:T(8,128)(2,1)}, bf16[512,768]{1,0:T(8,128)(2,1)}, u32[]{:S(2)}, u32[]{:S(2)}) %collective-permute-start.14) | collective-permute-done | bytes 786464 | tf_op jit(solution)/shard_map/ppermute | solution.py:21
  105.2 7.5 %collective-permute-done.5 = bf16[512,768]{1,0:T(8,128)(2,1)S(1)} collective-permute-done((bf16[512,768]{1,0:T(8,128)(2,1)S(1)}, bf16[512,768]{1,0:T(8,128)(2,1)S(1)}, u32[]{:S(2)}, u32[]{:S(2)}) %collective-permute-start.5) | collective-permute-done | bytes 786464 | tf_op jit(solution)/shard_map/ppermute | solution.py:21
  113.7 5.1 %collective-permute-start.17 = (bf16[256,768]{1,0:T(8,128)(2,1)S(1)}, bf16[256,768]{1,0:T(8,128)(2,1)S(1)}, u32[]{:S(2)}, u32[]{:S(2)}) collective-permute-start(bf16[256,768]{1,0:T(8,128)(2,1)S(1)} %get-tuple-element.8), channel_id=1, source_target_pairs={{0,124},{4,0},{8,4},{12,8},{16,12},{20,16},{24,20},{28,24},{32,28}... | collective-permute-start | bytes 1179656 | tf_op jit(solution)/shard_map/ppermute | solution.py:31
  121.3 3.2 %collective-permute-start.1 = (bf16[8,2,128,128]{3,2,1,0:T(8,128)(2,1)}, bf16[8,2,128,128]{3,2,1,0:T(8,128)(2,1)}, u32[]{:S(2)}, u32[]{:S(2)}) collective-permute-start(bf16[8,2,128,128]{3,2,1,0:T(8,128)(2,1)} %get-tuple-element.22), channel_id=1, source_target_pairs={{0,2},{1,3},{2,0},{3,1},{4,6},{5,7},{6,4},{7,5},{8,10},{9,11},{10,... | collective-permute-start | bytes 1572872 | tf_op jit(solution)/shard_map/ppermute | solution.py:59
  125.7 4.8 %collective-permute-start.8 = (bf16[256,768]{1,0:T(8,128)(2,1)S(1)}, bf16[256,768]{1,0:T(8,128)(2,1)S(1)}, u32[]{:S(2)}, u32[]{:S(2)}) collective-permute-start(bf16[256,768]{1,0:T(8,128)(2,1)S(1)} %get-tuple-element.6), channel_id=1, source_target_pairs={{0,124},{4,0},{8,4},{12,8},{16,12},{20,16},{24,20},{28,24},{32,28}... | collective-permute-start | bytes 1179656 | tf_op jit(solution)/shard_map/ppermute | solution.py:31
  132.1 10.2 %gather_fusion.1 = bf16[64,128,768]{2,1,0:T(8,128)(2,1)} fusion(bf16[36,128,768]{2,1,0:T(8,128)(2,1)} %bitcast.60, s32[1024]{0:T(1024)S(1)} %pad_clamp_fusion), kind=kCustom, calls=%fused_computation.1 | custom fusion | bytes 25166080 | tf_op jit(solution)/shard_map/gather | solution.py:39
  143.9 10.3 %gather_fusion = bf16[64,128,768]{2,1,0:T(8,128)(2,1)} fusion(bf16[36,128,768]{2,1,0:T(8,128)(2,1)} %bitcast.5, s32[1024]{0:T(1024)S(1)} %pad_clamp_fusion), kind=kCustom, calls=%fused_computation | custom fusion | bytes 25166080 | tf_op jit(solution)/shard_map/gather | solution.py:39
  154.2 7.3 %bitcast_multiply_fusion.2 = f32[8,128,768]{2,1,0:T(8,128)S(1)} fusion(bf16[8,8,128,768]{3,2,1,0:T(8,128)(2,1)} %bitcast.61, bf16[8,2,128,128]{3,2,1,0:T(8,128)(2,1)} %collective-permute-done.2, bf16[8,2,128,128]{3,2,1,0:T(8,128)(2,1)} %collective-permute-done.1, bf16[8,2,128,128]{3,2,1,0:T(8,128)(2,1)} %collective-permute-done, ...), kind=kOutput, calls=%fused_computation.14 | convolution fusion | flops 1614544896 | bytes 17825792 | tf_op jit(solution)/shard_map/rsij,rsjc->ric/dot_general | solution.py:40
  162.8 3.6 %bitcast_multiply_fusion.3 = f32[8,128,768]{2,1,0:T(8,128)S(1)} fusion(bf16[8,8,128,768]{3,2,1,0:T(8,128)(2,1)S(1)} %bitcast.63, bf16[8,2,128,128]{3,2,1,0:T(8,128)(2,1)} %collective-permute-done.2, bf16[8,2,128,128]{3,2,1,0:T(8,128)(2,1)} %collective-permute-done.1, bf16[8,2,128,128]{3,2,1,0:T(8,128)(2,1)} %collective-permute-done, ...), kind=kOutput, calls=%fused_computation.17 | convolution fusion | flops 1614544896 | bytes 17825792 | tf_op jit(solution)/shard_map/rsij,rsjc->ric/dot_general | solution.py:40
  168.2 2.2 collective-permute-start.24
  170.4 3.2 %collective-permute-start.18 = (bf16[1024,768]{1,0:T(8,128)(2,1)S(1)}, bf16[1024,768]{1,0:T(8,128)(2,1)S(1)}, u32[]{:S(2)}, u32[]{:S(2)}) collective-permute-start(bf16[1024,768]{1,0:T(8,128)(2,1)S(1)} %get-tuple-element.12), channel_id=1, source_target_pairs={{0,3},{1,0},{2,1},{3,2},{4,7},{5,4},{6,5},{7,6},{8,11},{9,8},{10,9... | collective-permute-start | bytes 4718600 | tf_op jit(solution)/shard_map/ppermute | solution.py:20
  173.7 32.0 %collective-permute-done.25 = bf16[1024,768]{1,0:T(8,128)(2,1)S(1)} collective-permute-done((bf16[1024,768]{1,0:T(8,128)(2,1)S(1)}, bf16[1024,768]{1,0:T(8,128)(2,1)S(1)}, u32[]{:S(2)}, u32[]{:S(2)}) %collective-permute-start.25) | collective-permute-done | bytes 1572896 | tf_op jit(solution)/shard_map/ppermute | solution.py:19
  205.9 3.3 %collective-permute-start.27 = (bf16[512,768]{1,0:T(8,128)(2,1)S(1)}, bf16[512,768]{1,0:T(8,128)(2,1)S(1)}, u32[]{:S(2)}, u32[]{:S(2)}) collective-permute-start(bf16[512,768]{1,0:T(8,128)(2,1)S(1)} %slice.63), channel_id=1, source_target_pairs={{0,3},{1,0},{2,1},{3,2},{4,7},{5,4},{6,5},{7,6},{8,11},{9,8},{10,9... | collective-permute-start | bytes 2359304 | tf_op jit(solution)/shard_map/ppermute | solution.py:22
  211.2 28.2 %collective-permute-done.19 = bf16[1024,768]{1,0:T(8,128)(2,1)S(1)} collective-permute-done((bf16[1024,768]{1,0:T(8,128)(2,1)S(1)}, bf16[1024,768]{1,0:T(8,128)(2,1)S(1)}, u32[]{:S(2)}, u32[]{:S(2)}) %collective-permute-start.19) | collective-permute-done | bytes 1572896 | tf_op jit(solution)/shard_map/ppermute | solution.py:19
  239.6 3.5 %collective-permute-start.21 = (bf16[512,768]{1,0:T(8,128)(2,1)S(1)}, bf16[512,768]{1,0:T(8,128)(2,1)S(1)}, u32[]{:S(2)}, u32[]{:S(2)}) collective-permute-start(bf16[512,768]{1,0:T(8,128)(2,1)S(1)} %slice.61), channel_id=1, source_target_pairs={{0,3},{1,0},{2,1},{3,2},{4,7},{5,4},{6,5},{7,6},{8,11},{9,8},{10,9... | collective-permute-start | bytes 2359304 | tf_op jit(solution)/shard_map/ppermute | solution.py:22
  245.8 10.4 %collective-permute-done.26 = bf16[512,768]{1,0:T(8,128)(2,1)S(1)} collective-permute-done((bf16[512,768]{1,0:T(8,128)(2,1)S(1)}, bf16[512,768]{1,0:T(8,128)(2,1)S(1)}, u32[]{:S(2)}, u32[]{:S(2)}) %collective-permute-start.26) | collective-permute-done | bytes 786464 | tf_op jit(solution)/shard_map/ppermute | solution.py:21
  259.7 5.1 %collective-permute-start.29 = (bf16[256,768]{1,0:T(8,128)(2,1)S(1)}, bf16[256,768]{1,0:T(8,128)(2,1)S(1)}, u32[]{:S(2)}, u32[]{:S(2)}) collective-permute-start(bf16[256,768]{1,0:T(8,128)(2,1)S(1)} %get-tuple-element.4), channel_id=1, source_target_pairs={{0,124},{4,0},{8,4},{12,8},{16,12},{20,16},{24,20},{28,24},{32,28}... | collective-permute-start | bytes 1179656 | tf_op jit(solution)/shard_map/ppermute | solution.py:31
  264.8 3.1 collective-permute-done.20
  271.4 5.1 %collective-permute-start.23 = (bf16[256,768]{1,0:T(8,128)(2,1)S(1)}, bf16[256,768]{1,0:T(8,128)(2,1)S(1)}, u32[]{:S(2)}, u32[]{:S(2)}) collective-permute-start(bf16[256,768]{1,0:T(8,128)(2,1)S(1)} %get-tuple-element.2), channel_id=1, source_target_pairs={{0,124},{4,0},{8,4},{12,8},{16,12},{20,16},{24,20},{28,24},{32,28}... | collective-permute-start | bytes 1179656 | tf_op jit(solution)/shard_map/ppermute | solution.py:31
  279.9 10.2 %gather_fusion.3 = bf16[64,128,768]{2,1,0:T(8,128)(2,1)} fusion(bf16[36,128,768]{2,1,0:T(8,128)(2,1)} %bitcast.27, s32[1024]{0:T(1024)S(1)} %pad_clamp_fusion), kind=kCustom, calls=%fused_computation.3 | custom fusion | bytes 25166080 | tf_op jit(solution)/shard_map/gather | solution.py:39
  291.7 10.2 %gather_fusion.2 = bf16[64,128,768]{2,1,0:T(8,128)(2,1)} fusion(bf16[36,128,768]{2,1,0:T(8,128)(2,1)} %bitcast.22, s32[1024]{0:T(1024)S(1)} %pad_clamp_fusion), kind=kCustom, calls=%fused_computation.2 | custom fusion | bytes 25166080 | tf_op jit(solution)/shard_map/gather | solution.py:39
  301.9 7.3 %bitcast_multiply_fusion = f32[8,128,768]{2,1,0:T(8,128)S(1)} fusion(bf16[8,8,128,768]{3,2,1,0:T(8,128)(2,1)} %bitcast.62, bf16[8,2,128,128]{3,2,1,0:T(8,128)(2,1)} %collective-permute-done.2, bf16[8,2,128,128]{3,2,1,0:T(8,128)(2,1)} %collective-permute-done.1, bf16[8,2,128,128]{3,2,1,0:T(8,128)(2,1)} %collective-permute-done, ...), kind=kOutput, calls=%fused_computation.8 | convolution fusion | flops 1614544896 | bytes 17825792 | tf_op jit(solution)/shard_map/rsij,rsjc->ric/dot_general | solution.py:40
  310.5 3.6 %bitcast_multiply_fusion.1 = f32[8,128,768]{2,1,0:T(8,128)S(1)} fusion(bf16[8,8,128,768]{3,2,1,0:T(8,128)(2,1)S(1)} %bitcast.64, bf16[8,2,128,128]{3,2,1,0:T(8,128)(2,1)} %collective-permute-done.2, bf16[8,2,128,128]{3,2,1,0:T(8,128)(2,1)} %collective-permute-done.1, bf16[8,2,128,128]{3,2,1,0:T(8,128)(2,1)} %collective-permute-done, ...), kind=kOutput, calls=%fused_computation.11 | convolution fusion | flops 1614544896 | bytes 17825792 | tf_op jit(solution)/shard_map/rsij,rsjc->ric/dot_general | solution.py:40
  (104 shorter events, 49.9 us)
Async XLA Ops:
  0.6 46.5 %copy-start.8 = (s32[32,2]{0,1:T(2,128)S(1)}, s32[32,2]{0,1:T(2,128)}, u32[]{:S(2)}) copy-start(s32[32,2]{0,1:T(2,128)} %param.5) | copy-start | bytes 772
  6.5 39.6 %collective-permute-start.13 = (bf16[1024,768]{1,0:T(8,128)(2,1)}, bf16[1024,768]{1,0:T(8,128)(2,1)S(1)}, u32[]{:S(2)}, u32[]{:S(2)}) collective-permute-start(bf16[1024,768]{1,0:T(8,128)(2,1)} %get-tuple-element.18), channel_id=1, source_target_pairs={{0,1},{1,2},{2,3},{3,0},{4,5},{5,6},{6,7},{7,4},{8,9},{9,10},{10,1... | collective-permute-start | bytes 4718600 | tf_op jit(solution)/shard_map/ppermute | solution.py:19
  8.5 38.7 %collective-permute-start.12 = (bf16[1024,768]{1,0:T(8,128)(2,1)}, bf16[1024,768]{1,0:T(8,128)(2,1)}, u32[]{:S(2)}, u32[]{:S(2)}) collective-permute-start(bf16[1024,768]{1,0:T(8,128)(2,1)} %get-tuple-element.18), channel_id=1, source_target_pairs={{0,3},{1,0},{2,1},{3,2},{4,7},{5,4},{6,5},{7,6},{8,11},{9,8},{10,9... | collective-permute-start | bytes 4718600 | tf_op jit(solution)/shard_map/ppermute | solution.py:20
  10.6 69.2 %collective-permute-start.4 = (bf16[1024,768]{1,0:T(8,128)(2,1)}, bf16[1024,768]{1,0:T(8,128)(2,1)S(1)}, u32[]{:S(2)}, u32[]{:S(2)}) collective-permute-start(bf16[1024,768]{1,0:T(8,128)(2,1)} %get-tuple-element.19), channel_id=1, source_target_pairs={{0,1},{1,2},{2,3},{3,0},{4,5},{5,6},{6,7},{7,4},{8,9},{9,10},{10,1... | collective-permute-start | bytes 4718600 | tf_op jit(solution)/shard_map/ppermute | solution.py:19
  10.6 69.3 %collective-permute-start.3 = (bf16[1024,768]{1,0:T(8,128)(2,1)}, bf16[1024,768]{1,0:T(8,128)(2,1)}, u32[]{:S(2)}, u32[]{:S(2)}) collective-permute-start(bf16[1024,768]{1,0:T(8,128)(2,1)} %get-tuple-element.19), channel_id=1, source_target_pairs={{0,3},{1,0},{2,1},{3,2},{4,7},{5,4},{6,5},{7,6},{8,11},{9,8},{10,9... | collective-permute-start | bytes 4718600 | tf_op jit(solution)/shard_map/ppermute | solution.py:20
  47.1 49.7 %collective-permute-start.14 = (bf16[512,768]{1,0:T(8,128)(2,1)}, bf16[512,768]{1,0:T(8,128)(2,1)}, u32[]{:S(2)}, u32[]{:S(2)}) collective-permute-start(bf16[512,768]{1,0:T(8,128)(2,1)} %slice.58), channel_id=1, source_target_pairs={{0,1},{1,2},{2,3},{3,0},{4,5},{5,6},{6,7},{7,4},{8,9},{9,10},{10,1... | collective-permute-start | bytes 2359304 | tf_op jit(solution)/shard_map/ppermute | solution.py:21
  49.3 51.6 %collective-permute-start.15 = (bf16[512,768]{1,0:T(8,128)(2,1)}, bf16[512,768]{1,0:T(8,128)(2,1)}, u32[]{:S(2)}, u32[]{:S(2)}) collective-permute-start(bf16[512,768]{1,0:T(8,128)(2,1)} %slice.59), channel_id=1, source_target_pairs={{0,3},{1,0},{2,1},{3,2},{4,7},{5,4},{6,5},{7,6},{8,11},{9,8},{10,9... | collective-permute-start | bytes 2359304 | tf_op jit(solution)/shard_map/ppermute | solution.py:22
  52.5 68.6 %collective-permute-start.10 = (s32[8,2]{0,1:T(2,128)S(1)}, s32[8,2]{0,1:T(2,128)S(1)}, u32[]{:S(2)}, u32[]{:S(2)}) collective-permute-start(s32[8,2]{0,1:T(2,128)S(1)} %bitcast.70), channel_id=1, source_target_pairs={{0,2},{1,3},{2,0},{3,1},{4,6},{5,7},{6,4},{7,5},{8,10},{9,11},{10,... | collective-permute-start | bytes 200 | tf_op jit(solution)/shard_map/ppermute | solution.py:60
  53.2 31.2 %copy-start.5 = (bf16[4096,768]{1,0:T(8,128)(2,1)S(1)}, bf16[4096,768]{1,0:T(8,128)(2,1)}, u32[]{:S(2)}) copy-start(bf16[4096,768]{1,0:T(8,128)(2,1)} %get-tuple-element.16) | copy-start | bytes 18874372
  79.8 32.8 %collective-permute-start.5 = (bf16[512,768]{1,0:T(8,128)(2,1)S(1)}, bf16[512,768]{1,0:T(8,128)(2,1)S(1)}, u32[]{:S(2)}, u32[]{:S(2)}) collective-permute-start(bf16[512,768]{1,0:T(8,128)(2,1)S(1)} %slice.56), channel_id=1, source_target_pairs={{0,1},{1,2},{2,3},{3,0},{4,5},{5,6},{6,7},{7,4},{8,9},{9,10},{10,1... | collective-permute-start | bytes 2359304 | tf_op jit(solution)/shard_map/ppermute | solution.py:21
  81.1 32.6 %collective-permute-start.6 = (bf16[512,768]{1,0:T(8,128)(2,1)S(1)}, bf16[512,768]{1,0:T(8,128)(2,1)S(1)}, u32[]{:S(2)}, u32[]{:S(2)}) collective-permute-start(bf16[512,768]{1,0:T(8,128)(2,1)S(1)} %slice.57), channel_id=1, source_target_pairs={{0,3},{1,0},{2,1},{3,2},{4,7},{5,4},{6,5},{7,6},{8,11},{9,8},{10,9... | collective-permute-start | bytes 2359304 | tf_op jit(solution)/shard_map/ppermute | solution.py:22
  96.8 24.5 %collective-permute-start.11 = (s32[8,2]{0,1:T(2,128)S(1)}, s32[8,2]{0,1:T(2,128)S(1)}, u32[]{:S(2)}, u32[]{:S(2)}) collective-permute-start(s32[8,2]{0,1:T(2,128)S(1)} %bitcast.69), channel_id=1, source_target_pairs={{0,3},{1,0},{2,1},{3,2},{4,7},{5,4},{6,5},{7,6},{8,11},{9,8},{10,9... | collective-permute-start | bytes 200 | tf_op jit(solution)/shard_map/ppermute | solution.py:60
  100.9 23.5 %collective-permute-start.9 = (s32[8,2]{0,1:T(2,128)S(1)}, s32[8,2]{0,1:T(2,128)S(1)}, u32[]{:S(2)}, u32[]{:S(2)}) collective-permute-start(s32[8,2]{0,1:T(2,128)S(1)} %bitcast.68), channel_id=1, source_target_pairs={{0,1},{1,2},{2,3},{3,0},{4,5},{5,6},{6,7},{7,4},{8,9},{9,10},{10,1... | collective-permute-start | bytes 200 | tf_op jit(solution)/shard_map/ppermute | solution.py:60
  112.7 12.0 %collective-permute-start.16 = (bf16[256,768]{1,0:T(8,128)(2,1)}, bf16[256,768]{1,0:T(8,128)(2,1)S(1)}, u32[]{:S(2)}, u32[]{:S(2)}) collective-permute-start(bf16[256,768]{1,0:T(8,128)(2,1)} %get-tuple-element.9), channel_id=1, source_target_pairs={{0,4},{4,8},{8,12},{12,16},{16,20},{20,24},{24,28},{28,32},{32,36}... | collective-permute-start | bytes 1179656 | tf_op jit(solution)/shard_map/ppermute | solution.py:30
  113.7 12.0 %collective-permute-start.17 = (bf16[256,768]{1,0:T(8,128)(2,1)S(1)}, bf16[256,768]{1,0:T(8,128)(2,1)S(1)}, u32[]{:S(2)}, u32[]{:S(2)}) collective-permute-start(bf16[256,768]{1,0:T(8,128)(2,1)S(1)} %get-tuple-element.8), channel_id=1, source_target_pairs={{0,124},{4,0},{8,4},{12,8},{16,12},{20,16},{24,20},{28,24},{32,28}... | collective-permute-start | bytes 1179656 | tf_op jit(solution)/shard_map/ppermute | solution.py:31
  121.2 33.0 %collective-permute-start = (bf16[8,2,128,128]{3,2,1,0:T(8,128)(2,1)}, bf16[8,2,128,128]{3,2,1,0:T(8,128)(2,1)}, u32[]{:S(2)}, u32[]{:S(2)}) collective-permute-start(bf16[8,2,128,128]{3,2,1,0:T(8,128)(2,1)} %get-tuple-element.23), channel_id=1, source_target_pairs={{0,1},{1,2},{2,3},{3,0},{4,5},{5,6},{6,7},{7,4},{8,9},{9,10},{10,1... | collective-permute-start | bytes 1572872 | tf_op jit(solution)/shard_map/ppermute | solution.py:59
  121.3 32.9 %collective-permute-start.1 = (bf16[8,2,128,128]{3,2,1,0:T(8,128)(2,1)}, bf16[8,2,128,128]{3,2,1,0:T(8,128)(2,1)}, u32[]{:S(2)}, u32[]{:S(2)}) collective-permute-start(bf16[8,2,128,128]{3,2,1,0:T(8,128)(2,1)} %get-tuple-element.22), channel_id=1, source_target_pairs={{0,2},{1,3},{2,0},{3,1},{4,6},{5,7},{6,4},{7,5},{8,10},{9,11},{10,... | collective-permute-start | bytes 1572872 | tf_op jit(solution)/shard_map/ppermute | solution.py:59
  124.4 17.9 %collective-permute-start.7 = (bf16[256,768]{1,0:T(8,128)(2,1)S(1)}, bf16[256,768]{1,0:T(8,128)(2,1)S(1)}, u32[]{:S(2)}, u32[]{:S(2)}) collective-permute-start(bf16[256,768]{1,0:T(8,128)(2,1)S(1)} %get-tuple-element.7), channel_id=1, source_target_pairs={{0,4},{4,8},{8,12},{12,16},{16,20},{20,24},{24,28},{28,32},{32,36}... | collective-permute-start | bytes 1179656 | tf_op jit(solution)/shard_map/ppermute | solution.py:30
  124.6 29.5 %collective-permute-start.2 = (bf16[8,2,128,128]{3,2,1,0:T(8,128)(2,1)S(1)}, bf16[8,2,128,128]{3,2,1,0:T(8,128)(2,1)}, u32[]{:S(2)}, u32[]{:S(2)}) collective-permute-start(bf16[8,2,128,128]{3,2,1,0:T(8,128)(2,1)S(1)} %copy-done.7), channel_id=1, source_target_pairs={{0,3},{1,0},{2,1},{3,2},{4,7},{5,4},{6,5},{7,6},{8,11},{9,8},{10,9... | collective-permute-start | bytes 1572872 | tf_op jit(solution)/shard_map/ppermute | solution.py:59
  125.7 17.4 %collective-permute-start.8 = (bf16[256,768]{1,0:T(8,128)(2,1)S(1)}, bf16[256,768]{1,0:T(8,128)(2,1)S(1)}, u32[]{:S(2)}, u32[]{:S(2)}) collective-permute-start(bf16[256,768]{1,0:T(8,128)(2,1)S(1)} %get-tuple-element.6), channel_id=1, source_target_pairs={{0,124},{4,0},{8,4},{12,8},{16,12},{20,16},{24,20},{28,24},{32,28}... | collective-permute-start | bytes 1179656 | tf_op jit(solution)/shard_map/ppermute | solution.py:31
  167.1 38.5 %collective-permute-start.25 = (bf16[1024,768]{1,0:T(8,128)(2,1)S(1)}, bf16[1024,768]{1,0:T(8,128)(2,1)S(1)}, u32[]{:S(2)}, u32[]{:S(2)}) collective-permute-start(bf16[1024,768]{1,0:T(8,128)(2,1)S(1)} %get-tuple-element.13), channel_id=1, source_target_pairs={{0,1},{1,2},{2,3},{3,0},{4,5},{5,6},{6,7},{7,4},{8,9},{9,10},{10,1... | collective-permute-start | bytes 4718600 | tf_op jit(solution)/shard_map/ppermute | solution.py:19
  168.2 37.6 %collective-permute-start.24 = (bf16[1024,768]{1,0:T(8,128)(2,1)S(1)}, bf16[1024,768]{1,0:T(8,128)(2,1)S(1)}, u32[]{:S(2)}, u32[]{:S(2)}) collective-permute-start(bf16[1024,768]{1,0:T(8,128)(2,1)S(1)} %get-tuple-element.13), channel_id=1, source_target_pairs={{0,3},{1,0},{2,1},{3,2},{4,7},{5,4},{6,5},{7,6},{8,11},{9,8},{10,9... | collective-permute-start | bytes 4718600 | tf_op jit(solution)/shard_map/ppermute | solution.py:20
  170.4 68.9 %collective-permute-start.19 = (bf16[1024,768]{1,0:T(8,128)(2,1)S(1)}, bf16[1024,768]{1,0:T(8,128)(2,1)S(1)}, u32[]{:S(2)}, u32[]{:S(2)}) collective-permute-start(bf16[1024,768]{1,0:T(8,128)(2,1)S(1)} %get-tuple-element.12), channel_id=1, source_target_pairs={{0,1},{1,2},{2,3},{3,0},{4,5},{5,6},{6,7},{7,4},{8,9},{9,10},{10,1... | collective-permute-start | bytes 4718600 | tf_op jit(solution)/shard_map/ppermute | solution.py:19
  170.4 69.1 %collective-permute-start.18 = (bf16[1024,768]{1,0:T(8,128)(2,1)S(1)}, bf16[1024,768]{1,0:T(8,128)(2,1)S(1)}, u32[]{:S(2)}, u32[]{:S(2)}) collective-permute-start(bf16[1024,768]{1,0:T(8,128)(2,1)S(1)} %get-tuple-element.12), channel_id=1, source_target_pairs={{0,3},{1,0},{2,1},{3,2},{4,7},{5,4},{6,5},{7,6},{8,11},{9,8},{10,9... | collective-permute-start | bytes 4718600 | tf_op jit(solution)/shard_map/ppermute | solution.py:20
  205.7 50.5 %collective-permute-start.26 = (bf16[512,768]{1,0:T(8,128)(2,1)S(1)}, bf16[512,768]{1,0:T(8,128)(2,1)S(1)}, u32[]{:S(2)}, u32[]{:S(2)}) collective-permute-start(bf16[512,768]{1,0:T(8,128)(2,1)S(1)} %slice.62), channel_id=1, source_target_pairs={{0,1},{1,2},{2,3},{3,0},{4,5},{5,6},{6,7},{7,4},{8,9},{9,10},{10,1... | collective-permute-start | bytes 2359304 | tf_op jit(solution)/shard_map/ppermute | solution.py:21
  205.9 51.4 %collective-permute-start.27 = (bf16[512,768]{1,0:T(8,128)(2,1)S(1)}, bf16[512,768]{1,0:T(8,128)(2,1)S(1)}, u32[]{:S(2)}, u32[]{:S(2)}) collective-permute-start(bf16[512,768]{1,0:T(8,128)(2,1)S(1)} %slice.63), channel_id=1, source_target_pairs={{0,3},{1,0},{2,1},{3,2},{4,7},{5,4},{6,5},{7,6},{8,11},{9,8},{10,9... | collective-permute-start | bytes 2359304 | tf_op jit(solution)/shard_map/ppermute | solution.py:22
  239.4 28.4 %collective-permute-start.20 = (bf16[512,768]{1,0:T(8,128)(2,1)S(1)}, bf16[512,768]{1,0:T(8,128)(2,1)S(1)}, u32[]{:S(2)}, u32[]{:S(2)}) collective-permute-start(bf16[512,768]{1,0:T(8,128)(2,1)S(1)} %slice.60), channel_id=1, source_target_pairs={{0,1},{1,2},{2,3},{3,0},{4,5},{5,6},{6,7},{7,4},{8,9},{9,10},{10,1... | collective-permute-start | bytes 2359304 | tf_op jit(solution)/shard_map/ppermute | solution.py:21
  239.6 29.3 %collective-permute-start.21 = (bf16[512,768]{1,0:T(8,128)(2,1)S(1)}, bf16[512,768]{1,0:T(8,128)(2,1)S(1)}, u32[]{:S(2)}, u32[]{:S(2)}) collective-permute-start(bf16[512,768]{1,0:T(8,128)(2,1)S(1)} %slice.61), channel_id=1, source_target_pairs={{0,3},{1,0},{2,1},{3,2},{4,7},{5,4},{6,5},{7,6},{8,11},{9,8},{10,9... | collective-permute-start | bytes 2359304 | tf_op jit(solution)/shard_map/ppermute | solution.py:22
  259.7 18.7 %collective-permute-start.28 = (bf16[256,768]{1,0:T(8,128)(2,1)S(1)}, bf16[256,768]{1,0:T(8,128)(2,1)S(1)}, u32[]{:S(2)}, u32[]{:S(2)}) collective-permute-start(bf16[256,768]{1,0:T(8,128)(2,1)S(1)} %get-tuple-element.5), channel_id=1, source_target_pairs={{0,4},{4,8},{8,12},{12,16},{16,20},{20,24},{24,28},{28,32},{32,36}... | collective-permute-start | bytes 1179656 | tf_op jit(solution)/shard_map/ppermute | solution.py:30
  259.7 19.3 %collective-permute-start.29 = (bf16[256,768]{1,0:T(8,128)(2,1)S(1)}, bf16[256,768]{1,0:T(8,128)(2,1)S(1)}, u32[]{:S(2)}, u32[]{:S(2)}) collective-permute-start(bf16[256,768]{1,0:T(8,128)(2,1)S(1)} %get-tuple-element.4), channel_id=1, source_target_pairs={{0,124},{4,0},{8,4},{12,8},{16,12},{20,16},{24,20},{28,24},{32,28}... | collective-permute-start | bytes 1179656 | tf_op jit(solution)/shard_map/ppermute | solution.py:31
  271.3 18.8 %collective-permute-start.22 = (bf16[256,768]{1,0:T(8,128)(2,1)S(1)}, bf16[256,768]{1,0:T(8,128)(2,1)S(1)}, u32[]{:S(2)}, u32[]{:S(2)}) collective-permute-start(bf16[256,768]{1,0:T(8,128)(2,1)S(1)} %get-tuple-element.3), channel_id=1, source_target_pairs={{0,4},{4,8},{8,12},{12,16},{16,20},{20,24},{24,28},{28,32},{32,36}... | collective-permute-start | bytes 1179656 | tf_op jit(solution)/shard_map/ppermute | solution.py:30
  271.4 19.6 %collective-permute-start.23 = (bf16[256,768]{1,0:T(8,128)(2,1)S(1)}, bf16[256,768]{1,0:T(8,128)(2,1)S(1)}, u32[]{:S(2)}, u32[]{:S(2)}) collective-permute-start(bf16[256,768]{1,0:T(8,128)(2,1)S(1)} %get-tuple-element.2), channel_id=1, source_target_pairs={{0,124},{4,0},{8,4},{12,8},{16,12},{20,16},{24,20},{28,24},{32,28}... | collective-permute-start | bytes 1179656 | tf_op jit(solution)/shard_map/ppermute | solution.py:31
  (7 other events, 77.3 us)

commit v3 on v2

--- a/solution.py
+++ b/solution.py
@@ -2,6 +2,8 @@
 import jax.numpy as jnp
 from jax import lax
 from jax.sharding import PartitionSpec as P
+from jax.experimental import pallas as pl
+from jax.experimental.pallas import tpu as pltpu
 
 KB = 8
 HB = 2
@@ -32,13 +34,38 @@
     return jnp.concatenate([panel, lo, hi], axis=0)
 
 
-def own_rows(h_own, pos_own, chunk, lidx):
-    block_size = h_own.shape[2]
+def step_kernel(pos_ref, h_ref, *refs):
+    slots = h_ref.shape[1]
+    panel_refs, prev_ref, out_ref = refs[:slots], refs[slots], refs[slots + 1]
+    acc = jnp.dot(h_ref[0, 0], panel_refs[0][0], preferred_element_type=jnp.float32)
+    for s in range(1, slots):
+        acc = acc + jnp.dot(h_ref[0, s], panel_refs[s][0], preferred_element_type=jnp.float32)
+    out_ref[...] = (2.0 * acc - prev_ref[...].astype(jnp.float32)).astype(out_ref.dtype)
+
+
+def own_rows(h_own, pos_flat, chunk, previous, lidx):
+    rows, slots, block_size = h_own.shape[0], h_own.shape[1], h_own.shape[2]
+    width = chunk.shape[1]
     wide = exchange(chunk, lidx, block_size)
-    blocks = wide.reshape(wide.shape[0] // block_size, block_size, chunk.shape[1])
-    picked = blocks[pos_own]
-    acc = jnp.einsum("rsij,rsjc->ric", h_own, picked, preferred_element_type=jnp.float32)
-    return acc.reshape(chunk.shape[0], chunk.shape[1])
+    blocks = wide.reshape(wide.shape[0] // block_size, block_size, width)
+
+    def panel_map(s):
+        return lambda i, p: (p[i * slots + s], 0, 0)
+
+    in_specs = [pl.BlockSpec((1, slots, block_size, block_size), lambda i, p: (i, 0, 0, 0))]
+    in_specs += [pl.BlockSpec((1, block_size, width), panel_map(s)) for s in range(slots)]
+    in_specs += [pl.BlockSpec((block_size, width), lambda i, p: (i, 0))]
+    grid_spec = pltpu.PrefetchScalarGridSpec(
+        num_scalar_prefetch=1,
+        grid=(rows,),
+        in_specs=in_specs,
+        out_specs=pl.BlockSpec((block_size, width), lambda i, p: (i, 0)),
+    )
+    return pl.pallas_call(
+        step_kernel,
+        grid_spec=grid_spec,
+        out_shape=jax.ShapeDtypeStruct(chunk.shape, jnp.bfloat16),
+    )(pos_flat, h_own, *([blocks] * slots), previous)
 
 
 def shards(h_blocks, block_cols, t_now, t_prev):
@@ -66,14 +93,14 @@
     pos_own = jnp.where(rel_own < HB, nl * per_dev + rel_own, pos_own)
     pos_own = jnp.where(rel_own >= HB + group_rows, rel_own, pos_own)
 
+    pos_flat = pos_own.reshape(-1).astype(jnp.int32)
     width = t_now.shape[1]
     step = width // NCH
 
     def recur(current, previous):
         outs = []
         for c in range(NCH):
-            acc = own_rows(h_own, pos_own, current[c], lidx)
-            outs.append((2.0 * acc - previous[c].astype(jnp.float32)).astype(jnp.bfloat16))
+            outs.append(own_rows(h_own, pos_flat, current[c], previous[c], lidx))
         return outs
 
     now_chunks = [t_now[:, c * step:(c + 1) * step] for c in range(NCH)]

time: 317 us -> 311 us (0.981)
  Pallas kernels: 0 us -> 42.5 us
  local copies, waits for them, and re-layouts: 90.9 us -> 54 us
  matrix products: 21.8 us -> 0 us
  other arithmetic: 5.23 us -> 8.96 us
  starting transfers between devices: 54.7 us -> 58.4 us
    ppermute x4, waiting for transfers between devices: 116 us -> 46.2 us  [exchange(): from_prev = lax.ppermute(own, 'layer', shift(nl, 1))]
    ppermute x3, waiting for transfers between devices: 0.01 us -> 66 us  [shards(): lax.ppermute(lax.dynamic_index_in_dim(p_split, dest, 0, keepdims=False),...]
    pallas_call x0 -> x4, Pallas kernels: none -> 42.5 us  [own_rows(): pl.pallas_call(step_kernel, grid_spec=grid_spec, out_shape=jax.ShapeDtype...]
    gather x4 -> x0, local copies, waits for them, and re-layouts: 41 us -> none  [own_rows(): picked = blocks[pos_own]]
    dot_general x4 -> x0, matrix products: 21.8 us -> none  [own_rows(): jnp.einsum('rsij,rsjc->ric', h_own, picked, preferred_element_type=jnp.fl...]
    ppermute x3, waiting for transfers between devices: 0.01 us -> 11.3 us  [shards(): lax.ppermute(lax.dynamic_index_in_dim(h_split, dest, 0, keepdims=False),...]
    ppermute x4, waiting for transfers between devices: 27.3 us -> 20.9 us  [exchange(): far_a = lax.ppermute(from_prev[:half], 'layer', shift(nl, 1))]
    unnamed x36 -> x37, local copies, waits for them, and re-layouts: 32.7 us -> 28.4 us
  transfers between devices with their start and end apart: 30 -> 30, of which waited for: 8 -> 10; matrix products, arithmetic and copies ran while one was open for 23% -> 17% of each run, Pallas kernels for 0% -> 10%
where the time goes in v3:
time: 311 us; the launch traced here: 309 us
  waiting for transfers between devices  144 us (46%)
  starting transfers between devices  58.4 us (19%)
  local copies, waits for them, and re-layouts  54 us (17%)
  Pallas kernels  42.5 us (14%)
  other arithmetic  8.96 us (3%)
    ppermute x3, waiting for transfers between devices, shards(): lax.ppermute(lax.dynamic_index_in_dim(p_split, dest, 0, keepdims=False),...  66 us
    ppermute x4, waiting for transfers between devices, exchange(): from_prev = lax.ppermute(own, 'layer', shift(nl, 1))  46.2 us
    pallas_call x4, Pallas kernels, own_rows(): pl.pallas_call(step_kernel, grid_spec=grid_spec, out_shape=jax.ShapeDtype...  42.5 us
    unnamed x37, local copies, waits for them, and re-layouts  28.4 us
    ppermute x4, waiting for transfers between devices, exchange(): far_a = lax.ppermute(from_prev[:half], 'layer', shift(nl, 1))  20.9 us
    ppermute x4, starting transfers between devices, exchange(): hi = lax.ppermute(first, 'grid', shift(ng, ng - 1))  20.2 us
    ppermute x4, starting transfers between devices, exchange(): from_next = lax.ppermute(own, 'layer', shift(nl, nl - 1))  13.6 us
    ppermute x4, starting transfers between devices, exchange(): far_b = lax.ppermute(from_next[half:], 'layer', shift(nl, nl - 1))  11.7 us
  transfers between devices with their start and end apart: 30, of which 10 were waited for; matrix products, arithmetic and copies ran while one was open for 17% of the time, Pallas kernels for 10%

profile of v3, /device:TPU:0, one launch (start us, length us, event | category | flops | bytes accessed | tf_op | source)
XLA Modules:
  0.0 309.1 jit_solution(4550157446224212914)
XLA Ops:
  0.6 5.0 %constant_dynamic-update-slice_fusion.4 = (bf16[4096,768]{1,0:T(8,128)(2,1)}, bf16[4608,768]{1,0:T(8,128)(2,1)}, bf16[4096,768]{1,0:T(8,128)(2,1)}, bf16[4608,76...) fusion(bf16[1024,1536]{1,0:T(8,128)(2,1)} %param.6), kind=kLoop, calls=%fused_computation.11 | loop fusion | bytes 12582912
  5.6 4.1 %collective-permute-start.12 = (bf16[1024,768]{1,0:T(8,128)(2,1)S(1)}, bf16[1024,768]{1,0:T(8,128)(2,1)}, u32[]{:S(2)}, u32[]{:S(2)}) collective-permute-start(bf16[1024,768]{1,0:T(8,128)(2,1)S(1)} %get-tuple-element.16.refs_8_), channel_id=1, source_target_pairs={{0,3},{1,0},{2,1},{3,2},{4,7},{5,4},{6,5},{7,6},{8,11},{9,8},{10,9... | collective-permute-start | bytes 4718600 | tf_op jit(solution)/shard_map/ppermute | solution.py:22
  9.8 3.3 %collective-permute-start.6 = (bf16[1024,768]{1,0:T(8,128)(2,1)S(1)}, bf16[1024,768]{1,0:T(8,128)(2,1)}, u32[]{:S(2)}, u32[]{:S(2)}) collective-permute-start(bf16[1024,768]{1,0:T(8,128)(2,1)S(1)} %get-tuple-element.17.refs_8_), channel_id=1, source_target_pairs={{0,3},{1,0},{2,1},{3,2},{4,7},{5,4},{6,5},{7,6},{8,11},{9,8},{10,9... | collective-permute-start | bytes 4718600 | tf_op jit(solution)/shard_map/ppermute | solution.py:22
  15.2 62.0 %collective-permute-done.2 = s32[8,2]{0,1:T(2,128)S(1)} collective-permute-done((s32[8,2]{0,1:T(2,128)S(1)}, s32[8,2]{0,1:T(2,128)S(1)}, u32[]{:S(2)}, u32[]{:S(2)}) %collective-permute-start.2) | collective-permute-done | bytes 96 | tf_op jit(solution)/shard_map/ppermute | solution.py:87
  83.3 2.9 dynamic-slice_bitcast_fusion.3
  91.8 3.8 %fusion.4 = (bf16[1024,768]{1,0:T(8,128)(2,1)}, bf16[1024,768]{1,0:T(8,128)(2,1)}) fusion(bf16[1024,1536]{1,0:T(8,128)(2,1)} %param.7), kind=kLoop, calls=%fused_computation.86 | loop fusion | bytes 6291456 | tf_op jit(solution)/shard_map/slice | solution.py:107
  98.9 11.3 %collective-permute-done.5 = bf16[8,2,128,128]{3,2,1,0:T(8,128)(2,1)} collective-permute-done((bf16[8,2,128,128]{3,2,1,0:T(8,128)(2,1)}, bf16[8,2,128,128]{3,2,1,0:T(8,128)(2,1)}, u32[]{:S(2)}, u32[]{:S(2)}) %collective-permute-start.5) | collective-permute-done | bytes 524320 | tf_op jit(solution)/shard_map/ppermute | solution.py:86
  110.1 3.8 %collective-permute-start.15 = (bf16[512,768]{1,0:T(8,128)(2,1)S(1)}, bf16[512,768]{1,0:T(8,128)(2,1)S(1)}, u32[]{:S(2)}, u32[]{:S(2)}) collective-permute-start(bf16[512,768]{1,0:T(8,128)(2,1)S(1)} %slice.51), channel_id=1, source_target_pairs={{0,3},{1,0},{2,1},{3,2},{4,7},{5,4},{6,5},{7,6},{8,11},{9,8},{10,9... | collective-permute-start | bytes 2359304 | tf_op jit(solution)/shard_map/ppermute | solution.py:24
  114.6 3.1 %pad_maximum_fusion.2.h_ref = bf16[8,8,128,128]{3,2,1,0:T(8,128)(2,1)} fusion(bf16[8,2,128,128]{3,2,1,0:T(8,128)(2,1)} %collective-permute-done.5, bf16[8,2,128,128]{3,2,1,0:T(8,128)(2,1)} %collective-permute-done.4, bf16[8,2,128,128]{3,2,1,0:T(8,128)(2,1)} %collective-permute-done.3, bf16[8,2,128,128]{3,2,1,0:T(8,128)(2,1)} %get-tuple-element.18), kind=kLoop, calls=%fused_computation.2 | loop fusion | flops 3145728 | bytes 4194304 | tf_op jit(solution)/shard_map/concatenate | solution.py:88
  123.8 2.8 constant_dynamic-update-slice_fusion.15
  126.6 2.8 constant_dynamic-update-slice_fusion.3
  129.4 3.0 collective-permute-done.14
  134.3 2.8 constant_dynamic-update-slice_fusion.12
  137.3 5.1 %collective-permute-start.17 = (bf16[256,768]{1,0:T(8,128)(2,1)S(1)}, bf16[256,768]{1,0:T(8,128)(2,1)S(1)}, u32[]{:S(2)}, u32[]{:S(2)}) collective-permute-start(bf16[256,768]{1,0:T(8,128)(2,1)S(1)} %get-tuple-element.8), channel_id=1, source_target_pairs={{0,124},{4,0},{8,4},{12,8},{16,12},{20,16},{24,20},{28,24},{32,28}... | collective-permute-start | bytes 1179656 | tf_op jit(solution)/shard_map/ppermute | solution.py:33
  142.3 4.6 %collective-permute-done.8 = bf16[512,768]{1,0:T(8,128)(2,1)S(1)} collective-permute-done((bf16[512,768]{1,0:T(8,128)(2,1)S(1)}, bf16[512,768]{1,0:T(8,128)(2,1)S(1)}, u32[]{:S(2)}, u32[]{:S(2)}) %collective-permute-start.8) | collective-permute-done | bytes 786464 | tf_op jit(solution)/shard_map/ppermute | solution.py:23
  149.0 2.8 constant_dynamic-update-slice_fusion
  151.9 5.1 %collective-permute-start.11 = (bf16[256,768]{1,0:T(8,128)(2,1)S(1)}, bf16[256,768]{1,0:T(8,128)(2,1)S(1)}, u32[]{:S(2)}, u32[]{:S(2)}) collective-permute-start(bf16[256,768]{1,0:T(8,128)(2,1)S(1)} %get-tuple-element.6), channel_id=1, source_target_pairs={{0,124},{4,0},{8,4},{12,8},{16,12},{20,16},{24,20},{28,24},{32,28}... | collective-permute-start | bytes 1179656 | tf_op jit(solution)/shard_map/ppermute | solution.py:33
  158.5 10.6 %shard_map.60 = bf16[1024,768]{1,0:T(8,128)(2,1)} custom-call(s32[64]{0:T(128)} %compare_select_fusion.pos_ref, bf16[8,8,128,128]{3,2,1,0:T(8,128)(2,1)} %pad_maximum_fusion.2.h_ref, bf16[36,128,768]{2,1,0:T(8,128)(2,1)} %bitcast.10.refs_0_.refs_1_.refs_2_.refs_3_.refs_4_.refs_5_.refs_6_.refs_7_, ...), custom_call_target="tpu_custom_call" | custom-call | tf_op jit(solution)/shard_map/pallas_call | solution.py:64
  169.4 2.9 collective-permute-start.24
  173.9 10.7 %shard_map.59 = bf16[1024,768]{1,0:T(8,128)(2,1)} custom-call(s32[64]{0:T(128)} %compare_select_fusion.pos_ref, bf16[8,8,128,128]{3,2,1,0:T(8,128)(2,1)} %pad_maximum_fusion.2.h_ref, bf16[36,128,768]{2,1,0:T(8,128)(2,1)} %bitcast.9.refs_0_.refs_1_.refs_2_.refs_3_.refs_4_.refs_5_.refs_6_.refs_7_, ...), custom_call_target="tpu_custom_call" | custom-call | tf_op jit(solution)/shard_map/pallas_call | solution.py:64
  184.7 3.2 %collective-permute-start.18 = (bf16[1024,768]{1,0:T(8,128)(2,1)}, bf16[1024,768]{1,0:T(8,128)(2,1)S(1)}, u32[]{:S(2)}, u32[]{:S(2)}) collective-permute-start(bf16[1024,768]{1,0:T(8,128)(2,1)} %shard_map.59), channel_id=1, source_target_pairs={{0,3},{1,0},{2,1},{3,2},{4,7},{5,4},{6,5},{7,6},{8,11},{9,8},{10,9... | collective-permute-start | bytes 4718600 | tf_op jit(solution)/shard_map/ppermute | solution.py:22
  187.9 19.9 %collective-permute-done.25 = bf16[1024,768]{1,0:T(8,128)(2,1)S(1)} collective-permute-done((bf16[1024,768]{1,0:T(8,128)(2,1)}, bf16[1024,768]{1,0:T(8,128)(2,1)S(1)}, u32[]{:S(2)}, u32[]{:S(2)}) %collective-permute-start.25) | collective-permute-done | bytes 1572896 | tf_op jit(solution)/shard_map/ppermute | solution.py:21
  209.1 3.3 %collective-permute-start.27 = (bf16[512,768]{1,0:T(8,128)(2,1)S(1)}, bf16[512,768]{1,0:T(8,128)(2,1)S(1)}, u32[]{:S(2)}, u32[]{:S(2)}) collective-permute-start(bf16[512,768]{1,0:T(8,128)(2,1)S(1)} %slice.55), channel_id=1, source_target_pairs={{0,3},{1,0},{2,1},{3,2},{4,7},{5,4},{6,5},{7,6},{8,11},{9,8},{10,9... | collective-permute-start | bytes 2359304 | tf_op jit(solution)/shard_map/ppermute | solution.py:24
  215.2 26.3 %collective-permute-done.19 = bf16[1024,768]{1,0:T(8,128)(2,1)S(1)} collective-permute-done((bf16[1024,768]{1,0:T(8,128)(2,1)}, bf16[1024,768]{1,0:T(8,128)(2,1)S(1)}, u32[]{:S(2)}, u32[]{:S(2)}) %collective-permute-start.19) | collective-permute-done | bytes 1572896 | tf_op jit(solution)/shard_map/ppermute | solution.py:21
  241.7 3.3 %collective-permute-start.21 = (bf16[512,768]{1,0:T(8,128)(2,1)S(1)}, bf16[512,768]{1,0:T(8,128)(2,1)S(1)}, u32[]{:S(2)}, u32[]{:S(2)}) collective-permute-start(bf16[512,768]{1,0:T(8,128)(2,1)S(1)} %slice.53), channel_id=1, source_target_pairs={{0,3},{1,0},{2,1},{3,2},{4,7},{5,4},{6,5},{7,6},{8,11},{9,8},{10,9... | collective-permute-start | bytes 2359304 | tf_op jit(solution)/shard_map/ppermute | solution.py:24
  249.1 9.3 %collective-permute-done.26 = bf16[512,768]{1,0:T(8,128)(2,1)S(1)} collective-permute-done((bf16[512,768]{1,0:T(8,128)(2,1)S(1)}, bf16[512,768]{1,0:T(8,128)(2,1)S(1)}, u32[]{:S(2)}, u32[]{:S(2)}) %collective-permute-start.26) | collective-permute-done | bytes 786464 | tf_op jit(solution)/shard_map/ppermute | solution.py:23
  261.8 5.1 %collective-permute-start.29 = (bf16[256,768]{1,0:T(8,128)(2,1)S(1)}, bf16[256,768]{1,0:T(8,128)(2,1)S(1)}, u32[]{:S(2)}, u32[]{:S(2)}) collective-permute-start(bf16[256,768]{1,0:T(8,128)(2,1)S(1)} %get-tuple-element.4), channel_id=1, source_target_pairs={{0,124},{4,0},{8,4},{12,8},{16,12},{20,16},{24,20},{28,24},{32,28}... | collective-permute-start | bytes 1179656 | tf_op jit(solution)/shard_map/ppermute | solution.py:33
  266.9 4.0 %collective-permute-done.20 = bf16[512,768]{1,0:T(8,128)(2,1)S(1)} collective-permute-done((bf16[512,768]{1,0:T(8,128)(2,1)S(1)}, bf16[512,768]{1,0:T(8,128)(2,1)S(1)}, u32[]{:S(2)}, u32[]{:S(2)}) %collective-permute-start.20) | collective-permute-done | bytes 786464 | tf_op jit(solution)/shard_map/ppermute | solution.py:23
  274.4 5.1 %collective-permute-start.23 = (bf16[256,768]{1,0:T(8,128)(2,1)S(1)}, bf16[256,768]{1,0:T(8,128)(2,1)S(1)}, u32[]{:S(2)}, u32[]{:S(2)}) collective-permute-start(bf16[256,768]{1,0:T(8,128)(2,1)S(1)} %get-tuple-element.2), channel_id=1, source_target_pairs={{0,124},{4,0},{8,4},{12,8},{16,12},{20,16},{24,20},{28,24},{32,28}... | collective-permute-start | bytes 1179656 | tf_op jit(solution)/shard_map/ppermute | solution.py:33
  282.9 10.6 %shard_map.62 = bf16[1024,768]{1,0:T(8,128)(2,1)} custom-call(s32[64]{0:T(128)} %compare_select_fusion.pos_ref, bf16[8,8,128,128]{3,2,1,0:T(8,128)(2,1)} %pad_maximum_fusion.2.h_ref, bf16[36,128,768]{2,1,0:T(8,128)(2,1)} %bitcast.12.refs_0_.refs_1_.refs_2_.refs_3_.refs_4_.refs_5_.refs_6_.refs_7_, ...), custom_call_target="tpu_custom_call" | custom-call | tf_op jit(solution)/shard_map/pallas_call | solution.py:64
  295.1 10.7 %shard_map.61 = bf16[1024,768]{1,0:T(8,128)(2,1)} custom-call(s32[64]{0:T(128)} %compare_select_fusion.pos_ref, bf16[8,8,128,128]{3,2,1,0:T(8,128)(2,1)} %pad_maximum_fusion.2.h_ref, bf16[36,128,768]{2,1,0:T(8,128)(2,1)} %bitcast.11.refs_0_.refs_1_.refs_2_.refs_3_.refs_4_.refs_5_.refs_6_.refs_7_, ...), custom_call_target="tpu_custom_call" | custom-call | tf_op jit(solution)/shard_map/pallas_call | solution.py:64
  305.8 3.3 %pad_maximum_fusion.1 = bf16[1024,1536]{1,0:T(8,128)(2,1)} fusion(bf16[1024,768]{1,0:T(8,128)(2,1)S(1)} %copy-done.4, bf16[1024,768]{1,0:T(8,128)(2,1)} %shard_map.61), kind=kLoop, calls=%fused_computation.1 | loop fusion | flops 6291456 | bytes 6291456 | tf_op jit(solution)/shard_map/concatenate | solution.py:110
  (102 shorter events, 52.1 us)
Async XLA Ops:
  5.6 93.2 %copy-start.2 = (bf16[1024,768]{1,0:T(8,128)(2,1)}, bf16[1024,768]{1,0:T(8,128)(2,1)S(1)}, u32[]{:S(2)}) copy-start(bf16[1024,768]{1,0:T(8,128)(2,1)S(1)} %get-tuple-element.17.refs_8_) | copy-start | bytes 4718596
  5.6 93.3 %copy-start.3 = (bf16[1024,768]{1,0:T(8,128)(2,1)}, bf16[1024,768]{1,0:T(8,128)(2,1)S(1)}, u32[]{:S(2)}) copy-start(bf16[1024,768]{1,0:T(8,128)(2,1)S(1)} %get-tuple-element.16.refs_8_) | copy-start | bytes 4718596
  5.6 84.0 %collective-permute-start.12 = (bf16[1024,768]{1,0:T(8,128)(2,1)S(1)}, bf16[1024,768]{1,0:T(8,128)(2,1)}, u32[]{:S(2)}, u32[]{:S(2)}) collective-permute-start(bf16[1024,768]{1,0:T(8,128)(2,1)S(1)} %get-tuple-element.16.refs_8_), channel_id=1, source_target_pairs={{0,3},{1,0},{2,1},{3,2},{4,7},{5,4},{6,5},{7,6},{8,11},{9,8},{10,9... | collective-permute-start | bytes 4718600 | tf_op jit(solution)/shard_map/ppermute | solution.py:22
  9.7 80.7 %collective-permute-start.13 = (bf16[1024,768]{1,0:T(8,128)(2,1)S(1)}, bf16[1024,768]{1,0:T(8,128)(2,1)}, u32[]{:S(2)}, u32[]{:S(2)}) collective-permute-start(bf16[1024,768]{1,0:T(8,128)(2,1)S(1)} %get-tuple-element.16.refs_8_), channel_id=1, source_target_pairs={{0,1},{1,2},{2,3},{3,0},{4,5},{5,6},{6,7},{7,4},{8,9},{9,10},{10,1... | collective-permute-start | bytes 4718600 | tf_op jit(solution)/shard_map/ppermute | solution.py:21
  9.7 108.0 %collective-permute-start.7 = (bf16[1024,768]{1,0:T(8,128)(2,1)S(1)}, bf16[1024,768]{1,0:T(8,128)(2,1)}, u32[]{:S(2)}, u32[]{:S(2)}) collective-permute-start(bf16[1024,768]{1,0:T(8,128)(2,1)S(1)} %get-tuple-element.17.refs_8_), channel_id=1, source_target_pairs={{0,1},{1,2},{2,3},{3,0},{4,5},{5,6},{6,7},{7,4},{8,9},{9,10},{10,1... | collective-permute-start | bytes 4718600 | tf_op jit(solution)/shard_map/ppermute | solution.py:21
  9.8 111.6 %collective-permute-start.6 = (bf16[1024,768]{1,0:T(8,128)(2,1)S(1)}, bf16[1024,768]{1,0:T(8,128)(2,1)}, u32[]{:S(2)}, u32[]{:S(2)}) collective-permute-start(bf16[1024,768]{1,0:T(8,128)(2,1)S(1)} %get-tuple-element.17.refs_8_), channel_id=1, source_target_pairs={{0,3},{1,0},{2,1},{3,2},{4,7},{5,4},{6,5},{7,6},{8,11},{9,8},{10,9... | collective-permute-start | bytes 4718600 | tf_op jit(solution)/shard_map/ppermute | solution.py:22
  13.1 64.0 %collective-permute-start.2 = (s32[8,2]{0,1:T(2,128)S(1)}, s32[8,2]{0,1:T(2,128)S(1)}, u32[]{:S(2)}, u32[]{:S(2)}) collective-permute-start(s32[8,2]{0,1:T(2,128)S(1)} %bitcast.25), channel_id=1, source_target_pairs={{0,3},{1,0},{2,1},{3,2},{4,7},{5,4},{6,5},{7,6},{8,11},{9,8},{10,9... | collective-permute-start | bytes 200 | tf_op jit(solution)/shard_map/ppermute | solution.py:87
  77.1 5.1 %collective-permute-start.1 = (s32[8,2]{0,1:T(2,128)S(1)}, s32[8,2]{0,1:T(2,128)S(1)}, u32[]{:S(2)}, u32[]{:S(2)}) collective-permute-start(s32[8,2]{0,1:T(2,128)S(1)} %bitcast.24), channel_id=1, source_target_pairs={{0,2},{1,3},{2,0},{3,1},{4,6},{5,7},{6,4},{7,5},{8,10},{9,11},{10,... | collective-permute-start | bytes 200 | tf_op jit(solution)/shard_map/ppermute | solution.py:87
  82.2 5.3 %collective-permute-start = (s32[8,2]{0,1:T(2,128)S(1)}, s32[8,2]{0,1:T(2,128)S(1)}, u32[]{:S(2)}, u32[]{:S(2)}) collective-permute-start(s32[8,2]{0,1:T(2,128)S(1)} %bitcast.23), channel_id=1, source_target_pairs={{0,1},{1,2},{2,3},{3,0},{4,5},{5,6},{6,7},{7,4},{8,9},{9,10},{10,1... | collective-permute-start | bytes 200 | tf_op jit(solution)/shard_map/ppermute | solution.py:87
  87.5 22.6 %collective-permute-start.5 = (bf16[8,2,128,128]{3,2,1,0:T(8,128)(2,1)}, bf16[8,2,128,128]{3,2,1,0:T(8,128)(2,1)}, u32[]{:S(2)}, u32[]{:S(2)}) collective-permute-start(bf16[8,2,128,128]{3,2,1,0:T(8,128)(2,1)} %get-tuple-element.19), channel_id=1, source_target_pairs={{0,3},{1,0},{2,1},{3,2},{4,7},{5,4},{6,5},{7,6},{8,11},{9,8},{10,9... | collective-permute-start | bytes 1572872 | tf_op jit(solution)/shard_map/ppermute | solution.py:86
  89.6 20.6 %collective-permute-start.4 = (bf16[8,2,128,128]{3,2,1,0:T(8,128)(2,1)}, bf16[8,2,128,128]{3,2,1,0:T(8,128)(2,1)}, u32[]{:S(2)}, u32[]{:S(2)}) collective-permute-start(bf16[8,2,128,128]{3,2,1,0:T(8,128)(2,1)} %get-tuple-element.20), channel_id=1, source_target_pairs={{0,2},{1,3},{2,0},{3,1},{4,6},{5,7},{6,4},{7,5},{8,10},{9,11},{10,... | collective-permute-start | bytes 1572872 | tf_op jit(solution)/shard_map/ppermute | solution.py:86
  90.4 24.2 %collective-permute-start.3 = (bf16[8,2,128,128]{3,2,1,0:T(8,128)(2,1)}, bf16[8,2,128,128]{3,2,1,0:T(8,128)(2,1)}, u32[]{:S(2)}, u32[]{:S(2)}) collective-permute-start(bf16[8,2,128,128]{3,2,1,0:T(8,128)(2,1)} %get-tuple-element.21), channel_id=1, source_target_pairs={{0,1},{1,2},{2,3},{3,0},{4,5},{5,6},{6,7},{7,4},{8,9},{9,10},{10,1... | collective-permute-start | bytes 1572872 | tf_op jit(solution)/shard_map/ppermute | solution.py:86
  110.1 22.2 %collective-permute-start.14 = (bf16[512,768]{1,0:T(8,128)(2,1)S(1)}, bf16[512,768]{1,0:T(8,128)(2,1)S(1)}, u32[]{:S(2)}, u32[]{:S(2)}) collective-permute-start(bf16[512,768]{1,0:T(8,128)(2,1)S(1)} %slice.50), channel_id=1, source_target_pairs={{0,1},{1,2},{2,3},{3,0},{4,5},{5,6},{6,7},{7,4},{8,9},{9,10},{10,1... | collective-permute-start | bytes 2359304 | tf_op jit(solution)/shard_map/ppermute | solution.py:23
  110.1 23.2 %collective-permute-start.15 = (bf16[512,768]{1,0:T(8,128)(2,1)S(1)}, bf16[512,768]{1,0:T(8,128)(2,1)S(1)}, u32[]{:S(2)}, u32[]{:S(2)}) collective-permute-start(bf16[512,768]{1,0:T(8,128)(2,1)S(1)} %slice.51), channel_id=1, source_target_pairs={{0,3},{1,0},{2,1},{3,2},{4,7},{5,4},{6,5},{7,6},{8,11},{9,8},{10,9... | collective-permute-start | bytes 2359304 | tf_op jit(solution)/shard_map/ppermute | solution.py:24
  119.0 27.9 %collective-permute-start.8 = (bf16[512,768]{1,0:T(8,128)(2,1)S(1)}, bf16[512,768]{1,0:T(8,128)(2,1)S(1)}, u32[]{:S(2)}, u32[]{:S(2)}) collective-permute-start(bf16[512,768]{1,0:T(8,128)(2,1)S(1)} %slice.48), channel_id=1, source_target_pairs={{0,1},{1,2},{2,3},{3,0},{4,5},{5,6},{6,7},{7,4},{8,9},{9,10},{10,1... | collective-permute-start | bytes 2359304 | tf_op jit(solution)/shard_map/ppermute | solution.py:23
  122.5 25.4 %collective-permute-start.9 = (bf16[512,768]{1,0:T(8,128)(2,1)S(1)}, bf16[512,768]{1,0:T(8,128)(2,1)S(1)}, u32[]{:S(2)}, u32[]{:S(2)}) collective-permute-start(bf16[512,768]{1,0:T(8,128)(2,1)S(1)} %slice.49), channel_id=1, source_target_pairs={{0,3},{1,0},{2,1},{3,2},{4,7},{5,4},{6,5},{7,6},{8,11},{9,8},{10,9... | collective-permute-start | bytes 2359304 | tf_op jit(solution)/shard_map/ppermute | solution.py:24
  137.2 19.8 %collective-permute-start.16 = (bf16[256,768]{1,0:T(8,128)(2,1)S(1)}, bf16[256,768]{1,0:T(8,128)(2,1)S(1)}, u32[]{:S(2)}, u32[]{:S(2)}) collective-permute-start(bf16[256,768]{1,0:T(8,128)(2,1)S(1)} %get-tuple-element.9), channel_id=1, source_target_pairs={{0,4},{4,8},{8,12},{12,16},{16,20},{20,24},{24,28},{28,32},{32,36}... | collective-permute-start | bytes 1179656 | tf_op jit(solution)/shard_map/ppermute | solution.py:32
  137.3 20.5 %collective-permute-start.17 = (bf16[256,768]{1,0:T(8,128)(2,1)S(1)}, bf16[256,768]{1,0:T(8,128)(2,1)S(1)}, u32[]{:S(2)}, u32[]{:S(2)}) collective-permute-start(bf16[256,768]{1,0:T(8,128)(2,1)S(1)} %get-tuple-element.8), channel_id=1, source_target_pairs={{0,124},{4,0},{8,4},{12,8},{16,12},{20,16},{24,20},{28,24},{32,28}... | collective-permute-start | bytes 1179656 | tf_op jit(solution)/shard_map/ppermute | solution.py:33
  151.8 20.5 %collective-permute-start.10 = (bf16[256,768]{1,0:T(8,128)(2,1)S(1)}, bf16[256,768]{1,0:T(8,128)(2,1)S(1)}, u32[]{:S(2)}, u32[]{:S(2)}) collective-permute-start(bf16[256,768]{1,0:T(8,128)(2,1)S(1)} %get-tuple-element.7), channel_id=1, source_target_pairs={{0,4},{4,8},{8,12},{12,16},{16,20},{20,24},{24,28},{28,32},{32,36}... | collective-permute-start | bytes 1179656 | tf_op jit(solution)/shard_map/ppermute | solution.py:32
  151.9 21.2 %collective-permute-start.11 = (bf16[256,768]{1,0:T(8,128)(2,1)S(1)}, bf16[256,768]{1,0:T(8,128)(2,1)S(1)}, u32[]{:S(2)}, u32[]{:S(2)}) collective-permute-start(bf16[256,768]{1,0:T(8,128)(2,1)S(1)} %get-tuple-element.6), channel_id=1, source_target_pairs={{0,124},{4,0},{8,4},{12,8},{16,12},{20,16},{24,20},{28,24},{32,28}... | collective-permute-start | bytes 1179656 | tf_op jit(solution)/shard_map/ppermute | solution.py:33
  169.1 38.7 %collective-permute-start.25 = (bf16[1024,768]{1,0:T(8,128)(2,1)}, bf16[1024,768]{1,0:T(8,128)(2,1)S(1)}, u32[]{:S(2)}, u32[]{:S(2)}) collective-permute-start(bf16[1024,768]{1,0:T(8,128)(2,1)} %shard_map.60), channel_id=1, source_target_pairs={{0,1},{1,2},{2,3},{3,0},{4,5},{5,6},{6,7},{7,4},{8,9},{9,10},{10,1... | collective-permute-start | bytes 4718600 | tf_op jit(solution)/shard_map/ppermute | solution.py:21
  169.4 38.5 %collective-permute-start.24 = (bf16[1024,768]{1,0:T(8,128)(2,1)}, bf16[1024,768]{1,0:T(8,128)(2,1)}, u32[]{:S(2)}, u32[]{:S(2)}) collective-permute-start(bf16[1024,768]{1,0:T(8,128)(2,1)} %shard_map.60), channel_id=1, source_target_pairs={{0,3},{1,0},{2,1},{3,2},{4,7},{5,4},{6,5},{7,6},{8,11},{9,8},{10,9... | collective-permute-start | bytes 4718600 | tf_op jit(solution)/shard_map/ppermute | solution.py:22
  184.6 56.9 %collective-permute-start.19 = (bf16[1024,768]{1,0:T(8,128)(2,1)}, bf16[1024,768]{1,0:T(8,128)(2,1)S(1)}, u32[]{:S(2)}, u32[]{:S(2)}) collective-permute-start(bf16[1024,768]{1,0:T(8,128)(2,1)} %shard_map.59), channel_id=1, source_target_pairs={{0,1},{1,2},{2,3},{3,0},{4,5},{5,6},{6,7},{7,4},{8,9},{9,10},{10,1... | collective-permute-start | bytes 4718600 | tf_op jit(solution)/shard_map/ppermute | solution.py:21
  184.7 57.0 %collective-permute-start.18 = (bf16[1024,768]{1,0:T(8,128)(2,1)}, bf16[1024,768]{1,0:T(8,128)(2,1)S(1)}, u32[]{:S(2)}, u32[]{:S(2)}) collective-permute-start(bf16[1024,768]{1,0:T(8,128)(2,1)} %shard_map.59), channel_id=1, source_target_pairs={{0,3},{1,0},{2,1},{3,2},{4,7},{5,4},{6,5},{7,6},{8,11},{9,8},{10,9... | collective-permute-start | bytes 4718600 | tf_op jit(solution)/shard_map/ppermute | solution.py:22
  207.8 50.5 %collective-permute-start.26 = (bf16[512,768]{1,0:T(8,128)(2,1)S(1)}, bf16[512,768]{1,0:T(8,128)(2,1)S(1)}, u32[]{:S(2)}, u32[]{:S(2)}) collective-permute-start(bf16[512,768]{1,0:T(8,128)(2,1)S(1)} %slice.54), channel_id=1, source_target_pairs={{0,1},{1,2},{2,3},{3,0},{4,5},{5,6},{6,7},{7,4},{8,9},{9,10},{10,1... | collective-permute-start | bytes 2359304 | tf_op jit(solution)/shard_map/ppermute | solution.py:23
  209.1 50.2 %collective-permute-start.27 = (bf16[512,768]{1,0:T(8,128)(2,1)S(1)}, bf16[512,768]{1,0:T(8,128)(2,1)S(1)}, u32[]{:S(2)}, u32[]{:S(2)}) collective-permute-start(bf16[512,768]{1,0:T(8,128)(2,1)S(1)} %slice.55), channel_id=1, source_target_pairs={{0,3},{1,0},{2,1},{3,2},{4,7},{5,4},{6,5},{7,6},{8,11},{9,8},{10,9... | collective-permute-start | bytes 2359304 | tf_op jit(solution)/shard_map/ppermute | solution.py:24
  241.5 29.4 %collective-permute-start.20 = (bf16[512,768]{1,0:T(8,128)(2,1)S(1)}, bf16[512,768]{1,0:T(8,128)(2,1)S(1)}, u32[]{:S(2)}, u32[]{:S(2)}) collective-permute-start(bf16[512,768]{1,0:T(8,128)(2,1)S(1)} %slice.52), channel_id=1, source_target_pairs={{0,1},{1,2},{2,3},{3,0},{4,5},{5,6},{6,7},{7,4},{8,9},{9,10},{10,1... | collective-permute-start | bytes 2359304 | tf_op jit(solution)/shard_map/ppermute | solution.py:23
  241.7 30.2 %collective-permute-start.21 = (bf16[512,768]{1,0:T(8,128)(2,1)S(1)}, bf16[512,768]{1,0:T(8,128)(2,1)S(1)}, u32[]{:S(2)}, u32[]{:S(2)}) collective-permute-start(bf16[512,768]{1,0:T(8,128)(2,1)S(1)} %slice.53), channel_id=1, source_target_pairs={{0,3},{1,0},{2,1},{3,2},{4,7},{5,4},{6,5},{7,6},{8,11},{9,8},{10,9... | collective-permute-start | bytes 2359304 | tf_op jit(solution)/shard_map/ppermute | solution.py:24
  261.7 19.7 %collective-permute-start.28 = (bf16[256,768]{1,0:T(8,128)(2,1)S(1)}, bf16[256,768]{1,0:T(8,128)(2,1)S(1)}, u32[]{:S(2)}, u32[]{:S(2)}) collective-permute-start(bf16[256,768]{1,0:T(8,128)(2,1)S(1)} %get-tuple-element.5), channel_id=1, source_target_pairs={{0,4},{4,8},{8,12},{12,16},{16,20},{20,24},{24,28},{28,32},{32,36}... | collective-permute-start | bytes 1179656 | tf_op jit(solution)/shard_map/ppermute | solution.py:32
  261.8 20.3 %collective-permute-start.29 = (bf16[256,768]{1,0:T(8,128)(2,1)S(1)}, bf16[256,768]{1,0:T(8,128)(2,1)S(1)}, u32[]{:S(2)}, u32[]{:S(2)}) collective-permute-start(bf16[256,768]{1,0:T(8,128)(2,1)S(1)} %get-tuple-element.4), channel_id=1, source_target_pairs={{0,124},{4,0},{8,4},{12,8},{16,12},{20,16},{24,20},{28,24},{32,28}... | collective-permute-start | bytes 1179656 | tf_op jit(solution)/shard_map/ppermute | solution.py:33
  274.3 19.2 %collective-permute-start.22 = (bf16[256,768]{1,0:T(8,128)(2,1)S(1)}, bf16[256,768]{1,0:T(8,128)(2,1)S(1)}, u32[]{:S(2)}, u32[]{:S(2)}) collective-permute-start(bf16[256,768]{1,0:T(8,128)(2,1)S(1)} %get-tuple-element.3), channel_id=1, source_target_pairs={{0,4},{4,8},{8,12},{12,16},{16,20},{20,24},{24,28},{28,32},{32,36}... | collective-permute-start | bytes 1179656 | tf_op jit(solution)/shard_map/ppermute | solution.py:32
  274.4 19.9 %collective-permute-start.23 = (bf16[256,768]{1,0:T(8,128)(2,1)S(1)}, bf16[256,768]{1,0:T(8,128)(2,1)S(1)}, u32[]{:S(2)}, u32[]{:S(2)}) collective-permute-start(bf16[256,768]{1,0:T(8,128)(2,1)S(1)} %get-tuple-element.2), channel_id=1, source_target_pairs={{0,124},{4,0},{8,4},{12,8},{16,12},{20,16},{24,20},{28,24},{32,28}... | collective-permute-start | bytes 1179656 | tf_op jit(solution)/shard_map/ppermute | solution.py:33
  (7 other events, 157.4 us)

commit v4 on v3

--- a/solution.py
+++ b/solution.py
@@ -1,3 +1,5 @@
+import functools
+
 import jax
 import jax.numpy as jnp
 from jax import lax
@@ -8,6 +10,7 @@
 KB = 8
 HB = 2
 NCH = 2
+TILE = 256
 
 
 def shift(size, k):
@@ -18,54 +21,68 @@
     nl = lax.axis_size("layer")
     ng = lax.axis_size("grid")
     half = own.shape[0] // 2
+    width = HB * block_size
     from_prev = lax.ppermute(own, "layer", shift(nl, 1))
     from_next = lax.ppermute(own, "layer", shift(nl, nl - 1))
     far_a = lax.ppermute(from_prev[:half], "layer", shift(nl, 1))
     far_b = lax.ppermute(from_next[half:], "layer", shift(nl, nl - 1))
-    panel = jnp.concatenate([own, from_next, far_a, far_b, from_prev], axis=0)
-    rows = own.shape[0]
-    width = HB * block_size
-    last_at = ((nl - 1 - lidx) % nl) * rows + rows - width
-    first_at = ((0 - lidx) % nl) * rows
-    last = lax.dynamic_slice_in_dim(panel, last_at, width, axis=0)
-    first = lax.dynamic_slice_in_dim(panel, first_at, width, axis=0)
+    tails = jnp.concatenate([a[-width:] for a in (own, from_next, far_b, from_prev)], axis=0)
+    heads = jnp.concatenate([a[:width] for a in (own, from_next, far_a, from_prev)], axis=0)
+    last = lax.dynamic_slice_in_dim(tails, ((nl - 1 - lidx) % nl) * width, width, axis=0)
+    first = lax.dynamic_slice_in_dim(heads, ((0 - lidx) % nl) * width, width, axis=0)
     lo = lax.ppermute(last, "grid", shift(ng, 1))
     hi = lax.ppermute(first, "grid", shift(ng, ng - 1))
-    return jnp.concatenate([panel, lo, hi], axis=0)
+    return [own, from_next, far_a, far_b, from_prev, lo, hi]
 
 
-def step_kernel(pos_ref, h_ref, *refs):
-    slots = h_ref.shape[1]
-    panel_refs, prev_ref, out_ref = refs[:slots], refs[slots], refs[slots + 1]
-    acc = jnp.dot(h_ref[0, 0], panel_refs[0][0], preferred_element_type=jnp.float32)
-    for s in range(1, slots):
-        acc = acc + jnp.dot(h_ref[0, s], panel_refs[s][0], preferred_element_type=jnp.float32)
-    out_ref[...] = (2.0 * acc - prev_ref[...].astype(jnp.float32)).astype(out_ref.dtype)
+def step_kernel(pos_ref, h_ref, *refs, starts, tile_rows):
+    n_pieces = len(starts) - 1
+    pieces, prev_ref, out_ref, acc_ref = refs[:n_pieces], refs[n_pieces], refs[n_pieces + 1], refs[n_pieces + 2]
+    rows, slots = h_ref.shape[0], h_ref.shape[1]
+
+    def row(i, carry):
+        acc_ref[...] = jnp.zeros_like(acc_ref)
+        for s in range(slots):
+            p = pos_ref[i * slots + s]
+            for k in range(n_pieces):
+                lo, hi = starts[k], starts[k + 1]
+
+                @pl.when((p >= lo) & (p < hi))
+                def _():
+                    acc_ref[...] += jnp.dot(h_ref[i, s], pieces[k][p - lo], preferred_element_type=jnp.float32)
+
+        at = pl.multiple_of(i * tile_rows, tile_rows)
+        prev = prev_ref[pl.ds(at, tile_rows), :].astype(jnp.float32)
+        out_ref[pl.ds(at, tile_rows), :] = (2.0 * acc_ref[...] - prev).astype(out_ref.dtype)
+        return carry
+
+    lax.fori_loop(0, rows, row, 0)
 
 
 def own_rows(h_own, pos_flat, chunk, previous, lidx):
     rows, slots, block_size = h_own.shape[0], h_own.shape[1], h_own.shape[2]
     width = chunk.shape[1]
-    wide = exchange(chunk, lidx, block_size)
-    blocks = wide.reshape(wide.shape[0] // block_size, block_size, width)
-
-    def panel_map(s):
-        return lambda i, p: (p[i * slots + s], 0, 0)
-
-    in_specs = [pl.BlockSpec((1, slots, block_size, block_size), lambda i, p: (i, 0, 0, 0))]
-    in_specs += [pl.BlockSpec((1, block_size, width), panel_map(s)) for s in range(slots)]
-    in_specs += [pl.BlockSpec((block_size, width), lambda i, p: (i, 0))]
+    tile = TILE if width % TILE == 0 else width
+    pieces = [a.reshape(a.shape[0] // block_size, block_size, width) for a in exchange(chunk, lidx, block_size)]
+    starts = [0]
+    for a in pieces:
+        starts.append(starts[-1] + a.shape[0])
+    in_specs = [pl.BlockSpec(h_own.shape, lambda j, p: (0, 0, 0, 0))]
+    in_specs += [pl.BlockSpec((a.shape[0], block_size, tile), lambda j, p: (0, 0, j)) for a in pieces]
+    in_specs += [pl.BlockSpec((chunk.shape[0], tile), lambda j, p: (0, j))]
     grid_spec = pltpu.PrefetchScalarGridSpec(
         num_scalar_prefetch=1,
-        grid=(rows,),
+        grid=(width // tile,),
         in_specs=in_specs,
-        out_specs=pl.BlockSpec((block_size, width), lambda i, p: (i, 0)),
+        out_specs=pl.BlockSpec((chunk.shape[0], tile), lambda j, p: (0, j)),
+        scratch_shapes=[pltpu.VMEM((block_size, tile), jnp.float32)],
     )
+    kernel = functools.partial(step_kernel, starts=tuple(starts), tile_rows=block_size)
     return pl.pallas_call(
-        step_kernel,
+        kernel,
         grid_spec=grid_spec,
         out_shape=jax.ShapeDtypeStruct(chunk.shape, jnp.bfloat16),
-    )(pos_flat, h_own, *([blocks] * slots), previous)
+    )(pos_flat, h_own, *pieces, previous)
 
 
 def shards(h_blocks, block_cols, t_now, t_prev):

time: 311 us -> 400 us (1.29)
  Pallas kernels: 42.5 us -> 160 us
  local copies, waits for them, and re-layouts: 54 us -> 30.8 us
  starting transfers between devices: 58.4 us -> 43.8 us
  other arithmetic: 8.96 us -> 19.2 us
    pallas_call x4, Pallas kernels: 42.5 us -> 160 us  [own_rows(): pl.pallas_call(kernel, grid_spec=grid_spec, out_shape=jax.ShapeDtypeStruc...]
    ppermute x3, waiting for transfers between devices: 66 us -> 33.2 us  [shards(): lax.ppermute(lax.dynamic_index_in_dim(p_split, dest, 0, keepdims=False),...]
    ppermute x4, waiting for transfers between devices: 20.9 us -> 50 us  [exchange(): far_a = lax.ppermute(from_prev[:half], 'layer', shift(nl, 1))]
    ppermute x4, waiting for transfers between devices: 0.01 us -> 23.9 us  [exchange(): from_next = lax.ppermute(own, 'layer', shift(nl, nl - 1))]
    unnamed x37 -> x62, local copies, waits for them, and re-layouts: 28.4 us -> 5.77 us
    ppermute x4, waiting for transfers between devices: 46.2 us -> 29.6 us  [exchange(): from_prev = lax.ppermute(own, 'layer', shift(nl, 1))]
    slice x0 -> x20, local copies, waits for them, and re-layouts: none -> 11.6 us  [the longest x15 8.41 us: exchange(): a[:width]]
    concatenate x8 -> x0, local copies, waits for them, and re-layouts: 11.5 us -> none  [the longest x4 8.33 us: exchange(): panel = jnp.concatenate([own, from_next, far_a, far_b, from_prev], axis=0)]
  transfers between devices with their start and end apart: 30 -> 30, of which waited for: 10 -> 9; matrix products, arithmetic and copies ran while one was open for 17% -> 10% of each run, Pallas kernels for 10% -> 30%
where the time goes in v4:
time: 400 us; the launch traced here: 399 us
  Pallas kernels  160 us (40%)
  waiting for transfers between devices  144 us (36%)
  starting transfers between devices  43.8 us (11%)
  local copies, waits for them, and re-layouts  30.8 us (8%)
  other arithmetic  19.2 us (5%)
    pallas_call x4, Pallas kernels, own_rows(): pl.pallas_call(kernel, grid_spec=grid_spec, out_shape=jax.ShapeDtypeStruc...  160 us
    ppermute x4, waiting for transfers between devices, exchange(): far_a = lax.ppermute(from_prev[:half], 'layer', shift(nl, 1))  50 us
    ppermute x3, waiting for transfers between devices, shards(): lax.ppermute(lax.dynamic_index_in_dim(p_split, dest, 0, keepdims=False),...  33.2 us
    ppermute x4, waiting for transfers between devices, exchange(): from_prev = lax.ppermute(own, 'layer', shift(nl, 1))  29.6 us
    ppermute x4, waiting for transfers between devices, exchange(): from_next = lax.ppermute(own, 'layer', shift(nl, nl - 1))  23.9 us
    ppermute x4, starting transfers between devices, exchange(): from_next = lax.ppermute(own, 'layer', shift(nl, nl - 1))  13.9 us
    ppermute x4, starting transfers between devices, exchange(): hi = lax.ppermute(first, 'grid', shift(ng, ng - 1))  11.8 us
    ppermute x4, starting transfers between devices, exchange(): far_b = lax.ppermute(from_next[half:], 'layer', shift(nl, nl - 1))  11.1 us
  transfers between devices with their start and end apart: 30, of which 9 were waited for; matrix products, arithmetic and copies ran while one was open for 10% of the time, Pallas kernels for 30%

profile of v4, /device:TPU:0, one launch (start us, length us, event | category | flops | bytes accessed | tf_op | source)
XLA Modules:
  0.0 398.8 jit_solution(8360564466198738669)
XLA Ops:
  0.6 2.1 fusion.30
  2.8 4.2 %collective-permute-start.6 = (bf16[1024,768]{1,0:T(8,128)(2,1)S(1)}, bf16[1024,768]{1,0:T(8,128)(2,1)}, u32[]{:S(2)}, u32[]{:S(2)}) collective-permute-start(bf16[1024,768]{1,0:T(8,128)(2,1)S(1)} %get-tuple-element.8.refs_7_), channel_id=1, source_target_pairs={{0,3},{1,0},{2,1},{3,2},{4,7},{5,4},{6,5},{7,6},{8,11},{9,8},{10,9... | collective-permute-start | bytes 4718600 | tf_op jit(solution)/shard_map/ppermute | solution.py:26
  7.0 3.3 collective-permute-start.12
  10.5 3.1 dynamic-slice_bitcast_fusion.3
  15.9 2.0 fusion.28
  17.9 23.9 %collective-permute-done.6 = bf16[1024,768]{1,0:T(8,128)(2,1)} collective-permute-done((bf16[1024,768]{1,0:T(8,128)(2,1)S(1)}, bf16[1024,768]{1,0:T(8,128)(2,1)}, u32[]{:S(2)}, u32[]{:S(2)}) %collective-permute-start.6) | collective-permute-done | bytes 1572896 | tf_op jit(solution)/shard_map/ppermute | solution.py:26
  41.8 2.4 collective-permute-start.1
  44.2 2.1 slice.181
  46.2 31.6 %collective-permute-done = s32[8,2]{0,1:T(2,128)} collective-permute-done((s32[8,2]{0,1:T(2,128)S(1)}, s32[8,2]{0,1:T(2,128)}, u32[]{:S(2)}, u32[]{:S(2)}) %collective-permute-start) | collective-permute-done | bytes 96 | tf_op jit(solution)/shard_map/ppermute | solution.py:104
  77.9 2.0 collective-permute-start.3
  88.1 3.3 collective-permute-start.15
  94.9 7.3 %collective-permute-done.9 = bf16[512,768]{1,0:T(8,128)(2,1)} collective-permute-done((bf16[512,768]{1,0:T(8,128)(2,1)}, bf16[512,768]{1,0:T(8,128)(2,1)}, u32[]{:S(2)}, u32[]{:S(2)}) %collective-permute-start.9) | collective-permute-done | bytes 786464 | tf_op jit(solution)/shard_map/ppermute | solution.py:28
  105.0 5.9 %collective-permute-done.8 = bf16[512,768]{1,0:T(8,128)(2,1)S(1)} collective-permute-done((bf16[512,768]{1,0:T(8,128)(2,1)S(1)}, bf16[512,768]{1,0:T(8,128)(2,1)S(1)}, u32[]{:S(2)}, u32[]{:S(2)}) %collective-permute-start.8) | collective-permute-done | bytes 786464 | tf_op jit(solution)/shard_map/ppermute | solution.py:27
  113.0 23.7 %collective-permute-done.14 = bf16[512,768]{1,0:T(8,128)(2,1)S(1)} collective-permute-done((bf16[512,768]{1,0:T(8,128)(2,1)S(1)}, bf16[512,768]{1,0:T(8,128)(2,1)S(1)}, u32[]{:S(2)}, u32[]{:S(2)}) %collective-permute-start.14) | collective-permute-done | bytes 786464 | tf_op jit(solution)/shard_map/ppermute | solution.py:27
  136.8 5.1 %collective-permute-start.11 = (bf16[256,768]{1,0:T(8,128)(2,1)S(1)}, bf16[256,768]{1,0:T(8,128)(2,1)S(1)}, u32[]{:S(2)}, u32[]{:S(2)}) collective-permute-start(bf16[256,768]{1,0:T(8,128)(2,1)S(1)} %fusion.20), channel_id=1, source_target_pairs={{0,124},{4,0},{8,4},{12,8},{16,12},{20,16},{24,20},{28,24},{32,28}... | collective-permute-start | bytes 1179656 | tf_op jit(solution)/shard_map/ppermute | solution.py:34
  142.0 1.7 fusion.14
  146.5 2.6 pad_maximum_fusion.2.h_ref
  150.1 39.9 %shard_map.59 = bf16[1024,768]{1,0:T(8,128)(2,1)} custom-call(s32[64]{0:T(128)} %compare_select_fusion.pos_ref, bf16[8,8,128,128]{3,2,1,0:T(8,128)(2,1)} %pad_maximum_fusion.2.h_ref, bf16[8,128,768]{2,1,0:T(8,128)(2,1)} %bitcast.46, bf16[8,128,768]{2,1,0:T(8,128)(2,1)} %bitcast.10.refs_1_, bf16[4,128,768]{2,1,0:T(8,128)(2,1)} %bitcast.52, ...), custom_call_target="tpu_custom_call" | custom-call | tf_op jit(solution)/shard_map/pallas_call | solution.py:81
  190.0 3.2 collective-permute-start.18
  194.1 40.1 %shard_map.60 = bf16[1024,768]{1,0:T(8,128)(2,1)} custom-call(s32[64]{0:T(128)} %compare_select_fusion.pos_ref, bf16[8,8,128,128]{3,2,1,0:T(8,128)(2,1)} %pad_maximum_fusion.2.h_ref, bf16[8,128,768]{2,1,0:T(8,128)(2,1)} %bitcast.45, bf16[8,128,768]{2,1,0:T(8,128)(2,1)} %bitcast.17.refs_1_, bf16[4,128,768]{2,1,0:T(8,128)(2,1)} %bitcast.50, ...), custom_call_target="tpu_custom_call" | custom-call | tf_op jit(solution)/shard_map/pallas_call | solution.py:81
  234.3 3.2 collective-permute-start.24
  240.1 3.3 collective-permute-start.21
  243.4 29.6 %collective-permute-done.25 = bf16[1024,768]{1,0:T(8,128)(2,1)S(1)} collective-permute-done((bf16[1024,768]{1,0:T(8,128)(2,1)}, bf16[1024,768]{1,0:T(8,128)(2,1)S(1)}, u32[]{:S(2)}, u32[]{:S(2)}) %collective-permute-start.25) | collective-permute-done | bytes 1572896 | tf_op jit(solution)/shard_map/ppermute | solution.py:25
  273.2 3.3 collective-permute-start.27
  279.0 10.9 %collective-permute-done.20 = bf16[512,768]{1,0:T(8,128)(2,1)S(1)} collective-permute-done((bf16[512,768]{1,0:T(8,128)(2,1)S(1)}, bf16[512,768]{1,0:T(8,128)(2,1)S(1)}, u32[]{:S(2)}, u32[]{:S(2)}) %collective-permute-start.20) | collective-permute-done | bytes 786464 | tf_op jit(solution)/shard_map/ppermute | solution.py:27
  290.9 3.5 collective-permute-start.23
  295.7 9.5 %collective-permute-done.26 = bf16[512,768]{1,0:T(8,128)(2,1)S(1)} collective-permute-done((bf16[512,768]{1,0:T(8,128)(2,1)S(1)}, bf16[512,768]{1,0:T(8,128)(2,1)S(1)}, u32[]{:S(2)}, u32[]{:S(2)}) %collective-permute-start.26) | collective-permute-done | bytes 786464 | tf_op jit(solution)/shard_map/ppermute | solution.py:27
  307.0 2.9 collective-permute-start.29
  311.9 1.9 pad_maximum_fusion
  314.7 39.9 %shard_map.61 = bf16[1024,768]{1,0:T(8,128)(2,1)} custom-call(s32[64]{0:T(128)} %compare_select_fusion.pos_ref, bf16[8,8,128,128]{3,2,1,0:T(8,128)(2,1)} %pad_maximum_fusion.2.h_ref, bf16[8,128,768]{2,1,0:T(8,128)(2,1)} %bitcast.43, bf16[8,128,768]{2,1,0:T(8,128)(2,1)} %bitcast.24.refs_1_, bf16[4,128,768]{2,1,0:T(8,128)(2,1)} %bitcast.54, ...), custom_call_target="tpu_custom_call" | custom-call | tf_op jit(solution)/shard_map/pallas_call | solution.py:81
  355.5 40.0 %shard_map.62 = bf16[1024,768]{1,0:T(8,128)(2,1)} custom-call(s32[64]{0:T(128)} %compare_select_fusion.pos_ref, bf16[8,8,128,128]{3,2,1,0:T(8,128)(2,1)} %pad_maximum_fusion.2.h_ref, bf16[8,128,768]{2,1,0:T(8,128)(2,1)} %bitcast.44, bf16[8,128,768]{2,1,0:T(8,128)(2,1)} %bitcast.48, bf16[4,128,768]{2,1,0:T(8,128)(2,1)} %bitcast.53, ...), custom_call_target="tpu_custom_call" | custom-call | tf_op jit(solution)/shard_map/pallas_call | solution.py:81
  395.5 3.3 pad_maximum_fusion.1
  (142 shorter events, 36.8 us)
Async XLA Ops:
  2.8 39.0 %collective-permute-start.6 = (bf16[1024,768]{1,0:T(8,128)(2,1)S(1)}, bf16[1024,768]{1,0:T(8,128)(2,1)}, u32[]{:S(2)}, u32[]{:S(2)}) collective-permute-start(bf16[1024,768]{1,0:T(8,128)(2,1)S(1)} %get-tuple-element.8.refs_7_), channel_id=1, source_target_pairs={{0,3},{1,0},{2,1},{3,2},{4,7},{5,4},{6,5},{7,6},{8,11},{9,8},{10,9... | collective-permute-start | bytes 4718600 | tf_op jit(solution)/shard_map/ppermute | solution.py:26
  7.0 76.5 %collective-permute-start.7 = (bf16[1024,768]{1,0:T(8,128)(2,1)S(1)}, bf16[1024,768]{1,0:T(8,128)(2,1)}, u32[]{:S(2)}, u32[]{:S(2)}) collective-permute-start(bf16[1024,768]{1,0:T(8,128)(2,1)S(1)} %get-tuple-element.8.refs_7_), channel_id=1, source_target_pairs={{0,1},{1,2},{2,3},{3,0},{4,5},{5,6},{6,7},{7,4},{8,9},{9,10},{10,1... | collective-permute-start | bytes 4718600 | tf_op jit(solution)/shard_map/ppermute | solution.py:25
  7.0 78.6 %collective-permute-start.13 = (bf16[1024,768]{1,0:T(8,128)(2,1)S(1)}, bf16[1024,768]{1,0:T(8,128)(2,1)}, u32[]{:S(2)}, u32[]{:S(2)}) collective-permute-start(bf16[1024,768]{1,0:T(8,128)(2,1)S(1)} %get-tuple-element.9.refs_7_), channel_id=1, source_target_pairs={{0,1},{1,2},{2,3},{3,0},{4,5},{5,6},{6,7},{7,4},{8,9},{9,10},{10,1... | collective-permute-start | bytes 4718600 | tf_op jit(solution)/shard_map/ppermute | solution.py:25
  7.0 79.9 %collective-permute-start.12 = (bf16[1024,768]{1,0:T(8,128)(2,1)S(1)}, bf16[1024,768]{1,0:T(8,128)(2,1)}, u32[]{:S(2)}, u32[]{:S(2)}) collective-permute-start(bf16[1024,768]{1,0:T(8,128)(2,1)S(1)} %get-tuple-element.9.refs_7_), channel_id=1, source_target_pairs={{0,3},{1,0},{2,1},{3,2},{4,7},{5,4},{6,5},{7,6},{8,11},{9,8},{10,9... | collective-permute-start | bytes 4718600 | tf_op jit(solution)/shard_map/ppermute | solution.py:26
  10.3 67.5 %collective-permute-start = (s32[8,2]{0,1:T(2,128)S(1)}, s32[8,2]{0,1:T(2,128)}, u32[]{:S(2)}, u32[]{:S(2)}) collective-permute-start(s32[8,2]{0,1:T(2,128)S(1)} %bitcast.68), channel_id=1, source_target_pairs={{0,1},{1,2},{2,3},{3,0},{4,5},{5,6},{6,7},{7,4},{8,9},{9,10},{10,1... | collective-permute-start | bytes 200 | tf_op jit(solution)/shard_map/ppermute | solution.py:104
  41.8 36.1 %collective-permute-start.1 = (s32[8,2]{0,1:T(2,128)S(1)}, s32[8,2]{0,1:T(2,128)S(1)}, u32[]{:S(2)}, u32[]{:S(2)}) collective-permute-start(s32[8,2]{0,1:T(2,128)S(1)} %bitcast.67), channel_id=1, source_target_pairs={{0,2},{1,3},{2,0},{3,1},{4,6},{5,7},{6,4},{7,5},{8,10},{9,11},{10,... | collective-permute-start | bytes 200 | tf_op jit(solution)/shard_map/ppermute | solution.py:104
  77.9 3.6 collective-permute-start.2
  77.9 67.6 %collective-permute-start.3 = (bf16[8,2,128,128]{3,2,1,0:T(8,128)(2,1)}, bf16[8,2,128,128]{3,2,1,0:T(8,128)(2,1)}, u32[]{:S(2)}, u32[]{:S(2)}) collective-permute-start(bf16[8,2,128,128]{3,2,1,0:T(8,128)(2,1)} %get-tuple-element.13), channel_id=1, source_target_pairs={{0,1},{1,2},{2,3},{3,0},{4,5},{5,6},{6,7},{7,4},{8,9},{9,10},{10,1... | collective-permute-start | bytes 1572872 | tf_op jit(solution)/shard_map/ppermute | solution.py:103
  81.5 20.7 %collective-permute-start.9 = (bf16[512,768]{1,0:T(8,128)(2,1)}, bf16[512,768]{1,0:T(8,128)(2,1)}, u32[]{:S(2)}, u32[]{:S(2)}) collective-permute-start(bf16[512,768]{1,0:T(8,128)(2,1)} %slice.181), channel_id=1, source_target_pairs={{0,3},{1,0},{2,1},{3,2},{4,7},{5,4},{6,5},{7,6},{8,11},{9,8},{10,9... | collective-permute-start | bytes 2359304 | tf_op jit(solution)/shard_map/ppermute | solution.py:28
  84.7 26.2 %collective-permute-start.8 = (bf16[512,768]{1,0:T(8,128)(2,1)S(1)}, bf16[512,768]{1,0:T(8,128)(2,1)S(1)}, u32[]{:S(2)}, u32[]{:S(2)}) collective-permute-start(bf16[512,768]{1,0:T(8,128)(2,1)S(1)} %slice.180), channel_id=1, source_target_pairs={{0,1},{1,2},{2,3},{3,0},{4,5},{5,6},{6,7},{7,4},{8,9},{9,10},{10,1... | collective-permute-start | bytes 2359304 | tf_op jit(solution)/shard_map/ppermute | solution.py:27
  86.8 50.0 %collective-permute-start.14 = (bf16[512,768]{1,0:T(8,128)(2,1)S(1)}, bf16[512,768]{1,0:T(8,128)(2,1)S(1)}, u32[]{:S(2)}, u32[]{:S(2)}) collective-permute-start(bf16[512,768]{1,0:T(8,128)(2,1)S(1)} %slice.188), channel_id=1, source_target_pairs={{0,1},{1,2},{2,3},{3,0},{4,5},{5,6},{6,7},{7,4},{8,9},{9,10},{10,1... | collective-permute-start | bytes 2359304 | tf_op jit(solution)/shard_map/ppermute | solution.py:27
  88.1 48.8 %collective-permute-start.15 = (bf16[512,768]{1,0:T(8,128)(2,1)S(1)}, bf16[512,768]{1,0:T(8,128)(2,1)S(1)}, u32[]{:S(2)}, u32[]{:S(2)}) collective-permute-start(bf16[512,768]{1,0:T(8,128)(2,1)S(1)} %slice.189), channel_id=1, source_target_pairs={{0,3},{1,0},{2,1},{3,2},{4,7},{5,4},{6,5},{7,6},{8,11},{9,8},{10,9... | collective-permute-start | bytes 2359304 | tf_op jit(solution)/shard_map/ppermute | solution.py:28
  102.2 43.6 %collective-permute-start.4 = (bf16[8,2,128,128]{3,2,1,0:T(8,128)(2,1)S(1)}, bf16[8,2,128,128]{3,2,1,0:T(8,128)(2,1)S(1)}, u32[]{:S(2)}, u32[]{:S(2)}) collective-permute-start(bf16[8,2,128,128]{3,2,1,0:T(8,128)(2,1)S(1)} %copy-done.21), channel_id=1, source_target_pairs={{0,2},{1,3},{2,0},{3,1},{4,6},{5,7},{6,4},{7,5},{8,10},{9,11},{10,... | collective-permute-start | bytes 1572872 | tf_op jit(solution)/shard_map/ppermute | solution.py:103
  111.0 35.6 %collective-permute-start.5 = (bf16[8,2,128,128]{3,2,1,0:T(8,128)(2,1)S(1)}, bf16[8,2,128,128]{3,2,1,0:T(8,128)(2,1)S(1)}, u32[]{:S(2)}, u32[]{:S(2)}) collective-permute-start(bf16[8,2,128,128]{3,2,1,0:T(8,128)(2,1)S(1)} %copy-done.20), channel_id=1, source_target_pairs={{0,3},{1,0},{2,1},{3,2},{4,7},{5,4},{6,5},{7,6},{8,11},{9,8},{10,9... | collective-permute-start | bytes 1572872 | tf_op jit(solution)/shard_map/ppermute | solution.py:103
  136.8 12.4 %collective-permute-start.10 = (bf16[256,768]{1,0:T(8,128)(2,1)S(1)}, bf16[256,768]{1,0:T(8,128)(2,1)S(1)}, u32[]{:S(2)}, u32[]{:S(2)}) collective-permute-start(bf16[256,768]{1,0:T(8,128)(2,1)S(1)} %fusion.23), channel_id=1, source_target_pairs={{0,4},{4,8},{8,12},{12,16},{16,20},{20,24},{24,28},{28,32},{32,36}... | collective-permute-start | bytes 1179656 | tf_op jit(solution)/shard_map/ppermute | solution.py:33
  136.8 12.3 %collective-permute-start.11 = (bf16[256,768]{1,0:T(8,128)(2,1)S(1)}, bf16[256,768]{1,0:T(8,128)(2,1)S(1)}, u32[]{:S(2)}, u32[]{:S(2)}) collective-permute-start(bf16[256,768]{1,0:T(8,128)(2,1)S(1)} %fusion.20), channel_id=1, source_target_pairs={{0,124},{4,0},{8,4},{12,8},{16,12},{20,16},{24,20},{28,24},{32,28}... | collective-permute-start | bytes 1179656 | tf_op jit(solution)/shard_map/ppermute | solution.py:34
  145.5 47.7 %collective-permute-start.17 = (bf16[256,768]{1,0:T(8,128)(2,1)}, bf16[256,768]{1,0:T(8,128)(2,1)S(1)}, u32[]{:S(2)}, u32[]{:S(2)}) collective-permute-start(bf16[256,768]{1,0:T(8,128)(2,1)} %fusion.14), channel_id=1, source_target_pairs={{0,124},{4,0},{8,4},{12,8},{16,12},{20,16},{24,20},{28,24},{32,28}... | collective-permute-start | bytes 1179656 | tf_op jit(solution)/shard_map/ppermute | solution.py:34
  145.8 47.5 %collective-permute-start.16 = (bf16[256,768]{1,0:T(8,128)(2,1)}, bf16[256,768]{1,0:T(8,128)(2,1)S(1)}, u32[]{:S(2)}, u32[]{:S(2)}) collective-permute-start(bf16[256,768]{1,0:T(8,128)(2,1)} %fusion.17), channel_id=1, source_target_pairs={{0,4},{4,8},{8,12},{12,16},{16,20},{20,24},{24,28},{28,32},{32,36}... | collective-permute-start | bytes 1179656 | tf_op jit(solution)/shard_map/ppermute | solution.py:33
  190.0 47.7 %collective-permute-start.19 = (bf16[1024,768]{1,0:T(8,128)(2,1)}, bf16[1024,768]{1,0:T(8,128)(2,1)}, u32[]{:S(2)}, u32[]{:S(2)}) collective-permute-start(bf16[1024,768]{1,0:T(8,128)(2,1)} %shard_map.59), channel_id=1, source_target_pairs={{0,1},{1,2},{2,3},{3,0},{4,5},{5,6},{6,7},{7,4},{8,9},{9,10},{10,1... | collective-permute-start | bytes 4718600 | tf_op jit(solution)/shard_map/ppermute | solution.py:25
  190.0 49.0 %collective-permute-start.18 = (bf16[1024,768]{1,0:T(8,128)(2,1)}, bf16[1024,768]{1,0:T(8,128)(2,1)}, u32[]{:S(2)}, u32[]{:S(2)}) collective-permute-start(bf16[1024,768]{1,0:T(8,128)(2,1)} %shard_map.59), channel_id=1, source_target_pairs={{0,3},{1,0},{2,1},{3,2},{4,7},{5,4},{6,5},{7,6},{8,11},{9,8},{10,9... | collective-permute-start | bytes 4718600 | tf_op jit(solution)/shard_map/ppermute | solution.py:26
  194.1 43.4 %copy-start = (bf16[1024,768]{1,0:T(8,128)(2,1)S(1)}, bf16[1024,768]{1,0:T(8,128)(2,1)}, u32[]{:S(2)}) copy-start(bf16[1024,768]{1,0:T(8,128)(2,1)} %shard_map.59) | copy-start | bytes 4718596
  234.2 38.8 %collective-permute-start.25 = (bf16[1024,768]{1,0:T(8,128)(2,1)}, bf16[1024,768]{1,0:T(8,128)(2,1)S(1)}, u32[]{:S(2)}, u32[]{:S(2)}) collective-permute-start(bf16[1024,768]{1,0:T(8,128)(2,1)} %shard_map.60), channel_id=1, source_target_pairs={{0,1},{1,2},{2,3},{3,0},{4,5},{5,6},{6,7},{7,4},{8,9},{9,10},{10,1... | collective-permute-start | bytes 4718600 | tf_op jit(solution)/shard_map/ppermute | solution.py:25
  234.3 38.8 %collective-permute-start.24 = (bf16[1024,768]{1,0:T(8,128)(2,1)}, bf16[1024,768]{1,0:T(8,128)(2,1)S(1)}, u32[]{:S(2)}, u32[]{:S(2)}) collective-permute-start(bf16[1024,768]{1,0:T(8,128)(2,1)} %shard_map.60), channel_id=1, source_target_pairs={{0,3},{1,0},{2,1},{3,2},{4,7},{5,4},{6,5},{7,6},{8,11},{9,8},{10,9... | collective-permute-start | bytes 4718600 | tf_op jit(solution)/shard_map/ppermute | solution.py:26
  238.9 51.0 %collective-permute-start.20 = (bf16[512,768]{1,0:T(8,128)(2,1)S(1)}, bf16[512,768]{1,0:T(8,128)(2,1)S(1)}, u32[]{:S(2)}, u32[]{:S(2)}) collective-permute-start(bf16[512,768]{1,0:T(8,128)(2,1)S(1)} %slice.196), channel_id=1, source_target_pairs={{0,1},{1,2},{2,3},{3,0},{4,5},{5,6},{6,7},{7,4},{8,9},{9,10},{10,1... | collective-permute-start | bytes 2359304 | tf_op jit(solution)/shard_map/ppermute | solution.py:27
  240.1 54.2 %collective-permute-start.21 = (bf16[512,768]{1,0:T(8,128)(2,1)S(1)}, bf16[512,768]{1,0:T(8,128)(2,1)S(1)}, u32[]{:S(2)}, u32[]{:S(2)}) collective-permute-start(bf16[512,768]{1,0:T(8,128)(2,1)S(1)} %slice.197), channel_id=1, source_target_pairs={{0,3},{1,0},{2,1},{3,2},{4,7},{5,4},{6,5},{7,6},{8,11},{9,8},{10,9... | collective-permute-start | bytes 2359304 | tf_op jit(solution)/shard_map/ppermute | solution.py:28
  273.0 32.2 %collective-permute-start.26 = (bf16[512,768]{1,0:T(8,128)(2,1)S(1)}, bf16[512,768]{1,0:T(8,128)(2,1)S(1)}, u32[]{:S(2)}, u32[]{:S(2)}) collective-permute-start(bf16[512,768]{1,0:T(8,128)(2,1)S(1)} %slice.206), channel_id=1, source_target_pairs={{0,1},{1,2},{2,3},{3,0},{4,5},{5,6},{6,7},{7,4},{8,9},{9,10},{10,1... | collective-permute-start | bytes 2359304 | tf_op jit(solution)/shard_map/ppermute | solution.py:27
  273.2 36.7 %collective-permute-start.27 = (bf16[512,768]{1,0:T(8,128)(2,1)S(1)}, bf16[512,768]{1,0:T(8,128)(2,1)S(1)}, u32[]{:S(2)}, u32[]{:S(2)}) collective-permute-start(bf16[512,768]{1,0:T(8,128)(2,1)S(1)} %slice.207), channel_id=1, source_target_pairs={{0,3},{1,0},{2,1},{3,2},{4,7},{5,4},{6,5},{7,6},{8,11},{9,8},{10,9... | collective-permute-start | bytes 2359304 | tf_op jit(solution)/shard_map/ppermute | solution.py:28
  290.9 22.9 %collective-permute-start.23 = (bf16[256,768]{1,0:T(8,128)(2,1)S(1)}, bf16[256,768]{1,0:T(8,128)(2,1)S(1)}, u32[]{:S(2)}, u32[]{:S(2)}) collective-permute-start(bf16[256,768]{1,0:T(8,128)(2,1)S(1)} %fusion.8), channel_id=1, source_target_pairs={{0,124},{4,0},{8,4},{12,8},{16,12},{20,16},{24,20},{28,24},{32,28}... | collective-permute-start | bytes 1179656 | tf_op jit(solution)/shard_map/ppermute | solution.py:34
  295.4 18.4 %collective-permute-start.22 = (bf16[256,768]{1,0:T(8,128)(2,1)S(1)}, bf16[256,768]{1,0:T(8,128)(2,1)S(1)}, u32[]{:S(2)}, u32[]{:S(2)}) collective-permute-start(bf16[256,768]{1,0:T(8,128)(2,1)S(1)} %fusion.11), channel_id=1, source_target_pairs={{0,4},{4,8},{8,12},{12,16},{16,20},{20,24},{24,28},{28,32},{32,36}... | collective-permute-start | bytes 1179656 | tf_op jit(solution)/shard_map/ppermute | solution.py:33
  307.0 47.6 %collective-permute-start.29 = (bf16[256,768]{1,0:T(8,128)(2,1)}, bf16[256,768]{1,0:T(8,128)(2,1)S(1)}, u32[]{:S(2)}, u32[]{:S(2)}) collective-permute-start(bf16[256,768]{1,0:T(8,128)(2,1)} %fusion.2), channel_id=1, source_target_pairs={{0,124},{4,0},{8,4},{12,8},{16,12},{20,16},{24,20},{28,24},{32,28}... | collective-permute-start | bytes 1179656 | tf_op jit(solution)/shard_map/ppermute | solution.py:34
  311.8 42.8 %collective-permute-start.28 = (bf16[256,768]{1,0:T(8,128)(2,1)S(1)}, bf16[256,768]{1,0:T(8,128)(2,1)S(1)}, u32[]{:S(2)}, u32[]{:S(2)}) collective-permute-start(bf16[256,768]{1,0:T(8,128)(2,1)S(1)} %fusion.5), channel_id=1, source_target_pairs={{0,4},{4,8},{8,12},{12,16},{16,20},{20,24},{24,28},{28,32},{32,36}... | collective-permute-start | bytes 1179656 | tf_op jit(solution)/shard_map/ppermute | solution.py:33
  355.5 40.0 %copy-start.7 = (bf16[1024,768]{1,0:T(8,128)(2,1)S(1)}, bf16[1024,768]{1,0:T(8,128)(2,1)}, u32[]{:S(2)}) copy-start(bf16[1024,768]{1,0:T(8,128)(2,1)} %shard_map.61) | copy-start | bytes 4718596
  (29 other events, 173.1 us)

commit v5 on v3

--- a/solution.py
+++ b/solution.py
@@ -7,7 +7,7 @@
 
 KB = 8
 HB = 2
-NCH = 2
+NCH = 1
 
 
 def shift(size, k):

time: 311 us -> 322 us (1.035)
  waiting for transfers between devices: 144 us -> 221 us
  starting transfers between devices: 58.4 us -> 28 us
  local copies, waits for them, and re-layouts: 54 us -> 38.8 us
  Pallas kernels: 42.5 us -> 29.8 us
  other arithmetic: 8.96 us -> 3.58 us
    ppermute x4 -> x2, waiting for transfers between devices: 46.2 us -> 137 us  [exchange(): from_prev = lax.ppermute(own, 'layer', shift(nl, 1))]
    ppermute x3, waiting for transfers between devices: 66 us -> 10.7 us  [shards(): lax.ppermute(lax.dynamic_index_in_dim(p_split, dest, 0, keepdims=False),...]
    ppermute x4 -> x2, waiting for transfers between devices: 20.9 us -> 48.1 us  [exchange(): far_a = lax.ppermute(from_prev[:half], 'layer', shift(nl, 1))]
    ppermute x4 -> x2, starting transfers between devices: 20.2 us -> 7.24 us  [exchange(): hi = lax.ppermute(first, 'grid', shift(ng, ng - 1))]
    pallas_call x4 -> x2, Pallas kernels: 42.5 us -> 29.8 us  [own_rows(): pl.pallas_call(step_kernel, grid_spec=grid_spec, out_shape=jax.ShapeDtype...]
    ppermute x3, waiting for transfers between devices: 11.3 us -> 0.01 us  [shards(): lax.ppermute(lax.dynamic_index_in_dim(h_split, dest, 0, keepdims=False),...]
    ppermute x4 -> x2, waiting for transfers between devices: 0.01 us -> 10.9 us  [exchange(): far_b = lax.ppermute(from_next[half:], 'layer', shift(nl, nl - 1))]
    ppermute x4 -> x2, waiting for transfers between devices: 0.01 us -> 9.67 us  [exchange(): lo = lax.ppermute(last, 'grid', shift(ng, 1))]
  transfers between devices with their start and end apart: 30 -> 18, of which waited for: 10 -> 10; matrix products, arithmetic and copies ran while one was open for 17% -> 10% of each run, Pallas kernels for 10% -> 0%
where the time goes in v5:
time: 322 us
  waiting for transfers between devices  221 us (69%)
  local copies, waits for them, and re-layouts  38.8 us (12%)
  Pallas kernels  29.8 us (9%)
  starting transfers between devices  28 us (9%)
  other arithmetic  3.58 us (1%)
    ppermute x2, waiting for transfers between devices, exchange(): from_prev = lax.ppermute(own, 'layer', shift(nl, 1))  137 us
    ppermute x2, waiting for transfers between devices, exchange(): far_a = lax.ppermute(from_prev[:half], 'layer', shift(nl, 1))  48.1 us
    pallas_call x2, Pallas kernels, own_rows(): pl.pallas_call(step_kernel, grid_spec=grid_spec, out_shape=jax.ShapeDtype...  29.8 us
    unnamed x22, local copies, waits for them, and re-layouts  25.8 us
    ppermute x2, waiting for transfers between devices, exchange(): far_b = lax.ppermute(from_next[half:], 'layer', shift(nl, nl - 1))  10.9 us
    ppermute x3, waiting for transfers between devices, shards(): lax.ppermute(lax.dynamic_index_in_dim(p_split, dest, 0, keepdims=False),...  10.7 us
    ppermute x2, waiting for transfers between devices, exchange(): lo = lax.ppermute(last, 'grid', shift(ng, 1))  9.67 us
    ppermute x2, starting transfers between devices, exchange(): hi = lax.ppermute(first, 'grid', shift(ng, ng - 1))  7.24 us
  transfers between devices with their start and end apart: 18, of which 10 were waited for; matrix products, arithmetic and copies ran while one was open for 10% of the time, Pallas kernels for 0%

profile of v5, /device:TPU:0, one launch (start us, length us, event | category | flops | bytes accessed | tf_op | source)
XLA Modules:
  0.0 321.8 jit_solution(12172736741848627522)
XLA Ops:
  0.6 2.1 collective-permute-start.7
  2.7 2.2 collective-permute-start.6
  4.9 68.2 %collective-permute-done.7 = bf16[1024,1536]{1,0:T(8,128)(2,1)S(1)} collective-permute-done((bf16[1024,1536]{1,0:T(8,128)(2,1)}, bf16[1024,1536]{1,0:T(8,128)(2,1)S(1)}, u32[]{:S(2)}, u32[]{:S(2)}) %collective-permute-start.7) | collective-permute-done | bytes 3145760 | tf_op jit(solution)/shard_map/ppermute | solution.py:21
  73.2 1.7 copy-done.1
  76.1 1.7 copy-done.3
  79.0 3.2 %collective-permute-start.9 = (bf16[512,1536]{1,0:T(8,128)(2,1)}, bf16[512,1536]{1,0:T(8,128)(2,1)}, u32[]{:S(2)}, u32[]{:S(2)}) collective-permute-start(bf16[512,1536]{1,0:T(8,128)(2,1)} %slice.17), channel_id=1, source_target_pairs={{0,3},{1,0},{2,1},{3,2},{4,7},{5,4},{6,5},{7,6},{8,11},{9,8},{10,9... | collective-permute-start | bytes 4718600 | tf_op jit(solution)/shard_map/ppermute | solution.py:24
  82.2 2.9 dynamic-slice_bitcast_fusion.3
  85.1 2.0 collective-permute-start.4
  88.4 2.0 constant_dynamic-update-slice_fusion.4
  90.4 4.0 %constant_dynamic-update-slice_fusion.3 = (bf16[4096,1536]{1,0:T(8,128)(2,1)S(1)}, bf16[4608,1536]{1,0:T(8,128)(2,1)}) fusion(bf16[4096,1536]{1,0:T(8,128)(2,1)S(1)} %get-tuple-element.16, bf16[1024,1536]{1,0:T(8,128)(2,1)} %copy-done.3, bf16[4608,1536]{1,0:T(8,128)(2,1)} %get-tuple-element.17), kind=kLoop, calls=%fused_computation.8 | loop fusion | bytes 9437184
  94.4 20.4 %collective-permute-done.8 = bf16[512,1536]{1,0:T(8,128)(2,1)} collective-permute-done((bf16[512,1536]{1,0:T(8,128)(2,1)}, bf16[512,1536]{1,0:T(8,128)(2,1)}, u32[]{:S(2)}, u32[]{:S(2)}) %collective-permute-start.8) | collective-permute-done | bytes 1572896 | tf_op jit(solution)/shard_map/ppermute | solution.py:23
  114.9 2.8 constant_dynamic-update-slice_fusion.2
  117.6 10.9 %collective-permute-done.9 = bf16[512,1536]{1,0:T(8,128)(2,1)} collective-permute-done((bf16[512,1536]{1,0:T(8,128)(2,1)}, bf16[512,1536]{1,0:T(8,128)(2,1)}, u32[]{:S(2)}, u32[]{:S(2)}) %collective-permute-start.9) | collective-permute-done | bytes 1572896 | tf_op jit(solution)/shard_map/ppermute | solution.py:24
  128.6 2.8 constant_dynamic-update-slice_fusion.1
  131.4 2.1 constant_dynamic-update-slice_fusion
  134.7 5.2 %collective-permute-done = s32[8,2]{0,1:T(2,128)S(1)} collective-permute-done((s32[8,2]{0,1:T(2,128)S(1)}, s32[8,2]{0,1:T(2,128)S(1)}, u32[]{:S(2)}, u32[]{:S(2)}) %collective-permute-start) | collective-permute-done | bytes 96 | tf_op jit(solution)/shard_map/ppermute | solution.py:87
  141.1 3.9 %collective-permute-done.1 = s32[8,2]{0,1:T(2,128)S(1)} collective-permute-done((s32[8,2]{0,1:T(2,128)S(1)}, s32[8,2]{0,1:T(2,128)S(1)}, u32[]{:S(2)}, u32[]{:S(2)}) %collective-permute-start.1) | collective-permute-done | bytes 96 | tf_op jit(solution)/shard_map/ppermute | solution.py:87
  145.0 2.0 collective-permute-start.2
  148.6 2.2 collective-permute-start.11
  151.5 2.9 pad_maximum_fusion.h_ref
  155.5 4.8 %collective-permute-done.11 = bf16[256,1536]{1,0:T(8,128)(2,1)S(1)} collective-permute-done((bf16[256,1536]{1,0:T(8,128)(2,1)S(1)}, bf16[256,1536]{1,0:T(8,128)(2,1)S(1)}, u32[]{:S(2)}, u32[]{:S(2)}) %collective-permute-start.11) | collective-permute-done | bytes 786464 | tf_op jit(solution)/shard_map/ppermute | solution.py:33
  161.2 14.8 %shard_map.59 = bf16[1024,1536]{1,0:T(8,128)(2,1)} custom-call(s32[64]{0:T(128)} %compare_select_fusion.pos_ref, bf16[8,8,128,128]{3,2,1,0:T(8,128)(2,1)} %pad_maximum_fusion.h_ref, bf16[36,128,1536]{2,1,0:T(8,128)(2,1)} %bitcast.9.refs_0_.refs_1_.refs_2_.refs_3_.refs_4_.refs_5_.refs_6_.refs_7_, ...), custom_call_target="tpu_custom_call" | custom-call | tf_op jit(solution)/shard_map/pallas_call | solution.py:64
  176.0 3.2 %collective-permute-start.12 = (bf16[1024,1536]{1,0:T(8,128)(2,1)}, bf16[1024,1536]{1,0:T(8,128)(2,1)S(1)}, u32[]{:S(2)}, u32[]{:S(2)}) collective-permute-start(bf16[1024,1536]{1,0:T(8,128)(2,1)} %shard_map.59), channel_id=1, source_target_pairs={{0,3},{1,0},{2,1},{3,2},{4,7},{5,4},{6,5},{7,6},{8,11},{9,8},{10,9... | collective-permute-start | bytes 9437192 | tf_op jit(solution)/shard_map/ppermute | solution.py:22
  179.3 68.6 %collective-permute-done.13 = bf16[1024,1536]{1,0:T(8,128)(2,1)S(1)} collective-permute-done((bf16[1024,1536]{1,0:T(8,128)(2,1)}, bf16[1024,1536]{1,0:T(8,128)(2,1)S(1)}, u32[]{:S(2)}, u32[]{:S(2)}) %collective-permute-start.13) | collective-permute-done | bytes 3145760 | tf_op jit(solution)/shard_map/ppermute | solution.py:21
  248.2 3.3 %collective-permute-start.15 = (bf16[512,1536]{1,0:T(8,128)(2,1)S(1)}, bf16[512,1536]{1,0:T(8,128)(2,1)S(1)}, u32[]{:S(2)}, u32[]{:S(2)}) collective-permute-start(bf16[512,1536]{1,0:T(8,128)(2,1)S(1)} %slice.19), channel_id=1, source_target_pairs={{0,3},{1,0},{2,1},{3,2},{4,7},{5,4},{6,5},{7,6},{8,11},{9,8},{10,9... | collective-permute-start | bytes 4718600 | tf_op jit(solution)/shard_map/ppermute | solution.py:24
  251.5 3.9 %constant_dynamic-update-slice_fusion.16 = (bf16[4096,1536]{1,0:T(8,128)(2,1)S(1)}, bf16[4608,1536]{1,0:T(8,128)(2,1)}) fusion(bf16[1024,1536]{1,0:T(8,128)(2,1)} %shard_map.59), kind=kLoop, calls=%fused_computation.21 | loop fusion | bytes 9437184
  255.4 2.1 constant_dynamic-update-slice_fusion.15
  257.5 27.6 %collective-permute-done.14 = bf16[512,1536]{1,0:T(8,128)(2,1)S(1)} collective-permute-done((bf16[512,1536]{1,0:T(8,128)(2,1)S(1)}, bf16[512,1536]{1,0:T(8,128)(2,1)S(1)}, u32[]{:S(2)}, u32[]{:S(2)}) %collective-permute-start.14) | collective-permute-done | bytes 1572896 | tf_op jit(solution)/shard_map/ppermute | solution.py:23
  287.9 2.1 constant_dynamic-update-slice_fusion.12
  290.2 5.1 %collective-permute-start.17 = (bf16[256,1536]{1,0:T(8,128)(2,1)S(1)}, bf16[256,1536]{1,0:T(8,128)(2,1)S(1)}, u32[]{:S(2)}, u32[]{:S(2)}) collective-permute-start(bf16[256,1536]{1,0:T(8,128)(2,1)S(1)} %get-tuple-element.2), channel_id=1, source_target_pairs={{0,124},{4,0},{8,4},{12,8},{16,12},{20,16},{24,20},{28,24},{32,28}... | collective-permute-start | bytes 2359304 | tf_op jit(solution)/shard_map/ppermute | solution.py:33
  295.3 9.7 %collective-permute-done.16 = bf16[256,1536]{1,0:T(8,128)(2,1)S(1)} collective-permute-done((bf16[256,1536]{1,0:T(8,128)(2,1)S(1)}, bf16[256,1536]{1,0:T(8,128)(2,1)S(1)}, u32[]{:S(2)}, u32[]{:S(2)}) %collective-permute-start.16) | collective-permute-done | bytes 786464 | tf_op jit(solution)/shard_map/ppermute | solution.py:32
  306.9 14.9 %shard_map.60 = bf16[1024,1536]{1,0:T(8,128)(2,1)} custom-call(s32[64]{0:T(128)} %compare_select_fusion.pos_ref, bf16[8,8,128,128]{3,2,1,0:T(8,128)(2,1)} %pad_maximum_fusion.h_ref, bf16[36,128,1536]{2,1,0:T(8,128)(2,1)} %bitcast.10.refs_0_.refs_1_.refs_2_.refs_3_.refs_4_.refs_5_.refs_6_.refs_7_, ...), custom_call_target="tpu_custom_call" | custom-call | tf_op jit(solution)/shard_map/pallas_call | solution.py:64
  (47 shorter events, 15.6 us)
Async XLA Ops:
  0.6 87.7 %copy-start = (bf16[1024,1536]{1,0:T(8,128)(2,1)S(1)}, bf16[1024,1536]{1,0:T(8,128)(2,1)}, u32[]{:S(2)}) copy-start(bf16[1024,1536]{1,0:T(8,128)(2,1)} %refs_8_.3) | copy-start | bytes 9437188
  0.6 72.5 %collective-permute-start.7 = (bf16[1024,1536]{1,0:T(8,128)(2,1)}, bf16[1024,1536]{1,0:T(8,128)(2,1)S(1)}, u32[]{:S(2)}, u32[]{:S(2)}) collective-permute-start(bf16[1024,1536]{1,0:T(8,128)(2,1)} %refs_8_.3), channel_id=1, source_target_pairs={{0,1},{1,2},{2,3},{3,0},{4,5},{5,6},{6,7},{7,4},{8,9},{9,10},{10,1... | collective-permute-start | bytes 9437192 | tf_op jit(solution)/shard_map/ppermute | solution.py:21
  2.7 73.3 %collective-permute-start.6 = (bf16[1024,1536]{1,0:T(8,128)(2,1)}, bf16[1024,1536]{1,0:T(8,128)(2,1)S(1)}, u32[]{:S(2)}, u32[]{:S(2)}) collective-permute-start(bf16[1024,1536]{1,0:T(8,128)(2,1)} %refs_8_.3), channel_id=1, source_target_pairs={{0,3},{1,0},{2,1},{3,2},{4,7},{5,4},{6,5},{7,6},{8,11},{9,8},{10,9... | collective-permute-start | bytes 9437192 | tf_op jit(solution)/shard_map/ppermute | solution.py:22
  73.2 1.7 copy-start.1
  76.1 38.8 %collective-permute-start.8 = (bf16[512,1536]{1,0:T(8,128)(2,1)}, bf16[512,1536]{1,0:T(8,128)(2,1)}, u32[]{:S(2)}, u32[]{:S(2)}) collective-permute-start(bf16[512,1536]{1,0:T(8,128)(2,1)} %slice.16), channel_id=1, source_target_pairs={{0,1},{1,2},{2,3},{3,0},{4,5},{5,6},{6,7},{7,4},{8,9},{9,10},{10,1... | collective-permute-start | bytes 4718600 | tf_op jit(solution)/shard_map/ppermute | solution.py:23
  76.1 1.7 copy-start.3
  79.0 49.6 %collective-permute-start.9 = (bf16[512,1536]{1,0:T(8,128)(2,1)}, bf16[512,1536]{1,0:T(8,128)(2,1)}, u32[]{:S(2)}, u32[]{:S(2)}) collective-permute-start(bf16[512,1536]{1,0:T(8,128)(2,1)} %slice.17), channel_id=1, source_target_pairs={{0,3},{1,0},{2,1},{3,2},{4,7},{5,4},{6,5},{7,6},{8,11},{9,8},{10,9... | collective-permute-start | bytes 4718600 | tf_op jit(solution)/shard_map/ppermute | solution.py:24
  85.1 66.4 %collective-permute-start.3 = (bf16[8,2,128,128]{3,2,1,0:T(8,128)(2,1)}, bf16[8,2,128,128]{3,2,1,0:T(8,128)(2,1)}, u32[]{:S(2)}, u32[]{:S(2)}) collective-permute-start(bf16[8,2,128,128]{3,2,1,0:T(8,128)(2,1)} %get-tuple-element.21), channel_id=1, source_target_pairs={{0,1},{1,2},{2,3},{3,0},{4,5},{5,6},{6,7},{7,4},{8,9},{9,10},{10,1... | collective-permute-start | bytes 1572872 | tf_op jit(solution)/shard_map/ppermute | solution.py:86
  85.1 66.4 %collective-permute-start.4 = (bf16[8,2,128,128]{3,2,1,0:T(8,128)(2,1)}, bf16[8,2,128,128]{3,2,1,0:T(8,128)(2,1)}, u32[]{:S(2)}, u32[]{:S(2)}) collective-permute-start(bf16[8,2,128,128]{3,2,1,0:T(8,128)(2,1)} %get-tuple-element.20), channel_id=1, source_target_pairs={{0,2},{1,3},{2,0},{3,1},{4,6},{5,7},{6,4},{7,5},{8,10},{9,11},{10,... | collective-permute-start | bytes 1572872 | tf_op jit(solution)/shard_map/ppermute | solution.py:86
  87.1 64.4 %collective-permute-start.5 = (bf16[8,2,128,128]{3,2,1,0:T(8,128)(2,1)}, bf16[8,2,128,128]{3,2,1,0:T(8,128)(2,1)}, u32[]{:S(2)}, u32[]{:S(2)}) collective-permute-start(bf16[8,2,128,128]{3,2,1,0:T(8,128)(2,1)} %get-tuple-element.19), channel_id=1, source_target_pairs={{0,3},{1,0},{2,1},{3,2},{4,7},{5,4},{6,5},{7,6},{8,11},{9,8},{10,9... | collective-permute-start | bytes 1572872 | tf_op jit(solution)/shard_map/ppermute | solution.py:86
  88.3 43.0 %copy-start.2 = (bf16[1024,1536]{1,0:T(8,128)(2,1)S(1)}, bf16[1024,1536]{1,0:T(8,128)(2,1)}, u32[]{:S(2)}) copy-start(bf16[1024,1536]{1,0:T(8,128)(2,1)} %copy-done.1) | copy-start | bytes 9437188
  94.4 40.0 %copy-start.5 = (s32[32,2]{0,1:T(2,128)S(1)}, s32[32,2]{0,1:T(2,128)}, u32[]{:S(2)}) copy-start(s32[32,2]{0,1:T(2,128)} %param.5) | copy-start | bytes 772
  94.4 57.1 %copy-start.4 = (bf16[8,2,128,128]{3,2,1,0:T(8,128)(2,1)S(1)}, bf16[8,2,128,128]{3,2,1,0:T(8,128)(2,1)}, u32[]{:S(2)}) copy-start(bf16[8,2,128,128]{3,2,1,0:T(8,128)(2,1)} %get-tuple-element.18) | copy-start | bytes 1572868
  134.5 20.0 %collective-permute-start.10 = (bf16[256,1536]{1,0:T(8,128)(2,1)}, bf16[256,1536]{1,0:T(8,128)(2,1)S(1)}, u32[]{:S(2)}, u32[]{:S(2)}) collective-permute-start(bf16[256,1536]{1,0:T(8,128)(2,1)} %get-tuple-element.5), channel_id=1, source_target_pairs={{0,4},{4,8},{8,12},{12,16},{16,20},{20,24},{24,28},{28,32},{32,36}... | collective-permute-start | bytes 2359304 | tf_op jit(solution)/shard_map/ppermute | solution.py:32
  134.6 5.3 %collective-permute-start = (s32[8,2]{0,1:T(2,128)S(1)}, s32[8,2]{0,1:T(2,128)S(1)}, u32[]{:S(2)}, u32[]{:S(2)}) collective-permute-start(s32[8,2]{0,1:T(2,128)S(1)} %bitcast.21), channel_id=1, source_target_pairs={{0,1},{1,2},{2,3},{3,0},{4,5},{5,6},{6,7},{7,4},{8,9},{9,10},{10,1... | collective-permute-start | bytes 200 | tf_op jit(solution)/shard_map/ppermute | solution.py:87
  139.9 5.1 %collective-permute-start.1 = (s32[8,2]{0,1:T(2,128)S(1)}, s32[8,2]{0,1:T(2,128)S(1)}, u32[]{:S(2)}, u32[]{:S(2)}) collective-permute-start(s32[8,2]{0,1:T(2,128)S(1)} %bitcast.20), channel_id=1, source_target_pairs={{0,2},{1,3},{2,0},{3,1},{4,6},{5,7},{6,4},{7,5},{8,10},{9,11},{10,... | collective-permute-start | bytes 200 | tf_op jit(solution)/shard_map/ppermute | solution.py:87
  145.0 3.6 %collective-permute-start.2 = (s32[8,2]{0,1:T(2,128)S(1)}, s32[8,2]{0,1:T(2,128)S(1)}, u32[]{:S(2)}, u32[]{:S(2)}) collective-permute-start(s32[8,2]{0,1:T(2,128)S(1)} %bitcast.19), channel_id=1, source_target_pairs={{0,3},{1,0},{2,1},{3,2},{4,7},{5,4},{6,5},{7,6},{8,11},{9,8},{10,9... | collective-permute-start | bytes 200 | tf_op jit(solution)/shard_map/ppermute | solution.py:87
  148.6 11.7 %collective-permute-start.11 = (bf16[256,1536]{1,0:T(8,128)(2,1)S(1)}, bf16[256,1536]{1,0:T(8,128)(2,1)S(1)}, u32[]{:S(2)}, u32[]{:S(2)}) collective-permute-start(bf16[256,1536]{1,0:T(8,128)(2,1)S(1)} %get-tuple-element.4), channel_id=1, source_target_pairs={{0,124},{4,0},{8,4},{12,8},{16,12},{20,16},{24,20},{28,24},{32,28}... | collective-permute-start | bytes 2359304 | tf_op jit(solution)/shard_map/ppermute | solution.py:33
  176.0 71.9 %collective-permute-start.13 = (bf16[1024,1536]{1,0:T(8,128)(2,1)}, bf16[1024,1536]{1,0:T(8,128)(2,1)S(1)}, u32[]{:S(2)}, u32[]{:S(2)}) collective-permute-start(bf16[1024,1536]{1,0:T(8,128)(2,1)} %shard_map.59), channel_id=1, source_target_pairs={{0,1},{1,2},{2,3},{3,0},{4,5},{5,6},{6,7},{7,4},{8,9},{9,10},{10,1... | collective-permute-start | bytes 9437192 | tf_op jit(solution)/shard_map/ppermute | solution.py:21
  176.0 72.0 %collective-permute-start.12 = (bf16[1024,1536]{1,0:T(8,128)(2,1)}, bf16[1024,1536]{1,0:T(8,128)(2,1)S(1)}, u32[]{:S(2)}, u32[]{:S(2)}) collective-permute-start(bf16[1024,1536]{1,0:T(8,128)(2,1)} %shard_map.59), channel_id=1, source_target_pairs={{0,3},{1,0},{2,1},{3,2},{4,7},{5,4},{6,5},{7,6},{8,11},{9,8},{10,9... | collective-permute-start | bytes 9437192 | tf_op jit(solution)/shard_map/ppermute | solution.py:22
  248.0 37.2 %collective-permute-start.14 = (bf16[512,1536]{1,0:T(8,128)(2,1)S(1)}, bf16[512,1536]{1,0:T(8,128)(2,1)S(1)}, u32[]{:S(2)}, u32[]{:S(2)}) collective-permute-start(bf16[512,1536]{1,0:T(8,128)(2,1)S(1)} %slice.18), channel_id=1, source_target_pairs={{0,1},{1,2},{2,3},{3,0},{4,5},{5,6},{6,7},{7,4},{8,9},{9,10},{10,1... | collective-permute-start | bytes 4718600 | tf_op jit(solution)/shard_map/ppermute | solution.py:23
  248.2 38.3 %collective-permute-start.15 = (bf16[512,1536]{1,0:T(8,128)(2,1)S(1)}, bf16[512,1536]{1,0:T(8,128)(2,1)S(1)}, u32[]{:S(2)}, u32[]{:S(2)}) collective-permute-start(bf16[512,1536]{1,0:T(8,128)(2,1)S(1)} %slice.19), channel_id=1, source_target_pairs={{0,3},{1,0},{2,1},{3,2},{4,7},{5,4},{6,5},{7,6},{8,11},{9,8},{10,9... | collective-permute-start | bytes 4718600 | tf_op jit(solution)/shard_map/ppermute | solution.py:24
  290.1 14.8 %collective-permute-start.16 = (bf16[256,1536]{1,0:T(8,128)(2,1)S(1)}, bf16[256,1536]{1,0:T(8,128)(2,1)S(1)}, u32[]{:S(2)}, u32[]{:S(2)}) collective-permute-start(bf16[256,1536]{1,0:T(8,128)(2,1)S(1)} %get-tuple-element.3), channel_id=1, source_target_pairs={{0,4},{4,8},{8,12},{12,16},{16,20},{20,24},{24,28},{28,32},{32,36}... | collective-permute-start | bytes 2359304 | tf_op jit(solution)/shard_map/ppermute | solution.py:32
  290.2 15.7 %collective-permute-start.17 = (bf16[256,1536]{1,0:T(8,128)(2,1)S(1)}, bf16[256,1536]{1,0:T(8,128)(2,1)S(1)}, u32[]{:S(2)}, u32[]{:S(2)}) collective-permute-start(bf16[256,1536]{1,0:T(8,128)(2,1)S(1)} %get-tuple-element.2), channel_id=1, source_target_pairs={{0,124},{4,0},{8,4},{12,8},{16,12},{20,16},{24,20},{28,24},{32,28}... | collective-permute-start | bytes 2359304 | tf_op jit(solution)/shard_map/ppermute | solution.py:33

commit v6 on v5

--- a/solution.py
+++ b/solution.py
@@ -18,43 +18,50 @@
     nl = lax.axis_size("layer")
     ng = lax.axis_size("grid")
     half = own.shape[0] // 2
+    width = HB * block_size
     from_prev = lax.ppermute(own, "layer", shift(nl, 1))
     from_next = lax.ppermute(own, "layer", shift(nl, nl - 1))
     far_a = lax.ppermute(from_prev[:half], "layer", shift(nl, 1))
     far_b = lax.ppermute(from_next[half:], "layer", shift(nl, nl - 1))
-    panel = jnp.concatenate([own, from_next, far_a, far_b, from_prev], axis=0)
-    rows = own.shape[0]
-    width = HB * block_size
-    last_at = ((nl - 1 - lidx) % nl) * rows + rows - width
-    first_at = ((0 - lidx) % nl) * rows
-    last = lax.dynamic_slice_in_dim(panel, last_at, width, axis=0)
-    first = lax.dynamic_slice_in_dim(panel, first_at, width, axis=0)
+    tails = jnp.concatenate([a[-width:] for a in (own, from_next, far_b, from_prev)], axis=0)
+    heads = jnp.concatenate([a[:width] for a in (own, from_next, far_a, from_prev)], axis=0)
+    last = lax.dynamic_slice_in_dim(tails, ((nl - 1 - lidx) % nl) * width, width, axis=0)
+    first = lax.dynamic_slice_in_dim(heads, ((0 - lidx) % nl) * width, width, axis=0)
     lo = lax.ppermute(last, "grid", shift(ng, 1))
     hi = lax.ppermute(first, "grid", shift(ng, ng - 1))
-    return jnp.concatenate([panel, lo, hi], axis=0)
+    near = jnp.concatenate([own, from_next, from_prev], axis=0)
+    far = jnp.concatenate([far_a, far_b, lo, hi], axis=0)
+    return near, far
 
 
-def step_kernel(pos_ref, h_ref, *refs):
+def near_kernel(pos_ref, h_ref, *refs):
     slots = h_ref.shape[1]
-    panel_refs, prev_ref, out_ref = refs[:slots], refs[slots], refs[slots + 1]
+    panel_refs, out_ref = refs[:slots], refs[slots]
     acc = jnp.dot(h_ref[0, 0], panel_refs[0][0], preferred_element_type=jnp.float32)
     for s in range(1, slots):
+        acc = acc + jnp.dot(h_ref[0, s], panel_refs[s][0], preferred_element_type=jnp.float32)
+    out_ref[...] = acc
+
+
+def far_kernel(pos_ref, h_ref, *refs):
+    slots = h_ref.shape[1]
+    panel_refs, acc_ref, prev_ref, out_ref = refs[:slots], refs[slots], refs[slots + 1], refs[slots + 2]
+    acc = acc_ref[...]
+    for s in range(slots):
         acc = acc + jnp.dot(h_ref[0, s], panel_refs[s][0], preferred_element_type=jnp.float32)
     out_ref[...] = (2.0 * acc - prev_ref[...].astype(jnp.float32)).astype(out_ref.dtype)
 
 
-def own_rows(h_own, pos_flat, chunk, previous, lidx):
-    rows, slots, block_size = h_own.shape[0], h_own.shape[1], h_own.shape[2]
-    width = chunk.shape[1]
-    wide = exchange(chunk, lidx, block_size)
-    blocks = wide.reshape(wide.shape[0] // block_size, block_size, width)
+def picked_call(kernel, pos_flat, h_part, blocks, extra, out_dtype):
+    rows, slots, block_size = h_part.shape[0], h_part.shape[1], h_part.shape[2]
+    width = blocks.shape[2]
 
     def panel_map(s):
         return lambda i, p: (p[i * slots + s], 0, 0)
 
     in_specs = [pl.BlockSpec((1, slots, block_size, block_size), lambda i, p: (i, 0, 0, 0))]
     in_specs += [pl.BlockSpec((1, block_size, width), panel_map(s)) for s in range(slots)]
-    in_specs += [pl.BlockSpec((block_size, width), lambda i, p: (i, 0))]
+    in_specs += [pl.BlockSpec((block_size, width), lambda i, p: (i, 0)) for _ in extra]
     grid_spec = pltpu.PrefetchScalarGridSpec(
         num_scalar_prefetch=1,
         grid=(rows,),
@@ -62,10 +69,29 @@
         out_specs=pl.BlockSpec((block_size, width), lambda i, p: (i, 0)),
     )
     return pl.pallas_call(
-        step_kernel,
+        kernel,
         grid_spec=grid_spec,
-        out_shape=jax.ShapeDtypeStruct(chunk.shape, jnp.bfloat16),
-    )(pos_flat, h_own, *([blocks] * slots), previous)
+        out_shape=jax.ShapeDtypeStruct((rows * block_size, width), out_dtype),
+    )(pos_flat, h_part, *([blocks] * slots), *extra)
+
+
+def own_rows(parts, chunk, previous, lidx):
+    (h_near, near_pos), (h_far, far_pos) = parts
+    block_size = h_near.shape[2]
+    width = chunk.shape[1]
+    near, far = exchange(chunk, lidx, block_size)
+    near = near.reshape(near.shape[0] // block_size, block_size, width)
+    far = far.reshape(far.shape[0] // block_size, block_size, width)
+    acc = picked_call(near_kernel, near_pos, h_near, near, [], jnp.float32)
+    return picked_call(far_kernel, far_pos, h_far, far, [acc, previous], jnp.bfloat16)
+
+
+def carried(valid, pos):
+    out, last = [], jnp.zeros_like(pos[0])
+    for i in range(pos.shape[0]):
+        last = jnp.where(valid[i], pos[i], last)
+        out.append(last)
+    return jnp.stack(out).reshape(-1).astype(jnp.int32)
 
 
 def shards(h_blocks, block_cols, t_now, t_prev):
@@ -93,14 +119,23 @@
     pos_own = jnp.where(rel_own < HB, nl * per_dev + rel_own, pos_own)
     pos_own = jnp.where(rel_own >= HB + group_rows, rel_own, pos_own)
 
-    pos_flat = pos_own.reshape(-1).astype(jnp.int32)
+    is_near = (pos_own < 2 * per_dev) | ((pos_own >= 3 * per_dev) & (pos_own < nl * per_dev))
+    near_pos = jnp.where(pos_own < 2 * per_dev, pos_own, pos_own - per_dev)
+    near_pos = jnp.where(is_near, near_pos, 0)
+    far_pos = jnp.where(pos_own >= nl * per_dev, pos_own - 3 * per_dev, pos_own - 2 * per_dev)
+    far_pos = jnp.where(is_near, 0, far_pos)
+    zero = jnp.zeros((), h_own.dtype)
+    parts = (
+        (jnp.where(is_near[:, :, None, None], h_own, zero), carried(is_near, near_pos)),
+        (jnp.where(is_near[:, :, None, None], zero, h_own), carried(~is_near, far_pos)),
+    )
     width = t_now.shape[1]
     step = width // NCH
 
     def recur(current, previous):
         outs = []
         for c in range(NCH):
-            outs.append(own_rows(h_own, pos_flat, current[c], previous[c], lidx))
+            outs.append(own_rows(parts, current[c], previous[c], lidx))
         return outs
 
     now_chunks = [t_now[:, c * step:(c + 1) * step] for c in range(NCH)]

time: 322 us -> 344 us (1.068)
  other arithmetic: 3.58 us -> 38.7 us
  Pallas kernels: 29.8 us -> 59.6 us
  waiting for transfers between devices: 221 us -> 193 us
  local copies, waits for them, and re-layouts: 38.8 us -> 17.2 us
  starting transfers between devices: 28 us -> 32.8 us
    ppermute x2, waiting for transfers between devices: 137 us -> 0.01 us  [exchange(): from_prev = lax.ppermute(own, 'layer', shift(nl, 1))]
    ppermute x2, waiting for transfers between devices: 0.01 us -> 64.7 us  [exchange(): from_next = lax.ppermute(own, 'layer', shift(nl, nl - 1))]
    ppermute x3, waiting for transfers between devices: 10.7 us -> 58.5 us  [shards(): lax.ppermute(lax.dynamic_index_in_dim(p_split, dest, 0, keepdims=False),...]
    ppermute x2, waiting for transfers between devices: 48.1 us -> 0.89 us  [exchange(): far_a = lax.ppermute(from_prev[:half], 'layer', shift(nl, 1))]
    ppermute x2, waiting for transfers between devices: 10.9 us -> 52.4 us  [exchange(): far_b = lax.ppermute(from_next[half:], 'layer', shift(nl, nl - 1))]
    concatenate x2 -> x8, other arithmetic: 2.96 us -> 34.4 us  [the longest x2 13.1 us: exchange(): far = jnp.concatenate([far_a, far_b, lo, hi], axis=0)]
    pallas_call x2 -> x4, Pallas kernels: 29.8 us -> 59.6 us  [picked_call(): pl.pallas_call(kernel, grid_spec=grid_spec, out_shape=jax.ShapeDtypeStruc...]
    unnamed x22, local copies, waits for them, and re-layouts: 25.8 us -> 2.27 us
  transfers between devices with their start and end apart: 18 -> 18, of which waited for: 10 -> 7; matrix products, arithmetic and copies ran while one was open for 10% -> 12% of each run, Pallas kernels for 0% -> 9%
where the time goes in v6:
time: 344 us; the launch traced here: 342 us
  waiting for transfers between devices  193 us (56%)
  Pallas kernels  59.6 us (17%)
  other arithmetic  38.7 us (11%)
  starting transfers between devices  32.8 us (10%)
  local copies, waits for them, and re-layouts  17.2 us (5%)
    ppermute x2, waiting for transfers between devices, exchange(): from_next = lax.ppermute(own, 'layer', shift(nl, nl - 1))  64.7 us
    pallas_call x4, Pallas kernels, picked_call(): pl.pallas_call(kernel, grid_spec=grid_spec, out_shape=jax.ShapeDtypeStruc...  59.6 us
    ppermute x3, waiting for transfers between devices, shards(): lax.ppermute(lax.dynamic_index_in_dim(p_split, dest, 0, keepdims=False),...  58.5 us
    ppermute x2, waiting for transfers between devices, exchange(): far_b = lax.ppermute(from_next[half:], 'layer', shift(nl, nl - 1))  52.4 us
    ppermute x3, waiting for transfers between devices, shards(): lax.ppermute(lax.dynamic_index_in_dim(h_split, dest, 0, keepdims=False),...  16 us
    concatenate x2, other arithmetic, exchange(): far = jnp.concatenate([far_a, far_b, lo, hi], axis=0)  13.1 us
    concatenate x2, other arithmetic, exchange(): near = jnp.concatenate([own, from_next, from_prev], axis=0)  11.5 us
    ppermute x2, starting transfers between devices, exchange(): hi = lax.ppermute(first, 'grid', shift(ng, ng - 1))  9.24 us
  transfers between devices with their start and end apart: 18, of which 7 were waited for; matrix products, arithmetic and copies ran while one was open for 12% of the time, Pallas kernels for 9%

profile of v6, /device:TPU:0, one launch (start us, length us, event | category | flops | bytes accessed | tf_op | source)
XLA Modules:
  0.0 341.7 jit_solution(550123288597479185)
XLA Ops:
  0.6 4.2 %collective-permute-start.8 = (bf16[1024,1536]{1,0:T(8,128)(2,1)}, bf16[1024,1536]{1,0:T(8,128)(2,1)}, u32[]{:S(2)}, u32[]{:S(2)}) collective-permute-start(bf16[1024,1536]{1,0:T(8,128)(2,1)} %refs_9_.3), channel_id=1, source_target_pairs={{0,3},{1,0},{2,1},{3,2},{4,7},{5,4},{6,5},{7,6},{8,11},{9,8},{10,9... | collective-permute-start | bytes 9437192 | tf_op jit(solution)/shard_map/ppermute | solution.py:23
  5.7 3.3 collective-permute-start.2
  9.9 2.9 dynamic-slice_bitcast_fusion.3
  14.1 58.5 %collective-permute-done.2 = s32[8,2]{0,1:T(2,128)S(1)} collective-permute-done((s32[8,2]{0,1:T(2,128)S(1)}, s32[8,2]{0,1:T(2,128)S(1)}, u32[]{:S(2)}, u32[]{:S(2)}) %collective-permute-start.2) | collective-permute-done | bytes 96 | tf_op jit(solution)/shard_map/ppermute | solution.py:113
  72.6 3.7 %collective-permute-start.5 = (bf16[8,2,128,128]{3,2,1,0:T(8,128)(2,1)}, bf16[8,2,128,128]{3,2,1,0:T(8,128)(2,1)}, u32[]{:S(2)}, u32[]{:S(2)}) collective-permute-start(bf16[8,2,128,128]{3,2,1,0:T(8,128)(2,1)} %get-tuple-element.36), channel_id=1, source_target_pairs={{0,3},{1,0},{2,1},{3,2},{4,7},{5,4},{6,5},{7,6},{8,11},{9,8},{10,9... | collective-permute-start | bytes 1572872 | tf_op jit(solution)/shard_map/ppermute | solution.py:112
  77.3 2.7 slice.209
  79.9 2.6 collective-permute-start.9
  84.2 1.6 slice.208
  85.9 14.2 %collective-permute-done.5 = bf16[8,2,128,128]{3,2,1,0:T(8,128)(2,1)} collective-permute-done((bf16[8,2,128,128]{3,2,1,0:T(8,128)(2,1)}, bf16[8,2,128,128]{3,2,1,0:T(8,128)(2,1)}, u32[]{:S(2)}, u32[]{:S(2)}) %collective-permute-start.5) | collective-permute-done | bytes 524320 | tf_op jit(solution)/shard_map/ppermute | solution.py:112
  100.1 1.8 collective-permute-done.3
  102.0 3.4 broadcast_select_fusion
  105.3 1.5 fusion.24
  106.8 1.5 fusion.23
  108.4 23.5 %collective-permute-done.9 = bf16[512,1536]{1,0:T(8,128)(2,1)} collective-permute-done((bf16[512,1536]{1,0:T(8,128)(2,1)}, bf16[512,1536]{1,0:T(8,128)(2,1)}, u32[]{:S(2)}, u32[]{:S(2)}) %collective-permute-start.9) | collective-permute-done | bytes 1572896 | tf_op jit(solution)/shard_map/ppermute | solution.py:25
  133.1 2.5 fusion.11
  136.8 2.5 fusion.8
  139.3 5.1 %collective-permute-start.11 = (bf16[256,1536]{1,0:T(8,128)(2,1)}, bf16[256,1536]{1,0:T(8,128)(2,1)}, u32[]{:S(2)}, u32[]{:S(2)}) collective-permute-start(bf16[256,1536]{1,0:T(8,128)(2,1)} %fusion.8), channel_id=1, source_target_pairs={{0,124},{4,0},{8,4},{12,8},{16,12},{20,16},{24,20},{28,24},{32,28}... | collective-permute-start | bytes 2359304 | tf_op jit(solution)/shard_map/ppermute | solution.py:31
  144.3 7.1 %pad_maximum_fusion = bf16[3072,1536]{1,0:T(8,128)(2,1)} fusion(bf16[1024,1536]{1,0:T(8,128)(2,1)} %collective-permute-done.6, bf16[1024,1536]{1,0:T(8,128)(2,1)} %collective-permute-done.8, bf16[1024,1536]{1,0:T(8,128)(2,1)S(1)} %copy-done), kind=kLoop, calls=%fused_computation | loop fusion | flops 28311552 | bytes 18874368 | tf_op jit(solution)/shard_map/concatenate | solution.py:32
  151.4 14.8 %shard_map.59.refs_8_ = f32[1024,1536]{1,0:T(8,128)} custom-call(s32[64]{0:T(128)} %reshape.208.pos_ref, bf16[8,8,128,128]{3,2,1,0:T(8,128)(2,1)} %get-tuple-element.33.h_ref, bf16[24,128,1536]{2,1,0:T(8,128)(2,1)} %bitcast.27, bf16[24,128,1536]{2,1,0:T(8,128)(2,1)} %bitcast.28, bf16[24,128,1536]{2,1,0:T(8,128)(2,1)} %bitcast.29, ...), custom_call_target="tpu_custom_call" | custom-call | tf_op jit(solution)/shard_map/pallas_call | solution.py:71
  166.2 4.7 %pad_maximum_fusion.2 = bf16[1536,1536]{1,0:T(8,128)(2,1)} fusion(bf16[256,1536]{1,0:T(8,128)(2,1)} %collective-permute-done.11, bf16[256,1536]{1,0:T(8,128)(2,1)} %collective-permute-done.10, bf16[512,1536]{1,0:T(8,128)(2,1)} %collective-permute-done.9, bf16[512,1536]{1,0:T(8,128)(2,1)S(1)} %copy-done.3), kind=kLoop, calls=%fused_computation.2 | loop fusion | flops 18874368 | bytes 9437184 | tf_op jit(solution)/shard_map/concatenate | solution.py:33
  170.9 15.1 %shard_map.60 = bf16[1024,1536]{1,0:T(8,128)(2,1)} custom-call(s32[64]{0:T(128)} %reshape.205.pos_ref, bf16[8,8,128,128]{3,2,1,0:T(8,128)(2,1)} %get-tuple-element.34.h_ref, bf16[12,128,1536]{2,1,0:T(8,128)(2,1)} %bitcast.43, bf16[12,128,1536]{2,1,0:T(8,128)(2,1)} %bitcast.44, bf16[12,128,1536]{2,1,0:T(8,128)(2,1)} %bitcast.45, ...), custom_call_target="tpu_custom_call" | custom-call | tf_op jit(solution)/shard_map/pallas_call | solution.py:71
  186.0 4.1 %collective-permute-start.14 = (bf16[1024,1536]{1,0:T(8,128)(2,1)}, bf16[1024,1536]{1,0:T(8,128)(2,1)S(1)}, u32[]{:S(2)}, u32[]{:S(2)}) collective-permute-start(bf16[1024,1536]{1,0:T(8,128)(2,1)} %shard_map.60), channel_id=1, source_target_pairs={{0,3},{1,0},{2,1},{3,2},{4,7},{5,4},{6,5},{7,6},{8,11},{9,8},{10,9... | collective-permute-start | bytes 9437192 | tf_op jit(solution)/shard_map/ppermute | solution.py:23
  190.1 64.7 %collective-permute-done.14 = bf16[1024,1536]{1,0:T(8,128)(2,1)S(1)} collective-permute-done((bf16[1024,1536]{1,0:T(8,128)(2,1)}, bf16[1024,1536]{1,0:T(8,128)(2,1)S(1)}, u32[]{:S(2)}, u32[]{:S(2)}) %collective-permute-start.14) | collective-permute-done | bytes 3145760 | tf_op jit(solution)/shard_map/ppermute | solution.py:23
  254.9 3.7 %collective-permute-start.15 = (bf16[512,1536]{1,0:T(8,128)(2,1)S(1)}, bf16[512,1536]{1,0:T(8,128)(2,1)S(1)}, u32[]{:S(2)}, u32[]{:S(2)}) collective-permute-start(bf16[512,1536]{1,0:T(8,128)(2,1)S(1)} %slice.217), channel_id=1, source_target_pairs={{0,3},{1,0},{2,1},{3,2},{4,7},{5,4},{6,5},{7,6},{8,11},{9,8},{10,9... | collective-permute-start | bytes 4718600 | tf_op jit(solution)/shard_map/ppermute | solution.py:25
  259.1 28.9 %collective-permute-done.15 = bf16[512,1536]{1,0:T(8,128)(2,1)S(1)} collective-permute-done((bf16[512,1536]{1,0:T(8,128)(2,1)S(1)}, bf16[512,1536]{1,0:T(8,128)(2,1)S(1)}, u32[]{:S(2)}, u32[]{:S(2)}) %collective-permute-start.15) | collective-permute-done | bytes 1572896 | tf_op jit(solution)/shard_map/ppermute | solution.py:25
  288.0 2.5 fusion.5
  292.6 2.4 fusion.2
  295.0 4.2 %collective-permute-start.17 = (bf16[256,1536]{1,0:T(8,128)(2,1)}, bf16[256,1536]{1,0:T(8,128)(2,1)}, u32[]{:S(2)}, u32[]{:S(2)}) collective-permute-start(bf16[256,1536]{1,0:T(8,128)(2,1)} %fusion.2), channel_id=1, source_target_pairs={{0,124},{4,0},{8,4},{12,8},{16,12},{20,16},{24,20},{28,24},{32,28}... | collective-permute-start | bytes 2359304 | tf_op jit(solution)/shard_map/ppermute | solution.py:31
  299.2 4.4 %pad_maximum_fusion.1 = bf16[3072,1536]{1,0:T(8,128)(2,1)} fusion(bf16[1024,1536]{1,0:T(8,128)(2,1)S(1)} %collective-permute-done.12, bf16[1024,1536]{1,0:T(8,128)(2,1)S(1)} %collective-permute-done.14, bf16[1024,1536]{1,0:T(8,128)(2,1)S(1)} %copy-done.1), kind=kLoop, calls=%fused_computation.1 | loop fusion | flops 28311552 | bytes 18874368 | tf_op jit(solution)/shard_map/concatenate | solution.py:32
  303.6 14.8 %shard_map.61.refs_8_ = f32[1024,1536]{1,0:T(8,128)} custom-call(s32[64]{0:T(128)} %reshape.208.pos_ref, bf16[8,8,128,128]{3,2,1,0:T(8,128)(2,1)} %get-tuple-element.33.h_ref, bf16[24,128,1536]{2,1,0:T(8,128)(2,1)} %bitcast.19, bf16[24,128,1536]{2,1,0:T(8,128)(2,1)} %bitcast.20, bf16[24,128,1536]{2,1,0:T(8,128)(2,1)} %bitcast.21, ...), custom_call_target="tpu_custom_call" | custom-call | tf_op jit(solution)/shard_map/pallas_call | solution.py:71
  318.4 8.3 %pad_maximum_fusion.3 = bf16[1536,1536]{1,0:T(8,128)(2,1)} fusion(bf16[256,1536]{1,0:T(8,128)(2,1)} %collective-permute-done.17, bf16[256,1536]{1,0:T(8,128)(2,1)} %collective-permute-done.16, bf16[512,1536]{1,0:T(8,128)(2,1)S(1)} %copy-done.5, bf16[512,1536]{1,0:T(8,128)(2,1)S(1)} %copy-done.7), kind=kLoop, calls=%fused_computation.3 | loop fusion | flops 18874368 | bytes 9437184 | tf_op jit(solution)/shard_map/concatenate | solution.py:33
  326.7 15.0 %shard_map.62 = bf16[1024,1536]{1,0:T(8,128)(2,1)} custom-call(s32[64]{0:T(128)} %reshape.205.pos_ref, bf16[8,8,128,128]{3,2,1,0:T(8,128)(2,1)} %get-tuple-element.34.h_ref, bf16[12,128,1536]{2,1,0:T(8,128)(2,1)} %bitcast.35, bf16[12,128,1536]{2,1,0:T(8,128)(2,1)} %bitcast.36, bf16[12,128,1536]{2,1,0:T(8,128)(2,1)} %bitcast.37, ...), custom_call_target="tpu_custom_call" | custom-call | tf_op jit(solution)/shard_map/pallas_call | solution.py:71
  (69 shorter events, 10.9 us)
Async XLA Ops:
  0.6 12.2 %copy-start = (bf16[1024,1536]{1,0:T(8,128)(2,1)S(1)}, bf16[1024,1536]{1,0:T(8,128)(2,1)}, u32[]{:S(2)}) copy-start(bf16[1024,1536]{1,0:T(8,128)(2,1)} %refs_9_.3) | copy-start | bytes 9437188
  0.6 76.6 %collective-permute-start.8 = (bf16[1024,1536]{1,0:T(8,128)(2,1)}, bf16[1024,1536]{1,0:T(8,128)(2,1)}, u32[]{:S(2)}, u32[]{:S(2)}) collective-permute-start(bf16[1024,1536]{1,0:T(8,128)(2,1)} %refs_9_.3), channel_id=1, source_target_pairs={{0,3},{1,0},{2,1},{3,2},{4,7},{5,4},{6,5},{7,6},{8,11},{9,8},{10,9... | collective-permute-start | bytes 9437192 | tf_op jit(solution)/shard_map/ppermute | solution.py:23
  4.9 79.4 %collective-permute-start.6 = (bf16[1024,1536]{1,0:T(8,128)(2,1)}, bf16[1024,1536]{1,0:T(8,128)(2,1)}, u32[]{:S(2)}, u32[]{:S(2)}) collective-permute-start(bf16[1024,1536]{1,0:T(8,128)(2,1)} %refs_9_.3), channel_id=1, source_target_pairs={{0,1},{1,2},{2,3},{3,0},{4,5},{5,6},{6,7},{7,4},{8,9},{9,10},{10,1... | collective-permute-start | bytes 9437192 | tf_op jit(solution)/shard_map/ppermute | solution.py:22
  5.7 66.9 %collective-permute-start.2 = (s32[8,2]{0,1:T(2,128)S(1)}, s32[8,2]{0,1:T(2,128)S(1)}, u32[]{:S(2)}, u32[]{:S(2)}) collective-permute-start(s32[8,2]{0,1:T(2,128)S(1)} %bitcast.55), channel_id=1, source_target_pairs={{0,3},{1,0},{2,1},{3,2},{4,7},{5,4},{6,5},{7,6},{8,11},{9,8},{10,9... | collective-permute-start | bytes 200 | tf_op jit(solution)/shard_map/ppermute | solution.py:113
  9.0 67.3 %collective-permute-start.1 = (s32[8,2]{0,1:T(2,128)S(1)}, s32[8,2]{0,1:T(2,128)S(1)}, u32[]{:S(2)}, u32[]{:S(2)}) collective-permute-start(s32[8,2]{0,1:T(2,128)S(1)} %bitcast.54), channel_id=1, source_target_pairs={{0,2},{1,3},{2,0},{3,1},{4,6},{5,7},{6,4},{7,5},{8,10},{9,11},{10,... | collective-permute-start | bytes 200 | tf_op jit(solution)/shard_map/ppermute | solution.py:113
  9.0 67.5 %collective-permute-start = (s32[8,2]{0,1:T(2,128)S(1)}, s32[8,2]{0,1:T(2,128)S(1)}, u32[]{:S(2)}, u32[]{:S(2)}) collective-permute-start(s32[8,2]{0,1:T(2,128)S(1)} %bitcast.53), channel_id=1, source_target_pairs={{0,1},{1,2},{2,3},{3,0},{4,5},{5,6},{6,7},{7,4},{8,9},{9,10},{10,1... | collective-permute-start | bytes 200 | tf_op jit(solution)/shard_map/ppermute | solution.py:113
  72.6 27.6 %collective-permute-start.5 = (bf16[8,2,128,128]{3,2,1,0:T(8,128)(2,1)}, bf16[8,2,128,128]{3,2,1,0:T(8,128)(2,1)}, u32[]{:S(2)}, u32[]{:S(2)}) collective-permute-start(bf16[8,2,128,128]{3,2,1,0:T(8,128)(2,1)} %get-tuple-element.36), channel_id=1, source_target_pairs={{0,3},{1,0},{2,1},{3,2},{4,7},{5,4},{6,5},{7,6},{8,11},{9,8},{10,9... | collective-permute-start | bytes 1572872 | tf_op jit(solution)/shard_map/ppermute | solution.py:112
  76.3 23.9 %collective-permute-start.4 = (bf16[8,2,128,128]{3,2,1,0:T(8,128)(2,1)}, bf16[8,2,128,128]{3,2,1,0:T(8,128)(2,1)}, u32[]{:S(2)}, u32[]{:S(2)}) collective-permute-start(bf16[8,2,128,128]{3,2,1,0:T(8,128)(2,1)} %get-tuple-element.37), channel_id=1, source_target_pairs={{0,2},{1,3},{2,0},{3,1},{4,6},{5,7},{6,4},{7,5},{8,10},{9,11},{10,... | collective-permute-start | bytes 1572872 | tf_op jit(solution)/shard_map/ppermute | solution.py:112
  76.5 25.5 %collective-permute-start.3 = (bf16[8,2,128,128]{3,2,1,0:T(8,128)(2,1)}, bf16[8,2,128,128]{3,2,1,0:T(8,128)(2,1)}, u32[]{:S(2)}, u32[]{:S(2)}) collective-permute-start(bf16[8,2,128,128]{3,2,1,0:T(8,128)(2,1)} %get-tuple-element.38), channel_id=1, source_target_pairs={{0,1},{1,2},{2,3},{3,0},{4,5},{5,6},{6,7},{7,4},{8,9},{9,10},{10,1... | collective-permute-start | bytes 1572872 | tf_op jit(solution)/shard_map/ppermute | solution.py:112
  79.9 51.9 %collective-permute-start.9 = (bf16[512,1536]{1,0:T(8,128)(2,1)}, bf16[512,1536]{1,0:T(8,128)(2,1)}, u32[]{:S(2)}, u32[]{:S(2)}) collective-permute-start(bf16[512,1536]{1,0:T(8,128)(2,1)} %slice.209), channel_id=1, source_target_pairs={{0,3},{1,0},{2,1},{3,2},{4,7},{5,4},{6,5},{7,6},{8,11},{9,8},{10,9... | collective-permute-start | bytes 4718600 | tf_op jit(solution)/shard_map/ppermute | solution.py:25
  84.2 17.7 %copy-start.10 = (bf16[8,2,128,128]{3,2,1,0:T(8,128)(2,1)S(1)}, bf16[8,2,128,128]{3,2,1,0:T(8,128)(2,1)}, u32[]{:S(2)}) copy-start(bf16[8,2,128,128]{3,2,1,0:T(8,128)(2,1)} %get-tuple-element.35) | copy-start | bytes 1572868
  85.8 49.8 %collective-permute-start.7 = (bf16[512,1536]{1,0:T(8,128)(2,1)S(1)}, bf16[512,1536]{1,0:T(8,128)(2,1)S(1)}, u32[]{:S(2)}, u32[]{:S(2)}) collective-permute-start(bf16[512,1536]{1,0:T(8,128)(2,1)S(1)} %slice.208), channel_id=1, source_target_pairs={{0,1},{1,2},{2,3},{3,0},{4,5},{5,6},{6,7},{7,4},{8,9},{9,10},{10,1... | collective-permute-start | bytes 4718600 | tf_op jit(solution)/shard_map/ppermute | solution.py:24
  106.8 26.2 %copy-start.9 = (bf16[256,1536]{1,0:T(8,128)(2,1)S(1)}, bf16[256,1536]{1,0:T(8,128)(2,1)}, u32[]{:S(2)}) copy-start(bf16[256,1536]{1,0:T(8,128)(2,1)} %get-tuple-element.31) | copy-start | bytes 2359300
  133.0 3.8 %copy-start.8 = (bf16[256,1536]{1,0:T(8,128)(2,1)S(1)}, bf16[256,1536]{1,0:T(8,128)(2,1)}, u32[]{:S(2)}) copy-start(bf16[256,1536]{1,0:T(8,128)(2,1)} %get-tuple-element.32) | copy-start | bytes 2359300
  135.6 30.6 %collective-permute-start.10 = (bf16[256,1536]{1,0:T(8,128)(2,1)}, bf16[256,1536]{1,0:T(8,128)(2,1)}, u32[]{:S(2)}, u32[]{:S(2)}) collective-permute-start(bf16[256,1536]{1,0:T(8,128)(2,1)} %fusion.11), channel_id=1, source_target_pairs={{0,4},{4,8},{8,12},{12,16},{16,20},{20,24},{24,28},{28,32},{32,36}... | collective-permute-start | bytes 2359304 | tf_op jit(solution)/shard_map/ppermute | solution.py:30
  135.6 1.1 copy-start.2
  139.3 26.9 %collective-permute-start.11 = (bf16[256,1536]{1,0:T(8,128)(2,1)}, bf16[256,1536]{1,0:T(8,128)(2,1)}, u32[]{:S(2)}, u32[]{:S(2)}) collective-permute-start(bf16[256,1536]{1,0:T(8,128)(2,1)} %fusion.8), channel_id=1, source_target_pairs={{0,124},{4,0},{8,4},{12,8},{16,12},{20,16},{24,20},{28,24},{32,28}... | collective-permute-start | bytes 2359304 | tf_op jit(solution)/shard_map/ppermute | solution.py:31
  151.4 14.8 %copy-start.3 = (bf16[512,1536]{1,0:T(8,128)(2,1)S(1)}, bf16[512,1536]{1,0:T(8,128)(2,1)}, u32[]{:S(2)}) copy-start(bf16[512,1536]{1,0:T(8,128)(2,1)} %copy-done.2) | copy-start | bytes 4718596
  185.9 72.8 %copy-start.1 = (bf16[1024,1536]{1,0:T(8,128)(2,1)S(1)}, bf16[1024,1536]{1,0:T(8,128)(2,1)}, u32[]{:S(2)}) copy-start(bf16[1024,1536]{1,0:T(8,128)(2,1)} %shard_map.60) | copy-start | bytes 9437188
  186.0 68.8 %collective-permute-start.14 = (bf16[1024,1536]{1,0:T(8,128)(2,1)}, bf16[1024,1536]{1,0:T(8,128)(2,1)S(1)}, u32[]{:S(2)}, u32[]{:S(2)}) collective-permute-start(bf16[1024,1536]{1,0:T(8,128)(2,1)} %shard_map.60), channel_id=1, source_target_pairs={{0,3},{1,0},{2,1},{3,2},{4,7},{5,4},{6,5},{7,6},{8,11},{9,8},{10,9... | collective-permute-start | bytes 9437192 | tf_op jit(solution)/shard_map/ppermute | solution.py:23
  190.1 68.5 %collective-permute-start.12 = (bf16[1024,1536]{1,0:T(8,128)(2,1)}, bf16[1024,1536]{1,0:T(8,128)(2,1)S(1)}, u32[]{:S(2)}, u32[]{:S(2)}) collective-permute-start(bf16[1024,1536]{1,0:T(8,128)(2,1)} %shard_map.60), channel_id=1, source_target_pairs={{0,1},{1,2},{2,3},{3,0},{4,5},{5,6},{6,7},{7,4},{8,9},{9,10},{10,1... | collective-permute-start | bytes 9437192 | tf_op jit(solution)/shard_map/ppermute | solution.py:22
  254.9 33.1 %collective-permute-start.15 = (bf16[512,1536]{1,0:T(8,128)(2,1)S(1)}, bf16[512,1536]{1,0:T(8,128)(2,1)S(1)}, u32[]{:S(2)}, u32[]{:S(2)}) collective-permute-start(bf16[512,1536]{1,0:T(8,128)(2,1)S(1)} %slice.217), channel_id=1, source_target_pairs={{0,3},{1,0},{2,1},{3,2},{4,7},{5,4},{6,5},{7,6},{8,11},{9,8},{10,9... | collective-permute-start | bytes 4718600 | tf_op jit(solution)/shard_map/ppermute | solution.py:25
  258.6 32.8 %collective-permute-start.13 = (bf16[512,1536]{1,0:T(8,128)(2,1)S(1)}, bf16[512,1536]{1,0:T(8,128)(2,1)S(1)}, u32[]{:S(2)}, u32[]{:S(2)}) collective-permute-start(bf16[512,1536]{1,0:T(8,128)(2,1)S(1)} %slice.216), channel_id=1, source_target_pairs={{0,1},{1,2},{2,3},{3,0},{4,5},{5,6},{6,7},{7,4},{8,9},{9,10},{10,1... | collective-permute-start | bytes 4718600 | tf_op jit(solution)/shard_map/ppermute | solution.py:24
  288.0 3.5 %copy-start.4 = (bf16[512,1536]{1,0:T(8,128)(2,1)}, bf16[512,1536]{1,0:T(8,128)(2,1)S(1)}, u32[]{:S(2)}) copy-start(bf16[512,1536]{1,0:T(8,128)(2,1)S(1)} %collective-permute-done.15) | copy-start | bytes 4718596
  290.5 27.8 %collective-permute-start.16 = (bf16[256,1536]{1,0:T(8,128)(2,1)}, bf16[256,1536]{1,0:T(8,128)(2,1)}, u32[]{:S(2)}, u32[]{:S(2)}) collective-permute-start(bf16[256,1536]{1,0:T(8,128)(2,1)} %fusion.5), channel_id=1, source_target_pairs={{0,4},{4,8},{8,12},{12,16},{16,20},{20,24},{24,28},{28,32},{32,36}... | collective-permute-start | bytes 2359304 | tf_op jit(solution)/shard_map/ppermute | solution.py:30
  291.4 1.2 copy-start.6
  295.0 23.4 %collective-permute-start.17 = (bf16[256,1536]{1,0:T(8,128)(2,1)}, bf16[256,1536]{1,0:T(8,128)(2,1)}, u32[]{:S(2)}, u32[]{:S(2)}) collective-permute-start(bf16[256,1536]{1,0:T(8,128)(2,1)} %fusion.2), channel_id=1, source_target_pairs={{0,124},{4,0},{8,4},{12,8},{16,12},{20,16},{24,20},{28,24},{32,28}... | collective-permute-start | bytes 2359304 | tf_op jit(solution)/shard_map/ppermute | solution.py:31
  303.6 14.8 %copy-start.5 = (bf16[512,1536]{1,0:T(8,128)(2,1)S(1)}, bf16[512,1536]{1,0:T(8,128)(2,1)}, u32[]{:S(2)}) copy-start(bf16[512,1536]{1,0:T(8,128)(2,1)} %copy-done.4) | copy-start | bytes 4718596
  303.6 14.8 %copy-start.7 = (bf16[512,1536]{1,0:T(8,128)(2,1)S(1)}, bf16[512,1536]{1,0:T(8,128)(2,1)}, u32[]{:S(2)}) copy-start(bf16[512,1536]{1,0:T(8,128)(2,1)} %copy-done.6) | copy-start | bytes 4718596

commit v7 on v3

--- a/solution.py
+++ b/solution.py
@@ -18,20 +18,18 @@
     nl = lax.axis_size("layer")
     ng = lax.axis_size("grid")
     half = own.shape[0] // 2
+    width = HB * block_size
     from_prev = lax.ppermute(own, "layer", shift(nl, 1))
     from_next = lax.ppermute(own, "layer", shift(nl, nl - 1))
     far_a = lax.ppermute(from_prev[:half], "layer", shift(nl, 1))
     far_b = lax.ppermute(from_next[half:], "layer", shift(nl, nl - 1))
-    panel = jnp.concatenate([own, from_next, far_a, far_b, from_prev], axis=0)
-    rows = own.shape[0]
-    width = HB * block_size
-    last_at = ((nl - 1 - lidx) % nl) * rows + rows - width
-    first_at = ((0 - lidx) % nl) * rows
-    last = lax.dynamic_slice_in_dim(panel, last_at, width, axis=0)
-    first = lax.dynamic_slice_in_dim(panel, first_at, width, axis=0)
+    tails = jnp.concatenate([a[-width:] for a in (own, from_next, far_b, from_prev)], axis=0)
+    heads = jnp.concatenate([a[:width] for a in (own, from_next, far_a, from_prev)], axis=0)
+    last = lax.dynamic_slice_in_dim(tails, ((nl - 1 - lidx) % nl) * width, width, axis=0)
+    first = lax.dynamic_slice_in_dim(heads, ((0 - lidx) % nl) * width, width, axis=0)
     lo = lax.ppermute(last, "grid", shift(ng, 1))
     hi = lax.ppermute(first, "grid", shift(ng, ng - 1))
-    return jnp.concatenate([panel, lo, hi], axis=0)
+    return jnp.concatenate([own, from_next, far_a, far_b, from_prev, lo, hi], axis=0)
 
 
 def step_kernel(pos_ref, h_ref, *refs):

time: 311 us -> 362 us (1.16)
  starting transfers between devices: 58.4 us -> 80.7 us
  waiting for transfers between devices: 144 us -> 165 us
  other arithmetic: 8.96 us -> 18.5 us
    ppermute x3, starting transfers between devices: 4.23 us -> 34.8 us  [shards(): lax.ppermute(lax.dynamic_index_in_dim(h_split, dest, 0, keepdims=False),...]
    ppermute x4, waiting for transfers between devices: 0.01 us -> 20.4 us  [exchange(): far_b = lax.ppermute(from_next[half:], 'layer', shift(nl, nl - 1))]
    ppermute x4, waiting for transfers between devices: 20.9 us -> 4.65 us  [exchange(): far_a = lax.ppermute(from_prev[:half], 'layer', shift(nl, 1))]
    slice x0 -> x20, local copies, waits for them, and re-layouts: none -> 9.98 us  [the longest x15 5.14 us: exchange(): a[:width]]
    concatenate x0 -> x8, other arithmetic: none -> 9.54 us  [the longest x4 4.78 us: exchange(): jnp.concatenate([a[-width:] for a in (own, from_next, far_b, from_prev)],...]
    ppermute x3, waiting for transfers between devices: 11.3 us -> 19.8 us  [shards(): lax.ppermute(lax.dynamic_index_in_dim(h_split, dest, 0, keepdims=False),...]
    concatenate x8 -> x4, local copies, waits for them, and re-layouts: 11.5 us -> 3.12 us  [exchange(): jnp.concatenate([own, from_next, far_a, far_b, from_prev, lo, hi], axis=0)]
    ppermute x3, waiting for transfers between devices: 66 us -> 73.4 us  [shards(): lax.ppermute(lax.dynamic_index_in_dim(p_split, dest, 0, keepdims=False),...]
  transfers between devices with their start and end apart: 30 -> 30, of which waited for: 10 -> 12; matrix products, arithmetic and copies ran while one was open for 17% -> 17% of each run, Pallas kernels for 10% -> 9%
where the time goes in v7:
time: 362 us; the launch traced here: 360 us
  waiting for transfers between devices  165 us (46%)
  starting transfers between devices  80.7 us (22%)
  local copies, waits for them, and re-layouts  52.7 us (15%)
  Pallas kernels  42.7 us (12%)
  other arithmetic  18.5 us (5%)
    ppermute x3, waiting for transfers between devices, shards(): lax.ppermute(lax.dynamic_index_in_dim(p_split, dest, 0, keepdims=False),...  73.4 us
    ppermute x4, waiting for transfers between devices, exchange(): from_prev = lax.ppermute(own, 'layer', shift(nl, 1))  46.5 us
    pallas_call x4, Pallas kernels, own_rows(): pl.pallas_call(step_kernel, grid_spec=grid_spec, out_shape=jax.ShapeDtype...  42.7 us
    ppermute x3, starting transfers between devices, shards(): lax.ppermute(lax.dynamic_index_in_dim(h_split, dest, 0, keepdims=False),...  34.8 us
    unnamed x42, local copies, waits for them, and re-layouts  28.8 us
    ppermute x4, waiting for transfers between devices, exchange(): far_b = lax.ppermute(from_next[half:], 'layer', shift(nl, nl - 1))  20.4 us
    ppermute x3, waiting for transfers between devices, shards(): lax.ppermute(lax.dynamic_index_in_dim(h_split, dest, 0, keepdims=False),...  19.8 us
    ppermute x4, starting transfers between devices, exchange(): hi = lax.ppermute(first, 'grid', shift(ng, ng - 1))  15.8 us
  transfers between devices with their start and end apart: 30, of which 12 were waited for; matrix products, arithmetic and copies ran while one was open for 17% of the time, Pallas kernels for 9%

profile of v7, /device:TPU:0, one launch (start us, length us, event | category | flops | bytes accessed | tf_op | source)
XLA Modules:
  0.0 360.4 jit_solution(9036159095727992575)
XLA Ops:
  0.6 4.7 %fusion.30 = (bf16[1024,768]{1,0:T(8,128)(2,1)}, bf16[4608,768]{1,0:T(8,128)(2,1)}, bf16[4608,768]{1,0:T(8,128)(2,1)}, bf16[1024,768]{1,0:T(8,128)(2,1)}) fusion(bf16[1024,1536]{1,0:T(8,128)(2,1)} %param.6), kind=kLoop, calls=%fused_computation.116 | loop fusion | bytes 9437184 | tf_op jit(solution)/shard_map/slice | solution.py:104
  5.4 4.1 %collective-permute-start.12 = (bf16[1024,768]{1,0:T(8,128)(2,1)}, bf16[1024,768]{1,0:T(8,128)(2,1)S(1)}, u32[]{:S(2)}, u32[]{:S(2)}) collective-permute-start(bf16[1024,768]{1,0:T(8,128)(2,1)} %get-tuple-element.11.refs_8_), channel_id=1, source_target_pairs={{0,3},{1,0},{2,1},{3,2},{4,7},{5,4},{6,5},{7,6},{8,11},{9,8},{10,9... | collective-permute-start | bytes 4718600 | tf_op jit(solution)/shard_map/ppermute | solution.py:23
  9.5 2.9 dynamic-slice_bitcast_fusion.3
  12.4 3.2 collective-permute-start.5
  16.7 38.1 %collective-permute-done.2 = s32[8,2]{0,1:T(2,128)S(1)} collective-permute-done((s32[8,2]{0,1:T(2,128)S(1)}, s32[8,2]{0,1:T(2,128)S(1)}, u32[]{:S(2)}, u32[]{:S(2)}) %collective-permute-start.2) | collective-permute-done | bytes 96 | tf_op jit(solution)/shard_map/ppermute | solution.py:85
  57.0 35.3 %collective-permute-done = s32[8,2]{0,1:T(2,128)S(1)} collective-permute-done((s32[8,2]{0,1:T(2,128)S(1)}, s32[8,2]{0,1:T(2,128)S(1)}, u32[]{:S(2)}, u32[]{:S(2)}) %collective-permute-start) | collective-permute-done | bytes 96 | tf_op jit(solution)/shard_map/ppermute | solution.py:85
  94.1 3.9 %fusion.28 = (bf16[1024,768]{1,0:T(8,128)(2,1)}, bf16[1024,768]{1,0:T(8,128)(2,1)}) fusion(bf16[1024,1536]{1,0:T(8,128)(2,1)} %param.7), kind=kLoop, calls=%fused_computation.114 | loop fusion | bytes 6291456 | tf_op jit(solution)/shard_map/slice | solution.py:105
  98.0 9.6 %collective-permute-done.4 = bf16[8,2,128,128]{3,2,1,0:T(8,128)(2,1)} collective-permute-done((bf16[8,2,128,128]{3,2,1,0:T(8,128)(2,1)}, bf16[8,2,128,128]{3,2,1,0:T(8,128)(2,1)}, u32[]{:S(2)}, u32[]{:S(2)}) %collective-permute-start.4) | collective-permute-done | bytes 524320 | tf_op jit(solution)/shard_map/ppermute | solution.py:84
  107.6 31.6 %collective-permute-start.3 = (bf16[8,2,128,128]{3,2,1,0:T(8,128)(2,1)}, bf16[8,2,128,128]{3,2,1,0:T(8,128)(2,1)}, u32[]{:S(2)}, u32[]{:S(2)}) collective-permute-start(bf16[8,2,128,128]{3,2,1,0:T(8,128)(2,1)} %get-tuple-element.15), channel_id=1, source_target_pairs={{0,1},{1,2},{2,3},{3,0},{4,5},{5,6},{6,7},{7,4},{8,9},{9,10},{10,1... | collective-permute-start | bytes 1572872 | tf_op jit(solution)/shard_map/ppermute | solution.py:84
  141.1 10.2 %collective-permute-done.3 = bf16[8,2,128,128]{3,2,1,0:T(8,128)(2,1)} collective-permute-done((bf16[8,2,128,128]{3,2,1,0:T(8,128)(2,1)}, bf16[8,2,128,128]{3,2,1,0:T(8,128)(2,1)}, u32[]{:S(2)}, u32[]{:S(2)}) %collective-permute-start.3) | collective-permute-done | bytes 524320 | tf_op jit(solution)/shard_map/ppermute | solution.py:84
  151.2 3.1 pad_maximum_fusion.2.h_ref
  154.6 3.3 collective-permute-start.15
  160.3 3.3 collective-permute-start.9
  166.2 2.7 constant_dynamic-update-slice_fusion.5
  170.1 5.7 %collective-permute-done.15 = bf16[512,768]{1,0:T(8,128)(2,1)S(1)} collective-permute-done((bf16[512,768]{1,0:T(8,128)(2,1)S(1)}, bf16[512,768]{1,0:T(8,128)(2,1)S(1)}, u32[]{:S(2)}, u32[]{:S(2)}) %collective-permute-start.15) | collective-permute-done | bytes 786464 | tf_op jit(solution)/shard_map/ppermute | solution.py:25
  178.0 5.1 %collective-permute-start.17 = (bf16[256,768]{1,0:T(8,128)(2,1)S(1)}, bf16[256,768]{1,0:T(8,128)(2,1)S(1)}, u32[]{:S(2)}, u32[]{:S(2)}) collective-permute-start(bf16[256,768]{1,0:T(8,128)(2,1)S(1)} %fusion.14), channel_id=1, source_target_pairs={{0,124},{4,0},{8,4},{12,8},{16,12},{20,16},{24,20},{28,24},{32,28}... | collective-permute-start | bytes 1179656 | tf_op jit(solution)/shard_map/ppermute | solution.py:31
  183.1 5.3 %collective-permute-done.9 = bf16[512,768]{1,0:T(8,128)(2,1)S(1)} collective-permute-done((bf16[512,768]{1,0:T(8,128)(2,1)S(1)}, bf16[512,768]{1,0:T(8,128)(2,1)S(1)}, u32[]{:S(2)}, u32[]{:S(2)}) %collective-permute-start.9) | collective-permute-done | bytes 786464 | tf_op jit(solution)/shard_map/ppermute | solution.py:25
  192.0 5.1 %collective-permute-start.11 = (bf16[256,768]{1,0:T(8,128)(2,1)}, bf16[256,768]{1,0:T(8,128)(2,1)S(1)}, u32[]{:S(2)}, u32[]{:S(2)}) collective-permute-start(bf16[256,768]{1,0:T(8,128)(2,1)} %fusion.20), channel_id=1, source_target_pairs={{0,124},{4,0},{8,4},{12,8},{16,12},{20,16},{24,20},{28,24},{32,28}... | collective-permute-start | bytes 1179656 | tf_op jit(solution)/shard_map/ppermute | solution.py:31
  206.4 10.6 %shard_map.60 = bf16[1024,768]{1,0:T(8,128)(2,1)} custom-call(s32[64]{0:T(128)} %compare_select_fusion.pos_ref, bf16[8,8,128,128]{3,2,1,0:T(8,128)(2,1)} %pad_maximum_fusion.2.h_ref, bf16[36,128,768]{2,1,0:T(8,128)(2,1)} %bitcast.10.refs_0_.refs_1_.refs_2_.refs_3_.refs_4_.refs_5_.refs_6_.refs_7_, ...), custom_call_target="tpu_custom_call" | custom-call | tf_op jit(solution)/shard_map/pallas_call | solution.py:62
  217.0 3.8 %collective-permute-start.24 = (bf16[1024,768]{1,0:T(8,128)(2,1)}, bf16[1024,768]{1,0:T(8,128)(2,1)}, u32[]{:S(2)}, u32[]{:S(2)}) collective-permute-start(bf16[1024,768]{1,0:T(8,128)(2,1)} %shard_map.60), channel_id=1, source_target_pairs={{0,3},{1,0},{2,1},{3,2},{4,7},{5,4},{6,5},{7,6},{8,11},{9,8},{10,9... | collective-permute-start | bytes 4718600 | tf_op jit(solution)/shard_map/ppermute | solution.py:23
  223.3 10.7 %shard_map.59 = bf16[1024,768]{1,0:T(8,128)(2,1)} custom-call(s32[64]{0:T(128)} %compare_select_fusion.pos_ref, bf16[8,8,128,128]{3,2,1,0:T(8,128)(2,1)} %pad_maximum_fusion.2.h_ref, bf16[36,128,768]{2,1,0:T(8,128)(2,1)} %bitcast.9.refs_0_.refs_1_.refs_2_.refs_3_.refs_4_.refs_5_.refs_6_.refs_7_, ...), custom_call_target="tpu_custom_call" | custom-call | tf_op jit(solution)/shard_map/pallas_call | solution.py:62
  234.2 3.2 collective-permute-start.18
  242.0 17.4 %collective-permute-done.25 = bf16[1024,768]{1,0:T(8,128)(2,1)S(1)} collective-permute-done((bf16[1024,768]{1,0:T(8,128)(2,1)}, bf16[1024,768]{1,0:T(8,128)(2,1)S(1)}, u32[]{:S(2)}, u32[]{:S(2)}) %collective-permute-start.25) | collective-permute-done | bytes 1572896 | tf_op jit(solution)/shard_map/ppermute | solution.py:22
  260.8 3.3 collective-permute-start.27
  264.1 29.1 %collective-permute-done.19 = bf16[1024,768]{1,0:T(8,128)(2,1)S(1)} collective-permute-done((bf16[1024,768]{1,0:T(8,128)(2,1)}, bf16[1024,768]{1,0:T(8,128)(2,1)S(1)}, u32[]{:S(2)}, u32[]{:S(2)}) %collective-permute-start.19) | collective-permute-done | bytes 1572896 | tf_op jit(solution)/shard_map/ppermute | solution.py:22
  293.4 3.3 collective-permute-start.21
  301.9 4.4 %collective-permute-done.27 = bf16[512,768]{1,0:T(8,128)(2,1)S(1)} collective-permute-done((bf16[512,768]{1,0:T(8,128)(2,1)S(1)}, bf16[512,768]{1,0:T(8,128)(2,1)S(1)}, u32[]{:S(2)}, u32[]{:S(2)}) %collective-permute-start.27) | collective-permute-done | bytes 786464 | tf_op jit(solution)/shard_map/ppermute | solution.py:25
  313.6 5.1 %collective-permute-done.21 = bf16[512,768]{1,0:T(8,128)(2,1)S(1)} collective-permute-done((bf16[512,768]{1,0:T(8,128)(2,1)S(1)}, bf16[512,768]{1,0:T(8,128)(2,1)S(1)}, u32[]{:S(2)}, u32[]{:S(2)}) %collective-permute-start.21) | collective-permute-done | bytes 786464 | tf_op jit(solution)/shard_map/ppermute | solution.py:25
  323.1 3.1 collective-permute-start.23
  334.1 10.6 %shard_map.62 = bf16[1024,768]{1,0:T(8,128)(2,1)} custom-call(s32[64]{0:T(128)} %compare_select_fusion.pos_ref, bf16[8,8,128,128]{3,2,1,0:T(8,128)(2,1)} %pad_maximum_fusion.2.h_ref, bf16[36,128,768]{2,1,0:T(8,128)(2,1)} %bitcast.12.refs_0_.refs_1_.refs_2_.refs_3_.refs_4_.refs_5_.refs_6_.refs_7_, ...), custom_call_target="tpu_custom_call" | custom-call | tf_op jit(solution)/shard_map/pallas_call | solution.py:62
  346.3 10.8 %shard_map.61 = bf16[1024,768]{1,0:T(8,128)(2,1)} custom-call(s32[64]{0:T(128)} %compare_select_fusion.pos_ref, bf16[8,8,128,128]{3,2,1,0:T(8,128)(2,1)} %pad_maximum_fusion.2.h_ref, bf16[36,128,768]{2,1,0:T(8,128)(2,1)} %bitcast.11.refs_0_.refs_1_.refs_2_.refs_3_.refs_4_.refs_5_.refs_6_.refs_7_, ...), custom_call_target="tpu_custom_call" | custom-call | tf_op jit(solution)/shard_map/pallas_call | solution.py:62
  357.0 3.3 pad_maximum_fusion.1
  (126 shorter events, 63.6 us)
Async XLA Ops:
  5.4 149.1 %collective-permute-start.12 = (bf16[1024,768]{1,0:T(8,128)(2,1)}, bf16[1024,768]{1,0:T(8,128)(2,1)S(1)}, u32[]{:S(2)}, u32[]{:S(2)}) collective-permute-start(bf16[1024,768]{1,0:T(8,128)(2,1)} %get-tuple-element.11.refs_8_), channel_id=1, source_target_pairs={{0,3},{1,0},{2,1},{3,2},{4,7},{5,4},{6,5},{7,6},{8,11},{9,8},{10,9... | collective-permute-start | bytes 4718600 | tf_op jit(solution)/shard_map/ppermute | solution.py:23
  9.5 144.8 %collective-permute-start.13 = (bf16[1024,768]{1,0:T(8,128)(2,1)}, bf16[1024,768]{1,0:T(8,128)(2,1)S(1)}, u32[]{:S(2)}, u32[]{:S(2)}) collective-permute-start(bf16[1024,768]{1,0:T(8,128)(2,1)} %get-tuple-element.11.refs_8_), channel_id=1, source_target_pairs={{0,1},{1,2},{2,3},{3,0},{4,5},{5,6},{6,7},{7,4},{8,9},{9,10},{10,1... | collective-permute-start | bytes 4718600 | tf_op jit(solution)/shard_map/ppermute | solution.py:22
  12.4 81.7 %collective-permute-start.5 = (bf16[8,2,128,128]{3,2,1,0:T(8,128)(2,1)}, bf16[8,2,128,128]{3,2,1,0:T(8,128)(2,1)}, u32[]{:S(2)}, u32[]{:S(2)}) collective-permute-start(bf16[8,2,128,128]{3,2,1,0:T(8,128)(2,1)} %get-tuple-element.13), channel_id=1, source_target_pairs={{0,3},{1,0},{2,1},{3,2},{4,7},{5,4},{6,5},{7,6},{8,11},{9,8},{10,9... | collective-permute-start | bytes 1572872 | tf_op jit(solution)/shard_map/ppermute | solution.py:84
  15.8 39.0 %collective-permute-start.2 = (s32[8,2]{0,1:T(2,128)S(1)}, s32[8,2]{0,1:T(2,128)S(1)}, u32[]{:S(2)}, u32[]{:S(2)}) collective-permute-start(s32[8,2]{0,1:T(2,128)S(1)} %bitcast.23), channel_id=1, source_target_pairs={{0,3},{1,0},{2,1},{3,2},{4,7},{5,4},{6,5},{7,6},{8,11},{9,8},{10,9... | collective-permute-start | bytes 200 | tf_op jit(solution)/shard_map/ppermute | solution.py:85
  15.8 39.4 %collective-permute-start.1 = (s32[8,2]{0,1:T(2,128)S(1)}, s32[8,2]{0,1:T(2,128)S(1)}, u32[]{:S(2)}, u32[]{:S(2)}) collective-permute-start(s32[8,2]{0,1:T(2,128)S(1)} %bitcast.22), channel_id=1, source_target_pairs={{0,2},{1,3},{2,0},{3,1},{4,6},{5,7},{6,4},{7,5},{8,10},{9,11},{10,... | collective-permute-start | bytes 200 | tf_op jit(solution)/shard_map/ppermute | solution.py:85
  54.8 103.1 %collective-permute-start.7 = (bf16[1024,768]{1,0:T(8,128)(2,1)}, bf16[1024,768]{1,0:T(8,128)(2,1)}, u32[]{:S(2)}, u32[]{:S(2)}) collective-permute-start(bf16[1024,768]{1,0:T(8,128)(2,1)} %get-tuple-element.8.refs_8_), channel_id=1, source_target_pairs={{0,1},{1,2},{2,3},{3,0},{4,5},{5,6},{6,7},{7,4},{8,9},{9,10},{10,1... | collective-permute-start | bytes 4718600 | tf_op jit(solution)/shard_map/ppermute | solution.py:22
  55.3 37.0 %collective-permute-start = (s32[8,2]{0,1:T(2,128)S(1)}, s32[8,2]{0,1:T(2,128)S(1)}, u32[]{:S(2)}, u32[]{:S(2)}) collective-permute-start(s32[8,2]{0,1:T(2,128)S(1)} %bitcast.21), channel_id=1, source_target_pairs={{0,1},{1,2},{2,3},{3,0},{4,5},{5,6},{6,7},{7,4},{8,9},{9,10},{10,1... | collective-permute-start | bytes 200 | tf_op jit(solution)/shard_map/ppermute | solution.py:85
  92.3 66.8 %collective-permute-start.6 = (bf16[1024,768]{1,0:T(8,128)(2,1)}, bf16[1024,768]{1,0:T(8,128)(2,1)}, u32[]{:S(2)}, u32[]{:S(2)}) collective-permute-start(bf16[1024,768]{1,0:T(8,128)(2,1)} %get-tuple-element.8.refs_8_), channel_id=1, source_target_pairs={{0,3},{1,0},{2,1},{3,2},{4,7},{5,4},{6,5},{7,6},{8,11},{9,8},{10,9... | collective-permute-start | bytes 4718600 | tf_op jit(solution)/shard_map/ppermute | solution.py:23
  94.1 13.5 %collective-permute-start.4 = (bf16[8,2,128,128]{3,2,1,0:T(8,128)(2,1)}, bf16[8,2,128,128]{3,2,1,0:T(8,128)(2,1)}, u32[]{:S(2)}, u32[]{:S(2)}) collective-permute-start(bf16[8,2,128,128]{3,2,1,0:T(8,128)(2,1)} %get-tuple-element.14), channel_id=1, source_target_pairs={{0,2},{1,3},{2,0},{3,1},{4,6},{5,7},{6,4},{7,5},{8,10},{9,11},{10,... | collective-permute-start | bytes 1572872 | tf_op jit(solution)/shard_map/ppermute | solution.py:84
  94.1 45.1 %copy-start.2 = (bf16[1024,1536]{1,0:T(8,128)(2,1)S(1)}, bf16[1024,1536]{1,0:T(8,128)(2,1)}, u32[]{:S(2)}) copy-start(bf16[1024,1536]{1,0:T(8,128)(2,1)} %param.6) | copy-start | bytes 9437188
  107.6 32.7 %copy-start.9 = (s32[8,2]{0,1:T(2,128)S(1)}, s32[8,2]{0,1:T(2,128)}, u32[]{:S(2)}) copy-start(s32[8,2]{0,1:T(2,128)} %copy-done.8) | copy-start | bytes 196
  107.6 43.7 %collective-permute-start.3 = (bf16[8,2,128,128]{3,2,1,0:T(8,128)(2,1)}, bf16[8,2,128,128]{3,2,1,0:T(8,128)(2,1)}, u32[]{:S(2)}, u32[]{:S(2)}) collective-permute-start(bf16[8,2,128,128]{3,2,1,0:T(8,128)(2,1)} %get-tuple-element.15), channel_id=1, source_target_pairs={{0,1},{1,2},{2,3},{3,0},{4,5},{5,6},{6,7},{7,4},{8,9},{9,10},{10,1... | collective-permute-start | bytes 1572872 | tf_op jit(solution)/shard_map/ppermute | solution.py:84
  154.4 22.5 %collective-permute-start.14 = (bf16[512,768]{1,0:T(8,128)(2,1)S(1)}, bf16[512,768]{1,0:T(8,128)(2,1)S(1)}, u32[]{:S(2)}, u32[]{:S(2)}) collective-permute-start(bf16[512,768]{1,0:T(8,128)(2,1)S(1)} %slice.188), channel_id=1, source_target_pairs={{0,1},{1,2},{2,3},{3,0},{4,5},{5,6},{6,7},{7,4},{8,9},{9,10},{10,1... | collective-permute-start | bytes 2359304 | tf_op jit(solution)/shard_map/ppermute | solution.py:24
  154.6 21.2 %collective-permute-start.15 = (bf16[512,768]{1,0:T(8,128)(2,1)S(1)}, bf16[512,768]{1,0:T(8,128)(2,1)S(1)}, u32[]{:S(2)}, u32[]{:S(2)}) collective-permute-start(bf16[512,768]{1,0:T(8,128)(2,1)S(1)} %slice.189), channel_id=1, source_target_pairs={{0,3},{1,0},{2,1},{3,2},{4,7},{5,4},{6,5},{7,6},{8,11},{9,8},{10,9... | collective-permute-start | bytes 2359304 | tf_op jit(solution)/shard_map/ppermute | solution.py:25
  159.0 31.1 %collective-permute-start.8 = (bf16[512,768]{1,0:T(8,128)(2,1)S(1)}, bf16[512,768]{1,0:T(8,128)(2,1)S(1)}, u32[]{:S(2)}, u32[]{:S(2)}) collective-permute-start(bf16[512,768]{1,0:T(8,128)(2,1)S(1)} %slice.180), channel_id=1, source_target_pairs={{0,1},{1,2},{2,3},{3,0},{4,5},{5,6},{6,7},{7,4},{8,9},{9,10},{10,1... | collective-permute-start | bytes 2359304 | tf_op jit(solution)/shard_map/ppermute | solution.py:24
  160.3 28.1 %collective-permute-start.9 = (bf16[512,768]{1,0:T(8,128)(2,1)S(1)}, bf16[512,768]{1,0:T(8,128)(2,1)S(1)}, u32[]{:S(2)}, u32[]{:S(2)}) collective-permute-start(bf16[512,768]{1,0:T(8,128)(2,1)S(1)} %slice.181), channel_id=1, source_target_pairs={{0,3},{1,0},{2,1},{3,2},{4,7},{5,4},{6,5},{7,6},{8,11},{9,8},{10,9... | collective-permute-start | bytes 2359304 | tf_op jit(solution)/shard_map/ppermute | solution.py:25
  176.8 28.0 %collective-permute-start.16 = (bf16[256,768]{1,0:T(8,128)(2,1)S(1)}, bf16[256,768]{1,0:T(8,128)(2,1)S(1)}, u32[]{:S(2)}, u32[]{:S(2)}) collective-permute-start(bf16[256,768]{1,0:T(8,128)(2,1)S(1)} %fusion.17), channel_id=1, source_target_pairs={{0,4},{4,8},{8,12},{12,16},{16,20},{20,24},{24,28},{28,32},{32,36}... | collective-permute-start | bytes 1179656 | tf_op jit(solution)/shard_map/ppermute | solution.py:30
  178.0 27.6 %collective-permute-start.17 = (bf16[256,768]{1,0:T(8,128)(2,1)S(1)}, bf16[256,768]{1,0:T(8,128)(2,1)S(1)}, u32[]{:S(2)}, u32[]{:S(2)}) collective-permute-start(bf16[256,768]{1,0:T(8,128)(2,1)S(1)} %fusion.14), channel_id=1, source_target_pairs={{0,124},{4,0},{8,4},{12,8},{16,12},{20,16},{24,20},{28,24},{32,28}... | collective-permute-start | bytes 1179656 | tf_op jit(solution)/shard_map/ppermute | solution.py:31
  190.2 30.6 %collective-permute-start.10 = (bf16[256,768]{1,0:T(8,128)(2,1)}, bf16[256,768]{1,0:T(8,128)(2,1)}, u32[]{:S(2)}, u32[]{:S(2)}) collective-permute-start(bf16[256,768]{1,0:T(8,128)(2,1)} %fusion.23), channel_id=1, source_target_pairs={{0,4},{4,8},{8,12},{12,16},{16,20},{20,24},{24,28},{28,32},{32,36}... | collective-permute-start | bytes 1179656 | tf_op jit(solution)/shard_map/ppermute | solution.py:30
  192.0 30.6 %collective-permute-start.11 = (bf16[256,768]{1,0:T(8,128)(2,1)}, bf16[256,768]{1,0:T(8,128)(2,1)S(1)}, u32[]{:S(2)}, u32[]{:S(2)}) collective-permute-start(bf16[256,768]{1,0:T(8,128)(2,1)} %fusion.20), channel_id=1, source_target_pairs={{0,124},{4,0},{8,4},{12,8},{16,12},{20,16},{24,20},{28,24},{32,28}... | collective-permute-start | bytes 1179656 | tf_op jit(solution)/shard_map/ppermute | solution.py:31
  217.0 42.6 %collective-permute-start.24 = (bf16[1024,768]{1,0:T(8,128)(2,1)}, bf16[1024,768]{1,0:T(8,128)(2,1)}, u32[]{:S(2)}, u32[]{:S(2)}) collective-permute-start(bf16[1024,768]{1,0:T(8,128)(2,1)} %shard_map.60), channel_id=1, source_target_pairs={{0,3},{1,0},{2,1},{3,2},{4,7},{5,4},{6,5},{7,6},{8,11},{9,8},{10,9... | collective-permute-start | bytes 4718600 | tf_op jit(solution)/shard_map/ppermute | solution.py:23
  220.8 38.7 %collective-permute-start.25 = (bf16[1024,768]{1,0:T(8,128)(2,1)}, bf16[1024,768]{1,0:T(8,128)(2,1)S(1)}, u32[]{:S(2)}, u32[]{:S(2)}) collective-permute-start(bf16[1024,768]{1,0:T(8,128)(2,1)} %shard_map.60), channel_id=1, source_target_pairs={{0,1},{1,2},{2,3},{3,0},{4,5},{5,6},{6,7},{7,4},{8,9},{9,10},{10,1... | collective-permute-start | bytes 4718600 | tf_op jit(solution)/shard_map/ppermute | solution.py:22
  234.1 59.1 %collective-permute-start.19 = (bf16[1024,768]{1,0:T(8,128)(2,1)}, bf16[1024,768]{1,0:T(8,128)(2,1)S(1)}, u32[]{:S(2)}, u32[]{:S(2)}) collective-permute-start(bf16[1024,768]{1,0:T(8,128)(2,1)} %shard_map.59), channel_id=1, source_target_pairs={{0,1},{1,2},{2,3},{3,0},{4,5},{5,6},{6,7},{7,4},{8,9},{9,10},{10,1... | collective-permute-start | bytes 4718600 | tf_op jit(solution)/shard_map/ppermute | solution.py:22
  234.2 59.2 %collective-permute-start.18 = (bf16[1024,768]{1,0:T(8,128)(2,1)}, bf16[1024,768]{1,0:T(8,128)(2,1)S(1)}, u32[]{:S(2)}, u32[]{:S(2)}) collective-permute-start(bf16[1024,768]{1,0:T(8,128)(2,1)} %shard_map.59), channel_id=1, source_target_pairs={{0,3},{1,0},{2,1},{3,2},{4,7},{5,4},{6,5},{7,6},{8,11},{9,8},{10,9... | collective-permute-start | bytes 4718600 | tf_op jit(solution)/shard_map/ppermute | solution.py:23
  259.5 50.5 %collective-permute-start.26 = (bf16[512,768]{1,0:T(8,128)(2,1)S(1)}, bf16[512,768]{1,0:T(8,128)(2,1)S(1)}, u32[]{:S(2)}, u32[]{:S(2)}) collective-permute-start(bf16[512,768]{1,0:T(8,128)(2,1)S(1)} %slice.206), channel_id=1, source_target_pairs={{0,1},{1,2},{2,3},{3,0},{4,5},{5,6},{6,7},{7,4},{8,9},{9,10},{10,1... | collective-permute-start | bytes 2359304 | tf_op jit(solution)/shard_map/ppermute | solution.py:24
  260.8 45.5 %collective-permute-start.27 = (bf16[512,768]{1,0:T(8,128)(2,1)S(1)}, bf16[512,768]{1,0:T(8,128)(2,1)S(1)}, u32[]{:S(2)}, u32[]{:S(2)}) collective-permute-start(bf16[512,768]{1,0:T(8,128)(2,1)S(1)} %slice.207), channel_id=1, source_target_pairs={{0,3},{1,0},{2,1},{3,2},{4,7},{5,4},{6,5},{7,6},{8,11},{9,8},{10,9... | collective-permute-start | bytes 2359304 | tf_op jit(solution)/shard_map/ppermute | solution.py:25
  293.2 28.9 %collective-permute-start.20 = (bf16[512,768]{1,0:T(8,128)(2,1)S(1)}, bf16[512,768]{1,0:T(8,128)(2,1)S(1)}, u32[]{:S(2)}, u32[]{:S(2)}) collective-permute-start(bf16[512,768]{1,0:T(8,128)(2,1)S(1)} %slice.196), channel_id=1, source_target_pairs={{0,1},{1,2},{2,3},{3,0},{4,5},{5,6},{6,7},{7,4},{8,9},{9,10},{10,1... | collective-permute-start | bytes 2359304 | tf_op jit(solution)/shard_map/ppermute | solution.py:24
  293.4 25.3 %collective-permute-start.21 = (bf16[512,768]{1,0:T(8,128)(2,1)S(1)}, bf16[512,768]{1,0:T(8,128)(2,1)S(1)}, u32[]{:S(2)}, u32[]{:S(2)}) collective-permute-start(bf16[512,768]{1,0:T(8,128)(2,1)S(1)} %slice.197), channel_id=1, source_target_pairs={{0,3},{1,0},{2,1},{3,2},{4,7},{5,4},{6,5},{7,6},{8,11},{9,8},{10,9... | collective-permute-start | bytes 2359304 | tf_op jit(solution)/shard_map/ppermute | solution.py:25
  307.4 25.2 %collective-permute-start.28 = (bf16[256,768]{1,0:T(8,128)(2,1)S(1)}, bf16[256,768]{1,0:T(8,128)(2,1)S(1)}, u32[]{:S(2)}, u32[]{:S(2)}) collective-permute-start(bf16[256,768]{1,0:T(8,128)(2,1)S(1)} %fusion.5), channel_id=1, source_target_pairs={{0,4},{4,8},{8,12},{12,16},{16,20},{20,24},{24,28},{28,32},{32,36}... | collective-permute-start | bytes 1179656 | tf_op jit(solution)/shard_map/ppermute | solution.py:30
  311.1 22.3 %collective-permute-start.29 = (bf16[256,768]{1,0:T(8,128)(2,1)S(1)}, bf16[256,768]{1,0:T(8,128)(2,1)S(1)}, u32[]{:S(2)}, u32[]{:S(2)}) collective-permute-start(bf16[256,768]{1,0:T(8,128)(2,1)S(1)} %fusion.2), channel_id=1, source_target_pairs={{0,124},{4,0},{8,4},{12,8},{16,12},{20,16},{24,20},{28,24},{32,28}... | collective-permute-start | bytes 1179656 | tf_op jit(solution)/shard_map/ppermute | solution.py:31
  319.7 25.0 %collective-permute-start.22 = (bf16[256,768]{1,0:T(8,128)(2,1)S(1)}, bf16[256,768]{1,0:T(8,128)(2,1)S(1)}, u32[]{:S(2)}, u32[]{:S(2)}) collective-permute-start(bf16[256,768]{1,0:T(8,128)(2,1)S(1)} %fusion.11), channel_id=1, source_target_pairs={{0,4},{4,8},{8,12},{12,16},{16,20},{20,24},{24,28},{28,32},{32,36}... | collective-permute-start | bytes 1179656 | tf_op jit(solution)/shard_map/ppermute | solution.py:30
  323.1 22.4 %collective-permute-start.23 = (bf16[256,768]{1,0:T(8,128)(2,1)S(1)}, bf16[256,768]{1,0:T(8,128)(2,1)S(1)}, u32[]{:S(2)}, u32[]{:S(2)}) collective-permute-start(bf16[256,768]{1,0:T(8,128)(2,1)S(1)} %fusion.8), channel_id=1, source_target_pairs={{0,124},{4,0},{8,4},{12,8},{16,12},{20,16},{24,20},{28,24},{32,28}... | collective-permute-start | bytes 1179656 | tf_op jit(solution)/shard_map/ppermute | solution.py:31
  (8 other events, 81.5 us)

commit v8 on v3

--- a/solution.py
+++ b/solution.py
@@ -8,6 +8,7 @@
 KB = 8
 HB = 2
 NCH = 2
+TILE = 384
 
 
 def shift(size, k):
@@ -34,38 +35,38 @@
     return jnp.concatenate([panel, lo, hi], axis=0)
 
 
-def step_kernel(pos_ref, h_ref, *refs):
-    slots = h_ref.shape[1]
-    panel_refs, prev_ref, out_ref = refs[:slots], refs[slots], refs[slots + 1]
-    acc = jnp.dot(h_ref[0, 0], panel_refs[0][0], preferred_element_type=jnp.float32)
-    for s in range(1, slots):
-        acc = acc + jnp.dot(h_ref[0, s], panel_refs[s][0], preferred_element_type=jnp.float32)
-    out_ref[...] = (2.0 * acc - prev_ref[...].astype(jnp.float32)).astype(out_ref.dtype)
+def step_kernel(pos_ref, h_ref, panel_ref, prev_ref, out_ref):
+    rows, slots, block_size = h_ref.shape[0], h_ref.shape[1], h_ref.shape[2]
+    for i in range(rows):
+        acc = jnp.dot(h_ref[i, 0], panel_ref[pos_ref[i * slots]], preferred_element_type=jnp.float32)
+        for s in range(1, slots):
+            acc = acc + jnp.dot(h_ref[i, s], panel_ref[pos_ref[i * slots + s]], preferred_element_type=jnp.float32)
+        at = slice(i * block_size, (i + 1) * block_size)
+        out_ref[at, :] = (2.0 * acc - prev_ref[at, :].astype(jnp.float32)).astype(out_ref.dtype)
 
 
 def own_rows(h_own, pos_flat, chunk, previous, lidx):
-    rows, slots, block_size = h_own.shape[0], h_own.shape[1], h_own.shape[2]
+    block_size = h_own.shape[2]
     width = chunk.shape[1]
+    tile = TILE if width % TILE == 0 else width
     wide = exchange(chunk, lidx, block_size)
     blocks = wide.reshape(wide.shape[0] // block_size, block_size, width)
-
-    def panel_map(s):
-        return lambda i, p: (p[i * slots + s], 0, 0)
-
-    in_specs = [pl.BlockSpec((1, slots, block_size, block_size), lambda i, p: (i, 0, 0, 0))]
-    in_specs += [pl.BlockSpec((1, block_size, width), panel_map(s)) for s in range(slots)]
-    in_specs += [pl.BlockSpec((block_size, width), lambda i, p: (i, 0))]
     grid_spec = pltpu.PrefetchScalarGridSpec(
         num_scalar_prefetch=1,
-        grid=(rows,),
-        in_specs=in_specs,
-        out_specs=pl.BlockSpec((block_size, width), lambda i, p: (i, 0)),
+        grid=(width // tile,),
+        in_specs=[
+            pl.BlockSpec(h_own.shape, lambda j, p: (0, 0, 0, 0)),
+            pl.BlockSpec((blocks.shape[0], block_size, tile), lambda j, p: (0, 0, j)),
+            pl.BlockSpec((chunk.shape[0], tile), lambda j, p: (0, j)),
+        ],
+        out_specs=pl.BlockSpec((chunk.shape[0], tile), lambda j, p: (0, j)),
     )
     return pl.pallas_call(
         step_kernel,
         grid_spec=grid_spec,
         out_shape=jax.ShapeDtypeStruct(chunk.shape, jnp.bfloat16),
-    )(pos_flat, h_own, *([blocks] * slots), previous)
+        compiler_params=pltpu.CompilerParams(vmem_limit_bytes=48 * 1024 * 1024),
+    )(pos_flat, h_own, blocks, previous)
 
 
 def shards(h_blocks, block_cols, t_now, t_prev):

time: 311 us -> 296 us (0.952)
  Pallas kernels: 42.5 us -> 25.6 us
  waiting for transfers between devices: 144 us -> 154 us
  local copies, waits for them, and re-layouts: 54 us -> 50.5 us
  other arithmetic: 8.96 us -> 5.64 us
    pallas_call x4, Pallas kernels: 42.5 us -> 25.6 us  [own_rows(): pl.pallas_call(step_kernel, grid_spec=grid_spec, out_shape=jax.ShapeDtype...]
    ppermute x4, waiting for transfers between devices: 46.2 us -> 52.6 us  [exchange(): from_prev = lax.ppermute(own, 'layer', shift(nl, 1))]
    unnamed x37 -> x43, local copies, waits for them, and re-layouts: 28.4 us -> 27 us
  transfers between devices with their start and end apart: 30 -> 30, of which waited for: 10 -> 11; matrix products, arithmetic and copies ran while one was open for 17% -> 15% of each run, Pallas kernels for 10% -> 7%
where the time goes in v8:
time: 296 us; the launch traced here: 295 us
  waiting for transfers between devices  154 us (52%)
  starting transfers between devices  58.7 us (20%)
  local copies, waits for them, and re-layouts  50.5 us (17%)
  Pallas kernels  25.6 us (9%)
  other arithmetic  5.64 us (2%)
    ppermute x3, waiting for transfers between devices, shards(): lax.ppermute(lax.dynamic_index_in_dim(p_split, dest, 0, keepdims=False),...  66 us
    ppermute x4, waiting for transfers between devices, exchange(): from_prev = lax.ppermute(own, 'layer', shift(nl, 1))  52.6 us
    unnamed x43, local copies, waits for them, and re-layouts  27 us
    pallas_call x4, Pallas kernels, own_rows(): pl.pallas_call(step_kernel, grid_spec=grid_spec, out_shape=jax.ShapeDtype...  25.6 us
    ppermute x4, waiting for transfers between devices, exchange(): far_a = lax.ppermute(from_prev[:half], 'layer', shift(nl, 1))  23.5 us
    ppermute x4, starting transfers between devices, exchange(): hi = lax.ppermute(first, 'grid', shift(ng, ng - 1))  20.2 us
    ppermute x4, starting transfers between devices, exchange(): from_next = lax.ppermute(own, 'layer', shift(nl, nl - 1))  13.8 us
    ppermute x4, starting transfers between devices, exchange(): far_b = lax.ppermute(from_next[half:], 'layer', shift(nl, nl - 1))  11.7 us
  transfers between devices with their start and end apart: 30, of which 11 were waited for; matrix products, arithmetic and copies ran while one was open for 15% of the time, Pallas kernels for 7%

profile of v8, /device:TPU:0, one launch (start us, length us, event | category | flops | bytes accessed | tf_op | source)
XLA Modules:
  0.0 295.2 jit_solution(8505059508651141212)
XLA Ops:
  0.6 5.0 %constant_dynamic-update-slice_fusion.4 = (bf16[4096,768]{1,0:T(8,128)(2,1)}, bf16[4608,768]{1,0:T(8,128)(2,1)}, bf16[4096,768]{1,0:T(8,128)(2,1)}, bf16[4608,76...) fusion(bf16[1024,1536]{1,0:T(8,128)(2,1)} %param.6), kind=kLoop, calls=%fused_computation.11 | loop fusion | bytes 12582912
  5.6 4.1 %collective-permute-start.12 = (bf16[1024,768]{1,0:T(8,128)(2,1)S(1)}, bf16[1024,768]{1,0:T(8,128)(2,1)}, u32[]{:S(2)}, u32[]{:S(2)}) collective-permute-start(bf16[1024,768]{1,0:T(8,128)(2,1)S(1)} %get-tuple-element.16.prev_ref), channel_id=1, source_target_pairs={{0,3},{1,0},{2,1},{3,2},{4,7},{5,4},{6,5},{7,6},{8,11},{9,8},{10,9... | collective-permute-start | bytes 4718600 | tf_op jit(solution)/shard_map/ppermute | solution.py:23
  9.8 3.3 %collective-permute-start.6 = (bf16[1024,768]{1,0:T(8,128)(2,1)S(1)}, bf16[1024,768]{1,0:T(8,128)(2,1)}, u32[]{:S(2)}, u32[]{:S(2)}) collective-permute-start(bf16[1024,768]{1,0:T(8,128)(2,1)S(1)} %get-tuple-element.17.prev_ref), channel_id=1, source_target_pairs={{0,3},{1,0},{2,1},{3,2},{4,7},{5,4},{6,5},{7,6},{8,11},{9,8},{10,9... | collective-permute-start | bytes 4718600 | tf_op jit(solution)/shard_map/ppermute | solution.py:23
  15.2 62.0 %collective-permute-done.2 = s32[8,2]{0,1:T(2,128)S(1)} collective-permute-done((s32[8,2]{0,1:T(2,128)S(1)}, s32[8,2]{0,1:T(2,128)S(1)}, u32[]{:S(2)}, u32[]{:S(2)}) %collective-permute-start.2) | collective-permute-done | bytes 96 | tf_op jit(solution)/shard_map/ppermute | solution.py:88
  83.3 2.9 dynamic-slice_bitcast_fusion.3
  91.8 3.7 %fusion.4 = (bf16[1024,768]{1,0:T(8,128)(2,1)}, bf16[1024,768]{1,0:T(8,128)(2,1)}) fusion(bf16[1024,1536]{1,0:T(8,128)(2,1)} %param.7), kind=kLoop, calls=%fused_computation.86 | loop fusion | bytes 6291456 | tf_op jit(solution)/shard_map/slice | solution.py:108
  98.8 11.3 %collective-permute-done.5 = bf16[8,2,128,128]{3,2,1,0:T(8,128)(2,1)} collective-permute-done((bf16[8,2,128,128]{3,2,1,0:T(8,128)(2,1)}, bf16[8,2,128,128]{3,2,1,0:T(8,128)(2,1)}, u32[]{:S(2)}, u32[]{:S(2)}) %collective-permute-start.5) | collective-permute-done | bytes 524320 | tf_op jit(solution)/shard_map/ppermute | solution.py:87
  110.1 3.8 %collective-permute-start.15 = (bf16[512,768]{1,0:T(8,128)(2,1)S(1)}, bf16[512,768]{1,0:T(8,128)(2,1)S(1)}, u32[]{:S(2)}, u32[]{:S(2)}) collective-permute-start(bf16[512,768]{1,0:T(8,128)(2,1)S(1)} %slice.51), channel_id=1, source_target_pairs={{0,3},{1,0},{2,1},{3,2},{4,7},{5,4},{6,5},{7,6},{8,11},{9,8},{10,9... | collective-permute-start | bytes 2359304 | tf_op jit(solution)/shard_map/ppermute | solution.py:25
  122.5 2.8 constant_dynamic-update-slice_fusion.15
  125.3 2.7 constant_dynamic-update-slice_fusion.3
  128.1 4.3 %collective-permute-done.14 = bf16[512,768]{1,0:T(8,128)(2,1)S(1)} collective-permute-done((bf16[512,768]{1,0:T(8,128)(2,1)S(1)}, bf16[512,768]{1,0:T(8,128)(2,1)S(1)}, u32[]{:S(2)}, u32[]{:S(2)}) %collective-permute-start.14) | collective-permute-done | bytes 786464 | tf_op jit(solution)/shard_map/ppermute | solution.py:24
  134.3 2.8 constant_dynamic-update-slice_fusion.12
  137.2 5.1 %collective-permute-start.17 = (bf16[256,768]{1,0:T(8,128)(2,1)S(1)}, bf16[256,768]{1,0:T(8,128)(2,1)S(1)}, u32[]{:S(2)}, u32[]{:S(2)}) collective-permute-start(bf16[256,768]{1,0:T(8,128)(2,1)S(1)} %get-tuple-element.8), channel_id=1, source_target_pairs={{0,124},{4,0},{8,4},{12,8},{16,12},{20,16},{24,20},{28,24},{32,28}... | collective-permute-start | bytes 1179656 | tf_op jit(solution)/shard_map/ppermute | solution.py:34
  142.3 4.7 %collective-permute-done.8 = bf16[512,768]{1,0:T(8,128)(2,1)S(1)} collective-permute-done((bf16[512,768]{1,0:T(8,128)(2,1)S(1)}, bf16[512,768]{1,0:T(8,128)(2,1)S(1)}, u32[]{:S(2)}, u32[]{:S(2)}) %collective-permute-start.8) | collective-permute-done | bytes 786464 | tf_op jit(solution)/shard_map/ppermute | solution.py:24
  148.9 2.8 constant_dynamic-update-slice_fusion
  151.9 5.1 %collective-permute-start.11 = (bf16[256,768]{1,0:T(8,128)(2,1)S(1)}, bf16[256,768]{1,0:T(8,128)(2,1)S(1)}, u32[]{:S(2)}, u32[]{:S(2)}) collective-permute-start(bf16[256,768]{1,0:T(8,128)(2,1)S(1)} %get-tuple-element.6), channel_id=1, source_target_pairs={{0,124},{4,0},{8,4},{12,8},{16,12},{20,16},{24,20},{28,24},{32,28}... | collective-permute-start | bytes 1179656 | tf_op jit(solution)/shard_map/ppermute | solution.py:34
  158.5 6.4 %shard_map.60 = bf16[1024,768]{1,0:T(8,128)(2,1)S(1)} custom-call(s32[64]{0:T(128)S(1)} %compare_select_fusion.pos_ref, bf16[8,8,128,128]{3,2,1,0:T(8,128)(2,1)S(1)} %pad_maximum_fusion.2.h_ref, bf16[36,128,768]{2,1,0:T(8,128)(2,1)} %bitcast.20, bf16[1024,768]{1,0:T(8,128)(2,1)S(1)} %copy-done.1), custom_call_target="tpu_custom_call" | custom-call | tf_op jit(solution)/shard_map/pallas_call | solution.py:64
  165.1 3.2 %collective-permute-start.24 = (bf16[1024,768]{1,0:T(8,128)(2,1)S(1)}, bf16[1024,768]{1,0:T(8,128)(2,1)S(1)}, u32[]{:S(2)}, u32[]{:S(2)}) collective-permute-start(bf16[1024,768]{1,0:T(8,128)(2,1)S(1)} %shard_map.60), channel_id=1, source_target_pairs={{0,3},{1,0},{2,1},{3,2},{4,7},{5,4},{6,5},{7,6},{8,11},{9,8},{10,9... | collective-permute-start | bytes 4718600 | tf_op jit(solution)/shard_map/ppermute | solution.py:23
  169.8 6.4 %shard_map.59 = bf16[1024,768]{1,0:T(8,128)(2,1)S(1)} custom-call(s32[64]{0:T(128)S(1)} %compare_select_fusion.pos_ref, bf16[8,8,128,128]{3,2,1,0:T(8,128)(2,1)S(1)} %pad_maximum_fusion.2.h_ref, bf16[36,128,768]{2,1,0:T(8,128)(2,1)} %bitcast.19, bf16[1024,768]{1,0:T(8,128)(2,1)S(1)} %copy-done), custom_call_target="tpu_custom_call" | custom-call | tf_op jit(solution)/shard_map/pallas_call | solution.py:64
  176.2 3.2 %collective-permute-start.18 = (bf16[1024,768]{1,0:T(8,128)(2,1)S(1)}, bf16[1024,768]{1,0:T(8,128)(2,1)S(1)}, u32[]{:S(2)}, u32[]{:S(2)}) collective-permute-start(bf16[1024,768]{1,0:T(8,128)(2,1)S(1)} %shard_map.59), channel_id=1, source_target_pairs={{0,3},{1,0},{2,1},{3,2},{4,7},{5,4},{6,5},{7,6},{8,11},{9,8},{10,9... | collective-permute-start | bytes 4718600 | tf_op jit(solution)/shard_map/ppermute | solution.py:23
  179.5 24.0 %collective-permute-done.25 = bf16[1024,768]{1,0:T(8,128)(2,1)S(1)} collective-permute-done((bf16[1024,768]{1,0:T(8,128)(2,1)S(1)}, bf16[1024,768]{1,0:T(8,128)(2,1)S(1)}, u32[]{:S(2)}, u32[]{:S(2)}) %collective-permute-start.25) | collective-permute-done | bytes 1572896 | tf_op jit(solution)/shard_map/ppermute | solution.py:22
  203.7 3.3 %collective-permute-start.27 = (bf16[512,768]{1,0:T(8,128)(2,1)S(1)}, bf16[512,768]{1,0:T(8,128)(2,1)S(1)}, u32[]{:S(2)}, u32[]{:S(2)}) collective-permute-start(bf16[512,768]{1,0:T(8,128)(2,1)S(1)} %slice.55), channel_id=1, source_target_pairs={{0,3},{1,0},{2,1},{3,2},{4,7},{5,4},{6,5},{7,6},{8,11},{9,8},{10,9... | collective-permute-start | bytes 2359304 | tf_op jit(solution)/shard_map/ppermute | solution.py:25
  208.5 28.6 %collective-permute-done.19 = bf16[1024,768]{1,0:T(8,128)(2,1)S(1)} collective-permute-done((bf16[1024,768]{1,0:T(8,128)(2,1)S(1)}, bf16[1024,768]{1,0:T(8,128)(2,1)S(1)}, u32[]{:S(2)}, u32[]{:S(2)}) %collective-permute-start.19) | collective-permute-done | bytes 1572896 | tf_op jit(solution)/shard_map/ppermute | solution.py:22
  237.4 3.3 %collective-permute-start.21 = (bf16[512,768]{1,0:T(8,128)(2,1)S(1)}, bf16[512,768]{1,0:T(8,128)(2,1)S(1)}, u32[]{:S(2)}, u32[]{:S(2)}) collective-permute-start(bf16[512,768]{1,0:T(8,128)(2,1)S(1)} %slice.53), channel_id=1, source_target_pairs={{0,3},{1,0},{2,1},{3,2},{4,7},{5,4},{6,5},{7,6},{8,11},{9,8},{10,9... | collective-permute-start | bytes 2359304 | tf_op jit(solution)/shard_map/ppermute | solution.py:25
  242.2 11.8 %collective-permute-done.26 = bf16[512,768]{1,0:T(8,128)(2,1)S(1)} collective-permute-done((bf16[512,768]{1,0:T(8,128)(2,1)S(1)}, bf16[512,768]{1,0:T(8,128)(2,1)S(1)}, u32[]{:S(2)}, u32[]{:S(2)}) %collective-permute-start.26) | collective-permute-done | bytes 786464 | tf_op jit(solution)/shard_map/ppermute | solution.py:24
  258.6 5.1 %collective-permute-start.29 = (bf16[256,768]{1,0:T(8,128)(2,1)S(1)}, bf16[256,768]{1,0:T(8,128)(2,1)S(1)}, u32[]{:S(2)}, u32[]{:S(2)}) collective-permute-start(bf16[256,768]{1,0:T(8,128)(2,1)S(1)} %get-tuple-element.4), channel_id=1, source_target_pairs={{0,124},{4,0},{8,4},{12,8},{16,12},{20,16},{24,20},{28,24},{32,28}... | collective-permute-start | bytes 1179656 | tf_op jit(solution)/shard_map/ppermute | solution.py:34
  263.7 2.7 collective-permute-done.20
  267.7 5.1 %collective-permute-start.23 = (bf16[256,768]{1,0:T(8,128)(2,1)S(1)}, bf16[256,768]{1,0:T(8,128)(2,1)S(1)}, u32[]{:S(2)}, u32[]{:S(2)}) collective-permute-start(bf16[256,768]{1,0:T(8,128)(2,1)S(1)} %get-tuple-element.2), channel_id=1, source_target_pairs={{0,124},{4,0},{8,4},{12,8},{16,12},{20,16},{24,20},{28,24},{32,28}... | collective-permute-start | bytes 1179656 | tf_op jit(solution)/shard_map/ppermute | solution.py:34
  274.7 2.8 copy-done.3
  277.5 6.4 %shard_map.62 = bf16[1024,768]{1,0:T(8,128)(2,1)S(1)} custom-call(s32[64]{0:T(128)S(1)} %compare_select_fusion.pos_ref, bf16[8,8,128,128]{3,2,1,0:T(8,128)(2,1)S(1)} %pad_maximum_fusion.2.h_ref, bf16[36,128,768]{2,1,0:T(8,128)(2,1)} %bitcast.22, bf16[1024,768]{1,0:T(8,128)(2,1)S(1)} %get-tuple-element.16.prev_ref), custom_call_target="tpu_custom_call" | custom-call | tf_op jit(solution)/shard_map/pallas_call | solution.py:64
  284.1 2.8 copy-done.2
  286.9 6.4 %shard_map.61 = bf16[1024,768]{1,0:T(8,128)(2,1)S(1)} custom-call(s32[64]{0:T(128)S(1)} %compare_select_fusion.pos_ref, bf16[8,8,128,128]{3,2,1,0:T(8,128)(2,1)S(1)} %pad_maximum_fusion.2.h_ref, bf16[36,128,768]{2,1,0:T(8,128)(2,1)} %bitcast.21, bf16[1024,768]{1,0:T(8,128)(2,1)S(1)} %get-tuple-element.17.prev_ref), custom_call_target="tpu_custom_call" | custom-call | tf_op jit(solution)/shard_map/pallas_call | solution.py:64
  (108 shorter events, 46.6 us)
Async XLA Ops:
  5.6 84.0 %collective-permute-start.12 = (bf16[1024,768]{1,0:T(8,128)(2,1)S(1)}, bf16[1024,768]{1,0:T(8,128)(2,1)}, u32[]{:S(2)}, u32[]{:S(2)}) collective-permute-start(bf16[1024,768]{1,0:T(8,128)(2,1)S(1)} %get-tuple-element.16.prev_ref), channel_id=1, source_target_pairs={{0,3},{1,0},{2,1},{3,2},{4,7},{5,4},{6,5},{7,6},{8,11},{9,8},{10,9... | collective-permute-start | bytes 4718600 | tf_op jit(solution)/shard_map/ppermute | solution.py:23
  9.8 80.7 %collective-permute-start.13 = (bf16[1024,768]{1,0:T(8,128)(2,1)S(1)}, bf16[1024,768]{1,0:T(8,128)(2,1)}, u32[]{:S(2)}, u32[]{:S(2)}) collective-permute-start(bf16[1024,768]{1,0:T(8,128)(2,1)S(1)} %get-tuple-element.16.prev_ref), channel_id=1, source_target_pairs={{0,1},{1,2},{2,3},{3,0},{4,5},{5,6},{6,7},{7,4},{8,9},{9,10},{10,1... | collective-permute-start | bytes 4718600 | tf_op jit(solution)/shard_map/ppermute | solution.py:22
  9.8 106.3 %collective-permute-start.7 = (bf16[1024,768]{1,0:T(8,128)(2,1)S(1)}, bf16[1024,768]{1,0:T(8,128)(2,1)}, u32[]{:S(2)}, u32[]{:S(2)}) collective-permute-start(bf16[1024,768]{1,0:T(8,128)(2,1)S(1)} %get-tuple-element.17.prev_ref), channel_id=1, source_target_pairs={{0,1},{1,2},{2,3},{3,0},{4,5},{5,6},{6,7},{7,4},{8,9},{9,10},{10,1... | collective-permute-start | bytes 4718600 | tf_op jit(solution)/shard_map/ppermute | solution.py:22
  9.8 110.2 %collective-permute-start.6 = (bf16[1024,768]{1,0:T(8,128)(2,1)S(1)}, bf16[1024,768]{1,0:T(8,128)(2,1)}, u32[]{:S(2)}, u32[]{:S(2)}) collective-permute-start(bf16[1024,768]{1,0:T(8,128)(2,1)S(1)} %get-tuple-element.17.prev_ref), channel_id=1, source_target_pairs={{0,3},{1,0},{2,1},{3,2},{4,7},{5,4},{6,5},{7,6},{8,11},{9,8},{10,9... | collective-permute-start | bytes 4718600 | tf_op jit(solution)/shard_map/ppermute | solution.py:23
  13.1 64.0 %collective-permute-start.2 = (s32[8,2]{0,1:T(2,128)S(1)}, s32[8,2]{0,1:T(2,128)S(1)}, u32[]{:S(2)}, u32[]{:S(2)}) collective-permute-start(s32[8,2]{0,1:T(2,128)S(1)} %bitcast.29), channel_id=1, source_target_pairs={{0,3},{1,0},{2,1},{3,2},{4,7},{5,4},{6,5},{7,6},{8,11},{9,8},{10,9... | collective-permute-start | bytes 200 | tf_op jit(solution)/shard_map/ppermute | solution.py:88
  77.2 5.1 %collective-permute-start.1 = (s32[8,2]{0,1:T(2,128)S(1)}, s32[8,2]{0,1:T(2,128)S(1)}, u32[]{:S(2)}, u32[]{:S(2)}) collective-permute-start(s32[8,2]{0,1:T(2,128)S(1)} %bitcast.28), channel_id=1, source_target_pairs={{0,2},{1,3},{2,0},{3,1},{4,6},{5,7},{6,4},{7,5},{8,10},{9,11},{10,... | collective-permute-start | bytes 200 | tf_op jit(solution)/shard_map/ppermute | solution.py:88
  82.2 5.3 %collective-permute-start = (s32[8,2]{0,1:T(2,128)S(1)}, s32[8,2]{0,1:T(2,128)S(1)}, u32[]{:S(2)}, u32[]{:S(2)}) collective-permute-start(s32[8,2]{0,1:T(2,128)S(1)} %bitcast.27), channel_id=1, source_target_pairs={{0,1},{1,2},{2,3},{3,0},{4,5},{5,6},{6,7},{7,4},{8,9},{9,10},{10,1... | collective-permute-start | bytes 200 | tf_op jit(solution)/shard_map/ppermute | solution.py:88
  87.6 22.6 %collective-permute-start.5 = (bf16[8,2,128,128]{3,2,1,0:T(8,128)(2,1)}, bf16[8,2,128,128]{3,2,1,0:T(8,128)(2,1)}, u32[]{:S(2)}, u32[]{:S(2)}) collective-permute-start(bf16[8,2,128,128]{3,2,1,0:T(8,128)(2,1)} %get-tuple-element.19), channel_id=1, source_target_pairs={{0,3},{1,0},{2,1},{3,2},{4,7},{5,4},{6,5},{7,6},{8,11},{9,8},{10,9... | collective-permute-start | bytes 1572872 | tf_op jit(solution)/shard_map/ppermute | solution.py:87
  89.6 20.5 %collective-permute-start.4 = (bf16[8,2,128,128]{3,2,1,0:T(8,128)(2,1)}, bf16[8,2,128,128]{3,2,1,0:T(8,128)(2,1)}, u32[]{:S(2)}, u32[]{:S(2)}) collective-permute-start(bf16[8,2,128,128]{3,2,1,0:T(8,128)(2,1)} %get-tuple-element.20), channel_id=1, source_target_pairs={{0,2},{1,3},{2,0},{3,1},{4,6},{5,7},{6,4},{7,5},{8,10},{9,11},{10,... | collective-permute-start | bytes 1572872 | tf_op jit(solution)/shard_map/ppermute | solution.py:87
  90.5 23.9 %collective-permute-start.3 = (bf16[8,2,128,128]{3,2,1,0:T(8,128)(2,1)}, bf16[8,2,128,128]{3,2,1,0:T(8,128)(2,1)}, u32[]{:S(2)}, u32[]{:S(2)}) collective-permute-start(bf16[8,2,128,128]{3,2,1,0:T(8,128)(2,1)} %get-tuple-element.21), channel_id=1, source_target_pairs={{0,1},{1,2},{2,3},{3,0},{4,5},{5,6},{6,7},{7,4},{8,9},{9,10},{10,1... | collective-permute-start | bytes 1572872 | tf_op jit(solution)/shard_map/ppermute | solution.py:87
  97.0 28.3 %slice-start = ((s8[6291456]{0:T(1024)(128)(4,1)}), s8[2097152]{0:T(1024)(128)(4,1)S(1)}, s32[]{:S(2)}) async-start(s8[6291456]{0:T(1024)(128)(4,1)} %bitcast.24), calls=%async_computation | async-start | bytes 4194304
  110.1 22.2 %collective-permute-start.14 = (bf16[512,768]{1,0:T(8,128)(2,1)S(1)}, bf16[512,768]{1,0:T(8,128)(2,1)S(1)}, u32[]{:S(2)}, u32[]{:S(2)}) collective-permute-start(bf16[512,768]{1,0:T(8,128)(2,1)S(1)} %slice.50), channel_id=1, source_target_pairs={{0,1},{1,2},{2,3},{3,0},{4,5},{5,6},{6,7},{7,4},{8,9},{9,10},{10,1... | collective-permute-start | bytes 2359304 | tf_op jit(solution)/shard_map/ppermute | solution.py:24
  110.1 23.2 %collective-permute-start.15 = (bf16[512,768]{1,0:T(8,128)(2,1)S(1)}, bf16[512,768]{1,0:T(8,128)(2,1)S(1)}, u32[]{:S(2)}, u32[]{:S(2)}) collective-permute-start(bf16[512,768]{1,0:T(8,128)(2,1)S(1)} %slice.51), channel_id=1, source_target_pairs={{0,3},{1,0},{2,1},{3,2},{4,7},{5,4},{6,5},{7,6},{8,11},{9,8},{10,9... | collective-permute-start | bytes 2359304 | tf_op jit(solution)/shard_map/ppermute | solution.py:25
  117.5 29.5 %collective-permute-start.8 = (bf16[512,768]{1,0:T(8,128)(2,1)S(1)}, bf16[512,768]{1,0:T(8,128)(2,1)S(1)}, u32[]{:S(2)}, u32[]{:S(2)}) collective-permute-start(bf16[512,768]{1,0:T(8,128)(2,1)S(1)} %slice.48), channel_id=1, source_target_pairs={{0,1},{1,2},{2,3},{3,0},{4,5},{5,6},{6,7},{7,4},{8,9},{9,10},{10,1... | collective-permute-start | bytes 2359304 | tf_op jit(solution)/shard_map/ppermute | solution.py:24
  121.2 26.7 %collective-permute-start.9 = (bf16[512,768]{1,0:T(8,128)(2,1)S(1)}, bf16[512,768]{1,0:T(8,128)(2,1)S(1)}, u32[]{:S(2)}, u32[]{:S(2)}) collective-permute-start(bf16[512,768]{1,0:T(8,128)(2,1)S(1)} %slice.49), channel_id=1, source_target_pairs={{0,3},{1,0},{2,1},{3,2},{4,7},{5,4},{6,5},{7,6},{8,11},{9,8},{10,9... | collective-permute-start | bytes 2359304 | tf_op jit(solution)/shard_map/ppermute | solution.py:25
  137.2 19.8 %collective-permute-start.16 = (bf16[256,768]{1,0:T(8,128)(2,1)S(1)}, bf16[256,768]{1,0:T(8,128)(2,1)S(1)}, u32[]{:S(2)}, u32[]{:S(2)}) collective-permute-start(bf16[256,768]{1,0:T(8,128)(2,1)S(1)} %get-tuple-element.9), channel_id=1, source_target_pairs={{0,4},{4,8},{8,12},{12,16},{16,20},{20,24},{24,28},{28,32},{32,36}... | collective-permute-start | bytes 1179656 | tf_op jit(solution)/shard_map/ppermute | solution.py:33
  137.2 20.5 %collective-permute-start.17 = (bf16[256,768]{1,0:T(8,128)(2,1)S(1)}, bf16[256,768]{1,0:T(8,128)(2,1)S(1)}, u32[]{:S(2)}, u32[]{:S(2)}) collective-permute-start(bf16[256,768]{1,0:T(8,128)(2,1)S(1)} %get-tuple-element.8), channel_id=1, source_target_pairs={{0,124},{4,0},{8,4},{12,8},{16,12},{20,16},{24,20},{28,24},{32,28}... | collective-permute-start | bytes 1179656 | tf_op jit(solution)/shard_map/ppermute | solution.py:34
  151.8 16.4 %collective-permute-start.10 = (bf16[256,768]{1,0:T(8,128)(2,1)S(1)}, bf16[256,768]{1,0:T(8,128)(2,1)S(1)}, u32[]{:S(2)}, u32[]{:S(2)}) collective-permute-start(bf16[256,768]{1,0:T(8,128)(2,1)S(1)} %get-tuple-element.7), channel_id=1, source_target_pairs={{0,4},{4,8},{8,12},{12,16},{16,20},{20,24},{24,28},{28,32},{32,36}... | collective-permute-start | bytes 1179656 | tf_op jit(solution)/shard_map/ppermute | solution.py:33
  151.9 17.1 %collective-permute-start.11 = (bf16[256,768]{1,0:T(8,128)(2,1)S(1)}, bf16[256,768]{1,0:T(8,128)(2,1)S(1)}, u32[]{:S(2)}, u32[]{:S(2)}) collective-permute-start(bf16[256,768]{1,0:T(8,128)(2,1)S(1)} %get-tuple-element.6), channel_id=1, source_target_pairs={{0,124},{4,0},{8,4},{12,8},{16,12},{20,16},{24,20},{28,24},{32,28}... | collective-permute-start | bytes 1179656 | tf_op jit(solution)/shard_map/ppermute | solution.py:34
  164.9 38.5 %collective-permute-start.25 = (bf16[1024,768]{1,0:T(8,128)(2,1)S(1)}, bf16[1024,768]{1,0:T(8,128)(2,1)S(1)}, u32[]{:S(2)}, u32[]{:S(2)}) collective-permute-start(bf16[1024,768]{1,0:T(8,128)(2,1)S(1)} %shard_map.60), channel_id=1, source_target_pairs={{0,1},{1,2},{2,3},{3,0},{4,5},{5,6},{6,7},{7,4},{8,9},{9,10},{10,1... | collective-permute-start | bytes 4718600 | tf_op jit(solution)/shard_map/ppermute | solution.py:22
  165.1 38.5 %collective-permute-start.24 = (bf16[1024,768]{1,0:T(8,128)(2,1)S(1)}, bf16[1024,768]{1,0:T(8,128)(2,1)S(1)}, u32[]{:S(2)}, u32[]{:S(2)}) collective-permute-start(bf16[1024,768]{1,0:T(8,128)(2,1)S(1)} %shard_map.60), channel_id=1, source_target_pairs={{0,3},{1,0},{2,1},{3,2},{4,7},{5,4},{6,5},{7,6},{8,11},{9,8},{10,9... | collective-permute-start | bytes 4718600 | tf_op jit(solution)/shard_map/ppermute | solution.py:23
  176.2 61.0 %collective-permute-start.19 = (bf16[1024,768]{1,0:T(8,128)(2,1)S(1)}, bf16[1024,768]{1,0:T(8,128)(2,1)S(1)}, u32[]{:S(2)}, u32[]{:S(2)}) collective-permute-start(bf16[1024,768]{1,0:T(8,128)(2,1)S(1)} %shard_map.59), channel_id=1, source_target_pairs={{0,1},{1,2},{2,3},{3,0},{4,5},{5,6},{6,7},{7,4},{8,9},{9,10},{10,1... | collective-permute-start | bytes 4718600 | tf_op jit(solution)/shard_map/ppermute | solution.py:22
  176.2 61.0 %collective-permute-start.18 = (bf16[1024,768]{1,0:T(8,128)(2,1)S(1)}, bf16[1024,768]{1,0:T(8,128)(2,1)S(1)}, u32[]{:S(2)}, u32[]{:S(2)}) collective-permute-start(bf16[1024,768]{1,0:T(8,128)(2,1)S(1)} %shard_map.59), channel_id=1, source_target_pairs={{0,3},{1,0},{2,1},{3,2},{4,7},{5,4},{6,5},{7,6},{8,11},{9,8},{10,9... | collective-permute-start | bytes 4718600 | tf_op jit(solution)/shard_map/ppermute | solution.py:23
  203.5 50.5 %collective-permute-start.26 = (bf16[512,768]{1,0:T(8,128)(2,1)S(1)}, bf16[512,768]{1,0:T(8,128)(2,1)S(1)}, u32[]{:S(2)}, u32[]{:S(2)}) collective-permute-start(bf16[512,768]{1,0:T(8,128)(2,1)S(1)} %slice.54), channel_id=1, source_target_pairs={{0,1},{1,2},{2,3},{3,0},{4,5},{5,6},{6,7},{7,4},{8,9},{9,10},{10,1... | collective-permute-start | bytes 2359304 | tf_op jit(solution)/shard_map/ppermute | solution.py:24
  203.7 51.3 %collective-permute-start.27 = (bf16[512,768]{1,0:T(8,128)(2,1)S(1)}, bf16[512,768]{1,0:T(8,128)(2,1)S(1)}, u32[]{:S(2)}, u32[]{:S(2)}) collective-permute-start(bf16[512,768]{1,0:T(8,128)(2,1)S(1)} %slice.55), channel_id=1, source_target_pairs={{0,3},{1,0},{2,1},{3,2},{4,7},{5,4},{6,5},{7,6},{8,11},{9,8},{10,9... | collective-permute-start | bytes 2359304 | tf_op jit(solution)/shard_map/ppermute | solution.py:25
  208.3 32.3 %copy-start.7 = (bf16[1024,768]{1,0:T(8,128)(2,1)S(1)}, bf16[1024,768]{1,0:T(8,128)(2,1)}, u32[]{:S(2)}) copy-start(bf16[1024,768]{1,0:T(8,128)(2,1)} %copy-done.6) | copy-start | bytes 4718596
  237.2 29.2 %collective-permute-start.20 = (bf16[512,768]{1,0:T(8,128)(2,1)S(1)}, bf16[512,768]{1,0:T(8,128)(2,1)S(1)}, u32[]{:S(2)}, u32[]{:S(2)}) collective-permute-start(bf16[512,768]{1,0:T(8,128)(2,1)S(1)} %slice.52), channel_id=1, source_target_pairs={{0,1},{1,2},{2,3},{3,0},{4,5},{5,6},{6,7},{7,4},{8,9},{9,10},{10,1... | collective-permute-start | bytes 2359304 | tf_op jit(solution)/shard_map/ppermute | solution.py:24
  237.4 29.2 %collective-permute-start.21 = (bf16[512,768]{1,0:T(8,128)(2,1)S(1)}, bf16[512,768]{1,0:T(8,128)(2,1)S(1)}, u32[]{:S(2)}, u32[]{:S(2)}) collective-permute-start(bf16[512,768]{1,0:T(8,128)(2,1)S(1)} %slice.53), channel_id=1, source_target_pairs={{0,3},{1,0},{2,1},{3,2},{4,7},{5,4},{6,5},{7,6},{8,11},{9,8},{10,9... | collective-permute-start | bytes 2359304 | tf_op jit(solution)/shard_map/ppermute | solution.py:25
  258.6 16.1 %collective-permute-start.28 = (bf16[256,768]{1,0:T(8,128)(2,1)S(1)}, bf16[256,768]{1,0:T(8,128)(2,1)S(1)}, u32[]{:S(2)}, u32[]{:S(2)}) collective-permute-start(bf16[256,768]{1,0:T(8,128)(2,1)S(1)} %get-tuple-element.5), channel_id=1, source_target_pairs={{0,4},{4,8},{8,12},{12,16},{16,20},{20,24},{24,28},{28,32},{32,36}... | collective-permute-start | bytes 1179656 | tf_op jit(solution)/shard_map/ppermute | solution.py:33
  258.6 16.1 %collective-permute-start.29 = (bf16[256,768]{1,0:T(8,128)(2,1)S(1)}, bf16[256,768]{1,0:T(8,128)(2,1)S(1)}, u32[]{:S(2)}, u32[]{:S(2)}) collective-permute-start(bf16[256,768]{1,0:T(8,128)(2,1)S(1)} %get-tuple-element.4), channel_id=1, source_target_pairs={{0,124},{4,0},{8,4},{12,8},{16,12},{20,16},{24,20},{28,24},{32,28}... | collective-permute-start | bytes 1179656 | tf_op jit(solution)/shard_map/ppermute | solution.py:34
  267.7 16.3 %collective-permute-start.22 = (bf16[256,768]{1,0:T(8,128)(2,1)}, bf16[256,768]{1,0:T(8,128)(2,1)S(1)}, u32[]{:S(2)}, u32[]{:S(2)}) collective-permute-start(bf16[256,768]{1,0:T(8,128)(2,1)} %get-tuple-element.3), channel_id=1, source_target_pairs={{0,4},{4,8},{8,12},{12,16},{16,20},{20,24},{24,28},{28,32},{32,36}... | collective-permute-start | bytes 1179656 | tf_op jit(solution)/shard_map/ppermute | solution.py:33
  267.7 16.3 %collective-permute-start.23 = (bf16[256,768]{1,0:T(8,128)(2,1)S(1)}, bf16[256,768]{1,0:T(8,128)(2,1)S(1)}, u32[]{:S(2)}, u32[]{:S(2)}) collective-permute-start(bf16[256,768]{1,0:T(8,128)(2,1)S(1)} %get-tuple-element.2), channel_id=1, source_target_pairs={{0,124},{4,0},{8,4},{12,8},{16,12},{20,16},{24,20},{28,24},{32,28}... | collective-permute-start | bytes 1179656 | tf_op jit(solution)/shard_map/ppermute | solution.py:34
  (10 other events, 99.1 us)

commit v9 on v8

--- a/solution.py
+++ b/solution.py
@@ -26,12 +26,9 @@
     panel = jnp.concatenate([own, from_next, far_a, far_b, from_prev], axis=0)
     rows = own.shape[0]
     width = HB * block_size
-    last_at = ((nl - 1 - lidx) % nl) * rows + rows - width
-    first_at = ((0 - lidx) % nl) * rows
-    last = lax.dynamic_slice_in_dim(panel, last_at, width, axis=0)
-    first = lax.dynamic_slice_in_dim(panel, first_at, width, axis=0)
-    lo = lax.ppermute(last, "grid", shift(ng, 1))
-    hi = lax.ppermute(first, "grid", shift(ng, ng - 1))
+    flat = ("grid", "layer")
+    lo = sum(lax.ppermute(own[rows - width:], flat, [(((g - 1) % ng) * nl + nl - 1, g * nl + k) for g in range(ng)]) for k in range(nl))
+    hi = sum(lax.ppermute(own[:width], flat, [(((g + 1) % ng) * nl, g * nl + k) for g in range(ng)]) for k in range(nl))
     return jnp.concatenate([panel, lo, hi], axis=0)
 
 

time: 296 us -> 403 us (1.36)
  starting transfers between devices: 58.7 us -> 182 us
  waiting for transfers between devices: 154 us -> 139 us
  local copies, waits for them, and re-layouts: 50.5 us -> 41.9 us
  other arithmetic: 5.64 us -> 11.8 us
    ppermute x8 -> x32, starting transfers between devices: 20.4 us -> 104 us  [the longest x16 90.1 us: exchange(): lax.ppermute(own[:width], flat, [((g + 1) % ng * nl, g * nl + k) for g in...]
    ppermute x4, starting transfers between devices: 0.24 us -> 33 us  [exchange(): from_prev = lax.ppermute(own, 'layer', shift(nl, 1))]
    ppermute x4, waiting for transfers between devices: 52.6 us -> 26.3 us  [exchange(): from_prev = lax.ppermute(own, 'layer', shift(nl, 1))]
    ppermute x8 -> x32, waiting for transfers between devices: 0.02 us -> 25.6 us  [the longest x16 25.5 us: exchange(): lax.ppermute(own[:width], flat, [((g + 1) % ng * nl, g * nl + k) for g in...]
    ppermute x4, starting transfers between devices: 11.7 us -> 29.6 us  [exchange(): far_b = lax.ppermute(from_next[half:], 'layer', shift(nl, nl - 1))]
    ppermute x4, waiting for transfers between devices: 23.5 us -> 9.17 us  [exchange(): far_a = lax.ppermute(from_prev[:half], 'layer', shift(nl, 1))]
    ppermute x4, starting transfers between devices: 13.8 us -> 2.13 us  [exchange(): from_next = lax.ppermute(own, 'layer', shift(nl, nl - 1))]
    concatenate x8 -> x0, local copies, waits for them, and re-layouts: 8.78 us -> none  [the longest x4 7.17 us: exchange(): panel = jnp.concatenate([own, from_next, far_a, far_b, from_prev], axis=0)]
  transfers between devices with their start and end apart: 30 -> 54, of which waited for: 11 -> 18; matrix products, arithmetic and copies ran while one was open for 15% -> 11% of each run, Pallas kernels for 7% -> 5%
where the time goes in v9:
time: 403 us; the launch traced here: 401 us
  starting transfers between devices  182 us (45%)
  waiting for transfers between devices  139 us (34%)
  local copies, waits for them, and re-layouts  41.9 us (10%)
  Pallas kernels  25.6 us (6%)
  other arithmetic  11.8 us (3%)
    ppermute x16, starting transfers between devices, exchange(): lax.ppermute(own[:width], flat, [((g + 1) % ng * nl, g * nl + k) for g in...  90.1 us
    ppermute x3, waiting for transfers between devices, shards(): lax.ppermute(lax.dynamic_index_in_dim(p_split, dest, 0, keepdims=False),...  63.6 us
    ppermute x4, starting transfers between devices, exchange(): from_prev = lax.ppermute(own, 'layer', shift(nl, 1))  33 us
    ppermute x4, starting transfers between devices, exchange(): far_b = lax.ppermute(from_next[half:], 'layer', shift(nl, nl - 1))  29.6 us
    ppermute x4, waiting for transfers between devices, exchange(): from_prev = lax.ppermute(own, 'layer', shift(nl, 1))  26.3 us
    pallas_call x4, Pallas kernels, own_rows(): pl.pallas_call(step_kernel, grid_spec=grid_spec, out_shape=jax.ShapeDtype...  25.6 us
    ppermute x16, waiting for transfers between devices, exchange(): lax.ppermute(own[:width], flat, [((g + 1) % ng * nl, g * nl + k) for g in...  25.5 us
    unnamed x36, local copies, waits for them, and re-layouts  22.3 us
  transfers between devices with their start and end apart: 54, of which 18 were waited for; matrix products, arithmetic and copies ran while one was open for 11% of the time, Pallas kernels for 5%

profile of v9, /device:TPU:0, one launch (start us, length us, event | category | flops | bytes accessed | tf_op | source)
XLA Modules:
  0.0 401.4 jit_solution(7308989365739100399)
XLA Ops:
  0.6 4.0 %fusion.6 = (bf16[1024,768]{1,0:T(8,128)(2,1)S(1)}, bf16[4608,768]{1,0:T(8,128)(2,1)}, bf16[4608,768]{1,0:T(8,128)(2,1)}, bf16[1024,768]{1,0:T(8,128)(2,1)S(1)}) fusion(bf16[1024,1536]{1,0:T(8,128)(2,1)} %param.6), kind=kLoop, calls=%fused_computation.60 | loop fusion | bytes 9437184 | tf_op jit(solution)/shard_map/slice | solution.py:104
  8.8 2.9 dynamic-slice_bitcast_fusion.3
  11.7 3.2 collective-permute-start.5
  15.9 38.2 %collective-permute-done.2 = s32[8,2]{0,1:T(2,128)S(1)} collective-permute-done((s32[8,2]{0,1:T(2,128)S(1)}, s32[8,2]{0,1:T(2,128)S(1)}, u32[]{:S(2)}, u32[]{:S(2)}) %collective-permute-start.2) | collective-permute-done | bytes 96 | tf_op jit(solution)/shard_map/ppermute | solution.py:85
  54.1 3.4 collective-permute-start.1
  57.5 20.6 %collective-permute-done.1 = s32[8,2]{0,1:T(2,128)S(1)} collective-permute-done((s32[8,2]{0,1:T(2,128)S(1)}, s32[8,2]{0,1:T(2,128)S(1)}, u32[]{:S(2)}, u32[]{:S(2)}) %collective-permute-start.1) | collective-permute-done | bytes 96 | tf_op jit(solution)/shard_map/ppermute | solution.py:85
  78.1 4.8 %collective-permute-done = s32[8,2]{0,1:T(2,128)S(1)} collective-permute-done((s32[8,2]{0,1:T(2,128)S(1)}, s32[8,2]{0,1:T(2,128)S(1)}, u32[]{:S(2)}, u32[]{:S(2)}) %collective-permute-start) | collective-permute-done | bytes 96 | tf_op jit(solution)/shard_map/ppermute | solution.py:85
  85.0 3.7 fusion.4
  94.7 4.8 %collective-permute-done.4 = bf16[8,2,128,128]{3,2,1,0:T(8,128)(2,1)} collective-permute-done((bf16[8,2,128,128]{3,2,1,0:T(8,128)(2,1)}, bf16[8,2,128,128]{3,2,1,0:T(8,128)(2,1)}, u32[]{:S(2)}, u32[]{:S(2)}) %collective-permute-start.4) | collective-permute-done | bytes 524320 | tf_op jit(solution)/shard_map/ppermute | solution.py:84
  100.2 7.4 %collective-permute-done.3 = bf16[8,2,128,128]{3,2,1,0:T(8,128)(2,1)} collective-permute-done((bf16[8,2,128,128]{3,2,1,0:T(8,128)(2,1)}, bf16[8,2,128,128]{3,2,1,0:T(8,128)(2,1)}, u32[]{:S(2)}, u32[]{:S(2)}) %collective-permute-start.3) | collective-permute-done | bytes 524320 | tf_op jit(solution)/shard_map/ppermute | solution.py:84
  108.4 26.9 %collective-permute-start.21 = (bf16[512,768]{1,0:T(8,128)(2,1)S(1)}, bf16[512,768]{1,0:T(8,128)(2,1)S(1)}, u32[]{:S(2)}, u32[]{:S(2)}) collective-permute-start(bf16[512,768]{1,0:T(8,128)(2,1)S(1)} %slice.111), channel_id=1, source_target_pairs={{0,3},{1,0},{2,1},{3,2},{4,7},{5,4},{6,5},{7,6},{8,11},{9,8},{10,9... | collective-permute-start | bytes 2359304 | tf_op jit(solution)/shard_map/ppermute | solution.py:25
  144.3 10.4 %collective-permute-start.29 = (bf16[256,768]{1,0:T(8,128)(2,1)S(1)}, bf16[256,768]{1,0:T(8,128)(2,1)S(1)}, u32[]{:S(2)}, u32[]{:S(2)}) collective-permute-start(bf16[256,768]{1,0:T(8,128)(2,1)S(1)} %copy-done.6), channel_id=1, source_target_pairs={{4,3},{8,7},{12,11},{16,15},{20,19},{24,23},{28,27},{32,31},{36,35... | collective-permute-start | bytes 1179656 | tf_op jit(solution)/shard_map/ppermute | solution.py:31
  154.7 3.0 collective-permute-start.28
  165.3 11.6 %collective-permute-start.27 = (bf16[256,768]{1,0:T(8,128)(2,1)S(1)}, bf16[256,768]{1,0:T(8,128)(2,1)S(1)}, u32[]{:S(2)}, u32[]{:S(2)}) collective-permute-start(bf16[256,768]{1,0:T(8,128)(2,1)S(1)} %copy-done.6), channel_id=1, source_target_pairs={{4,1},{8,5},{12,9},{16,13},{20,17},{24,21},{28,25},{32,29},{36,33}... | collective-permute-start | bytes 1179656 | tf_op jit(solution)/shard_map/ppermute | solution.py:31
  177.7 2.7 constant_dynamic-update-slice_fusion.5
  185.1 6.4 %shard_map.60 = bf16[1024,768]{1,0:T(8,128)(2,1)S(1)} custom-call(s32[64]{0:T(128)S(1)} %compare_select_fusion.pos_ref, bf16[8,8,128,128]{3,2,1,0:T(8,128)(2,1)S(1)} %pad_maximum_fusion.2.h_ref, bf16[36,128,768]{2,1,0:T(8,128)(2,1)} %bitcast.20, bf16[1024,768]{1,0:T(8,128)(2,1)S(1)} %copy-done.1), custom_call_target="tpu_custom_call" | custom-call | tf_op jit(solution)/shard_map/pallas_call | solution.py:61
  191.5 16.8 %collective-permute-start.17 = (bf16[256,768]{1,0:T(8,128)(2,1)S(1)}, bf16[256,768]{1,0:T(8,128)(2,1)S(1)}, u32[]{:S(2)}, u32[]{:S(2)}) collective-permute-start(bf16[256,768]{1,0:T(8,128)(2,1)S(1)} %get-tuple-element.4), channel_id=1, source_target_pairs={{4,3},{8,7},{12,11},{16,15},{20,19},{24,23},{28,27},{32,31},{36,35... | collective-permute-start | bytes 1179656 | tf_op jit(solution)/shard_map/ppermute | solution.py:31
  216.0 2.7 constant_dynamic-update-slice_fusion
  222.2 4.2 %collective-permute-done.15 = bf16[256,768]{1,0:T(8,128)(2,1)S(1)} collective-permute-done((bf16[256,768]{1,0:T(8,128)(2,1)S(1)}, bf16[256,768]{1,0:T(8,128)(2,1)S(1)}, u32[]{:S(2)}, u32[]{:S(2)}) %collective-permute-start.15) | collective-permute-done | bytes 393248 | tf_op jit(solution)/shard_map/ppermute | solution.py:31
  227.4 6.4 %shard_map.59 = bf16[1024,768]{1,0:T(8,128)(2,1)S(1)} custom-call(s32[64]{0:T(128)S(1)} %compare_select_fusion.pos_ref, bf16[8,8,128,128]{3,2,1,0:T(8,128)(2,1)S(1)} %pad_maximum_fusion.2.h_ref, bf16[36,128,768]{2,1,0:T(8,128)(2,1)} %bitcast.19, bf16[1024,768]{1,0:T(8,128)(2,1)S(1)} %copy-done), custom_call_target="tpu_custom_call" | custom-call | tf_op jit(solution)/shard_map/pallas_call | solution.py:61
  233.8 31.0 %collective-permute-start.31 = (bf16[1024,768]{1,0:T(8,128)(2,1)S(1)}, bf16[1024,768]{1,0:T(8,128)(2,1)S(1)}, u32[]{:S(2)}, u32[]{:S(2)}) collective-permute-start(bf16[1024,768]{1,0:T(8,128)(2,1)S(1)} %shard_map.59), channel_id=1, source_target_pairs={{0,1},{1,2},{2,3},{3,0},{4,5},{5,6},{6,7},{7,4},{8,9},{9,10},{10,1... | collective-permute-start | bytes 4718600 | tf_op jit(solution)/shard_map/ppermute | solution.py:22
  273.2 26.3 %collective-permute-done.31 = bf16[1024,768]{1,0:T(8,128)(2,1)S(1)} collective-permute-done((bf16[1024,768]{1,0:T(8,128)(2,1)S(1)}, bf16[1024,768]{1,0:T(8,128)(2,1)S(1)}, u32[]{:S(2)}, u32[]{:S(2)}) %collective-permute-start.31) | collective-permute-done | bytes 1572896 | tf_op jit(solution)/shard_map/ppermute | solution.py:22
  304.2 9.2 %collective-permute-done.44 = bf16[512,768]{1,0:T(8,128)(2,1)S(1)} collective-permute-done((bf16[512,768]{1,0:T(8,128)(2,1)S(1)}, bf16[512,768]{1,0:T(8,128)(2,1)S(1)}, u32[]{:S(2)}, u32[]{:S(2)}) %collective-permute-start.44) | collective-permute-done | bytes 786464 | tf_op jit(solution)/shard_map/ppermute | solution.py:24
  316.9 18.4 %collective-permute-start.52 = (bf16[256,768]{1,0:T(8,128)(2,1)S(1)}, bf16[256,768]{1,0:T(8,128)(2,1)S(1)}, u32[]{:S(2)}, u32[]{:S(2)}) collective-permute-start(bf16[256,768]{1,0:T(8,128)(2,1)S(1)} %get-tuple-element.18), channel_id=1, source_target_pairs={{4,2},{8,6},{12,10},{16,14},{20,18},{24,22},{28,26},{32,30},{36,34... | collective-permute-start | bytes 1179656 | tf_op jit(solution)/shard_map/ppermute | solution.py:31
  341.2 3.5 collective-permute-done.50
  345.4 3.5 collective-permute-done.51
  350.5 2.9 copy-done.3
  353.4 6.4 %shard_map.62 = bf16[1024,768]{1,0:T(8,128)(2,1)S(1)} custom-call(s32[64]{0:T(128)S(1)} %compare_select_fusion.pos_ref, bf16[8,8,128,128]{3,2,1,0:T(8,128)(2,1)S(1)} %pad_maximum_fusion.2.h_ref, bf16[36,128,768]{2,1,0:T(8,128)(2,1)} %bitcast.22, bf16[1024,768]{1,0:T(8,128)(2,1)S(1)} %get-tuple-element.11.prev_ref), custom_call_target="tpu_custom_call" | custom-call | tf_op jit(solution)/shard_map/pallas_call | solution.py:61
  361.5 12.8 %collective-permute-start.41 = (bf16[256,768]{1,0:T(8,128)(2,1)S(1)}, bf16[256,768]{1,0:T(8,128)(2,1)S(1)}, u32[]{:S(2)}, u32[]{:S(2)}) collective-permute-start(bf16[256,768]{1,0:T(8,128)(2,1)S(1)} %get-tuple-element.16), channel_id=1, source_target_pairs={{4,3},{8,7},{12,11},{16,15},{20,19},{24,23},{28,27},{32,31},{36,35... | collective-permute-start | bytes 1179656 | tf_op jit(solution)/shard_map/ppermute | solution.py:31
  383.7 4.2 %collective-permute-done.38 = bf16[256,768]{1,0:T(8,128)(2,1)S(1)} collective-permute-done((bf16[256,768]{1,0:T(8,128)(2,1)S(1)}, bf16[256,768]{1,0:T(8,128)(2,1)S(1)}, u32[]{:S(2)}, u32[]{:S(2)}) %collective-permute-start.38) | collective-permute-done | bytes 393248 | tf_op jit(solution)/shard_map/ppermute | solution.py:31
  387.9 4.2 %collective-permute-done.39 = bf16[256,768]{1,0:T(8,128)(2,1)S(1)} collective-permute-done((bf16[256,768]{1,0:T(8,128)(2,1)S(1)}, bf16[256,768]{1,0:T(8,128)(2,1)S(1)}, u32[]{:S(2)}, u32[]{:S(2)}) %collective-permute-start.39) | collective-permute-done | bytes 393248 | tf_op jit(solution)/shard_map/ppermute | solution.py:31
  393.1 6.4 %shard_map.61 = bf16[1024,768]{1,0:T(8,128)(2,1)S(1)} custom-call(s32[64]{0:T(128)S(1)} %compare_select_fusion.pos_ref, bf16[8,8,128,128]{3,2,1,0:T(8,128)(2,1)S(1)} %pad_maximum_fusion.2.h_ref, bf16[36,128,768]{2,1,0:T(8,128)(2,1)} %bitcast.21, bf16[1024,768]{1,0:T(8,128)(2,1)S(1)} %get-tuple-element.8.prev_ref), custom_call_target="tpu_custom_call" | custom-call | tf_op jit(solution)/shard_map/pallas_call | solution.py:61
  (148 shorter events, 87.0 us)
Async XLA Ops:
  4.7 79.1 %collective-permute-start.19 = (bf16[1024,768]{1,0:T(8,128)(2,1)S(1)}, bf16[1024,768]{1,0:T(8,128)(2,1)}, u32[]{:S(2)}, u32[]{:S(2)}) collective-permute-start(bf16[1024,768]{1,0:T(8,128)(2,1)S(1)} %get-tuple-element.11.prev_ref), channel_id=1, source_target_pairs={{0,1},{1,2},{2,3},{3,0},{4,5},{5,6},{6,7},{7,4},{8,9},{9,10},{10,1... | collective-permute-start | bytes 4718600 | tf_op jit(solution)/shard_map/ppermute | solution.py:22
  6.7 84.1 %collective-permute-start.18 = (bf16[1024,768]{1,0:T(8,128)(2,1)S(1)}, bf16[1024,768]{1,0:T(8,128)(2,1)}, u32[]{:S(2)}, u32[]{:S(2)}) collective-permute-start(bf16[1024,768]{1,0:T(8,128)(2,1)S(1)} %get-tuple-element.11.prev_ref), channel_id=1, source_target_pairs={{0,3},{1,0},{2,1},{3,2},{4,7},{5,4},{6,5},{7,6},{8,11},{9,8},{10,9... | collective-permute-start | bytes 4718600 | tf_op jit(solution)/shard_map/ppermute | solution.py:23
  8.8 99.5 %collective-permute-start.7 = (bf16[1024,768]{1,0:T(8,128)(2,1)S(1)}, bf16[1024,768]{1,0:T(8,128)(2,1)}, u32[]{:S(2)}, u32[]{:S(2)}) collective-permute-start(bf16[1024,768]{1,0:T(8,128)(2,1)S(1)} %get-tuple-element.8.prev_ref), channel_id=1, source_target_pairs={{0,1},{1,2},{2,3},{3,0},{4,5},{5,6},{6,7},{7,4},{8,9},{9,10},{10,1... | collective-permute-start | bytes 4718600 | tf_op jit(solution)/shard_map/ppermute | solution.py:22
  11.7 71.2 %collective-permute-start.5 = (bf16[8,2,128,128]{3,2,1,0:T(8,128)(2,1)}, bf16[8,2,128,128]{3,2,1,0:T(8,128)(2,1)}, u32[]{:S(2)}, u32[]{:S(2)}) collective-permute-start(bf16[8,2,128,128]{3,2,1,0:T(8,128)(2,1)} %get-tuple-element.13), channel_id=1, source_target_pairs={{0,3},{1,0},{2,1},{3,2},{4,7},{5,4},{6,5},{7,6},{8,11},{9,8},{10,9... | collective-permute-start | bytes 1572872 | tf_op jit(solution)/shard_map/ppermute | solution.py:84
  15.1 39.0 %collective-permute-start.2 = (s32[8,2]{0,1:T(2,128)S(1)}, s32[8,2]{0,1:T(2,128)S(1)}, u32[]{:S(2)}, u32[]{:S(2)}) collective-permute-start(s32[8,2]{0,1:T(2,128)S(1)} %bitcast.27), channel_id=1, source_target_pairs={{0,3},{1,0},{2,1},{3,2},{4,7},{5,4},{6,5},{7,6},{8,11},{9,8},{10,9... | collective-permute-start | bytes 200 | tf_op jit(solution)/shard_map/ppermute | solution.py:85
  82.9 55.4 %collective-permute-start.6 = (bf16[1024,768]{1,0:T(8,128)(2,1)S(1)}, bf16[1024,768]{1,0:T(8,128)(2,1)}, u32[]{:S(2)}, u32[]{:S(2)}) collective-permute-start(bf16[1024,768]{1,0:T(8,128)(2,1)S(1)} %get-tuple-element.8.prev_ref), channel_id=1, source_target_pairs={{0,3},{1,0},{2,1},{3,2},{4,7},{5,4},{6,5},{7,6},{8,11},{9,8},{10,9... | collective-permute-start | bytes 4718600 | tf_op jit(solution)/shard_map/ppermute | solution.py:23
  90.9 63.8 %collective-permute-start.20 = (bf16[512,768]{1,0:T(8,128)(2,1)}, bf16[512,768]{1,0:T(8,128)(2,1)}, u32[]{:S(2)}, u32[]{:S(2)}) collective-permute-start(bf16[512,768]{1,0:T(8,128)(2,1)} %slice.110), channel_id=1, source_target_pairs={{0,1},{1,2},{2,3},{3,0},{4,5},{5,6},{6,7},{7,4},{8,9},{9,10},{10,1... | collective-permute-start | bytes 2359304 | tf_op jit(solution)/shard_map/ppermute | solution.py:24
  99.6 43.9 %collective-permute-start.25 = (bf16[256,768]{1,0:T(8,128)(2,1)}, bf16[256,768]{1,0:T(8,128)(2,1)S(1)}, u32[]{:S(2)}, u32[]{:S(2)}) collective-permute-start(bf16[256,768]{1,0:T(8,128)(2,1)} %get-tuple-element.7), channel_id=1, source_target_pairs={{127,3},{3,7},{7,11},{11,15},{15,19},{19,23},{23,27},{27,31},{31,3... | collective-permute-start | bytes 1179656 | tf_op jit(solution)/shard_map/ppermute | solution.py:30
  107.7 36.6 %collective-permute-start.24 = (bf16[256,768]{1,0:T(8,128)(2,1)}, bf16[256,768]{1,0:T(8,128)(2,1)S(1)}, u32[]{:S(2)}, u32[]{:S(2)}) collective-permute-start(bf16[256,768]{1,0:T(8,128)(2,1)} %get-tuple-element.7), channel_id=1, source_target_pairs={{127,2},{3,6},{7,10},{11,14},{15,18},{19,22},{23,26},{27,30},{31,3... | collective-permute-start | bytes 1179656 | tf_op jit(solution)/shard_map/ppermute | solution.py:30
  108.4 54.0 %collective-permute-start.21 = (bf16[512,768]{1,0:T(8,128)(2,1)S(1)}, bf16[512,768]{1,0:T(8,128)(2,1)S(1)}, u32[]{:S(2)}, u32[]{:S(2)}) collective-permute-start(bf16[512,768]{1,0:T(8,128)(2,1)S(1)} %slice.111), channel_id=1, source_target_pairs={{0,3},{1,0},{2,1},{3,2},{4,7},{5,4},{6,5},{7,6},{8,11},{9,8},{10,9... | collective-permute-start | bytes 2359304 | tf_op jit(solution)/shard_map/ppermute | solution.py:25
  138.3 25.0 %collective-permute-start.22 = (bf16[256,768]{1,0:T(8,128)(2,1)S(1)}, bf16[256,768]{1,0:T(8,128)(2,1)S(1)}, u32[]{:S(2)}, u32[]{:S(2)}) collective-permute-start(bf16[256,768]{1,0:T(8,128)(2,1)S(1)} %copy-done.7), channel_id=1, source_target_pairs={{127,0},{3,4},{7,8},{11,12},{15,16},{19,20},{23,24},{27,28},{31,32... | collective-permute-start | bytes 1179656 | tf_op jit(solution)/shard_map/ppermute | solution.py:30
  144.3 32.6 %collective-permute-start.29 = (bf16[256,768]{1,0:T(8,128)(2,1)S(1)}, bf16[256,768]{1,0:T(8,128)(2,1)S(1)}, u32[]{:S(2)}, u32[]{:S(2)}) collective-permute-start(bf16[256,768]{1,0:T(8,128)(2,1)S(1)} %copy-done.6), channel_id=1, source_target_pairs={{4,3},{8,7},{12,11},{16,15},{20,19},{24,23},{28,27},{32,31},{36,35... | collective-permute-start | bytes 1179656 | tf_op jit(solution)/shard_map/ppermute | solution.py:31
  162.4 29.2 %collective-permute-start.8 = (bf16[512,768]{1,0:T(8,128)(2,1)S(1)}, bf16[512,768]{1,0:T(8,128)(2,1)S(1)}, u32[]{:S(2)}, u32[]{:S(2)}) collective-permute-start(bf16[512,768]{1,0:T(8,128)(2,1)S(1)} %slice.108), channel_id=1, source_target_pairs={{0,1},{1,2},{2,3},{3,0},{4,5},{5,6},{6,7},{7,4},{8,9},{9,10},{10,1... | collective-permute-start | bytes 2359304 | tf_op jit(solution)/shard_map/ppermute | solution.py:24
  177.6 31.7 %collective-permute-start.9 = (bf16[512,768]{1,0:T(8,128)(2,1)S(1)}, bf16[512,768]{1,0:T(8,128)(2,1)S(1)}, u32[]{:S(2)}, u32[]{:S(2)}) collective-permute-start(bf16[512,768]{1,0:T(8,128)(2,1)S(1)} %slice.109), channel_id=1, source_target_pairs={{0,3},{1,0},{2,1},{3,2},{4,7},{5,4},{6,5},{7,6},{8,11},{9,8},{10,9... | collective-permute-start | bytes 2359304 | tf_op jit(solution)/shard_map/ppermute | solution.py:25
  181.3 28.9 %collective-permute-start.12 = (bf16[256,768]{1,0:T(8,128)(2,1)S(1)}, bf16[256,768]{1,0:T(8,128)(2,1)S(1)}, u32[]{:S(2)}, u32[]{:S(2)}) collective-permute-start(bf16[256,768]{1,0:T(8,128)(2,1)S(1)} %copy-done.5), channel_id=1, source_target_pairs={{127,2},{3,6},{7,10},{11,14},{15,18},{19,22},{23,26},{27,30},{31,3... | collective-permute-start | bytes 1179656 | tf_op jit(solution)/shard_map/ppermute | solution.py:30
  182.2 30.6 %collective-permute-start.10 = (bf16[256,768]{1,0:T(8,128)(2,1)S(1)}, bf16[256,768]{1,0:T(8,128)(2,1)S(1)}, u32[]{:S(2)}, u32[]{:S(2)}) collective-permute-start(bf16[256,768]{1,0:T(8,128)(2,1)S(1)} %copy-done.5), channel_id=1, source_target_pairs={{127,0},{3,4},{7,8},{11,12},{15,16},{19,20},{23,24},{27,28},{31,32... | collective-permute-start | bytes 1179656 | tf_op jit(solution)/shard_map/ppermute | solution.py:30
  183.5 31.2 %collective-permute-start.11 = (bf16[256,768]{1,0:T(8,128)(2,1)S(1)}, bf16[256,768]{1,0:T(8,128)(2,1)S(1)}, u32[]{:S(2)}, u32[]{:S(2)}) collective-permute-start(bf16[256,768]{1,0:T(8,128)(2,1)S(1)} %copy-done.5), channel_id=1, source_target_pairs={{127,1},{3,5},{7,9},{11,13},{15,17},{19,21},{23,25},{27,29},{31,33... | collective-permute-start | bytes 1179656 | tf_op jit(solution)/shard_map/ppermute | solution.py:30
  191.5 27.1 %collective-permute-start.17 = (bf16[256,768]{1,0:T(8,128)(2,1)S(1)}, bf16[256,768]{1,0:T(8,128)(2,1)S(1)}, u32[]{:S(2)}, u32[]{:S(2)}) collective-permute-start(bf16[256,768]{1,0:T(8,128)(2,1)S(1)} %get-tuple-element.4), channel_id=1, source_target_pairs={{4,3},{8,7},{12,11},{16,15},{20,19},{24,23},{28,27},{32,31},{36,35... | collective-permute-start | bytes 1179656 | tf_op jit(solution)/shard_map/ppermute | solution.py:31
  209.3 57.4 %collective-permute-start.43 = (bf16[1024,768]{1,0:T(8,128)(2,1)S(1)}, bf16[1024,768]{1,0:T(8,128)(2,1)S(1)}, u32[]{:S(2)}, u32[]{:S(2)}) collective-permute-start(bf16[1024,768]{1,0:T(8,128)(2,1)S(1)} %shard_map.60), channel_id=1, source_target_pairs={{0,1},{1,2},{2,3},{3,0},{4,5},{5,6},{6,7},{7,4},{8,9},{9,10},{10,1... | collective-permute-start | bytes 4718600 | tf_op jit(solution)/shard_map/ppermute | solution.py:22
  218.7 51.0 %collective-permute-start.42 = (bf16[1024,768]{1,0:T(8,128)(2,1)S(1)}, bf16[1024,768]{1,0:T(8,128)(2,1)S(1)}, u32[]{:S(2)}, u32[]{:S(2)}) collective-permute-start(bf16[1024,768]{1,0:T(8,128)(2,1)S(1)} %shard_map.60), channel_id=1, source_target_pairs={{0,3},{1,0},{2,1},{3,2},{4,7},{5,4},{6,5},{7,6},{8,11},{9,8},{10,9... | collective-permute-start | bytes 4718600 | tf_op jit(solution)/shard_map/ppermute | solution.py:23
  233.8 65.8 %collective-permute-start.31 = (bf16[1024,768]{1,0:T(8,128)(2,1)S(1)}, bf16[1024,768]{1,0:T(8,128)(2,1)S(1)}, u32[]{:S(2)}, u32[]{:S(2)}) collective-permute-start(bf16[1024,768]{1,0:T(8,128)(2,1)S(1)} %shard_map.59), channel_id=1, source_target_pairs={{0,1},{1,2},{2,3},{3,0},{4,5},{5,6},{6,7},{7,4},{8,9},{9,10},{10,1... | collective-permute-start | bytes 4718600 | tf_op jit(solution)/shard_map/ppermute | solution.py:22
  264.8 37.3 %collective-permute-start.30 = (bf16[1024,768]{1,0:T(8,128)(2,1)S(1)}, bf16[1024,768]{1,0:T(8,128)(2,1)S(1)}, u32[]{:S(2)}, u32[]{:S(2)}) collective-permute-start(bf16[1024,768]{1,0:T(8,128)(2,1)S(1)} %shard_map.59), channel_id=1, source_target_pairs={{0,3},{1,0},{2,1},{3,2},{4,7},{5,4},{6,5},{7,6},{8,11},{9,8},{10,9... | collective-permute-start | bytes 4718600 | tf_op jit(solution)/shard_map/ppermute | solution.py:23
  266.7 46.6 %collective-permute-start.44 = (bf16[512,768]{1,0:T(8,128)(2,1)S(1)}, bf16[512,768]{1,0:T(8,128)(2,1)S(1)}, u32[]{:S(2)}, u32[]{:S(2)}) collective-permute-start(bf16[512,768]{1,0:T(8,128)(2,1)S(1)} %slice.116), channel_id=1, source_target_pairs={{0,1},{1,2},{2,3},{3,0},{4,5},{5,6},{6,7},{7,4},{8,9},{9,10},{10,1... | collective-permute-start | bytes 2359304 | tf_op jit(solution)/shard_map/ppermute | solution.py:24
  268.9 34.6 %collective-permute-start.49 = (bf16[256,768]{1,0:T(8,128)(2,1)S(1)}, bf16[256,768]{1,0:T(8,128)(2,1)S(1)}, u32[]{:S(2)}, u32[]{:S(2)}) collective-permute-start(bf16[256,768]{1,0:T(8,128)(2,1)S(1)} %get-tuple-element.19), channel_id=1, source_target_pairs={{127,3},{3,7},{7,11},{11,15},{15,19},{19,23},{23,27},{27,31},{31,3... | collective-permute-start | bytes 1179656 | tf_op jit(solution)/shard_map/ppermute | solution.py:30
  269.8 46.7 %collective-permute-start.45 = (bf16[512,768]{1,0:T(8,128)(2,1)S(1)}, bf16[512,768]{1,0:T(8,128)(2,1)S(1)}, u32[]{:S(2)}, u32[]{:S(2)}) collective-permute-start(bf16[512,768]{1,0:T(8,128)(2,1)S(1)} %slice.117), channel_id=1, source_target_pairs={{0,3},{1,0},{2,1},{3,2},{4,7},{5,4},{6,5},{7,6},{8,11},{9,8},{10,9... | collective-permute-start | bytes 2359304 | tf_op jit(solution)/shard_map/ppermute | solution.py:25
  302.0 33.2 %collective-permute-start.46 = (bf16[256,768]{1,0:T(8,128)(2,1)S(1)}, bf16[256,768]{1,0:T(8,128)(2,1)S(1)}, u32[]{:S(2)}, u32[]{:S(2)}) collective-permute-start(bf16[256,768]{1,0:T(8,128)(2,1)S(1)} %get-tuple-element.19), channel_id=1, source_target_pairs={{127,0},{3,4},{7,8},{11,12},{15,16},{19,20},{23,24},{27,28},{31,32... | collective-permute-start | bytes 1179656 | tf_op jit(solution)/shard_map/ppermute | solution.py:30
  303.5 33.7 %collective-permute-start.47 = (bf16[256,768]{1,0:T(8,128)(2,1)S(1)}, bf16[256,768]{1,0:T(8,128)(2,1)S(1)}, u32[]{:S(2)}, u32[]{:S(2)}) collective-permute-start(bf16[256,768]{1,0:T(8,128)(2,1)S(1)} %get-tuple-element.19), channel_id=1, source_target_pairs={{127,1},{3,5},{7,9},{11,13},{15,17},{19,21},{23,25},{27,29},{31,33... | collective-permute-start | bytes 1179656 | tf_op jit(solution)/shard_map/ppermute | solution.py:30
  313.4 25.3 %collective-permute-start.53 = (bf16[256,768]{1,0:T(8,128)(2,1)S(1)}, bf16[256,768]{1,0:T(8,128)(2,1)S(1)}, u32[]{:S(2)}, u32[]{:S(2)}) collective-permute-start(bf16[256,768]{1,0:T(8,128)(2,1)S(1)} %get-tuple-element.18), channel_id=1, source_target_pairs={{4,3},{8,7},{12,11},{16,15},{20,19},{24,23},{28,27},{32,31},{36,35... | collective-permute-start | bytes 1179656 | tf_op jit(solution)/shard_map/ppermute | solution.py:31
  316.4 43.4 %collective-permute-start.32 = (bf16[512,768]{1,0:T(8,128)(2,1)}, bf16[512,768]{1,0:T(8,128)(2,1)S(1)}, u32[]{:S(2)}, u32[]{:S(2)}) collective-permute-start(bf16[512,768]{1,0:T(8,128)(2,1)} %slice.112), channel_id=1, source_target_pairs={{0,1},{1,2},{2,3},{3,0},{4,5},{5,6},{6,7},{7,4},{8,9},{9,10},{10,1... | collective-permute-start | bytes 2359304 | tf_op jit(solution)/shard_map/ppermute | solution.py:24
  340.5 34.7 %collective-permute-start.37 = (bf16[256,768]{1,0:T(8,128)(2,1)}, bf16[256,768]{1,0:T(8,128)(2,1)S(1)}, u32[]{:S(2)}, u32[]{:S(2)}) collective-permute-start(bf16[256,768]{1,0:T(8,128)(2,1)} %get-tuple-element.17), channel_id=1, source_target_pairs={{127,3},{3,7},{7,11},{11,15},{15,19},{19,23},{23,27},{27,31},{31,3... | collective-permute-start | bytes 1179656 | tf_op jit(solution)/shard_map/ppermute | solution.py:30
  344.7 31.8 %collective-permute-start.36 = (bf16[256,768]{1,0:T(8,128)(2,1)}, bf16[256,768]{1,0:T(8,128)(2,1)S(1)}, u32[]{:S(2)}, u32[]{:S(2)}) collective-permute-start(bf16[256,768]{1,0:T(8,128)(2,1)} %get-tuple-element.17), channel_id=1, source_target_pairs={{127,2},{3,6},{7,10},{11,14},{15,18},{19,22},{23,26},{27,30},{31,3... | collective-permute-start | bytes 1179656 | tf_op jit(solution)/shard_map/ppermute | solution.py:30
  348.9 29.5 %collective-permute-start.34 = (bf16[256,768]{1,0:T(8,128)(2,1)}, bf16[256,768]{1,0:T(8,128)(2,1)S(1)}, u32[]{:S(2)}, u32[]{:S(2)}) collective-permute-start(bf16[256,768]{1,0:T(8,128)(2,1)} %get-tuple-element.17), channel_id=1, source_target_pairs={{127,0},{3,4},{7,8},{11,12},{15,16},{19,20},{23,24},{27,28},{31,32... | collective-permute-start | bytes 1179656 | tf_op jit(solution)/shard_map/ppermute | solution.py:30
  (31 other events, 689.2 us)

commit v10 on v8

--- a/solution.py
+++ b/solution.py
@@ -7,8 +7,8 @@
 
 KB = 8
 HB = 2
-NCH = 2
-TILE = 384
+NCH = 3
+TILE = 256
 
 
 def shift(size, k):

time: 296 us -> 311 us (1.051)
  waiting for transfers between devices: 154 us -> 142 us
  local copies, waits for them, and re-layouts: 50.5 us -> 62.4 us
  starting transfers between devices: 58.7 us -> 70 us
  Pallas kernels: 25.6 us -> 29 us
    ppermute x4 -> x6, waiting for transfers between devices: 0.01 us -> 61.8 us  [exchange(): from_next = lax.ppermute(own, 'layer', shift(nl, nl - 1))]
    ppermute x4 -> x6, waiting for transfers between devices: 52.6 us -> 24.3 us  [exchange(): from_prev = lax.ppermute(own, 'layer', shift(nl, 1))]
    ppermute x3, waiting for transfers between devices: 66 us -> 40.1 us  [shards(): lax.ppermute(lax.dynamic_index_in_dim(p_split, dest, 0, keepdims=False),...]
    ppermute x4 -> x6, waiting for transfers between devices: 23.5 us -> 2.05 us  [exchange(): far_a = lax.ppermute(from_prev[:half], 'layer', shift(nl, 1))]
    ppermute x4 -> x6, waiting for transfers between devices: 0.01 us -> 13.7 us  [exchange(): far_b = lax.ppermute(from_next[half:], 'layer', shift(nl, nl - 1))]
    ppermute x3, waiting for transfers between devices: 11.6 us -> 0.01 us  [shards(): lax.ppermute(lax.dynamic_index_in_dim(h_split, dest, 0, keepdims=False),...]
    ppermute x4 -> x6, starting transfers between devices: 20.2 us -> 28.3 us  [exchange(): hi = lax.ppermute(first, 'grid', shift(ng, ng - 1))]
    ppermute x4 -> x6, starting transfers between devices: 0.24 us -> 7.02 us  [exchange(): from_prev = lax.ppermute(own, 'layer', shift(nl, 1))]
  transfers between devices with their start and end apart: 30 -> 42, of which waited for: 11 -> 17; matrix products, arithmetic and copies ran while one was open for 15% -> 18% of each run, Pallas kernels for 7% -> 8%
where the time goes in v10:
time: 311 us; the launch traced here: 310 us
  waiting for transfers between devices  142 us (46%)
  starting transfers between devices  70 us (23%)
  local copies, waits for them, and re-layouts  62.4 us (20%)
  Pallas kernels  29 us (9%)
  other arithmetic  5.4 us (2%)
    ppermute x6, waiting for transfers between devices, exchange(): from_next = lax.ppermute(own, 'layer', shift(nl, nl - 1))  61.8 us
    ppermute x3, waiting for transfers between devices, shards(): lax.ppermute(lax.dynamic_index_in_dim(p_split, dest, 0, keepdims=False),...  40.1 us
    unnamed x46, local copies, waits for them, and re-layouts  31.9 us
    pallas_call x6, Pallas kernels, own_rows(): pl.pallas_call(step_kernel, grid_spec=grid_spec, out_shape=jax.ShapeDtype...  29 us
    ppermute x6, starting transfers between devices, exchange(): hi = lax.ppermute(first, 'grid', shift(ng, ng - 1))  28.3 us
    ppermute x6, waiting for transfers between devices, exchange(): from_prev = lax.ppermute(own, 'layer', shift(nl, 1))  24.3 us
    ppermute x6, waiting for transfers between devices, exchange(): far_b = lax.ppermute(from_next[half:], 'layer', shift(nl, nl - 1))  13.7 us
    ppermute x6, starting transfers between devices, exchange(): far_b = lax.ppermute(from_next[half:], 'layer', shift(nl, nl - 1))  13.4 us
  transfers between devices with their start and end apart: 42, of which 17 were waited for; matrix products, arithmetic and copies ran while one was open for 18% of the time, Pallas kernels for 8%

profile of v10, /device:TPU:0, one launch (start us, length us, event | category | flops | bytes accessed | tf_op | source)
XLA Modules:
  0.0 309.8 jit_solution(13104237396456541959)
XLA Ops:
  0.6 4.7 %constant_dynamic-update-slice_fusion.4 = (bf16[4096,512]{1,0:T(8,128)(2,1)}, bf16[4608,512]{1,0:T(8,128)(2,1)}, bf16[4096,512]{1,0:T(8,128)(2,1)}, bf16[4608,51...) fusion(bf16[1024,1536]{1,0:T(8,128)(2,1)} %param.6), kind=kLoop, calls=%fused_computation.11 | loop fusion | bytes 12582912
  17.7 17.7 %collective-permute-done.2 = s32[8,2]{0,1:T(2,128)S(1)} collective-permute-done((s32[8,2]{0,1:T(2,128)S(1)}, s32[8,2]{0,1:T(2,128)S(1)}, u32[]{:S(2)}, u32[]{:S(2)}) %collective-permute-start.2) | collective-permute-done | bytes 96 | tf_op jit(solution)/shard_map/ppermute | solution.py:88
  35.4 3.4 %collective-permute-start.1 = (s32[8,2]{0,1:T(2,128)S(1)}, s32[8,2]{0,1:T(2,128)S(1)}, u32[]{:S(2)}, u32[]{:S(2)}) collective-permute-start(s32[8,2]{0,1:T(2,128)S(1)} %bitcast.28), channel_id=1, source_target_pairs={{0,2},{1,3},{2,0},{3,1},{4,6},{5,7},{6,4},{7,5},{8,10},{9,11},{10,... | collective-permute-start | bytes 200 | tf_op jit(solution)/shard_map/ppermute | solution.py:88
  38.7 17.7 %collective-permute-done.1 = s32[8,2]{0,1:T(2,128)S(1)} collective-permute-done((s32[8,2]{0,1:T(2,128)S(1)}, s32[8,2]{0,1:T(2,128)S(1)}, u32[]{:S(2)}, u32[]{:S(2)}) %collective-permute-start.1) | collective-permute-done | bytes 96 | tf_op jit(solution)/shard_map/ppermute | solution.py:88
  56.4 4.8 %collective-permute-done = s32[8,2]{0,1:T(2,128)S(1)} collective-permute-done((s32[8,2]{0,1:T(2,128)S(1)}, s32[8,2]{0,1:T(2,128)S(1)}, u32[]{:S(2)}, u32[]{:S(2)}) %collective-permute-start) | collective-permute-done | bytes 96 | tf_op jit(solution)/shard_map/ppermute | solution.py:88
  67.7 3.6 %fusion.4 = (bf16[1024,512]{1,0:T(8,128)(2,1)}, bf16[1024,512]{1,0:T(8,128)(2,1)}, bf16[1024,512]{1,0:T(8,128)(2,1)}) fusion(bf16[1024,1536]{1,0:T(8,128)(2,1)} %param.7), kind=kLoop, calls=%fused_computation.114 | loop fusion | bytes 6291456 | tf_op jit(solution)/shard_map/slice | solution.py:108
  72.7 14.6 %collective-permute-done.18 = bf16[1024,512]{1,0:T(8,128)(2,1)} collective-permute-done((bf16[1024,512]{1,0:T(8,128)(2,1)S(1)}, bf16[1024,512]{1,0:T(8,128)(2,1)}, u32[]{:S(2)}, u32[]{:S(2)}) %collective-permute-start.18) | collective-permute-done | bytes 1048608 | tf_op jit(solution)/shard_map/ppermute | solution.py:23
  90.3 3.3 %collective-permute-start.21 = (bf16[512,512]{1,0:T(8,128)(2,1)S(1)}, bf16[512,512]{1,0:T(8,128)(2,1)S(1)}, u32[]{:S(2)}, u32[]{:S(2)}) collective-permute-start(bf16[512,512]{1,0:T(8,128)(2,1)S(1)} %slice.77), channel_id=1, source_target_pairs={{0,3},{1,0},{2,1},{3,2},{4,7},{5,4},{6,5},{7,6},{8,11},{9,8},{10,9... | collective-permute-start | bytes 1572872 | tf_op jit(solution)/shard_map/ppermute | solution.py:25
  97.3 12.5 %collective-permute-done.12 = bf16[1024,512]{1,0:T(8,128)(2,1)} collective-permute-done((bf16[1024,512]{1,0:T(8,128)(2,1)S(1)}, bf16[1024,512]{1,0:T(8,128)(2,1)}, u32[]{:S(2)}, u32[]{:S(2)}) %collective-permute-start.12) | collective-permute-done | bytes 1048608 | tf_op jit(solution)/shard_map/ppermute | solution.py:23
  116.0 16.2 %collective-permute-done.6 = bf16[1024,512]{1,0:T(8,128)(2,1)} collective-permute-done((bf16[1024,512]{1,0:T(8,128)(2,1)S(1)}, bf16[1024,512]{1,0:T(8,128)(2,1)}, u32[]{:S(2)}, u32[]{:S(2)}) %collective-permute-start.6) | collective-permute-done | bytes 1048608 | tf_op jit(solution)/shard_map/ppermute | solution.py:23
  138.0 3.2 %collective-permute-start.9 = (bf16[512,512]{1,0:T(8,128)(2,1)S(1)}, bf16[512,512]{1,0:T(8,128)(2,1)S(1)}, u32[]{:S(2)}, u32[]{:S(2)}) collective-permute-start(bf16[512,512]{1,0:T(8,128)(2,1)S(1)} %slice.73), channel_id=1, source_target_pairs={{0,3},{1,0},{2,1},{3,2},{4,7},{5,4},{6,5},{7,6},{8,11},{9,8},{10,9... | collective-permute-start | bytes 1572872 | tf_op jit(solution)/shard_map/ppermute | solution.py:25
  146.8 5.0 %collective-permute-start.23 = (bf16[256,512]{1,0:T(8,128)(2,1)S(1)}, bf16[256,512]{1,0:T(8,128)(2,1)S(1)}, u32[]{:S(2)}, u32[]{:S(2)}) collective-permute-start(bf16[256,512]{1,0:T(8,128)(2,1)S(1)} %get-tuple-element.12), channel_id=1, source_target_pairs={{0,124},{4,0},{8,4},{12,8},{16,12},{20,16},{24,20},{28,24},{32,28}... | collective-permute-start | bytes 786440 | tf_op jit(solution)/shard_map/ppermute | solution.py:34
  158.0 5.0 %collective-permute-start.17 = (bf16[256,512]{1,0:T(8,128)(2,1)S(1)}, bf16[256,512]{1,0:T(8,128)(2,1)S(1)}, u32[]{:S(2)}, u32[]{:S(2)}) collective-permute-start(bf16[256,512]{1,0:T(8,128)(2,1)S(1)} %get-tuple-element.10), channel_id=1, source_target_pairs={{0,124},{4,0},{8,4},{12,8},{16,12},{20,16},{24,20},{28,24},{32,28}... | collective-permute-start | bytes 786440 | tf_op jit(solution)/shard_map/ppermute | solution.py:34
  164.5 4.8 %shard_map.61 = bf16[1024,512]{1,0:T(8,128)(2,1)S(1)} custom-call(s32[64]{0:T(128)S(1)} %compare_select_fusion.pos_ref, bf16[8,8,128,128]{3,2,1,0:T(8,128)(2,1)S(1)} %pad_maximum_fusion.2.h_ref, bf16[36,128,512]{2,1,0:T(8,128)(2,1)} %bitcast.22, bf16[1024,512]{1,0:T(8,128)(2,1)S(1)} %copy-done.2), custom_call_target="tpu_custom_call" | custom-call | tf_op jit(solution)/shard_map/pallas_call | solution.py:64
  173.6 5.1 %collective-permute-start.11 = (bf16[256,512]{1,0:T(8,128)(2,1)S(1)}, bf16[256,512]{1,0:T(8,128)(2,1)S(1)}, u32[]{:S(2)}, u32[]{:S(2)}) collective-permute-start(bf16[256,512]{1,0:T(8,128)(2,1)S(1)} %get-tuple-element.8), channel_id=1, source_target_pairs={{0,124},{4,0},{8,4},{12,8},{16,12},{20,16},{24,20},{28,24},{32,28}... | collective-permute-start | bytes 786440 | tf_op jit(solution)/shard_map/ppermute | solution.py:34
  178.7 3.2 %collective-permute-start.36 = (bf16[1024,512]{1,0:T(8,128)(2,1)S(1)}, bf16[1024,512]{1,0:T(8,128)(2,1)}, u32[]{:S(2)}, u32[]{:S(2)}) collective-permute-start(bf16[1024,512]{1,0:T(8,128)(2,1)S(1)} %shard_map.61), channel_id=1, source_target_pairs={{0,3},{1,0},{2,1},{3,2},{4,7},{5,4},{6,5},{7,6},{8,11},{9,8},{10,9... | collective-permute-start | bytes 3145736 | tf_op jit(solution)/shard_map/ppermute | solution.py:23
  183.3 4.8 %shard_map.60 = bf16[1024,512]{1,0:T(8,128)(2,1)S(1)} custom-call(s32[64]{0:T(128)S(1)} %compare_select_fusion.pos_ref, bf16[8,8,128,128]{3,2,1,0:T(8,128)(2,1)S(1)} %pad_maximum_fusion.2.h_ref, bf16[36,128,512]{2,1,0:T(8,128)(2,1)} %bitcast.10.panel_ref, bf16[1024,512]{1,0:T(8,128)(2,1)S(1)} %copy-done.1), custom_call_target="tpu_custom_call" | custom-call | tf_op jit(solution)/shard_map/pallas_call | solution.py:64
  191.7 4.8 %shard_map.59 = bf16[1024,512]{1,0:T(8,128)(2,1)S(1)} custom-call(s32[64]{0:T(128)S(1)} %compare_select_fusion.pos_ref, bf16[8,8,128,128]{3,2,1,0:T(8,128)(2,1)S(1)} %pad_maximum_fusion.2.h_ref, bf16[36,128,512]{2,1,0:T(8,128)(2,1)} %bitcast.21, bf16[1024,512]{1,0:T(8,128)(2,1)S(1)} %copy-done), custom_call_target="tpu_custom_call" | custom-call | tf_op jit(solution)/shard_map/pallas_call | solution.py:64
  196.6 3.2 %collective-permute-start.24 = (bf16[1024,512]{1,0:T(8,128)(2,1)S(1)}, bf16[1024,512]{1,0:T(8,128)(2,1)S(1)}, u32[]{:S(2)}, u32[]{:S(2)}) collective-permute-start(bf16[1024,512]{1,0:T(8,128)(2,1)S(1)} %shard_map.59), channel_id=1, source_target_pairs={{0,3},{1,0},{2,1},{3,2},{4,7},{5,4},{6,5},{7,6},{8,11},{9,8},{10,9... | collective-permute-start | bytes 3145736 | tf_op jit(solution)/shard_map/ppermute | solution.py:23
  202.0 3.5 %collective-permute-done.36 = bf16[1024,512]{1,0:T(8,128)(2,1)} collective-permute-done((bf16[1024,512]{1,0:T(8,128)(2,1)S(1)}, bf16[1024,512]{1,0:T(8,128)(2,1)}, u32[]{:S(2)}, u32[]{:S(2)}) %collective-permute-start.36) | collective-permute-done | bytes 1048608 | tf_op jit(solution)/shard_map/ppermute | solution.py:23
  207.6 11.6 %collective-permute-done.31 = bf16[1024,512]{1,0:T(8,128)(2,1)} collective-permute-done((bf16[1024,512]{1,0:T(8,128)(2,1)S(1)}, bf16[1024,512]{1,0:T(8,128)(2,1)}, u32[]{:S(2)}, u32[]{:S(2)}) %collective-permute-start.31) | collective-permute-done | bytes 1048608 | tf_op jit(solution)/shard_map/ppermute | solution.py:22
  221.7 6.2 %collective-permute-done.30 = bf16[1024,512]{1,0:T(8,128)(2,1)} collective-permute-done((bf16[1024,512]{1,0:T(8,128)(2,1)S(1)}, bf16[1024,512]{1,0:T(8,128)(2,1)}, u32[]{:S(2)}, u32[]{:S(2)}) %collective-permute-start.30) | collective-permute-done | bytes 1048608 | tf_op jit(solution)/shard_map/ppermute | solution.py:23
  229.0 12.6 %collective-permute-done.25 = bf16[1024,512]{1,0:T(8,128)(2,1)S(1)} collective-permute-done((bf16[1024,512]{1,0:T(8,128)(2,1)S(1)}, bf16[1024,512]{1,0:T(8,128)(2,1)S(1)}, u32[]{:S(2)}, u32[]{:S(2)}) %collective-permute-start.25) | collective-permute-done | bytes 1048608 | tf_op jit(solution)/shard_map/ppermute | solution.py:22
  241.6 8.8 %collective-permute-done.24 = bf16[1024,512]{1,0:T(8,128)(2,1)S(1)} collective-permute-done((bf16[1024,512]{1,0:T(8,128)(2,1)S(1)}, bf16[1024,512]{1,0:T(8,128)(2,1)S(1)}, u32[]{:S(2)}, u32[]{:S(2)}) %collective-permute-start.24) | collective-permute-done | bytes 1048608 | tf_op jit(solution)/shard_map/ppermute | solution.py:23
  252.9 3.7 %collective-permute-start.27 = (bf16[512,512]{1,0:T(8,128)(2,1)S(1)}, bf16[512,512]{1,0:T(8,128)(2,1)S(1)}, u32[]{:S(2)}, u32[]{:S(2)}) collective-permute-start(bf16[512,512]{1,0:T(8,128)(2,1)S(1)} %slice.79), channel_id=1, source_target_pairs={{0,3},{1,0},{2,1},{3,2},{4,7},{5,4},{6,5},{7,6},{8,11},{9,8},{10,9... | collective-permute-start | bytes 1572872 | tf_op jit(solution)/shard_map/ppermute | solution.py:25
  256.7 4.9 %collective-permute-done.39 = bf16[512,512]{1,0:T(8,128)(2,1)S(1)} collective-permute-done((bf16[512,512]{1,0:T(8,128)(2,1)S(1)}, bf16[512,512]{1,0:T(8,128)(2,1)S(1)}, u32[]{:S(2)}, u32[]{:S(2)}) %collective-permute-start.39) | collective-permute-done | bytes 524320 | tf_op jit(solution)/shard_map/ppermute | solution.py:25
  267.1 5.7 %collective-permute-done.33 = bf16[512,512]{1,0:T(8,128)(2,1)S(1)} collective-permute-done((bf16[512,512]{1,0:T(8,128)(2,1)S(1)}, bf16[512,512]{1,0:T(8,128)(2,1)S(1)}, u32[]{:S(2)}, u32[]{:S(2)}) %collective-permute-start.33) | collective-permute-done | bytes 524320 | tf_op jit(solution)/shard_map/ppermute | solution.py:25
  274.5 5.0 %collective-permute-start.35 = (bf16[256,512]{1,0:T(8,128)(2,1)S(1)}, bf16[256,512]{1,0:T(8,128)(2,1)S(1)}, u32[]{:S(2)}, u32[]{:S(2)}) collective-permute-start(bf16[256,512]{1,0:T(8,128)(2,1)S(1)} %get-tuple-element.4), channel_id=1, source_target_pairs={{0,124},{4,0},{8,4},{12,8},{16,12},{20,16},{24,20},{28,24},{32,28}... | collective-permute-start | bytes 786440 | tf_op jit(solution)/shard_map/ppermute | solution.py:34
  282.5 5.0 %collective-permute-start.29 = (bf16[256,512]{1,0:T(8,128)(2,1)S(1)}, bf16[256,512]{1,0:T(8,128)(2,1)S(1)}, u32[]{:S(2)}, u32[]{:S(2)}) collective-permute-start(bf16[256,512]{1,0:T(8,128)(2,1)S(1)} %get-tuple-element.2), channel_id=1, source_target_pairs={{0,124},{4,0},{8,4},{12,8},{16,12},{20,16},{24,20},{28,24},{32,28}... | collective-permute-start | bytes 786440 | tf_op jit(solution)/shard_map/ppermute | solution.py:34
  289.8 4.8 %shard_map.64 = bf16[1024,512]{1,0:T(8,128)(2,1)S(1)} custom-call(s32[64]{0:T(128)S(1)} %compare_select_fusion.pos_ref, bf16[8,8,128,128]{3,2,1,0:T(8,128)(2,1)S(1)} %pad_maximum_fusion.2.h_ref, bf16[36,128,512]{2,1,0:T(8,128)(2,1)} %bitcast.24, bf16[1024,512]{1,0:T(8,128)(2,1)S(1)} %get-tuple-element.24.prev_ref), custom_call_target="tpu_custom_call" | custom-call | tf_op jit(solution)/shard_map/pallas_call | solution.py:64
  296.9 4.8 %shard_map.63 = bf16[1024,512]{1,0:T(8,128)(2,1)S(1)} custom-call(s32[64]{0:T(128)S(1)} %compare_select_fusion.pos_ref, bf16[8,8,128,128]{3,2,1,0:T(8,128)(2,1)S(1)} %pad_maximum_fusion.2.h_ref, bf16[36,128,512]{2,1,0:T(8,128)(2,1)} %bitcast.23, bf16[1024,512]{1,0:T(8,128)(2,1)S(1)} %get-tuple-element.25.prev_ref), custom_call_target="tpu_custom_call" | custom-call | tf_op jit(solution)/shard_map/pallas_call | solution.py:64
  303.2 4.8 %shard_map.62 = bf16[1024,512]{1,0:T(8,128)(2,1)S(1)} custom-call(s32[64]{0:T(128)S(1)} %compare_select_fusion.pos_ref, bf16[8,8,128,128]{3,2,1,0:T(8,128)(2,1)S(1)} %pad_maximum_fusion.2.h_ref, bf16[36,128,512]{2,1,0:T(8,128)(2,1)} %bitcast.12.panel_ref, bf16[1024,512]{1,0:T(8,128)(2,1)S(1)} %get-tuple-element.23.prev_ref), custom_call_target="tpu_custom_call" | custom-call | tf_op jit(solution)/shard_map/pallas_call | solution.py:64
  (146 shorter events, 89.5 us)
Async XLA Ops:
  5.4 59.9 %collective-permute-start.19 = (bf16[1024,512]{1,0:T(8,128)(2,1)S(1)}, bf16[1024,512]{1,0:T(8,128)(2,1)}, u32[]{:S(2)}, u32[]{:S(2)}) collective-permute-start(bf16[1024,512]{1,0:T(8,128)(2,1)S(1)} %get-tuple-element.24.prev_ref), channel_id=1, source_target_pairs={{0,1},{1,2},{2,3},{3,0},{4,5},{5,6},{6,7},{7,4},{8,9},{9,10},{10,1... | collective-permute-start | bytes 3145736 | tf_op jit(solution)/shard_map/ppermute | solution.py:22
  10.3 50.9 %collective-permute-start.5 = (bf16[8,2,128,128]{3,2,1,0:T(8,128)(2,1)}, bf16[8,2,128,128]{3,2,1,0:T(8,128)(2,1)}, u32[]{:S(2)}, u32[]{:S(2)}) collective-permute-start(bf16[8,2,128,128]{3,2,1,0:T(8,128)(2,1)} %get-tuple-element.27), channel_id=1, source_target_pairs={{0,3},{1,0},{2,1},{3,2},{4,7},{5,4},{6,5},{7,6},{8,11},{9,8},{10,9... | collective-permute-start | bytes 1572872 | tf_op jit(solution)/shard_map/ppermute | solution.py:87
  12.4 50.8 %collective-permute-start.4 = (bf16[8,2,128,128]{3,2,1,0:T(8,128)(2,1)}, bf16[8,2,128,128]{3,2,1,0:T(8,128)(2,1)}, u32[]{:S(2)}, u32[]{:S(2)}) collective-permute-start(bf16[8,2,128,128]{3,2,1,0:T(8,128)(2,1)} %get-tuple-element.28), channel_id=1, source_target_pairs={{0,2},{1,3},{2,0},{3,1},{4,6},{5,7},{6,4},{7,5},{8,10},{9,11},{10,... | collective-permute-start | bytes 1572872 | tf_op jit(solution)/shard_map/ppermute | solution.py:87
  14.3 50.2 %collective-permute-start.3 = (bf16[8,2,128,128]{3,2,1,0:T(8,128)(2,1)}, bf16[8,2,128,128]{3,2,1,0:T(8,128)(2,1)}, u32[]{:S(2)}, u32[]{:S(2)}) collective-permute-start(bf16[8,2,128,128]{3,2,1,0:T(8,128)(2,1)} %get-tuple-element.29), channel_id=1, source_target_pairs={{0,1},{1,2},{2,3},{3,0},{4,5},{5,6},{6,7},{7,4},{8,9},{9,10},{10,1... | collective-permute-start | bytes 1572872 | tf_op jit(solution)/shard_map/ppermute | solution.py:87
  35.4 21.0 %collective-permute-start.1 = (s32[8,2]{0,1:T(2,128)S(1)}, s32[8,2]{0,1:T(2,128)S(1)}, u32[]{:S(2)}, u32[]{:S(2)}) collective-permute-start(s32[8,2]{0,1:T(2,128)S(1)} %bitcast.28), channel_id=1, source_target_pairs={{0,2},{1,3},{2,0},{3,1},{4,6},{5,7},{6,4},{7,5},{8,10},{9,11},{10,... | collective-permute-start | bytes 200 | tf_op jit(solution)/shard_map/ppermute | solution.py:88
  61.2 26.1 %collective-permute-start.18 = (bf16[1024,512]{1,0:T(8,128)(2,1)S(1)}, bf16[1024,512]{1,0:T(8,128)(2,1)}, u32[]{:S(2)}, u32[]{:S(2)}) collective-permute-start(bf16[1024,512]{1,0:T(8,128)(2,1)S(1)} %get-tuple-element.24.prev_ref), channel_id=1, source_target_pairs={{0,3},{1,0},{2,1},{3,2},{4,7},{5,4},{6,5},{7,6},{8,11},{9,8},{10,9... | collective-permute-start | bytes 3145736 | tf_op jit(solution)/shard_map/ppermute | solution.py:23
  61.2 29.2 %collective-permute-start.13 = (bf16[1024,512]{1,0:T(8,128)(2,1)S(1)}, bf16[1024,512]{1,0:T(8,128)(2,1)}, u32[]{:S(2)}, u32[]{:S(2)}) collective-permute-start(bf16[1024,512]{1,0:T(8,128)(2,1)S(1)} %get-tuple-element.25.prev_ref), channel_id=1, source_target_pairs={{0,1},{1,2},{2,3},{3,0},{4,5},{5,6},{6,7},{7,4},{8,9},{9,10},{10,1... | collective-permute-start | bytes 3145736 | tf_op jit(solution)/shard_map/ppermute | solution.py:22
  63.2 46.6 %collective-permute-start.12 = (bf16[1024,512]{1,0:T(8,128)(2,1)S(1)}, bf16[1024,512]{1,0:T(8,128)(2,1)}, u32[]{:S(2)}, u32[]{:S(2)}) collective-permute-start(bf16[1024,512]{1,0:T(8,128)(2,1)S(1)} %get-tuple-element.25.prev_ref), channel_id=1, source_target_pairs={{0,3},{1,0},{2,1},{3,2},{4,7},{5,4},{6,5},{7,6},{8,11},{9,8},{10,9... | collective-permute-start | bytes 3145736 | tf_op jit(solution)/shard_map/ppermute | solution.py:23
  64.4 46.6 %collective-permute-start.7 = (bf16[1024,512]{1,0:T(8,128)(2,1)S(1)}, bf16[1024,512]{1,0:T(8,128)(2,1)}, u32[]{:S(2)}, u32[]{:S(2)}) collective-permute-start(bf16[1024,512]{1,0:T(8,128)(2,1)S(1)} %get-tuple-element.23.prev_ref), channel_id=1, source_target_pairs={{0,1},{1,2},{2,3},{3,0},{4,5},{5,6},{6,7},{7,4},{8,9},{9,10},{10,1... | collective-permute-start | bytes 3145736 | tf_op jit(solution)/shard_map/ppermute | solution.py:22
  65.2 67.0 %collective-permute-start.6 = (bf16[1024,512]{1,0:T(8,128)(2,1)S(1)}, bf16[1024,512]{1,0:T(8,128)(2,1)}, u32[]{:S(2)}, u32[]{:S(2)}) collective-permute-start(bf16[1024,512]{1,0:T(8,128)(2,1)S(1)} %get-tuple-element.23.prev_ref), channel_id=1, source_target_pairs={{0,3},{1,0},{2,1},{3,2},{4,7},{5,4},{6,5},{7,6},{8,11},{9,8},{10,9... | collective-permute-start | bytes 3145736 | tf_op jit(solution)/shard_map/ppermute | solution.py:23
  87.3 50.7 %collective-permute-start.20 = (bf16[512,512]{1,0:T(8,128)(2,1)S(1)}, bf16[512,512]{1,0:T(8,128)(2,1)S(1)}, u32[]{:S(2)}, u32[]{:S(2)}) collective-permute-start(bf16[512,512]{1,0:T(8,128)(2,1)S(1)} %slice.76), channel_id=1, source_target_pairs={{0,1},{1,2},{2,3},{3,0},{4,5},{5,6},{6,7},{7,4},{8,9},{9,10},{10,1... | collective-permute-start | bytes 1572872 | tf_op jit(solution)/shard_map/ppermute | solution.py:24
  90.3 53.0 %collective-permute-start.21 = (bf16[512,512]{1,0:T(8,128)(2,1)S(1)}, bf16[512,512]{1,0:T(8,128)(2,1)S(1)}, u32[]{:S(2)}, u32[]{:S(2)}) collective-permute-start(bf16[512,512]{1,0:T(8,128)(2,1)S(1)} %slice.77), channel_id=1, source_target_pairs={{0,3},{1,0},{2,1},{3,2},{4,7},{5,4},{6,5},{7,6},{8,11},{9,8},{10,9... | collective-permute-start | bytes 1572872 | tf_op jit(solution)/shard_map/ppermute | solution.py:25
  109.8 37.0 %collective-permute-start.14 = (bf16[512,512]{1,0:T(8,128)(2,1)S(1)}, bf16[512,512]{1,0:T(8,128)(2,1)S(1)}, u32[]{:S(2)}, u32[]{:S(2)}) collective-permute-start(bf16[512,512]{1,0:T(8,128)(2,1)S(1)} %slice.74), channel_id=1, source_target_pairs={{0,1},{1,2},{2,3},{3,0},{4,5},{5,6},{6,7},{7,4},{8,9},{9,10},{10,1... | collective-permute-start | bytes 1572872 | tf_op jit(solution)/shard_map/ppermute | solution.py:24
  111.0 43.6 %collective-permute-start.15 = (bf16[512,512]{1,0:T(8,128)(2,1)S(1)}, bf16[512,512]{1,0:T(8,128)(2,1)S(1)}, u32[]{:S(2)}, u32[]{:S(2)}) collective-permute-start(bf16[512,512]{1,0:T(8,128)(2,1)S(1)} %slice.75), channel_id=1, source_target_pairs={{0,3},{1,0},{2,1},{3,2},{4,7},{5,4},{6,5},{7,6},{8,11},{9,8},{10,9... | collective-permute-start | bytes 1572872 | tf_op jit(solution)/shard_map/ppermute | solution.py:25
  132.3 37.1 %collective-permute-start.8 = (bf16[512,512]{1,0:T(8,128)(2,1)}, bf16[512,512]{1,0:T(8,128)(2,1)S(1)}, u32[]{:S(2)}, u32[]{:S(2)}) collective-permute-start(bf16[512,512]{1,0:T(8,128)(2,1)} %slice.72), channel_id=1, source_target_pairs={{0,1},{1,2},{2,3},{3,0},{4,5},{5,6},{6,7},{7,4},{8,9},{9,10},{10,1... | collective-permute-start | bytes 1572872 | tf_op jit(solution)/shard_map/ppermute | solution.py:24
  138.0 32.2 %collective-permute-start.9 = (bf16[512,512]{1,0:T(8,128)(2,1)S(1)}, bf16[512,512]{1,0:T(8,128)(2,1)S(1)}, u32[]{:S(2)}, u32[]{:S(2)}) collective-permute-start(bf16[512,512]{1,0:T(8,128)(2,1)S(1)} %slice.73), channel_id=1, source_target_pairs={{0,3},{1,0},{2,1},{3,2},{4,7},{5,4},{6,5},{7,6},{8,11},{9,8},{10,9... | collective-permute-start | bytes 1572872 | tf_op jit(solution)/shard_map/ppermute | solution.py:25
  157.9 20.8 %collective-permute-start.16 = (bf16[256,512]{1,0:T(8,128)(2,1)S(1)}, bf16[256,512]{1,0:T(8,128)(2,1)S(1)}, u32[]{:S(2)}, u32[]{:S(2)}) collective-permute-start(bf16[256,512]{1,0:T(8,128)(2,1)S(1)} %get-tuple-element.11), channel_id=1, source_target_pairs={{0,4},{4,8},{8,12},{12,16},{16,20},{20,24},{24,28},{28,32},{32,36}... | collective-permute-start | bytes 786440 | tf_op jit(solution)/shard_map/ppermute | solution.py:33
  158.0 24.6 %collective-permute-start.17 = (bf16[256,512]{1,0:T(8,128)(2,1)S(1)}, bf16[256,512]{1,0:T(8,128)(2,1)S(1)}, u32[]{:S(2)}, u32[]{:S(2)}) collective-permute-start(bf16[256,512]{1,0:T(8,128)(2,1)S(1)} %get-tuple-element.10), channel_id=1, source_target_pairs={{0,124},{4,0},{8,4},{12,8},{16,12},{20,16},{24,20},{28,24},{32,28}... | collective-permute-start | bytes 786440 | tf_op jit(solution)/shard_map/ppermute | solution.py:34
  169.3 27.3 %collective-permute-start.37 = (bf16[1024,512]{1,0:T(8,128)(2,1)S(1)}, bf16[1024,512]{1,0:T(8,128)(2,1)S(1)}, u32[]{:S(2)}, u32[]{:S(2)}) collective-permute-start(bf16[1024,512]{1,0:T(8,128)(2,1)S(1)} %shard_map.61), channel_id=1, source_target_pairs={{0,1},{1,2},{2,3},{3,0},{4,5},{5,6},{6,7},{7,4},{8,9},{9,10},{10,1... | collective-permute-start | bytes 3145736 | tf_op jit(solution)/shard_map/ppermute | solution.py:22
  178.7 26.8 %collective-permute-start.36 = (bf16[1024,512]{1,0:T(8,128)(2,1)S(1)}, bf16[1024,512]{1,0:T(8,128)(2,1)}, u32[]{:S(2)}, u32[]{:S(2)}) collective-permute-start(bf16[1024,512]{1,0:T(8,128)(2,1)S(1)} %shard_map.61), channel_id=1, source_target_pairs={{0,3},{1,0},{2,1},{3,2},{4,7},{5,4},{6,5},{7,6},{8,11},{9,8},{10,9... | collective-permute-start | bytes 3145736 | tf_op jit(solution)/shard_map/ppermute | solution.py:23
  188.2 39.7 %collective-permute-start.30 = (bf16[1024,512]{1,0:T(8,128)(2,1)S(1)}, bf16[1024,512]{1,0:T(8,128)(2,1)}, u32[]{:S(2)}, u32[]{:S(2)}) collective-permute-start(bf16[1024,512]{1,0:T(8,128)(2,1)S(1)} %shard_map.60), channel_id=1, source_target_pairs={{0,3},{1,0},{2,1},{3,2},{4,7},{5,4},{6,5},{7,6},{8,11},{9,8},{10,9... | collective-permute-start | bytes 3145736 | tf_op jit(solution)/shard_map/ppermute | solution.py:23
  188.3 30.9 %collective-permute-start.31 = (bf16[1024,512]{1,0:T(8,128)(2,1)S(1)}, bf16[1024,512]{1,0:T(8,128)(2,1)}, u32[]{:S(2)}, u32[]{:S(2)}) collective-permute-start(bf16[1024,512]{1,0:T(8,128)(2,1)S(1)} %shard_map.60), channel_id=1, source_target_pairs={{0,1},{1,2},{2,3},{3,0},{4,5},{5,6},{6,7},{7,4},{8,9},{9,10},{10,1... | collective-permute-start | bytes 3145736 | tf_op jit(solution)/shard_map/ppermute | solution.py:22
  196.5 45.0 %collective-permute-start.25 = (bf16[1024,512]{1,0:T(8,128)(2,1)S(1)}, bf16[1024,512]{1,0:T(8,128)(2,1)S(1)}, u32[]{:S(2)}, u32[]{:S(2)}) collective-permute-start(bf16[1024,512]{1,0:T(8,128)(2,1)S(1)} %shard_map.59), channel_id=1, source_target_pairs={{0,1},{1,2},{2,3},{3,0},{4,5},{5,6},{6,7},{7,4},{8,9},{9,10},{10,1... | collective-permute-start | bytes 3145736 | tf_op jit(solution)/shard_map/ppermute | solution.py:22
  196.6 53.7 %collective-permute-start.24 = (bf16[1024,512]{1,0:T(8,128)(2,1)S(1)}, bf16[1024,512]{1,0:T(8,128)(2,1)S(1)}, u32[]{:S(2)}, u32[]{:S(2)}) collective-permute-start(bf16[1024,512]{1,0:T(8,128)(2,1)S(1)} %shard_map.59), channel_id=1, source_target_pairs={{0,3},{1,0},{2,1},{3,2},{4,7},{5,4},{6,5},{7,6},{8,11},{9,8},{10,9... | collective-permute-start | bytes 3145736 | tf_op jit(solution)/shard_map/ppermute | solution.py:23
  205.4 47.5 %collective-permute-start.38 = (bf16[512,512]{1,0:T(8,128)(2,1)S(1)}, bf16[512,512]{1,0:T(8,128)(2,1)S(1)}, u32[]{:S(2)}, u32[]{:S(2)}) collective-permute-start(bf16[512,512]{1,0:T(8,128)(2,1)S(1)} %slice.82), channel_id=1, source_target_pairs={{0,1},{1,2},{2,3},{3,0},{4,5},{5,6},{6,7},{7,4},{8,9},{9,10},{10,1... | collective-permute-start | bytes 1572872 | tf_op jit(solution)/shard_map/ppermute | solution.py:24
  219.2 42.4 %collective-permute-start.39 = (bf16[512,512]{1,0:T(8,128)(2,1)S(1)}, bf16[512,512]{1,0:T(8,128)(2,1)S(1)}, u32[]{:S(2)}, u32[]{:S(2)}) collective-permute-start(bf16[512,512]{1,0:T(8,128)(2,1)S(1)} %slice.83), channel_id=1, source_target_pairs={{0,3},{1,0},{2,1},{3,2},{4,7},{5,4},{6,5},{7,6},{8,11},{9,8},{10,9... | collective-permute-start | bytes 1572872 | tf_op jit(solution)/shard_map/ppermute | solution.py:25
  227.9 36.1 %collective-permute-start.32 = (bf16[512,512]{1,0:T(8,128)(2,1)S(1)}, bf16[512,512]{1,0:T(8,128)(2,1)S(1)}, u32[]{:S(2)}, u32[]{:S(2)}) collective-permute-start(bf16[512,512]{1,0:T(8,128)(2,1)S(1)} %slice.80), channel_id=1, source_target_pairs={{0,1},{1,2},{2,3},{3,0},{4,5},{5,6},{6,7},{7,4},{8,9},{9,10},{10,1... | collective-permute-start | bytes 1572872 | tf_op jit(solution)/shard_map/ppermute | solution.py:24
  241.6 31.3 %collective-permute-start.33 = (bf16[512,512]{1,0:T(8,128)(2,1)S(1)}, bf16[512,512]{1,0:T(8,128)(2,1)S(1)}, u32[]{:S(2)}, u32[]{:S(2)}) collective-permute-start(bf16[512,512]{1,0:T(8,128)(2,1)S(1)} %slice.81), channel_id=1, source_target_pairs={{0,3},{1,0},{2,1},{3,2},{4,7},{5,4},{6,5},{7,6},{8,11},{9,8},{10,9... | collective-permute-start | bytes 1572872 | tf_op jit(solution)/shard_map/ppermute | solution.py:25
  250.4 24.1 %collective-permute-start.26 = (bf16[512,512]{1,0:T(8,128)(2,1)S(1)}, bf16[512,512]{1,0:T(8,128)(2,1)S(1)}, u32[]{:S(2)}, u32[]{:S(2)}) collective-permute-start(bf16[512,512]{1,0:T(8,128)(2,1)S(1)} %slice.78), channel_id=1, source_target_pairs={{0,1},{1,2},{2,3},{3,0},{4,5},{5,6},{6,7},{7,4},{8,9},{9,10},{10,1... | collective-permute-start | bytes 1572872 | tf_op jit(solution)/shard_map/ppermute | solution.py:24
  252.9 27.4 %collective-permute-start.27 = (bf16[512,512]{1,0:T(8,128)(2,1)S(1)}, bf16[512,512]{1,0:T(8,128)(2,1)S(1)}, u32[]{:S(2)}, u32[]{:S(2)}) collective-permute-start(bf16[512,512]{1,0:T(8,128)(2,1)S(1)} %slice.79), channel_id=1, source_target_pairs={{0,3},{1,0},{2,1},{3,2},{4,7},{5,4},{6,5},{7,6},{8,11},{9,8},{10,9... | collective-permute-start | bytes 1572872 | tf_op jit(solution)/shard_map/ppermute | solution.py:25
  261.9 20.6 %collective-permute-start.40 = (bf16[256,512]{1,0:T(8,128)(2,1)S(1)}, bf16[256,512]{1,0:T(8,128)(2,1)S(1)}, u32[]{:S(2)}, u32[]{:S(2)}) collective-permute-start(bf16[256,512]{1,0:T(8,128)(2,1)S(1)} %get-tuple-element.7), channel_id=1, source_target_pairs={{0,4},{4,8},{8,12},{12,16},{16,20},{20,24},{24,28},{28,32},{32,36}... | collective-permute-start | bytes 786440 | tf_op jit(solution)/shard_map/ppermute | solution.py:33
  264.0 23.5 %collective-permute-start.41 = (bf16[256,512]{1,0:T(8,128)(2,1)S(1)}, bf16[256,512]{1,0:T(8,128)(2,1)S(1)}, u32[]{:S(2)}, u32[]{:S(2)}) collective-permute-start(bf16[256,512]{1,0:T(8,128)(2,1)S(1)} %get-tuple-element.6), channel_id=1, source_target_pairs={{0,124},{4,0},{8,4},{12,8},{16,12},{20,16},{24,20},{28,24},{32,28}... | collective-permute-start | bytes 786440 | tf_op jit(solution)/shard_map/ppermute | solution.py:34
  (19 other events, 325.7 us)

commit v11 on v8

--- a/solution.py
+++ b/solution.py
@@ -88,6 +88,7 @@
         p_parts.append(lax.ppermute(lax.dynamic_index_in_dim(p_split, dest, 0, keepdims=False), "layer", shift(nl, k)))
     h_own = jnp.concatenate(h_parts, axis=1)
     rel_own = jnp.concatenate(p_parts, axis=1)
+    t_now, h_own, rel_own = lax.optimization_barrier((t_now, h_own, rel_own))
     inner = rel_own - HB
     owner = inner // per_dev
     pos_own = ((owner - lidx) % nl) * per_dev + inner % per_dev

time: 296 us -> 293 us (0.990)
    ppermute x4, waiting for transfers between devices: 52.6 us -> 110 us  [exchange(): from_prev = lax.ppermute(own, 'layer', shift(nl, 1))]
    ppermute x3, waiting for transfers between devices: 66 us -> 21.5 us  [shards(): lax.ppermute(lax.dynamic_index_in_dim(p_split, dest, 0, keepdims=False),...]
    ppermute x3, waiting for transfers between devices: 11.6 us -> 0.01 us  [shards(): lax.ppermute(lax.dynamic_index_in_dim(h_split, dest, 0, keepdims=False),...]
    unnamed x43 -> x55, local copies, waits for them, and re-layouts: 27 us -> 33.9 us
    ppermute x4, waiting for transfers between devices: 23.5 us -> 20.2 us  [exchange(): far_a = lax.ppermute(from_prev[:half], 'layer', shift(nl, 1))]
  transfers between devices with their start and end apart: 30 -> 30, of which waited for: 11 -> 11; matrix products, arithmetic and copies ran while one was open for 15% -> 13% of each run, Pallas kernels for 7% -> 6%
where the time goes in v11:
time: 293 us
  waiting for transfers between devices  152 us (52%)
  starting transfers between devices  56.4 us (19%)
  local copies, waits for them, and re-layouts  52.4 us (18%)
  Pallas kernels  25.4 us (9%)
  other arithmetic  5.99 us (2%)
    ppermute x4, waiting for transfers between devices, exchange(): from_prev = lax.ppermute(own, 'layer', shift(nl, 1))  110 us
    unnamed x55, local copies, waits for them, and re-layouts  33.9 us
    pallas_call x4, Pallas kernels, own_rows(): pl.pallas_call(step_kernel, grid_spec=grid_spec, out_shape=jax.ShapeDtype...  25.4 us
    ppermute x3, waiting for transfers between devices, shards(): lax.ppermute(lax.dynamic_index_in_dim(p_split, dest, 0, keepdims=False),...  21.5 us
    ppermute x4, starting transfers between devices, exchange(): hi = lax.ppermute(first, 'grid', shift(ng, ng - 1))  20.2 us
    ppermute x4, waiting for transfers between devices, exchange(): far_a = lax.ppermute(from_prev[:half], 'layer', shift(nl, 1))  20.2 us
    ppermute x4, starting transfers between devices, exchange(): from_next = lax.ppermute(own, 'layer', shift(nl, nl - 1))  12.9 us
    ppermute x4, starting transfers between devices, exchange(): far_b = lax.ppermute(from_next[half:], 'layer', shift(nl, nl - 1))  12.7 us
  transfers between devices with their start and end apart: 30, of which 11 were waited for; matrix products, arithmetic and copies ran while one was open for 13% of the time, Pallas kernels for 6%

profile of v11, /device:TPU:0, one launch (start us, length us, event | category | flops | bytes accessed | tf_op | source)
XLA Modules:
  0.0 293.0 jit_solution(11089985398192263062)
XLA Ops:
  3.2 4.1 %collective-permute-start.2 = (bf16[8,2,128,128]{3,2,1,0:T(8,128)(2,1)}, bf16[8,2,128,128]{3,2,1,0:T(8,128)(2,1)S(1)}, u32[]{:S(2)}, u32[]{:S(2)}) collective-permute-start(bf16[8,2,128,128]{3,2,1,0:T(8,128)(2,1)} %get-tuple-element.25), channel_id=1, source_target_pairs={{0,3},{1,0},{2,1},{3,2},{4,7},{5,4},{6,5},{7,6},{8,11},{9,8},{10,9... | collective-permute-start | bytes 1572872 | tf_op jit(solution)/shard_map/ppermute | solution.py:87
  13.8 16.3 %collective-permute-done.5 = s32[8,2]{0,1:T(2,128)S(1)} collective-permute-done((s32[8,2]{0,1:T(2,128)S(1)}, s32[8,2]{0,1:T(2,128)S(1)}, u32[]{:S(2)}, u32[]{:S(2)}) %collective-permute-start.5) | collective-permute-done | bytes 96 | tf_op jit(solution)/shard_map/ppermute | solution.py:88
  30.1 3.4 %collective-permute-done.4 = s32[8,2]{0,1:T(2,128)S(1)} collective-permute-done((s32[8,2]{0,1:T(2,128)S(1)}, s32[8,2]{0,1:T(2,128)S(1)}, u32[]{:S(2)}, u32[]{:S(2)}) %collective-permute-start.4) | collective-permute-done | bytes 96 | tf_op jit(solution)/shard_map/ppermute | solution.py:88
  38.4 3.6 %constant_dynamic-update-slice_fusion.4 = (bf16[4096,768]{1,0:T(8,128)(2,1)}, bf16[4608,768]{1,0:T(8,128)(2,1)}, bf16[4096,768]{1,0:T(8,128)(2,1)}, bf16[4608,76...) fusion(bf16[1024,1536]{1,0:T(8,128)(2,1)S(1)} %copy-done.14), kind=kLoop, calls=%fused_computation.11 | loop fusion | bytes 12582912
  42.0 3.2 %collective-permute-start.12 = (bf16[1024,768]{1,0:T(8,128)(2,1)S(1)}, bf16[1024,768]{1,0:T(8,128)(2,1)S(1)}, u32[]{:S(2)}, u32[]{:S(2)}) collective-permute-start(bf16[1024,768]{1,0:T(8,128)(2,1)S(1)} %get-tuple-element.22.prev_ref), channel_id=1, source_target_pairs={{0,3},{1,0},{2,1},{3,2},{4,7},{5,4},{6,5},{7,6},{8,11},{9,8},{10,9... | collective-permute-start | bytes 4718600 | tf_op jit(solution)/shard_map/ppermute | solution.py:23
  46.4 3.2 %collective-permute-start.6 = (bf16[1024,768]{1,0:T(8,128)(2,1)}, bf16[1024,768]{1,0:T(8,128)(2,1)}, u32[]{:S(2)}, u32[]{:S(2)}) collective-permute-start(bf16[1024,768]{1,0:T(8,128)(2,1)} %get-tuple-element.23.prev_ref), channel_id=1, source_target_pairs={{0,3},{1,0},{2,1},{3,2},{4,7},{5,4},{6,5},{7,6},{8,11},{9,8},{10,9... | collective-permute-start | bytes 4718600 | tf_op jit(solution)/shard_map/ppermute | solution.py:23
  49.7 30.8 %collective-permute-done.13 = bf16[1024,768]{1,0:T(8,128)(2,1)S(1)} collective-permute-done((bf16[1024,768]{1,0:T(8,128)(2,1)S(1)}, bf16[1024,768]{1,0:T(8,128)(2,1)S(1)}, u32[]{:S(2)}, u32[]{:S(2)}) %collective-permute-start.13) | collective-permute-done | bytes 1572896 | tf_op jit(solution)/shard_map/ppermute | solution.py:22
  83.1 2.8 collective-permute-start.15
  87.9 26.4 %collective-permute-done.7 = bf16[1024,768]{1,0:T(8,128)(2,1)} collective-permute-done((bf16[1024,768]{1,0:T(8,128)(2,1)}, bf16[1024,768]{1,0:T(8,128)(2,1)}, u32[]{:S(2)}, u32[]{:S(2)}) %collective-permute-start.7) | collective-permute-done | bytes 1572896 | tf_op jit(solution)/shard_map/ppermute | solution.py:22
  116.8 3.3 %collective-permute-start.9 = (bf16[512,768]{1,0:T(8,128)(2,1)S(1)}, bf16[512,768]{1,0:T(8,128)(2,1)S(1)}, u32[]{:S(2)}, u32[]{:S(2)}) collective-permute-start(bf16[512,768]{1,0:T(8,128)(2,1)S(1)} %slice.49), channel_id=1, source_target_pairs={{0,3},{1,0},{2,1},{3,2},{4,7},{5,4},{6,5},{7,6},{8,11},{9,8},{10,9... | collective-permute-start | bytes 2359304 | tf_op jit(solution)/shard_map/ppermute | solution.py:25
  120.1 3.4 %constant_dynamic-update-slice_fusion.15 = (bf16[4096,768]{1,0:T(8,128)(2,1)}, bf16[4608,768]{1,0:T(8,128)(2,1)}) fusion(bf16[4096,768]{1,0:T(8,128)(2,1)} %get-tuple-element.20, bf16[1024,768]{1,0:T(8,128)(2,1)} %copy-done.8, bf16[4608,768]{1,0:T(8,128)(2,1)} %get-tuple-element.21), kind=kLoop, calls=%fused_computation.22 | loop fusion | bytes 4718592
  123.5 3.2 %constant_dynamic-update-slice_fusion.3 = (bf16[4096,768]{1,0:T(8,128)(2,1)}, bf16[4608,768]{1,0:T(8,128)(2,1)}) fusion(bf16[4096,768]{1,0:T(8,128)(2,1)} %get-tuple-element.18, bf16[1024,768]{1,0:T(8,128)(2,1)} %collective-permute-done.6, bf16[4608,768]{1,0:T(8,128)(2,1)} %get-tuple-element.19), kind=kLoop, calls=%fused_computation.10 | loop fusion | bytes 4718592
  126.7 4.5 %collective-permute-done.14 = bf16[512,768]{1,0:T(8,128)(2,1)} collective-permute-done((bf16[512,768]{1,0:T(8,128)(2,1)}, bf16[512,768]{1,0:T(8,128)(2,1)}, u32[]{:S(2)}, u32[]{:S(2)}) %collective-permute-start.14) | collective-permute-done | bytes 786464 | tf_op jit(solution)/shard_map/ppermute | solution.py:24
  139.1 5.1 %collective-permute-start.17 = (bf16[256,768]{1,0:T(8,128)(2,1)S(1)}, bf16[256,768]{1,0:T(8,128)(2,1)S(1)}, u32[]{:S(2)}, u32[]{:S(2)}) collective-permute-start(bf16[256,768]{1,0:T(8,128)(2,1)S(1)} %get-tuple-element.14), channel_id=1, source_target_pairs={{0,124},{4,0},{8,4},{12,8},{16,12},{20,16},{24,20},{28,24},{32,28}... | collective-permute-start | bytes 1179656 | tf_op jit(solution)/shard_map/ppermute | solution.py:34
  147.3 2.8 constant_dynamic-update-slice_fusion
  150.2 5.1 %collective-permute-start.11 = (bf16[256,768]{1,0:T(8,128)(2,1)S(1)}, bf16[256,768]{1,0:T(8,128)(2,1)S(1)}, u32[]{:S(2)}, u32[]{:S(2)}) collective-permute-start(bf16[256,768]{1,0:T(8,128)(2,1)S(1)} %get-tuple-element.12), channel_id=1, source_target_pairs={{0,124},{4,0},{8,4},{12,8},{16,12},{20,16},{24,20},{28,24},{32,28}... | collective-permute-start | bytes 1179656 | tf_op jit(solution)/shard_map/ppermute | solution.py:34
  156.8 6.3 %shard_map.60 = bf16[1024,768]{1,0:T(8,128)(2,1)S(1)} custom-call(s32[64]{0:T(128)S(1)} %reshape.27.pos_ref, bf16[8,8,128,128]{3,2,1,0:T(8,128)(2,1)S(1)} %pad_maximum_fusion.2.h_ref, bf16[36,128,768]{2,1,0:T(8,128)(2,1)} %bitcast.20, bf16[1024,768]{1,0:T(8,128)(2,1)S(1)} %copy-done.3), custom_call_target="tpu_custom_call" | custom-call | tf_op jit(solution)/shard_map/pallas_call | solution.py:64
  163.4 3.2 %collective-permute-start.24 = (bf16[1024,768]{1,0:T(8,128)(2,1)S(1)}, bf16[1024,768]{1,0:T(8,128)(2,1)S(1)}, u32[]{:S(2)}, u32[]{:S(2)}) collective-permute-start(bf16[1024,768]{1,0:T(8,128)(2,1)S(1)} %shard_map.60), channel_id=1, source_target_pairs={{0,3},{1,0},{2,1},{3,2},{4,7},{5,4},{6,5},{7,6},{8,11},{9,8},{10,9... | collective-permute-start | bytes 4718600 | tf_op jit(solution)/shard_map/ppermute | solution.py:23
  168.2 6.3 %shard_map.59 = bf16[1024,768]{1,0:T(8,128)(2,1)S(1)} custom-call(s32[64]{0:T(128)S(1)} %reshape.27.pos_ref, bf16[8,8,128,128]{3,2,1,0:T(8,128)(2,1)S(1)} %pad_maximum_fusion.2.h_ref, bf16[36,128,768]{2,1,0:T(8,128)(2,1)} %bitcast.19, bf16[1024,768]{1,0:T(8,128)(2,1)S(1)} %copy-done.2), custom_call_target="tpu_custom_call" | custom-call | tf_op jit(solution)/shard_map/pallas_call | solution.py:64
  174.6 3.2 %collective-permute-start.18 = (bf16[1024,768]{1,0:T(8,128)(2,1)S(1)}, bf16[1024,768]{1,0:T(8,128)(2,1)S(1)}, u32[]{:S(2)}, u32[]{:S(2)}) collective-permute-start(bf16[1024,768]{1,0:T(8,128)(2,1)S(1)} %shard_map.59), channel_id=1, source_target_pairs={{0,3},{1,0},{2,1},{3,2},{4,7},{5,4},{6,5},{7,6},{8,11},{9,8},{10,9... | collective-permute-start | bytes 4718600 | tf_op jit(solution)/shard_map/ppermute | solution.py:23
  177.8 24.1 %collective-permute-done.25 = bf16[1024,768]{1,0:T(8,128)(2,1)S(1)} collective-permute-done((bf16[1024,768]{1,0:T(8,128)(2,1)S(1)}, bf16[1024,768]{1,0:T(8,128)(2,1)S(1)}, u32[]{:S(2)}, u32[]{:S(2)}) %collective-permute-start.25) | collective-permute-done | bytes 1572896 | tf_op jit(solution)/shard_map/ppermute | solution.py:22
  202.1 3.3 %collective-permute-start.27 = (bf16[512,768]{1,0:T(8,128)(2,1)S(1)}, bf16[512,768]{1,0:T(8,128)(2,1)S(1)}, u32[]{:S(2)}, u32[]{:S(2)}) collective-permute-start(bf16[512,768]{1,0:T(8,128)(2,1)S(1)} %slice.55), channel_id=1, source_target_pairs={{0,3},{1,0},{2,1},{3,2},{4,7},{5,4},{6,5},{7,6},{8,11},{9,8},{10,9... | collective-permute-start | bytes 2359304 | tf_op jit(solution)/shard_map/ppermute | solution.py:25
  207.0 28.6 %collective-permute-done.19 = bf16[1024,768]{1,0:T(8,128)(2,1)S(1)} collective-permute-done((bf16[1024,768]{1,0:T(8,128)(2,1)S(1)}, bf16[1024,768]{1,0:T(8,128)(2,1)S(1)}, u32[]{:S(2)}, u32[]{:S(2)}) %collective-permute-start.19) | collective-permute-done | bytes 1572896 | tf_op jit(solution)/shard_map/ppermute | solution.py:22
  235.8 3.3 %collective-permute-start.21 = (bf16[512,768]{1,0:T(8,128)(2,1)S(1)}, bf16[512,768]{1,0:T(8,128)(2,1)S(1)}, u32[]{:S(2)}, u32[]{:S(2)}) collective-permute-start(bf16[512,768]{1,0:T(8,128)(2,1)S(1)} %slice.53), channel_id=1, source_target_pairs={{0,3},{1,0},{2,1},{3,2},{4,7},{5,4},{6,5},{7,6},{8,11},{9,8},{10,9... | collective-permute-start | bytes 2359304 | tf_op jit(solution)/shard_map/ppermute | solution.py:25
  240.6 11.8 %collective-permute-done.26 = bf16[512,768]{1,0:T(8,128)(2,1)S(1)} collective-permute-done((bf16[512,768]{1,0:T(8,128)(2,1)S(1)}, bf16[512,768]{1,0:T(8,128)(2,1)S(1)}, u32[]{:S(2)}, u32[]{:S(2)}) %collective-permute-start.26) | collective-permute-done | bytes 786464 | tf_op jit(solution)/shard_map/ppermute | solution.py:24
  257.1 5.1 %collective-permute-start.29 = (bf16[256,768]{1,0:T(8,128)(2,1)S(1)}, bf16[256,768]{1,0:T(8,128)(2,1)S(1)}, u32[]{:S(2)}, u32[]{:S(2)}) collective-permute-start(bf16[256,768]{1,0:T(8,128)(2,1)S(1)} %get-tuple-element.10), channel_id=1, source_target_pairs={{0,124},{4,0},{8,4},{12,8},{16,12},{20,16},{24,20},{28,24},{32,28}... | collective-permute-start | bytes 1179656 | tf_op jit(solution)/shard_map/ppermute | solution.py:34
  262.1 2.8 collective-permute-done.20
  265.5 5.1 %collective-permute-start.23 = (bf16[256,768]{1,0:T(8,128)(2,1)S(1)}, bf16[256,768]{1,0:T(8,128)(2,1)S(1)}, u32[]{:S(2)}, u32[]{:S(2)}) collective-permute-start(bf16[256,768]{1,0:T(8,128)(2,1)S(1)} %get-tuple-element.8), channel_id=1, source_target_pairs={{0,124},{4,0},{8,4},{12,8},{16,12},{20,16},{24,20},{28,24},{32,28}... | collective-permute-start | bytes 1179656 | tf_op jit(solution)/shard_map/ppermute | solution.py:34
  272.5 2.8 copy-done.5
  275.3 6.3 %shard_map.62 = bf16[1024,768]{1,0:T(8,128)(2,1)S(1)} custom-call(s32[64]{0:T(128)S(1)} %reshape.27.pos_ref, bf16[8,8,128,128]{3,2,1,0:T(8,128)(2,1)S(1)} %pad_maximum_fusion.2.h_ref, bf16[36,128,768]{2,1,0:T(8,128)(2,1)} %bitcast.22, bf16[1024,768]{1,0:T(8,128)(2,1)S(1)} %copy-done.1), custom_call_target="tpu_custom_call" | custom-call | tf_op jit(solution)/shard_map/pallas_call | solution.py:64
  281.8 2.8 copy-done.4
  284.6 6.5 %shard_map.61 = bf16[1024,768]{1,0:T(8,128)(2,1)S(1)} custom-call(s32[64]{0:T(128)S(1)} %reshape.27.pos_ref, bf16[8,8,128,128]{3,2,1,0:T(8,128)(2,1)S(1)} %pad_maximum_fusion.2.h_ref, bf16[36,128,768]{2,1,0:T(8,128)(2,1)} %bitcast.21, bf16[1024,768]{1,0:T(8,128)(2,1)} %get-tuple-element.23.prev_ref), custom_call_target="tpu_custom_call" | custom-call | tf_op jit(solution)/shard_map/pallas_call | solution.py:64
  (119 shorter events, 49.2 us)
Async XLA Ops:
  3.2 32.1 %collective-permute-start.2 = (bf16[8,2,128,128]{3,2,1,0:T(8,128)(2,1)}, bf16[8,2,128,128]{3,2,1,0:T(8,128)(2,1)S(1)}, u32[]{:S(2)}, u32[]{:S(2)}) collective-permute-start(bf16[8,2,128,128]{3,2,1,0:T(8,128)(2,1)} %get-tuple-element.25), channel_id=1, source_target_pairs={{0,3},{1,0},{2,1},{3,2},{4,7},{5,4},{6,5},{7,6},{8,11},{9,8},{10,9... | collective-permute-start | bytes 1572872 | tf_op jit(solution)/shard_map/ppermute | solution.py:87
  7.4 28.0 %collective-permute-start.1 = (bf16[8,2,128,128]{3,2,1,0:T(8,128)(2,1)S(1)}, bf16[8,2,128,128]{3,2,1,0:T(8,128)(2,1)S(1)}, u32[]{:S(2)}, u32[]{:S(2)}) collective-permute-start(bf16[8,2,128,128]{3,2,1,0:T(8,128)(2,1)S(1)} %get-tuple-element.26), channel_id=1, source_target_pairs={{0,2},{1,3},{2,0},{3,1},{4,6},{5,7},{6,4},{7,5},{8,10},{9,11},{10,... | collective-permute-start | bytes 1572872 | tf_op jit(solution)/shard_map/ppermute | solution.py:87
  7.4 28.0 %collective-permute-start = (bf16[8,2,128,128]{3,2,1,0:T(8,128)(2,1)S(1)}, bf16[8,2,128,128]{3,2,1,0:T(8,128)(2,1)S(1)}, u32[]{:S(2)}, u32[]{:S(2)}) collective-permute-start(bf16[8,2,128,128]{3,2,1,0:T(8,128)(2,1)S(1)} %get-tuple-element.27), channel_id=1, source_target_pairs={{0,1},{1,2},{2,3},{3,0},{4,5},{5,6},{6,7},{7,4},{8,9},{9,10},{10,1... | collective-permute-start | bytes 1572872 | tf_op jit(solution)/shard_map/ppermute | solution.py:87
  9.4 20.7 %collective-permute-start.5 = (s32[8,2]{0,1:T(2,128)S(1)}, s32[8,2]{0,1:T(2,128)S(1)}, u32[]{:S(2)}, u32[]{:S(2)}) collective-permute-start(s32[8,2]{0,1:T(2,128)S(1)} %bitcast.27), channel_id=1, source_target_pairs={{0,3},{1,0},{2,1},{3,2},{4,7},{5,4},{6,5},{7,6},{8,11},{9,8},{10,9... | collective-permute-start | bytes 200 | tf_op jit(solution)/shard_map/ppermute | solution.py:88
  11.5 22.1 %collective-permute-start.4 = (s32[8,2]{0,1:T(2,128)S(1)}, s32[8,2]{0,1:T(2,128)S(1)}, u32[]{:S(2)}, u32[]{:S(2)}) collective-permute-start(s32[8,2]{0,1:T(2,128)S(1)} %bitcast.26), channel_id=1, source_target_pairs={{0,2},{1,3},{2,0},{3,1},{4,6},{5,7},{6,4},{7,5},{8,10},{9,11},{10,... | collective-permute-start | bytes 200 | tf_op jit(solution)/shard_map/ppermute | solution.py:88
  30.1 5.2 %collective-permute-start.3 = (s32[8,2]{0,1:T(2,128)S(1)}, s32[8,2]{0,1:T(2,128)S(1)}, u32[]{:S(2)}, u32[]{:S(2)}) collective-permute-start(s32[8,2]{0,1:T(2,128)S(1)} %bitcast.25), channel_id=1, source_target_pairs={{0,1},{1,2},{2,3},{3,0},{4,5},{5,6},{6,7},{7,4},{8,9},{9,10},{10,1... | collective-permute-start | bytes 200 | tf_op jit(solution)/shard_map/ppermute | solution.py:88
  38.4 47.5 %copy-start.13 = (bf16[1024,1536]{1,0:T(8,128)(2,1)S(1)}, bf16[1024,1536]{1,0:T(8,128)(2,1)}, u32[]{:S(2)}) copy-start(bf16[1024,1536]{1,0:T(8,128)(2,1)} %param.7) | copy-start | bytes 9437188
  42.0 38.5 %collective-permute-start.13 = (bf16[1024,768]{1,0:T(8,128)(2,1)S(1)}, bf16[1024,768]{1,0:T(8,128)(2,1)S(1)}, u32[]{:S(2)}, u32[]{:S(2)}) collective-permute-start(bf16[1024,768]{1,0:T(8,128)(2,1)S(1)} %get-tuple-element.22.prev_ref), channel_id=1, source_target_pairs={{0,1},{1,2},{2,3},{3,0},{4,5},{5,6},{6,7},{7,4},{8,9},{9,10},{10,1... | collective-permute-start | bytes 4718600 | tf_op jit(solution)/shard_map/ppermute | solution.py:22
  42.0 39.5 %collective-permute-start.12 = (bf16[1024,768]{1,0:T(8,128)(2,1)S(1)}, bf16[1024,768]{1,0:T(8,128)(2,1)S(1)}, u32[]{:S(2)}, u32[]{:S(2)}) collective-permute-start(bf16[1024,768]{1,0:T(8,128)(2,1)S(1)} %get-tuple-element.22.prev_ref), channel_id=1, source_target_pairs={{0,3},{1,0},{2,1},{3,2},{4,7},{5,4},{6,5},{7,6},{8,11},{9,8},{10,9... | collective-permute-start | bytes 4718600 | tf_op jit(solution)/shard_map/ppermute | solution.py:23
  46.4 67.9 %collective-permute-start.7 = (bf16[1024,768]{1,0:T(8,128)(2,1)}, bf16[1024,768]{1,0:T(8,128)(2,1)}, u32[]{:S(2)}, u32[]{:S(2)}) collective-permute-start(bf16[1024,768]{1,0:T(8,128)(2,1)} %get-tuple-element.23.prev_ref), channel_id=1, source_target_pairs={{0,1},{1,2},{2,3},{3,0},{4,5},{5,6},{6,7},{7,4},{8,9},{9,10},{10,1... | collective-permute-start | bytes 4718600 | tf_op jit(solution)/shard_map/ppermute | solution.py:22
  46.4 69.1 %collective-permute-start.6 = (bf16[1024,768]{1,0:T(8,128)(2,1)}, bf16[1024,768]{1,0:T(8,128)(2,1)}, u32[]{:S(2)}, u32[]{:S(2)}) collective-permute-start(bf16[1024,768]{1,0:T(8,128)(2,1)} %get-tuple-element.23.prev_ref), channel_id=1, source_target_pairs={{0,3},{1,0},{2,1},{3,2},{4,7},{5,4},{6,5},{7,6},{8,11},{9,8},{10,9... | collective-permute-start | bytes 4718600 | tf_op jit(solution)/shard_map/ppermute | solution.py:23
  81.5 49.7 %collective-permute-start.14 = (bf16[512,768]{1,0:T(8,128)(2,1)}, bf16[512,768]{1,0:T(8,128)(2,1)}, u32[]{:S(2)}, u32[]{:S(2)}) collective-permute-start(bf16[512,768]{1,0:T(8,128)(2,1)} %slice.50), channel_id=1, source_target_pairs={{0,1},{1,2},{2,3},{3,0},{4,5},{5,6},{6,7},{7,4},{8,9},{9,10},{10,1... | collective-permute-start | bytes 2359304 | tf_op jit(solution)/shard_map/ppermute | solution.py:24
  83.1 50.5 %collective-permute-start.15 = (bf16[512,768]{1,0:T(8,128)(2,1)S(1)}, bf16[512,768]{1,0:T(8,128)(2,1)}, u32[]{:S(2)}, u32[]{:S(2)}) collective-permute-start(bf16[512,768]{1,0:T(8,128)(2,1)S(1)} %slice.51), channel_id=1, source_target_pairs={{0,3},{1,0},{2,1},{3,2},{4,7},{5,4},{6,5},{7,6},{8,11},{9,8},{10,9... | collective-permute-start | bytes 2359304 | tf_op jit(solution)/shard_map/ppermute | solution.py:25
  115.5 29.8 %collective-permute-start.8 = (bf16[512,768]{1,0:T(8,128)(2,1)S(1)}, bf16[512,768]{1,0:T(8,128)(2,1)S(1)}, u32[]{:S(2)}, u32[]{:S(2)}) collective-permute-start(bf16[512,768]{1,0:T(8,128)(2,1)S(1)} %slice.48), channel_id=1, source_target_pairs={{0,1},{1,2},{2,3},{3,0},{4,5},{5,6},{6,7},{7,4},{8,9},{9,10},{10,1... | collective-permute-start | bytes 2359304 | tf_op jit(solution)/shard_map/ppermute | solution.py:24
  116.8 29.5 %collective-permute-start.9 = (bf16[512,768]{1,0:T(8,128)(2,1)S(1)}, bf16[512,768]{1,0:T(8,128)(2,1)S(1)}, u32[]{:S(2)}, u32[]{:S(2)}) collective-permute-start(bf16[512,768]{1,0:T(8,128)(2,1)S(1)} %slice.49), channel_id=1, source_target_pairs={{0,3},{1,0},{2,1},{3,2},{4,7},{5,4},{6,5},{7,6},{8,11},{9,8},{10,9... | collective-permute-start | bytes 2359304 | tf_op jit(solution)/shard_map/ppermute | solution.py:25
  139.0 16.2 %collective-permute-start.16 = (bf16[256,768]{1,0:T(8,128)(2,1)S(1)}, bf16[256,768]{1,0:T(8,128)(2,1)S(1)}, u32[]{:S(2)}, u32[]{:S(2)}) collective-permute-start(bf16[256,768]{1,0:T(8,128)(2,1)S(1)} %get-tuple-element.15), channel_id=1, source_target_pairs={{0,4},{4,8},{8,12},{12,16},{16,20},{20,24},{24,28},{28,32},{32,36}... | collective-permute-start | bytes 1179656 | tf_op jit(solution)/shard_map/ppermute | solution.py:33
  139.1 17.0 %collective-permute-start.17 = (bf16[256,768]{1,0:T(8,128)(2,1)S(1)}, bf16[256,768]{1,0:T(8,128)(2,1)S(1)}, u32[]{:S(2)}, u32[]{:S(2)}) collective-permute-start(bf16[256,768]{1,0:T(8,128)(2,1)S(1)} %get-tuple-element.14), channel_id=1, source_target_pairs={{0,124},{4,0},{8,4},{12,8},{16,12},{20,16},{24,20},{28,24},{32,28}... | collective-permute-start | bytes 1179656 | tf_op jit(solution)/shard_map/ppermute | solution.py:34
  150.1 16.5 %collective-permute-start.10 = (bf16[256,768]{1,0:T(8,128)(2,1)S(1)}, bf16[256,768]{1,0:T(8,128)(2,1)S(1)}, u32[]{:S(2)}, u32[]{:S(2)}) collective-permute-start(bf16[256,768]{1,0:T(8,128)(2,1)S(1)} %get-tuple-element.13), channel_id=1, source_target_pairs={{0,4},{4,8},{8,12},{12,16},{16,20},{20,24},{24,28},{28,32},{32,36}... | collective-permute-start | bytes 1179656 | tf_op jit(solution)/shard_map/ppermute | solution.py:33
  150.2 17.2 %collective-permute-start.11 = (bf16[256,768]{1,0:T(8,128)(2,1)S(1)}, bf16[256,768]{1,0:T(8,128)(2,1)S(1)}, u32[]{:S(2)}, u32[]{:S(2)}) collective-permute-start(bf16[256,768]{1,0:T(8,128)(2,1)S(1)} %get-tuple-element.12), channel_id=1, source_target_pairs={{0,124},{4,0},{8,4},{12,8},{16,12},{20,16},{24,20},{28,24},{32,28}... | collective-permute-start | bytes 1179656 | tf_op jit(solution)/shard_map/ppermute | solution.py:34
  163.2 38.7 %collective-permute-start.25 = (bf16[1024,768]{1,0:T(8,128)(2,1)S(1)}, bf16[1024,768]{1,0:T(8,128)(2,1)S(1)}, u32[]{:S(2)}, u32[]{:S(2)}) collective-permute-start(bf16[1024,768]{1,0:T(8,128)(2,1)S(1)} %shard_map.60), channel_id=1, source_target_pairs={{0,1},{1,2},{2,3},{3,0},{4,5},{5,6},{6,7},{7,4},{8,9},{9,10},{10,1... | collective-permute-start | bytes 4718600 | tf_op jit(solution)/shard_map/ppermute | solution.py:22
  163.4 38.6 %collective-permute-start.24 = (bf16[1024,768]{1,0:T(8,128)(2,1)S(1)}, bf16[1024,768]{1,0:T(8,128)(2,1)S(1)}, u32[]{:S(2)}, u32[]{:S(2)}) collective-permute-start(bf16[1024,768]{1,0:T(8,128)(2,1)S(1)} %shard_map.60), channel_id=1, source_target_pairs={{0,3},{1,0},{2,1},{3,2},{4,7},{5,4},{6,5},{7,6},{8,11},{9,8},{10,9... | collective-permute-start | bytes 4718600 | tf_op jit(solution)/shard_map/ppermute | solution.py:23
  174.5 61.1 %collective-permute-start.19 = (bf16[1024,768]{1,0:T(8,128)(2,1)S(1)}, bf16[1024,768]{1,0:T(8,128)(2,1)S(1)}, u32[]{:S(2)}, u32[]{:S(2)}) collective-permute-start(bf16[1024,768]{1,0:T(8,128)(2,1)S(1)} %shard_map.59), channel_id=1, source_target_pairs={{0,1},{1,2},{2,3},{3,0},{4,5},{5,6},{6,7},{7,4},{8,9},{9,10},{10,1... | collective-permute-start | bytes 4718600 | tf_op jit(solution)/shard_map/ppermute | solution.py:22
  174.6 61.1 %collective-permute-start.18 = (bf16[1024,768]{1,0:T(8,128)(2,1)S(1)}, bf16[1024,768]{1,0:T(8,128)(2,1)S(1)}, u32[]{:S(2)}, u32[]{:S(2)}) collective-permute-start(bf16[1024,768]{1,0:T(8,128)(2,1)S(1)} %shard_map.59), channel_id=1, source_target_pairs={{0,3},{1,0},{2,1},{3,2},{4,7},{5,4},{6,5},{7,6},{8,11},{9,8},{10,9... | collective-permute-start | bytes 4718600 | tf_op jit(solution)/shard_map/ppermute | solution.py:23
  201.9 50.5 %collective-permute-start.26 = (bf16[512,768]{1,0:T(8,128)(2,1)S(1)}, bf16[512,768]{1,0:T(8,128)(2,1)S(1)}, u32[]{:S(2)}, u32[]{:S(2)}) collective-permute-start(bf16[512,768]{1,0:T(8,128)(2,1)S(1)} %slice.54), channel_id=1, source_target_pairs={{0,1},{1,2},{2,3},{3,0},{4,5},{5,6},{6,7},{7,4},{8,9},{9,10},{10,1... | collective-permute-start | bytes 2359304 | tf_op jit(solution)/shard_map/ppermute | solution.py:24
  202.1 51.3 %collective-permute-start.27 = (bf16[512,768]{1,0:T(8,128)(2,1)S(1)}, bf16[512,768]{1,0:T(8,128)(2,1)S(1)}, u32[]{:S(2)}, u32[]{:S(2)}) collective-permute-start(bf16[512,768]{1,0:T(8,128)(2,1)S(1)} %slice.55), channel_id=1, source_target_pairs={{0,3},{1,0},{2,1},{3,2},{4,7},{5,4},{6,5},{7,6},{8,11},{9,8},{10,9... | collective-permute-start | bytes 2359304 | tf_op jit(solution)/shard_map/ppermute | solution.py:25
  206.8 32.3 %copy-start.12 = (bf16[1024,768]{1,0:T(8,128)(2,1)S(1)}, bf16[1024,768]{1,0:T(8,128)(2,1)}, u32[]{:S(2)}) copy-start(bf16[1024,768]{1,0:T(8,128)(2,1)} %copy-done.11) | copy-start | bytes 4718596
  235.6 29.2 %collective-permute-start.20 = (bf16[512,768]{1,0:T(8,128)(2,1)S(1)}, bf16[512,768]{1,0:T(8,128)(2,1)S(1)}, u32[]{:S(2)}, u32[]{:S(2)}) collective-permute-start(bf16[512,768]{1,0:T(8,128)(2,1)S(1)} %slice.52), channel_id=1, source_target_pairs={{0,1},{1,2},{2,3},{3,0},{4,5},{5,6},{6,7},{7,4},{8,9},{9,10},{10,1... | collective-permute-start | bytes 2359304 | tf_op jit(solution)/shard_map/ppermute | solution.py:24
  235.8 29.2 %collective-permute-start.21 = (bf16[512,768]{1,0:T(8,128)(2,1)S(1)}, bf16[512,768]{1,0:T(8,128)(2,1)S(1)}, u32[]{:S(2)}, u32[]{:S(2)}) collective-permute-start(bf16[512,768]{1,0:T(8,128)(2,1)S(1)} %slice.53), channel_id=1, source_target_pairs={{0,3},{1,0},{2,1},{3,2},{4,7},{5,4},{6,5},{7,6},{8,11},{9,8},{10,9... | collective-permute-start | bytes 2359304 | tf_op jit(solution)/shard_map/ppermute | solution.py:25
  257.0 15.5 %collective-permute-start.28 = (bf16[256,768]{1,0:T(8,128)(2,1)S(1)}, bf16[256,768]{1,0:T(8,128)(2,1)S(1)}, u32[]{:S(2)}, u32[]{:S(2)}) collective-permute-start(bf16[256,768]{1,0:T(8,128)(2,1)S(1)} %get-tuple-element.11), channel_id=1, source_target_pairs={{0,4},{4,8},{8,12},{12,16},{16,20},{20,24},{24,28},{28,32},{32,36}... | collective-permute-start | bytes 1179656 | tf_op jit(solution)/shard_map/ppermute | solution.py:33
  257.1 15.4 %collective-permute-start.29 = (bf16[256,768]{1,0:T(8,128)(2,1)S(1)}, bf16[256,768]{1,0:T(8,128)(2,1)S(1)}, u32[]{:S(2)}, u32[]{:S(2)}) collective-permute-start(bf16[256,768]{1,0:T(8,128)(2,1)S(1)} %get-tuple-element.10), channel_id=1, source_target_pairs={{0,124},{4,0},{8,4},{12,8},{16,12},{20,16},{24,20},{28,24},{32,28}... | collective-permute-start | bytes 1179656 | tf_op jit(solution)/shard_map/ppermute | solution.py:34
  265.4 16.3 %collective-permute-start.22 = (bf16[256,768]{1,0:T(8,128)(2,1)S(1)}, bf16[256,768]{1,0:T(8,128)(2,1)S(1)}, u32[]{:S(2)}, u32[]{:S(2)}) collective-permute-start(bf16[256,768]{1,0:T(8,128)(2,1)S(1)} %get-tuple-element.9), channel_id=1, source_target_pairs={{0,4},{4,8},{8,12},{12,16},{16,20},{20,24},{24,28},{28,32},{32,36}... | collective-permute-start | bytes 1179656 | tf_op jit(solution)/shard_map/ppermute | solution.py:33
  265.5 16.2 %collective-permute-start.23 = (bf16[256,768]{1,0:T(8,128)(2,1)S(1)}, bf16[256,768]{1,0:T(8,128)(2,1)S(1)}, u32[]{:S(2)}, u32[]{:S(2)}) collective-permute-start(bf16[256,768]{1,0:T(8,128)(2,1)S(1)} %get-tuple-element.8), channel_id=1, source_target_pairs={{0,124},{4,0},{8,4},{12,8},{16,12},{20,16},{24,20},{28,24},{32,28}... | collective-permute-start | bytes 1179656 | tf_op jit(solution)/shard_map/ppermute | solution.py:34
  (16 other events, 129.8 us)

commit v12 on v8

--- a/solution.py
+++ b/solution.py
@@ -88,6 +88,7 @@
         p_parts.append(lax.ppermute(lax.dynamic_index_in_dim(p_split, dest, 0, keepdims=False), "layer", shift(nl, k)))
     h_own = jnp.concatenate(h_parts, axis=1)
     rel_own = jnp.concatenate(p_parts, axis=1)
+    t_now, rel_own = lax.optimization_barrier((t_now, rel_own))
     inner = rel_own - HB
     owner = inner // per_dev
     pos_own = ((owner - lidx) % nl) * per_dev + inner % per_dev

time: 296 us -> 291 us (0.983)
  waiting for transfers between devices: 154 us -> 143 us
  local copies, waits for them, and re-layouts: 50.5 us -> 54.2 us
    ppermute x3, waiting for transfers between devices: 66 us -> 3.82 us  [shards(): lax.ppermute(lax.dynamic_index_in_dim(p_split, dest, 0, keepdims=False),...]
    ppermute x4, waiting for transfers between devices: 0.01 us -> 30.1 us  [exchange(): from_next = lax.ppermute(own, 'layer', shift(nl, nl - 1))]
    ppermute x3, waiting for transfers between devices: 11.6 us -> 37.5 us  [shards(): lax.ppermute(lax.dynamic_index_in_dim(h_split, dest, 0, keepdims=False),...]
    ppermute x4, starting transfers between devices: 11.7 us -> 19.3 us  [exchange(): far_b = lax.ppermute(from_next[half:], 'layer', shift(nl, nl - 1))]
    ppermute x4, waiting for transfers between devices: 23.5 us -> 18.6 us  [exchange(): far_a = lax.ppermute(from_prev[:half], 'layer', shift(nl, 1))]
    ppermute x4, starting transfers between devices: 13.8 us -> 9.94 us  [exchange(): from_next = lax.ppermute(own, 'layer', shift(nl, nl - 1))]
    unnamed x43 -> x45, local copies, waits for them, and re-layouts: 27 us -> 30.6 us
  transfers between devices with their start and end apart: 30 -> 30, of which waited for: 11 -> 10; matrix products, arithmetic and copies ran while one was open for 15% -> 16% of each run, Pallas kernels for 7% -> 7%
where the time goes in v12:
time: 291 us; the launch traced here: 290 us
  waiting for transfers between devices  143 us (49%)
  starting transfers between devices  61 us (21%)
  local copies, waits for them, and re-layouts  54.2 us (19%)
  Pallas kernels  25.2 us (9%)
  other arithmetic  6.31 us (2%)
    ppermute x4, waiting for transfers between devices, exchange(): from_prev = lax.ppermute(own, 'layer', shift(nl, 1))  52.7 us
    ppermute x3, waiting for transfers between devices, shards(): lax.ppermute(lax.dynamic_index_in_dim(h_split, dest, 0, keepdims=False),...  37.5 us
    unnamed x45, local copies, waits for them, and re-layouts  30.6 us
    ppermute x4, waiting for transfers between devices, exchange(): from_next = lax.ppermute(own, 'layer', shift(nl, nl - 1))  30.1 us
    pallas_call x4, Pallas kernels, own_rows(): pl.pallas_call(step_kernel, grid_spec=grid_spec, out_shape=jax.ShapeDtype...  25.2 us
    ppermute x4, starting transfers between devices, exchange(): hi = lax.ppermute(first, 'grid', shift(ng, ng - 1))  20.2 us
    ppermute x4, starting transfers between devices, exchange(): far_b = lax.ppermute(from_next[half:], 'layer', shift(nl, nl - 1))  19.3 us
    ppermute x4, waiting for transfers between devices, exchange(): far_a = lax.ppermute(from_prev[:half], 'layer', shift(nl, 1))  18.6 us
  transfers between devices with their start and end apart: 30, of which 10 were waited for; matrix products, arithmetic and copies ran while one was open for 16% of the time, Pallas kernels for 7%

profile of v12, /device:TPU:0, one launch (start us, length us, event | category | flops | bytes accessed | tf_op | source)
XLA Modules:
  0.0 290.5 jit_solution(2683783074029846310)
XLA Ops:
  1.5 4.2 %collective-permute-start.2 = (s32[8,2]{0,1:T(2,128)S(1)}, s32[8,2]{0,1:T(2,128)S(1)}, u32[]{:S(2)}, u32[]{:S(2)}) collective-permute-start(s32[8,2]{0,1:T(2,128)S(1)} %bitcast.27), channel_id=1, source_target_pairs={{0,3},{1,0},{2,1},{3,2},{4,7},{5,4},{6,5},{7,6},{8,11},{9,8},{10,9... | collective-permute-start | bytes 200 | tf_op jit(solution)/shard_map/ppermute | solution.py:88
  7.0 3.8 %collective-permute-done.1 = s32[8,2]{0,1:T(2,128)S(1)} collective-permute-done((s32[8,2]{0,1:T(2,128)S(1)}, s32[8,2]{0,1:T(2,128)S(1)}, u32[]{:S(2)}, u32[]{:S(2)}) %collective-permute-start.1) | collective-permute-done | bytes 96 | tf_op jit(solution)/shard_map/ppermute | solution.py:88
  10.8 5.1 %constant_dynamic-update-slice_fusion.4 = (bf16[4096,768]{1,0:T(8,128)(2,1)}, bf16[4608,768]{1,0:T(8,128)(2,1)}, bf16[4096,768]{1,0:T(8,128)(2,1)}, bf16[4608,76...) fusion(bf16[1024,1536]{1,0:T(8,128)(2,1)} %param.6), kind=kLoop, calls=%fused_computation.11 | loop fusion | bytes 12582912
  18.0 3.2 %collective-permute-start.6 = (bf16[1024,768]{1,0:T(8,128)(2,1)S(1)}, bf16[1024,768]{1,0:T(8,128)(2,1)}, u32[]{:S(2)}, u32[]{:S(2)}) collective-permute-start(bf16[1024,768]{1,0:T(8,128)(2,1)S(1)} %get-tuple-element.21.prev_ref), channel_id=1, source_target_pairs={{0,3},{1,0},{2,1},{3,2},{4,7},{5,4},{6,5},{7,6},{8,11},{9,8},{10,9... | collective-permute-start | bytes 4718600 | tf_op jit(solution)/shard_map/ppermute | solution.py:23
  23.1 30.0 %collective-permute-done.12 = bf16[1024,768]{1,0:T(8,128)(2,1)S(1)} collective-permute-done((bf16[1024,768]{1,0:T(8,128)(2,1)S(1)}, bf16[1024,768]{1,0:T(8,128)(2,1)S(1)}, u32[]{:S(2)}, u32[]{:S(2)}) %collective-permute-start.12) | collective-permute-done | bytes 1572896 | tf_op jit(solution)/shard_map/ppermute | solution.py:23
  57.0 3.8 %fusion.7 = (bf16[1024,768]{1,0:T(8,128)(2,1)}, bf16[1024,768]{1,0:T(8,128)(2,1)}) fusion(bf16[1024,1536]{1,0:T(8,128)(2,1)} %param.7), kind=kLoop, calls=%fused_computation.88 | loop fusion | bytes 6291456 | tf_op jit(solution)/shard_map/slice | solution.py:109
  63.8 34.4 %collective-permute-done.5 = bf16[8,2,128,128]{3,2,1,0:T(8,128)(2,1)} collective-permute-done((bf16[8,2,128,128]{3,2,1,0:T(8,128)(2,1)}, bf16[8,2,128,128]{3,2,1,0:T(8,128)(2,1)}, u32[]{:S(2)}, u32[]{:S(2)}) %collective-permute-start.5) | collective-permute-done | bytes 524320 | tf_op jit(solution)/shard_map/ppermute | solution.py:87
  100.3 9.7 %collective-permute-start.15 = (bf16[512,768]{1,0:T(8,128)(2,1)}, bf16[512,768]{1,0:T(8,128)(2,1)}, u32[]{:S(2)}, u32[]{:S(2)}) collective-permute-start(bf16[512,768]{1,0:T(8,128)(2,1)} %slice.51), channel_id=1, source_target_pairs={{0,3},{1,0},{2,1},{3,2},{4,7},{5,4},{6,5},{7,6},{8,11},{9,8},{10,9... | collective-permute-start | bytes 2359304 | tf_op jit(solution)/shard_map/ppermute | solution.py:25
  115.8 3.0 %collective-permute-start.9 = (bf16[512,768]{1,0:T(8,128)(2,1)S(1)}, bf16[512,768]{1,0:T(8,128)(2,1)S(1)}, u32[]{:S(2)}, u32[]{:S(2)}) collective-permute-start(bf16[512,768]{1,0:T(8,128)(2,1)S(1)} %slice.49), channel_id=1, source_target_pairs={{0,3},{1,0},{2,1},{3,2},{4,7},{5,4},{6,5},{7,6},{8,11},{9,8},{10,9... | collective-permute-start | bytes 2359304 | tf_op jit(solution)/shard_map/ppermute | solution.py:25
  120.6 3.2 %constant_dynamic-update-slice_fusion.3 = (bf16[4096,768]{1,0:T(8,128)(2,1)}, bf16[4608,768]{1,0:T(8,128)(2,1)}) fusion(bf16[4096,768]{1,0:T(8,128)(2,1)} %get-tuple-element.16, bf16[1024,768]{1,0:T(8,128)(2,1)} %collective-permute-done.6, bf16[4608,768]{1,0:T(8,128)(2,1)} %get-tuple-element.17), kind=kLoop, calls=%fused_computation.10 | loop fusion | bytes 4718592
  123.9 4.2 %collective-permute-done.14 = bf16[512,768]{1,0:T(8,128)(2,1)} collective-permute-done((bf16[512,768]{1,0:T(8,128)(2,1)}, bf16[512,768]{1,0:T(8,128)(2,1)}, u32[]{:S(2)}, u32[]{:S(2)}) %collective-permute-start.14) | collective-permute-done | bytes 786464 | tf_op jit(solution)/shard_map/ppermute | solution.py:24
  128.1 2.4 constant_dynamic-update-slice_fusion.14
  132.8 3.3 %constant_dynamic-update-slice_fusion.12 = (bf16[4096,768]{1,0:T(8,128)(2,1)}, bf16[4608,768]{1,0:T(8,128)(2,1)}) fusion(bf16[4096,768]{1,0:T(8,128)(2,1)} %get-tuple-element.58, bf16[1024,768]{1,0:T(8,128)(2,1)} %collective-permute-done.13, bf16[4608,768]{1,0:T(8,128)(2,1)} %get-tuple-element.59), kind=kLoop, calls=%fused_computation.19 | loop fusion | bytes 4718592 | tf_op jit(solution)/shard_map/concatenate | solution.py:26
  137.4 5.1 %collective-permute-start.17 = (bf16[256,768]{1,0:T(8,128)(2,1)S(1)}, bf16[256,768]{1,0:T(8,128)(2,1)S(1)}, u32[]{:S(2)}, u32[]{:S(2)}) collective-permute-start(bf16[256,768]{1,0:T(8,128)(2,1)S(1)} %get-tuple-element.12), channel_id=1, source_target_pairs={{0,124},{4,0},{8,4},{12,8},{16,12},{20,16},{24,20},{28,24},{32,28}... | collective-permute-start | bytes 1179656 | tf_op jit(solution)/shard_map/ppermute | solution.py:34
  144.4 2.8 constant_dynamic-update-slice_fusion
  147.4 5.1 %collective-permute-start.11 = (bf16[256,768]{1,0:T(8,128)(2,1)S(1)}, bf16[256,768]{1,0:T(8,128)(2,1)S(1)}, u32[]{:S(2)}, u32[]{:S(2)}) collective-permute-start(bf16[256,768]{1,0:T(8,128)(2,1)S(1)} %get-tuple-element.10), channel_id=1, source_target_pairs={{0,124},{4,0},{8,4},{12,8},{16,12},{20,16},{24,20},{28,24},{32,28}... | collective-permute-start | bytes 1179656 | tf_op jit(solution)/shard_map/ppermute | solution.py:34
  154.0 6.3 %shard_map.60 = bf16[1024,768]{1,0:T(8,128)(2,1)S(1)} custom-call(s32[64]{0:T(128)S(1)} %reshape.26.pos_ref, bf16[8,8,128,128]{3,2,1,0:T(8,128)(2,1)S(1)} %pad_maximum_fusion.2.h_ref, bf16[36,128,768]{2,1,0:T(8,128)(2,1)} %bitcast.20, bf16[1024,768]{1,0:T(8,128)(2,1)S(1)} %copy-done.1), custom_call_target="tpu_custom_call" | custom-call | tf_op jit(solution)/shard_map/pallas_call | solution.py:64
  160.9 2.9 %collective-permute-start.24 = (bf16[1024,768]{1,0:T(8,128)(2,1)S(1)}, bf16[1024,768]{1,0:T(8,128)(2,1)S(1)}, u32[]{:S(2)}, u32[]{:S(2)}) collective-permute-start(bf16[1024,768]{1,0:T(8,128)(2,1)S(1)} %shard_map.60), channel_id=1, source_target_pairs={{0,3},{1,0},{2,1},{3,2},{4,7},{5,4},{6,5},{7,6},{8,11},{9,8},{10,9... | collective-permute-start | bytes 4718600 | tf_op jit(solution)/shard_map/ppermute | solution.py:23
  165.4 6.3 %shard_map.59 = bf16[1024,768]{1,0:T(8,128)(2,1)S(1)} custom-call(s32[64]{0:T(128)S(1)} %reshape.26.pos_ref, bf16[8,8,128,128]{3,2,1,0:T(8,128)(2,1)S(1)} %pad_maximum_fusion.2.h_ref, bf16[36,128,768]{2,1,0:T(8,128)(2,1)} %bitcast.19, bf16[1024,768]{1,0:T(8,128)(2,1)S(1)} %copy-done), custom_call_target="tpu_custom_call" | custom-call | tf_op jit(solution)/shard_map/pallas_call | solution.py:64
  171.8 3.2 %collective-permute-start.18 = (bf16[1024,768]{1,0:T(8,128)(2,1)S(1)}, bf16[1024,768]{1,0:T(8,128)(2,1)S(1)}, u32[]{:S(2)}, u32[]{:S(2)}) collective-permute-start(bf16[1024,768]{1,0:T(8,128)(2,1)S(1)} %shard_map.59), channel_id=1, source_target_pairs={{0,3},{1,0},{2,1},{3,2},{4,7},{5,4},{6,5},{7,6},{8,11},{9,8},{10,9... | collective-permute-start | bytes 4718600 | tf_op jit(solution)/shard_map/ppermute | solution.py:23
  175.0 24.1 %collective-permute-done.25 = bf16[1024,768]{1,0:T(8,128)(2,1)S(1)} collective-permute-done((bf16[1024,768]{1,0:T(8,128)(2,1)S(1)}, bf16[1024,768]{1,0:T(8,128)(2,1)S(1)}, u32[]{:S(2)}, u32[]{:S(2)}) %collective-permute-start.25) | collective-permute-done | bytes 1572896 | tf_op jit(solution)/shard_map/ppermute | solution.py:22
  199.3 3.3 %collective-permute-start.27 = (bf16[512,768]{1,0:T(8,128)(2,1)S(1)}, bf16[512,768]{1,0:T(8,128)(2,1)S(1)}, u32[]{:S(2)}, u32[]{:S(2)}) collective-permute-start(bf16[512,768]{1,0:T(8,128)(2,1)S(1)} %slice.55), channel_id=1, source_target_pairs={{0,3},{1,0},{2,1},{3,2},{4,7},{5,4},{6,5},{7,6},{8,11},{9,8},{10,9... | collective-permute-start | bytes 2359304 | tf_op jit(solution)/shard_map/ppermute | solution.py:25
  204.1 28.6 %collective-permute-done.19 = bf16[1024,768]{1,0:T(8,128)(2,1)S(1)} collective-permute-done((bf16[1024,768]{1,0:T(8,128)(2,1)S(1)}, bf16[1024,768]{1,0:T(8,128)(2,1)S(1)}, u32[]{:S(2)}, u32[]{:S(2)}) %collective-permute-start.19) | collective-permute-done | bytes 1572896 | tf_op jit(solution)/shard_map/ppermute | solution.py:22
  233.0 3.3 %collective-permute-start.21 = (bf16[512,768]{1,0:T(8,128)(2,1)S(1)}, bf16[512,768]{1,0:T(8,128)(2,1)S(1)}, u32[]{:S(2)}, u32[]{:S(2)}) collective-permute-start(bf16[512,768]{1,0:T(8,128)(2,1)S(1)} %slice.53), channel_id=1, source_target_pairs={{0,3},{1,0},{2,1},{3,2},{4,7},{5,4},{6,5},{7,6},{8,11},{9,8},{10,9... | collective-permute-start | bytes 2359304 | tf_op jit(solution)/shard_map/ppermute | solution.py:25
  237.8 11.8 %collective-permute-done.26 = bf16[512,768]{1,0:T(8,128)(2,1)S(1)} collective-permute-done((bf16[512,768]{1,0:T(8,128)(2,1)S(1)}, bf16[512,768]{1,0:T(8,128)(2,1)S(1)}, u32[]{:S(2)}, u32[]{:S(2)}) %collective-permute-start.26) | collective-permute-done | bytes 786464 | tf_op jit(solution)/shard_map/ppermute | solution.py:24
  254.2 5.1 %collective-permute-start.29 = (bf16[256,768]{1,0:T(8,128)(2,1)S(1)}, bf16[256,768]{1,0:T(8,128)(2,1)S(1)}, u32[]{:S(2)}, u32[]{:S(2)}) collective-permute-start(bf16[256,768]{1,0:T(8,128)(2,1)S(1)} %get-tuple-element.8), channel_id=1, source_target_pairs={{0,124},{4,0},{8,4},{12,8},{16,12},{20,16},{24,20},{28,24},{32,28}... | collective-permute-start | bytes 1179656 | tf_op jit(solution)/shard_map/ppermute | solution.py:34
  259.3 2.6 collective-permute-done.20
  263.1 5.1 %collective-permute-start.23 = (bf16[256,768]{1,0:T(8,128)(2,1)S(1)}, bf16[256,768]{1,0:T(8,128)(2,1)S(1)}, u32[]{:S(2)}, u32[]{:S(2)}) collective-permute-start(bf16[256,768]{1,0:T(8,128)(2,1)S(1)} %get-tuple-element.6), channel_id=1, source_target_pairs={{0,124},{4,0},{8,4},{12,8},{16,12},{20,16},{24,20},{28,24},{32,28}... | collective-permute-start | bytes 1179656 | tf_op jit(solution)/shard_map/ppermute | solution.py:34
  270.2 2.8 copy-done.3
  273.0 6.3 %shard_map.62 = bf16[1024,768]{1,0:T(8,128)(2,1)S(1)} custom-call(s32[64]{0:T(128)S(1)} %reshape.26.pos_ref, bf16[8,8,128,128]{3,2,1,0:T(8,128)(2,1)S(1)} %pad_maximum_fusion.2.h_ref, bf16[36,128,768]{2,1,0:T(8,128)(2,1)} %bitcast.22, bf16[1024,768]{1,0:T(8,128)(2,1)S(1)} %get-tuple-element.20.prev_ref), custom_call_target="tpu_custom_call" | custom-call | tf_op jit(solution)/shard_map/pallas_call | solution.py:64
  279.4 2.8 copy-done.2
  282.2 6.3 %shard_map.61 = bf16[1024,768]{1,0:T(8,128)(2,1)S(1)} custom-call(s32[64]{0:T(128)S(1)} %reshape.26.pos_ref, bf16[8,8,128,128]{3,2,1,0:T(8,128)(2,1)S(1)} %pad_maximum_fusion.2.h_ref, bf16[36,128,768]{2,1,0:T(8,128)(2,1)} %bitcast.21, bf16[1024,768]{1,0:T(8,128)(2,1)S(1)} %get-tuple-element.21.prev_ref), custom_call_target="tpu_custom_call" | custom-call | tf_op jit(solution)/shard_map/pallas_call | solution.py:64
  (109 shorter events, 45.4 us)
Async XLA Ops:
  1.5 5.5 %collective-permute-start.2 = (s32[8,2]{0,1:T(2,128)S(1)}, s32[8,2]{0,1:T(2,128)S(1)}, u32[]{:S(2)}, u32[]{:S(2)}) collective-permute-start(s32[8,2]{0,1:T(2,128)S(1)} %bitcast.27), channel_id=1, source_target_pairs={{0,3},{1,0},{2,1},{3,2},{4,7},{5,4},{6,5},{7,6},{8,11},{9,8},{10,9... | collective-permute-start | bytes 200 | tf_op jit(solution)/shard_map/ppermute | solution.py:88
  5.7 5.1 %collective-permute-start.1 = (s32[8,2]{0,1:T(2,128)S(1)}, s32[8,2]{0,1:T(2,128)S(1)}, u32[]{:S(2)}, u32[]{:S(2)}) collective-permute-start(s32[8,2]{0,1:T(2,128)S(1)} %bitcast.26), channel_id=1, source_target_pairs={{0,2},{1,3},{2,0},{3,1},{4,6},{5,7},{6,4},{7,5},{8,10},{9,11},{10,... | collective-permute-start | bytes 200 | tf_op jit(solution)/shard_map/ppermute | solution.py:88
  5.7 5.1 %collective-permute-start = (s32[8,2]{0,1:T(2,128)S(1)}, s32[8,2]{0,1:T(2,128)S(1)}, u32[]{:S(2)}, u32[]{:S(2)}) collective-permute-start(s32[8,2]{0,1:T(2,128)S(1)} %bitcast.25), channel_id=1, source_target_pairs={{0,1},{1,2},{2,3},{3,0},{4,5},{5,6},{6,7},{7,4},{8,9},{9,10},{10,1... | collective-permute-start | bytes 200 | tf_op jit(solution)/shard_map/ppermute | solution.py:88
  15.9 37.3 %collective-permute-start.12 = (bf16[1024,768]{1,0:T(8,128)(2,1)S(1)}, bf16[1024,768]{1,0:T(8,128)(2,1)S(1)}, u32[]{:S(2)}, u32[]{:S(2)}) collective-permute-start(bf16[1024,768]{1,0:T(8,128)(2,1)S(1)} %get-tuple-element.20.prev_ref), channel_id=1, source_target_pairs={{0,3},{1,0},{2,1},{3,2},{4,7},{5,4},{6,5},{7,6},{8,11},{9,8},{10,9... | collective-permute-start | bytes 4718600 | tf_op jit(solution)/shard_map/ppermute | solution.py:23
  16.5 39.9 %collective-permute-start.13 = (bf16[1024,768]{1,0:T(8,128)(2,1)S(1)}, bf16[1024,768]{1,0:T(8,128)(2,1)}, u32[]{:S(2)}, u32[]{:S(2)}) collective-permute-start(bf16[1024,768]{1,0:T(8,128)(2,1)S(1)} %get-tuple-element.20.prev_ref), channel_id=1, source_target_pairs={{0,1},{1,2},{2,3},{3,0},{4,5},{5,6},{6,7},{7,4},{8,9},{9,10},{10,1... | collective-permute-start | bytes 4718600 | tf_op jit(solution)/shard_map/ppermute | solution.py:22
  17.9 95.1 %collective-permute-start.7 = (bf16[1024,768]{1,0:T(8,128)(2,1)S(1)}, bf16[1024,768]{1,0:T(8,128)(2,1)}, u32[]{:S(2)}, u32[]{:S(2)}) collective-permute-start(bf16[1024,768]{1,0:T(8,128)(2,1)S(1)} %get-tuple-element.21.prev_ref), channel_id=1, source_target_pairs={{0,1},{1,2},{2,3},{3,0},{4,5},{5,6},{6,7},{7,4},{8,9},{9,10},{10,1... | collective-permute-start | bytes 4718600 | tf_op jit(solution)/shard_map/ppermute | solution.py:22
  18.0 96.6 %collective-permute-start.6 = (bf16[1024,768]{1,0:T(8,128)(2,1)S(1)}, bf16[1024,768]{1,0:T(8,128)(2,1)}, u32[]{:S(2)}, u32[]{:S(2)}) collective-permute-start(bf16[1024,768]{1,0:T(8,128)(2,1)S(1)} %get-tuple-element.21.prev_ref), channel_id=1, source_target_pairs={{0,3},{1,0},{2,1},{3,2},{4,7},{5,4},{6,5},{7,6},{8,11},{9,8},{10,9... | collective-permute-start | bytes 4718600 | tf_op jit(solution)/shard_map/ppermute | solution.py:23
  22.6 75.7 %collective-permute-start.5 = (bf16[8,2,128,128]{3,2,1,0:T(8,128)(2,1)}, bf16[8,2,128,128]{3,2,1,0:T(8,128)(2,1)}, u32[]{:S(2)}, u32[]{:S(2)}) collective-permute-start(bf16[8,2,128,128]{3,2,1,0:T(8,128)(2,1)} %get-tuple-element.23), channel_id=1, source_target_pairs={{0,3},{1,0},{2,1},{3,2},{4,7},{5,4},{6,5},{7,6},{8,11},{9,8},{10,9... | collective-permute-start | bytes 1572872 | tf_op jit(solution)/shard_map/ppermute | solution.py:87
  54.3 46.0 %collective-permute-start.4 = (bf16[8,2,128,128]{3,2,1,0:T(8,128)(2,1)}, bf16[8,2,128,128]{3,2,1,0:T(8,128)(2,1)}, u32[]{:S(2)}, u32[]{:S(2)}) collective-permute-start(bf16[8,2,128,128]{3,2,1,0:T(8,128)(2,1)} %get-tuple-element.24), channel_id=1, source_target_pairs={{0,2},{1,3},{2,0},{3,1},{4,6},{5,7},{6,4},{7,5},{8,10},{9,11},{10,... | collective-permute-start | bytes 1572872 | tf_op jit(solution)/shard_map/ppermute | solution.py:87
  56.4 54.9 %collective-permute-start.3 = (bf16[8,2,128,128]{3,2,1,0:T(8,128)(2,1)}, bf16[8,2,128,128]{3,2,1,0:T(8,128)(2,1)}, u32[]{:S(2)}, u32[]{:S(2)}) collective-permute-start(bf16[8,2,128,128]{3,2,1,0:T(8,128)(2,1)} %get-tuple-element.25), channel_id=1, source_target_pairs={{0,1},{1,2},{2,3},{3,0},{4,5},{5,6},{6,7},{7,4},{8,9},{9,10},{10,1... | collective-permute-start | bytes 1572872 | tf_op jit(solution)/shard_map/ppermute | solution.py:87
  98.2 29.9 %collective-permute-start.14 = (bf16[512,768]{1,0:T(8,128)(2,1)}, bf16[512,768]{1,0:T(8,128)(2,1)}, u32[]{:S(2)}, u32[]{:S(2)}) collective-permute-start(bf16[512,768]{1,0:T(8,128)(2,1)} %slice.50), channel_id=1, source_target_pairs={{0,1},{1,2},{2,3},{3,0},{4,5},{5,6},{6,7},{7,4},{8,9},{9,10},{10,1... | collective-permute-start | bytes 2359304 | tf_op jit(solution)/shard_map/ppermute | solution.py:24
  100.3 30.2 %collective-permute-start.15 = (bf16[512,768]{1,0:T(8,128)(2,1)}, bf16[512,768]{1,0:T(8,128)(2,1)}, u32[]{:S(2)}, u32[]{:S(2)}) collective-permute-start(bf16[512,768]{1,0:T(8,128)(2,1)} %slice.51), channel_id=1, source_target_pairs={{0,3},{1,0},{2,1},{3,2},{4,7},{5,4},{6,5},{7,6},{8,11},{9,8},{10,9... | collective-permute-start | bytes 2359304 | tf_op jit(solution)/shard_map/ppermute | solution.py:25
  114.2 28.2 %collective-permute-start.8 = (bf16[512,768]{1,0:T(8,128)(2,1)S(1)}, bf16[512,768]{1,0:T(8,128)(2,1)S(1)}, u32[]{:S(2)}, u32[]{:S(2)}) collective-permute-start(bf16[512,768]{1,0:T(8,128)(2,1)S(1)} %slice.48), channel_id=1, source_target_pairs={{0,1},{1,2},{2,3},{3,0},{4,5},{5,6},{6,7},{7,4},{8,9},{9,10},{10,1... | collective-permute-start | bytes 2359304 | tf_op jit(solution)/shard_map/ppermute | solution.py:24
  115.8 27.7 %collective-permute-start.9 = (bf16[512,768]{1,0:T(8,128)(2,1)S(1)}, bf16[512,768]{1,0:T(8,128)(2,1)S(1)}, u32[]{:S(2)}, u32[]{:S(2)}) collective-permute-start(bf16[512,768]{1,0:T(8,128)(2,1)S(1)} %slice.49), channel_id=1, source_target_pairs={{0,3},{1,0},{2,1},{3,2},{4,7},{5,4},{6,5},{7,6},{8,11},{9,8},{10,9... | collective-permute-start | bytes 2359304 | tf_op jit(solution)/shard_map/ppermute | solution.py:25
  123.9 18.6 %copy-start.12 = (bf16[4096,768]{1,0:T(8,128)(2,1)S(1)}, bf16[4096,768]{1,0:T(8,128)(2,1)}, u32[]{:S(2)}) copy-start(bf16[4096,768]{1,0:T(8,128)(2,1)} %get-tuple-element.40) | copy-start | bytes 18874372
  137.3 15.1 %collective-permute-start.16 = (bf16[256,768]{1,0:T(8,128)(2,1)S(1)}, bf16[256,768]{1,0:T(8,128)(2,1)S(1)}, u32[]{:S(2)}, u32[]{:S(2)}) collective-permute-start(bf16[256,768]{1,0:T(8,128)(2,1)S(1)} %get-tuple-element.13), channel_id=1, source_target_pairs={{0,4},{4,8},{8,12},{12,16},{16,20},{20,24},{24,28},{28,32},{32,36}... | collective-permute-start | bytes 1179656 | tf_op jit(solution)/shard_map/ppermute | solution.py:33
  137.4 15.8 %collective-permute-start.17 = (bf16[256,768]{1,0:T(8,128)(2,1)S(1)}, bf16[256,768]{1,0:T(8,128)(2,1)S(1)}, u32[]{:S(2)}, u32[]{:S(2)}) collective-permute-start(bf16[256,768]{1,0:T(8,128)(2,1)S(1)} %get-tuple-element.12), channel_id=1, source_target_pairs={{0,124},{4,0},{8,4},{12,8},{16,12},{20,16},{24,20},{28,24},{32,28}... | collective-permute-start | bytes 1179656 | tf_op jit(solution)/shard_map/ppermute | solution.py:34
  147.3 16.5 %collective-permute-start.10 = (bf16[256,768]{1,0:T(8,128)(2,1)S(1)}, bf16[256,768]{1,0:T(8,128)(2,1)S(1)}, u32[]{:S(2)}, u32[]{:S(2)}) collective-permute-start(bf16[256,768]{1,0:T(8,128)(2,1)S(1)} %get-tuple-element.11), channel_id=1, source_target_pairs={{0,4},{4,8},{8,12},{12,16},{16,20},{20,24},{24,28},{28,32},{32,36}... | collective-permute-start | bytes 1179656 | tf_op jit(solution)/shard_map/ppermute | solution.py:33
  147.4 17.2 %collective-permute-start.11 = (bf16[256,768]{1,0:T(8,128)(2,1)S(1)}, bf16[256,768]{1,0:T(8,128)(2,1)S(1)}, u32[]{:S(2)}, u32[]{:S(2)}) collective-permute-start(bf16[256,768]{1,0:T(8,128)(2,1)S(1)} %get-tuple-element.10), channel_id=1, source_target_pairs={{0,124},{4,0},{8,4},{12,8},{16,12},{20,16},{24,20},{28,24},{32,28}... | collective-permute-start | bytes 1179656 | tf_op jit(solution)/shard_map/ppermute | solution.py:34
  160.3 38.7 %collective-permute-start.25 = (bf16[1024,768]{1,0:T(8,128)(2,1)S(1)}, bf16[1024,768]{1,0:T(8,128)(2,1)S(1)}, u32[]{:S(2)}, u32[]{:S(2)}) collective-permute-start(bf16[1024,768]{1,0:T(8,128)(2,1)S(1)} %shard_map.60), channel_id=1, source_target_pairs={{0,1},{1,2},{2,3},{3,0},{4,5},{5,6},{6,7},{7,4},{8,9},{9,10},{10,1... | collective-permute-start | bytes 4718600 | tf_op jit(solution)/shard_map/ppermute | solution.py:22
  160.9 38.3 %collective-permute-start.24 = (bf16[1024,768]{1,0:T(8,128)(2,1)S(1)}, bf16[1024,768]{1,0:T(8,128)(2,1)S(1)}, u32[]{:S(2)}, u32[]{:S(2)}) collective-permute-start(bf16[1024,768]{1,0:T(8,128)(2,1)S(1)} %shard_map.60), channel_id=1, source_target_pairs={{0,3},{1,0},{2,1},{3,2},{4,7},{5,4},{6,5},{7,6},{8,11},{9,8},{10,9... | collective-permute-start | bytes 4718600 | tf_op jit(solution)/shard_map/ppermute | solution.py:23
  171.7 61.1 %collective-permute-start.19 = (bf16[1024,768]{1,0:T(8,128)(2,1)S(1)}, bf16[1024,768]{1,0:T(8,128)(2,1)S(1)}, u32[]{:S(2)}, u32[]{:S(2)}) collective-permute-start(bf16[1024,768]{1,0:T(8,128)(2,1)S(1)} %shard_map.59), channel_id=1, source_target_pairs={{0,1},{1,2},{2,3},{3,0},{4,5},{5,6},{6,7},{7,4},{8,9},{9,10},{10,1... | collective-permute-start | bytes 4718600 | tf_op jit(solution)/shard_map/ppermute | solution.py:22
  171.8 61.1 %collective-permute-start.18 = (bf16[1024,768]{1,0:T(8,128)(2,1)S(1)}, bf16[1024,768]{1,0:T(8,128)(2,1)S(1)}, u32[]{:S(2)}, u32[]{:S(2)}) collective-permute-start(bf16[1024,768]{1,0:T(8,128)(2,1)S(1)} %shard_map.59), channel_id=1, source_target_pairs={{0,3},{1,0},{2,1},{3,2},{4,7},{5,4},{6,5},{7,6},{8,11},{9,8},{10,9... | collective-permute-start | bytes 4718600 | tf_op jit(solution)/shard_map/ppermute | solution.py:23
  199.1 50.5 %collective-permute-start.26 = (bf16[512,768]{1,0:T(8,128)(2,1)S(1)}, bf16[512,768]{1,0:T(8,128)(2,1)S(1)}, u32[]{:S(2)}, u32[]{:S(2)}) collective-permute-start(bf16[512,768]{1,0:T(8,128)(2,1)S(1)} %slice.54), channel_id=1, source_target_pairs={{0,1},{1,2},{2,3},{3,0},{4,5},{5,6},{6,7},{7,4},{8,9},{9,10},{10,1... | collective-permute-start | bytes 2359304 | tf_op jit(solution)/shard_map/ppermute | solution.py:24
  199.3 51.3 %collective-permute-start.27 = (bf16[512,768]{1,0:T(8,128)(2,1)S(1)}, bf16[512,768]{1,0:T(8,128)(2,1)S(1)}, u32[]{:S(2)}, u32[]{:S(2)}) collective-permute-start(bf16[512,768]{1,0:T(8,128)(2,1)S(1)} %slice.55), channel_id=1, source_target_pairs={{0,3},{1,0},{2,1},{3,2},{4,7},{5,4},{6,5},{7,6},{8,11},{9,8},{10,9... | collective-permute-start | bytes 2359304 | tf_op jit(solution)/shard_map/ppermute | solution.py:25
  203.9 32.3 %copy-start.10 = (bf16[1024,768]{1,0:T(8,128)(2,1)S(1)}, bf16[1024,768]{1,0:T(8,128)(2,1)}, u32[]{:S(2)}) copy-start(bf16[1024,768]{1,0:T(8,128)(2,1)} %copy-done.9) | copy-start | bytes 4718596
  232.8 29.1 %collective-permute-start.20 = (bf16[512,768]{1,0:T(8,128)(2,1)S(1)}, bf16[512,768]{1,0:T(8,128)(2,1)S(1)}, u32[]{:S(2)}, u32[]{:S(2)}) collective-permute-start(bf16[512,768]{1,0:T(8,128)(2,1)S(1)} %slice.52), channel_id=1, source_target_pairs={{0,1},{1,2},{2,3},{3,0},{4,5},{5,6},{6,7},{7,4},{8,9},{9,10},{10,1... | collective-permute-start | bytes 2359304 | tf_op jit(solution)/shard_map/ppermute | solution.py:24
  233.0 29.0 %collective-permute-start.21 = (bf16[512,768]{1,0:T(8,128)(2,1)S(1)}, bf16[512,768]{1,0:T(8,128)(2,1)S(1)}, u32[]{:S(2)}, u32[]{:S(2)}) collective-permute-start(bf16[512,768]{1,0:T(8,128)(2,1)S(1)} %slice.53), channel_id=1, source_target_pairs={{0,3},{1,0},{2,1},{3,2},{4,7},{5,4},{6,5},{7,6},{8,11},{9,8},{10,9... | collective-permute-start | bytes 2359304 | tf_op jit(solution)/shard_map/ppermute | solution.py:25
  254.2 16.0 %collective-permute-start.28 = (bf16[256,768]{1,0:T(8,128)(2,1)S(1)}, bf16[256,768]{1,0:T(8,128)(2,1)S(1)}, u32[]{:S(2)}, u32[]{:S(2)}) collective-permute-start(bf16[256,768]{1,0:T(8,128)(2,1)S(1)} %get-tuple-element.9), channel_id=1, source_target_pairs={{0,4},{4,8},{8,12},{12,16},{16,20},{20,24},{24,28},{28,32},{32,36}... | collective-permute-start | bytes 1179656 | tf_op jit(solution)/shard_map/ppermute | solution.py:33
  254.2 15.9 %collective-permute-start.29 = (bf16[256,768]{1,0:T(8,128)(2,1)S(1)}, bf16[256,768]{1,0:T(8,128)(2,1)S(1)}, u32[]{:S(2)}, u32[]{:S(2)}) collective-permute-start(bf16[256,768]{1,0:T(8,128)(2,1)S(1)} %get-tuple-element.8), channel_id=1, source_target_pairs={{0,124},{4,0},{8,4},{12,8},{16,12},{20,16},{24,20},{28,24},{32,28}... | collective-permute-start | bytes 1179656 | tf_op jit(solution)/shard_map/ppermute | solution.py:34
  263.1 16.2 %collective-permute-start.22 = (bf16[256,768]{1,0:T(8,128)(2,1)}, bf16[256,768]{1,0:T(8,128)(2,1)S(1)}, u32[]{:S(2)}, u32[]{:S(2)}) collective-permute-start(bf16[256,768]{1,0:T(8,128)(2,1)} %get-tuple-element.7), channel_id=1, source_target_pairs={{0,4},{4,8},{8,12},{12,16},{16,20},{20,24},{24,28},{28,32},{32,36}... | collective-permute-start | bytes 1179656 | tf_op jit(solution)/shard_map/ppermute | solution.py:33
  263.1 16.2 %collective-permute-start.23 = (bf16[256,768]{1,0:T(8,128)(2,1)S(1)}, bf16[256,768]{1,0:T(8,128)(2,1)S(1)}, u32[]{:S(2)}, u32[]{:S(2)}) collective-permute-start(bf16[256,768]{1,0:T(8,128)(2,1)S(1)} %get-tuple-element.6), channel_id=1, source_target_pairs={{0,124},{4,0},{8,4},{12,8},{16,12},{20,16},{24,20},{28,24},{32,28}... | collective-permute-start | bytes 1179656 | tf_op jit(solution)/shard_map/ppermute | solution.py:34
  (11 other events, 77.4 us)

commit v13 on v12

--- a/solution.py
+++ b/solution.py
@@ -82,10 +82,16 @@
     p_split = rel.reshape(nl, per_dev, rel.shape[1])
     h_parts = [lax.dynamic_index_in_dim(h_split, lidx, 0, keepdims=False)]
     p_parts = [lax.dynamic_index_in_dim(p_split, lidx, 0, keepdims=False)]
+    h_size = h_parts[0].size
     for k in range(1, nl):
         dest = (lidx + k) % nl
-        h_parts.append(lax.ppermute(lax.dynamic_index_in_dim(h_split, dest, 0, keepdims=False), "layer", shift(nl, k)))
-        p_parts.append(lax.ppermute(lax.dynamic_index_in_dim(p_split, dest, 0, keepdims=False), "layer", shift(nl, k)))
+        piece = jnp.concatenate([
+            lax.dynamic_index_in_dim(h_split, dest, 0, keepdims=False).reshape(-1),
+            lax.dynamic_index_in_dim(p_split, dest, 0, keepdims=False).reshape(-1).astype(h_blocks.dtype),
+        ])
+        got = lax.ppermute(piece, "layer", shift(nl, k))
+        h_parts.append(got[:h_size].reshape(h_parts[0].shape))
+        p_parts.append(got[h_size:].astype(p_split.dtype).reshape(p_parts[0].shape))
     h_own = jnp.concatenate(h_parts, axis=1)
     rel_own = jnp.concatenate(p_parts, axis=1)
     t_now, rel_own = lax.optimization_barrier((t_now, rel_own))

time: 291 us -> 295 us (1.014)
  starting transfers between devices: 61 us -> 52.4 us
  local copies, waits for them, and re-layouts: 54.2 us -> 60.6 us
  waiting for transfers between devices: 143 us -> 146 us
    ppermute x4, waiting for transfers between devices: 52.7 us -> 102 us  [exchange(): from_prev = lax.ppermute(own, 'layer', shift(nl, 1))]
    ppermute x4, waiting for transfers between devices: 30.1 us -> 0.01 us  [exchange(): from_next = lax.ppermute(own, 'layer', shift(nl, nl - 1))]
    ppermute x6 -> x3, waiting for transfers between devices: 41.4 us -> 23.1 us  [shards(): got = lax.ppermute(piece, 'layer', shift(nl, k))]
    ppermute x4, starting transfers between devices: 19.3 us -> 13.1 us  [exchange(): far_b = lax.ppermute(from_next[half:], 'layer', shift(nl, nl - 1))]
    slice x0 -> x3, local copies, waits for them, and re-layouts: none -> 3.38 us  [shards(): h_parts.append(got[:h_size].reshape(h_parts[0].shape))]
    ppermute x6 -> x3, starting transfers between devices: 8.68 us -> 5.62 us  [shards(): got = lax.ppermute(piece, 'layer', shift(nl, k))]
    ppermute x4, starting transfers between devices: 9.94 us -> 12.9 us  [exchange(): from_next = lax.ppermute(own, 'layer', shift(nl, nl - 1))]
    unnamed x45 -> x39, local copies, waits for them, and re-layouts: 30.6 us -> 30.3 us
  transfers between devices with their start and end apart: 30 -> 27, of which waited for: 10 -> 10; matrix products, arithmetic and copies ran while one was open for 16% -> 18% of each run, Pallas kernels for 7% -> 6%
where the time goes in v13:
time: 295 us; the launch traced here: 294 us
  waiting for transfers between devices  146 us (49%)
  local copies, waits for them, and re-layouts  60.6 us (21%)
  starting transfers between devices  52.4 us (18%)
  Pallas kernels  25.2 us (9%)
  other arithmetic  8.14 us (3%)
    ppermute x4, waiting for transfers between devices, exchange(): from_prev = lax.ppermute(own, 'layer', shift(nl, 1))  102 us
    unnamed x39, local copies, waits for them, and re-layouts  30.3 us
    pallas_call x4, Pallas kernels, own_rows(): pl.pallas_call(step_kernel, grid_spec=grid_spec, out_shape=jax.ShapeDtype...  25.2 us
    ppermute x3, waiting for transfers between devices, shards(): got = lax.ppermute(piece, 'layer', shift(nl, k))  23.1 us
    ppermute x4, waiting for transfers between devices, exchange(): far_a = lax.ppermute(from_prev[:half], 'layer', shift(nl, 1))  21.1 us
    ppermute x4, starting transfers between devices, exchange(): hi = lax.ppermute(first, 'grid', shift(ng, ng - 1))  20.2 us
    ppermute x4, starting transfers between devices, exchange(): far_b = lax.ppermute(from_next[half:], 'layer', shift(nl, nl - 1))  13.1 us
    ppermute x4, starting transfers between devices, exchange(): from_next = lax.ppermute(own, 'layer', shift(nl, nl - 1))  12.9 us
  transfers between devices with their start and end apart: 27, of which 10 were waited for; matrix products, arithmetic and copies ran while one was open for 18% of the time, Pallas kernels for 6%

profile of v13, /device:TPU:0, one launch (start us, length us, event | category | flops | bytes accessed | tf_op | source)
XLA Modules:
  0.0 293.8 jit_solution(17996440161049913845)
XLA Ops:
  4.3 4.2 %collective-permute-start.2 = (bf16[262160]{0:T(1024)(128)(2,1)S(1)}, bf16[262160]{0:T(1024)(128)(2,1)}, u32[]{:S(2)}, u32[]{:S(2)}) collective-permute-start(bf16[262160]{0:T(1024)(128)(2,1)S(1)} %pad_maximum_fusion.5), channel_id=1, source_target_pairs={{0,3},{1,0},{2,1},{3,2},{4,7},{5,4},{6,5},{7,6},{8,11},{9,8},{10,9... | collective-permute-start | bytes 1572968 | tf_op jit(solution)/shard_map/ppermute | solution.py:92
  10.4 20.6 %collective-permute-done.2 = bf16[262160]{0:T(1024)(128)(2,1)} collective-permute-done((bf16[262160]{0:T(1024)(128)(2,1)S(1)}, bf16[262160]{0:T(1024)(128)(2,1)}, u32[]{:S(2)}, u32[]{:S(2)}) %collective-permute-start.2) | collective-permute-done | bytes 524352 | tf_op jit(solution)/shard_map/ppermute | solution.py:92
  36.0 4.9 %constant_dynamic-update-slice_fusion.4 = (bf16[4096,768]{1,0:T(8,128)(2,1)}, bf16[4608,768]{1,0:T(8,128)(2,1)}, bf16[4096,768]{1,0:T(8,128)(2,1)}, bf16[4608,76...) fusion(bf16[1024,1536]{1,0:T(8,128)(2,1)} %param.6), kind=kLoop, calls=%fused_computation.11 | loop fusion | bytes 12582912
  40.9 3.2 %collective-permute-start.9 = (bf16[1024,768]{1,0:T(8,128)(2,1)S(1)}, bf16[1024,768]{1,0:T(8,128)(2,1)}, u32[]{:S(2)}, u32[]{:S(2)}) collective-permute-start(bf16[1024,768]{1,0:T(8,128)(2,1)S(1)} %get-tuple-element.20.prev_ref), channel_id=1, source_target_pairs={{0,3},{1,0},{2,1},{3,2},{4,7},{5,4},{6,5},{7,6},{8,11},{9,8},{10,9... | collective-permute-start | bytes 4718600 | tf_op jit(solution)/shard_map/ppermute | solution.py:23
  44.2 3.2 %collective-permute-start.3 = (bf16[1024,768]{1,0:T(8,128)(2,1)S(1)}, bf16[1024,768]{1,0:T(8,128)(2,1)}, u32[]{:S(2)}, u32[]{:S(2)}) collective-permute-start(bf16[1024,768]{1,0:T(8,128)(2,1)S(1)} %get-tuple-element.21.prev_ref), channel_id=1, source_target_pairs={{0,3},{1,0},{2,1},{3,2},{4,7},{5,4},{6,5},{7,6},{8,11},{9,8},{10,9... | collective-permute-start | bytes 4718600 | tf_op jit(solution)/shard_map/ppermute | solution.py:23
  47.4 3.7 %fusion.10 = (bf16[1024,768]{1,0:T(8,128)(2,1)}, bf16[1024,768]{1,0:T(8,128)(2,1)}) fusion(bf16[1024,1536]{1,0:T(8,128)(2,1)} %param.7), kind=kLoop, calls=%fused_computation.97 | loop fusion | bytes 6291456 | tf_op jit(solution)/shard_map/slice | solution.py:115
  51.1 28.4 %collective-permute-done.10 = bf16[1024,768]{1,0:T(8,128)(2,1)} collective-permute-done((bf16[1024,768]{1,0:T(8,128)(2,1)S(1)}, bf16[1024,768]{1,0:T(8,128)(2,1)}, u32[]{:S(2)}, u32[]{:S(2)}) %collective-permute-start.10) | collective-permute-done | bytes 1572896 | tf_op jit(solution)/shard_map/ppermute | solution.py:22
  83.7 3.2 %collective-permute-start.12 = (bf16[512,768]{1,0:T(8,128)(2,1)}, bf16[512,768]{1,0:T(8,128)(2,1)}, u32[]{:S(2)}, u32[]{:S(2)}) collective-permute-start(bf16[512,768]{1,0:T(8,128)(2,1)} %slice.105), channel_id=1, source_target_pairs={{0,3},{1,0},{2,1},{3,2},{4,7},{5,4},{6,5},{7,6},{8,11},{9,8},{10,9... | collective-permute-start | bytes 2359304 | tf_op jit(solution)/shard_map/ppermute | solution.py:25
  92.0 21.2 %collective-permute-done.4 = bf16[1024,768]{1,0:T(8,128)(2,1)} collective-permute-done((bf16[1024,768]{1,0:T(8,128)(2,1)S(1)}, bf16[1024,768]{1,0:T(8,128)(2,1)}, u32[]{:S(2)}, u32[]{:S(2)}) %collective-permute-start.4) | collective-permute-done | bytes 1572896 | tf_op jit(solution)/shard_map/ppermute | solution.py:22
  115.7 3.3 %collective-permute-start.6 = (bf16[512,768]{1,0:T(8,128)(2,1)S(1)}, bf16[512,768]{1,0:T(8,128)(2,1)S(1)}, u32[]{:S(2)}, u32[]{:S(2)}) collective-permute-start(bf16[512,768]{1,0:T(8,128)(2,1)S(1)} %slice.103), channel_id=1, source_target_pairs={{0,3},{1,0},{2,1},{3,2},{4,7},{5,4},{6,5},{7,6},{8,11},{9,8},{10,9... | collective-permute-start | bytes 2359304 | tf_op jit(solution)/shard_map/ppermute | solution.py:25
  119.0 3.3 %constant_dynamic-update-slice_fusion.15 = (bf16[4096,768]{1,0:T(8,128)(2,1)}, bf16[4608,768]{1,0:T(8,128)(2,1)}) fusion(bf16[4096,768]{1,0:T(8,128)(2,1)} %get-tuple-element.18, bf16[1024,768]{1,0:T(8,128)(2,1)} %collective-permute-done.9, bf16[4608,768]{1,0:T(8,128)(2,1)} %get-tuple-element.19), kind=kLoop, calls=%fused_computation.22 | loop fusion | bytes 4718592
  122.2 2.8 constant_dynamic-update-slice_fusion.3
  125.0 5.1 %collective-permute-done.11 = bf16[512,768]{1,0:T(8,128)(2,1)} collective-permute-done((bf16[512,768]{1,0:T(8,128)(2,1)}, bf16[512,768]{1,0:T(8,128)(2,1)}, u32[]{:S(2)}, u32[]{:S(2)}) %collective-permute-start.11) | collective-permute-done | bytes 786464 | tf_op jit(solution)/shard_map/ppermute | solution.py:24
  134.8 3.3 %constant_dynamic-update-slice_fusion.12 = (bf16[4096,768]{1,0:T(8,128)(2,1)}, bf16[4608,768]{1,0:T(8,128)(2,1)}) fusion(bf16[4096,768]{1,0:T(8,128)(2,1)} %get-tuple-element.58, bf16[1024,768]{1,0:T(8,128)(2,1)} %collective-permute-done.10, bf16[4608,768]{1,0:T(8,128)(2,1)} %get-tuple-element.59), kind=kLoop, calls=%fused_computation.19 | loop fusion | bytes 4718592 | tf_op jit(solution)/shard_map/concatenate | solution.py:26
  139.3 5.1 %collective-permute-start.14 = (bf16[256,768]{1,0:T(8,128)(2,1)S(1)}, bf16[256,768]{1,0:T(8,128)(2,1)S(1)}, u32[]{:S(2)}, u32[]{:S(2)}) collective-permute-start(bf16[256,768]{1,0:T(8,128)(2,1)S(1)} %get-tuple-element.12), channel_id=1, source_target_pairs={{0,124},{4,0},{8,4},{12,8},{16,12},{20,16},{24,20},{28,24},{32,28}... | collective-permute-start | bytes 1179656 | tf_op jit(solution)/shard_map/ppermute | solution.py:34
  147.9 2.8 constant_dynamic-update-slice_fusion
  150.8 5.1 %collective-permute-start.8 = (bf16[256,768]{1,0:T(8,128)(2,1)S(1)}, bf16[256,768]{1,0:T(8,128)(2,1)S(1)}, u32[]{:S(2)}, u32[]{:S(2)}) collective-permute-start(bf16[256,768]{1,0:T(8,128)(2,1)S(1)} %get-tuple-element.10), channel_id=1, source_target_pairs={{0,124},{4,0},{8,4},{12,8},{16,12},{20,16},{24,20},{28,24},{32,28}... | collective-permute-start | bytes 1179656 | tf_op jit(solution)/shard_map/ppermute | solution.py:34
  157.4 6.3 %shard_map.60 = bf16[1024,768]{1,0:T(8,128)(2,1)S(1)} custom-call(s32[64]{0:T(128)S(1)} %reshape.93.pos_ref, bf16[8,8,128,128]{3,2,1,0:T(8,128)(2,1)S(1)} %pad_maximum_fusion.2.h_ref, bf16[36,128,768]{2,1,0:T(8,128)(2,1)} %bitcast.17, bf16[1024,768]{1,0:T(8,128)(2,1)S(1)} %copy-done.1), custom_call_target="tpu_custom_call" | custom-call | tf_op jit(solution)/shard_map/pallas_call | solution.py:64
  163.8 3.2 %collective-permute-start.21 = (bf16[1024,768]{1,0:T(8,128)(2,1)S(1)}, bf16[1024,768]{1,0:T(8,128)(2,1)S(1)}, u32[]{:S(2)}, u32[]{:S(2)}) collective-permute-start(bf16[1024,768]{1,0:T(8,128)(2,1)S(1)} %shard_map.60), channel_id=1, source_target_pairs={{0,3},{1,0},{2,1},{3,2},{4,7},{5,4},{6,5},{7,6},{8,11},{9,8},{10,9... | collective-permute-start | bytes 4718600 | tf_op jit(solution)/shard_map/ppermute | solution.py:23
  168.6 6.3 %shard_map.59 = bf16[1024,768]{1,0:T(8,128)(2,1)S(1)} custom-call(s32[64]{0:T(128)S(1)} %reshape.93.pos_ref, bf16[8,8,128,128]{3,2,1,0:T(8,128)(2,1)S(1)} %pad_maximum_fusion.2.h_ref, bf16[36,128,768]{2,1,0:T(8,128)(2,1)} %bitcast.16, bf16[1024,768]{1,0:T(8,128)(2,1)S(1)} %copy-done), custom_call_target="tpu_custom_call" | custom-call | tf_op jit(solution)/shard_map/pallas_call | solution.py:64
  175.0 3.2 %collective-permute-start.15 = (bf16[1024,768]{1,0:T(8,128)(2,1)S(1)}, bf16[1024,768]{1,0:T(8,128)(2,1)S(1)}, u32[]{:S(2)}, u32[]{:S(2)}) collective-permute-start(bf16[1024,768]{1,0:T(8,128)(2,1)S(1)} %shard_map.59), channel_id=1, source_target_pairs={{0,3},{1,0},{2,1},{3,2},{4,7},{5,4},{6,5},{7,6},{8,11},{9,8},{10,9... | collective-permute-start | bytes 4718600 | tf_op jit(solution)/shard_map/ppermute | solution.py:23
  178.2 24.1 %collective-permute-done.22 = bf16[1024,768]{1,0:T(8,128)(2,1)S(1)} collective-permute-done((bf16[1024,768]{1,0:T(8,128)(2,1)S(1)}, bf16[1024,768]{1,0:T(8,128)(2,1)S(1)}, u32[]{:S(2)}, u32[]{:S(2)}) %collective-permute-start.22) | collective-permute-done | bytes 1572896 | tf_op jit(solution)/shard_map/ppermute | solution.py:22
  202.5 3.3 %collective-permute-start.24 = (bf16[512,768]{1,0:T(8,128)(2,1)S(1)}, bf16[512,768]{1,0:T(8,128)(2,1)S(1)}, u32[]{:S(2)}, u32[]{:S(2)}) collective-permute-start(bf16[512,768]{1,0:T(8,128)(2,1)S(1)} %slice.109), channel_id=1, source_target_pairs={{0,3},{1,0},{2,1},{3,2},{4,7},{5,4},{6,5},{7,6},{8,11},{9,8},{10,9... | collective-permute-start | bytes 2359304 | tf_op jit(solution)/shard_map/ppermute | solution.py:25
  207.4 28.6 %collective-permute-done.16 = bf16[1024,768]{1,0:T(8,128)(2,1)S(1)} collective-permute-done((bf16[1024,768]{1,0:T(8,128)(2,1)S(1)}, bf16[1024,768]{1,0:T(8,128)(2,1)S(1)}, u32[]{:S(2)}, u32[]{:S(2)}) %collective-permute-start.16) | collective-permute-done | bytes 1572896 | tf_op jit(solution)/shard_map/ppermute | solution.py:22
  236.2 3.3 %collective-permute-start.18 = (bf16[512,768]{1,0:T(8,128)(2,1)S(1)}, bf16[512,768]{1,0:T(8,128)(2,1)S(1)}, u32[]{:S(2)}, u32[]{:S(2)}) collective-permute-start(bf16[512,768]{1,0:T(8,128)(2,1)S(1)} %slice.107), channel_id=1, source_target_pairs={{0,3},{1,0},{2,1},{3,2},{4,7},{5,4},{6,5},{7,6},{8,11},{9,8},{10,9... | collective-permute-start | bytes 2359304 | tf_op jit(solution)/shard_map/ppermute | solution.py:25
  241.0 11.8 %collective-permute-done.23 = bf16[512,768]{1,0:T(8,128)(2,1)S(1)} collective-permute-done((bf16[512,768]{1,0:T(8,128)(2,1)S(1)}, bf16[512,768]{1,0:T(8,128)(2,1)S(1)}, u32[]{:S(2)}, u32[]{:S(2)}) %collective-permute-start.23) | collective-permute-done | bytes 786464 | tf_op jit(solution)/shard_map/ppermute | solution.py:24
  257.5 5.1 %collective-permute-start.26 = (bf16[256,768]{1,0:T(8,128)(2,1)S(1)}, bf16[256,768]{1,0:T(8,128)(2,1)S(1)}, u32[]{:S(2)}, u32[]{:S(2)}) collective-permute-start(bf16[256,768]{1,0:T(8,128)(2,1)S(1)} %get-tuple-element.8), channel_id=1, source_target_pairs={{0,124},{4,0},{8,4},{12,8},{16,12},{20,16},{24,20},{28,24},{32,28}... | collective-permute-start | bytes 1179656 | tf_op jit(solution)/shard_map/ppermute | solution.py:34
  266.5 5.1 %collective-permute-start.20 = (bf16[256,768]{1,0:T(8,128)(2,1)S(1)}, bf16[256,768]{1,0:T(8,128)(2,1)S(1)}, u32[]{:S(2)}, u32[]{:S(2)}) collective-permute-start(bf16[256,768]{1,0:T(8,128)(2,1)S(1)} %get-tuple-element.6), channel_id=1, source_target_pairs={{0,124},{4,0},{8,4},{12,8},{16,12},{20,16},{24,20},{28,24},{32,28}... | collective-permute-start | bytes 1179656 | tf_op jit(solution)/shard_map/ppermute | solution.py:34
  273.6 2.8 copy-done.3
  276.4 6.3 %shard_map.62 = bf16[1024,768]{1,0:T(8,128)(2,1)S(1)} custom-call(s32[64]{0:T(128)S(1)} %reshape.93.pos_ref, bf16[8,8,128,128]{3,2,1,0:T(8,128)(2,1)S(1)} %pad_maximum_fusion.2.h_ref, bf16[36,128,768]{2,1,0:T(8,128)(2,1)} %bitcast.19, bf16[1024,768]{1,0:T(8,128)(2,1)S(1)} %get-tuple-element.20.prev_ref), custom_call_target="tpu_custom_call" | custom-call | tf_op jit(solution)/shard_map/pallas_call | solution.py:64
  282.8 2.8 copy-done.2
  285.6 6.3 %shard_map.61 = bf16[1024,768]{1,0:T(8,128)(2,1)S(1)} custom-call(s32[64]{0:T(128)S(1)} %reshape.93.pos_ref, bf16[8,8,128,128]{3,2,1,0:T(8,128)(2,1)S(1)} %pad_maximum_fusion.2.h_ref, bf16[36,128,768]{2,1,0:T(8,128)(2,1)} %bitcast.18, bf16[1024,768]{1,0:T(8,128)(2,1)S(1)} %get-tuple-element.21.prev_ref), custom_call_target="tpu_custom_call" | custom-call | tf_op jit(solution)/shard_map/pallas_call | solution.py:64
  (119 shorter events, 51.1 us)
Async XLA Ops:
  4.3 26.7 %collective-permute-start.2 = (bf16[262160]{0:T(1024)(128)(2,1)S(1)}, bf16[262160]{0:T(1024)(128)(2,1)}, u32[]{:S(2)}, u32[]{:S(2)}) collective-permute-start(bf16[262160]{0:T(1024)(128)(2,1)S(1)} %pad_maximum_fusion.5), channel_id=1, source_target_pairs={{0,3},{1,0},{2,1},{3,2},{4,7},{5,4},{6,5},{7,6},{8,11},{9,8},{10,9... | collective-permute-start | bytes 1572968 | tf_op jit(solution)/shard_map/ppermute | solution.py:92
  8.7 23.1 %collective-permute-start.1 = (bf16[262160]{0:T(1024)(128)(2,1)S(1)}, bf16[262160]{0:T(1024)(128)(2,1)}, u32[]{:S(2)}, u32[]{:S(2)}) collective-permute-start(bf16[262160]{0:T(1024)(128)(2,1)S(1)} %pad_maximum_fusion.4), channel_id=1, source_target_pairs={{0,2},{1,3},{2,0},{3,1},{4,6},{5,7},{6,4},{7,5},{8,10},{9,11},{10,... | collective-permute-start | bytes 1572968 | tf_op jit(solution)/shard_map/ppermute | solution.py:92
  9.0 26.1 %collective-permute-start = (bf16[262160]{0:T(1024)(128)(2,1)S(1)}, bf16[262160]{0:T(1024)(128)(2,1)}, u32[]{:S(2)}, u32[]{:S(2)}) collective-permute-start(bf16[262160]{0:T(1024)(128)(2,1)S(1)} %pad_maximum_fusion.3), channel_id=1, source_target_pairs={{0,1},{1,2},{2,3},{3,0},{4,5},{5,6},{6,7},{7,4},{8,9},{9,10},{10,1... | collective-permute-start | bytes 1572968 | tf_op jit(solution)/shard_map/ppermute | solution.py:92
  40.9 38.6 %collective-permute-start.10 = (bf16[1024,768]{1,0:T(8,128)(2,1)S(1)}, bf16[1024,768]{1,0:T(8,128)(2,1)}, u32[]{:S(2)}, u32[]{:S(2)}) collective-permute-start(bf16[1024,768]{1,0:T(8,128)(2,1)S(1)} %get-tuple-element.20.prev_ref), channel_id=1, source_target_pairs={{0,1},{1,2},{2,3},{3,0},{4,5},{5,6},{6,7},{7,4},{8,9},{9,10},{10,1... | collective-permute-start | bytes 4718600 | tf_op jit(solution)/shard_map/ppermute | solution.py:22
  40.9 40.7 %collective-permute-start.9 = (bf16[1024,768]{1,0:T(8,128)(2,1)S(1)}, bf16[1024,768]{1,0:T(8,128)(2,1)}, u32[]{:S(2)}, u32[]{:S(2)}) collective-permute-start(bf16[1024,768]{1,0:T(8,128)(2,1)S(1)} %get-tuple-element.20.prev_ref), channel_id=1, source_target_pairs={{0,3},{1,0},{2,1},{3,2},{4,7},{5,4},{6,5},{7,6},{8,11},{9,8},{10,9... | collective-permute-start | bytes 4718600 | tf_op jit(solution)/shard_map/ppermute | solution.py:23
  44.1 69.0 %collective-permute-start.4 = (bf16[1024,768]{1,0:T(8,128)(2,1)S(1)}, bf16[1024,768]{1,0:T(8,128)(2,1)}, u32[]{:S(2)}, u32[]{:S(2)}) collective-permute-start(bf16[1024,768]{1,0:T(8,128)(2,1)S(1)} %get-tuple-element.21.prev_ref), channel_id=1, source_target_pairs={{0,1},{1,2},{2,3},{3,0},{4,5},{5,6},{6,7},{7,4},{8,9},{9,10},{10,1... | collective-permute-start | bytes 4718600 | tf_op jit(solution)/shard_map/ppermute | solution.py:22
  44.2 70.3 %collective-permute-start.3 = (bf16[1024,768]{1,0:T(8,128)(2,1)S(1)}, bf16[1024,768]{1,0:T(8,128)(2,1)}, u32[]{:S(2)}, u32[]{:S(2)}) collective-permute-start(bf16[1024,768]{1,0:T(8,128)(2,1)S(1)} %get-tuple-element.21.prev_ref), channel_id=1, source_target_pairs={{0,3},{1,0},{2,1},{3,2},{4,7},{5,4},{6,5},{7,6},{8,11},{9,8},{10,9... | collective-permute-start | bytes 4718600 | tf_op jit(solution)/shard_map/ppermute | solution.py:23
  81.6 48.5 %collective-permute-start.11 = (bf16[512,768]{1,0:T(8,128)(2,1)}, bf16[512,768]{1,0:T(8,128)(2,1)}, u32[]{:S(2)}, u32[]{:S(2)}) collective-permute-start(bf16[512,768]{1,0:T(8,128)(2,1)} %slice.104), channel_id=1, source_target_pairs={{0,1},{1,2},{2,3},{3,0},{4,5},{5,6},{6,7},{7,4},{8,9},{9,10},{10,1... | collective-permute-start | bytes 2359304 | tf_op jit(solution)/shard_map/ppermute | solution.py:24
  83.7 48.7 %collective-permute-start.12 = (bf16[512,768]{1,0:T(8,128)(2,1)}, bf16[512,768]{1,0:T(8,128)(2,1)}, u32[]{:S(2)}, u32[]{:S(2)}) collective-permute-start(bf16[512,768]{1,0:T(8,128)(2,1)} %slice.105), channel_id=1, source_target_pairs={{0,3},{1,0},{2,1},{3,2},{4,7},{5,4},{6,5},{7,6},{8,11},{9,8},{10,9... | collective-permute-start | bytes 2359304 | tf_op jit(solution)/shard_map/ppermute | solution.py:25
  89.3 32.9 %slice-start = ((s8[6291456]{0:T(1024)(128)(4,1)}), s8[4194304]{0:T(1024)(128)(4,1)S(1)}, s32[]{:S(2)}) async-start(s8[6291456]{0:T(1024)(128)(4,1)} %bitcast.27), calls=%async_computation | async-start | bytes 8388608
  92.0 30.2 %slice-start.1 = ((s8[6291456]{0:T(1024)(128)(4,1)}), s8[2097152]{0:T(1024)(128)(4,1)S(1)}, s32[]{:S(2)}) async-start(s8[6291456]{0:T(1024)(128)(4,1)} %bitcast.27), calls=%async_computation.1 | async-start | bytes 4194304
  114.4 31.5 %collective-permute-start.5 = (bf16[512,768]{1,0:T(8,128)(2,1)S(1)}, bf16[512,768]{1,0:T(8,128)(2,1)S(1)}, u32[]{:S(2)}, u32[]{:S(2)}) collective-permute-start(bf16[512,768]{1,0:T(8,128)(2,1)S(1)} %slice.102), channel_id=1, source_target_pairs={{0,1},{1,2},{2,3},{3,0},{4,5},{5,6},{6,7},{7,4},{8,9},{9,10},{10,1... | collective-permute-start | bytes 2359304 | tf_op jit(solution)/shard_map/ppermute | solution.py:24
  115.7 31.2 %collective-permute-start.6 = (bf16[512,768]{1,0:T(8,128)(2,1)S(1)}, bf16[512,768]{1,0:T(8,128)(2,1)S(1)}, u32[]{:S(2)}, u32[]{:S(2)}) collective-permute-start(bf16[512,768]{1,0:T(8,128)(2,1)S(1)} %slice.103), channel_id=1, source_target_pairs={{0,3},{1,0},{2,1},{3,2},{4,7},{5,4},{6,5},{7,6},{8,11},{9,8},{10,9... | collective-permute-start | bytes 2359304 | tf_op jit(solution)/shard_map/ppermute | solution.py:25
  139.3 16.6 %collective-permute-start.13 = (bf16[256,768]{1,0:T(8,128)(2,1)S(1)}, bf16[256,768]{1,0:T(8,128)(2,1)S(1)}, u32[]{:S(2)}, u32[]{:S(2)}) collective-permute-start(bf16[256,768]{1,0:T(8,128)(2,1)S(1)} %get-tuple-element.13), channel_id=1, source_target_pairs={{0,4},{4,8},{8,12},{12,16},{16,20},{20,24},{24,28},{28,32},{32,36}... | collective-permute-start | bytes 1179656 | tf_op jit(solution)/shard_map/ppermute | solution.py:33
  139.3 17.3 %collective-permute-start.14 = (bf16[256,768]{1,0:T(8,128)(2,1)S(1)}, bf16[256,768]{1,0:T(8,128)(2,1)S(1)}, u32[]{:S(2)}, u32[]{:S(2)}) collective-permute-start(bf16[256,768]{1,0:T(8,128)(2,1)S(1)} %get-tuple-element.12), channel_id=1, source_target_pairs={{0,124},{4,0},{8,4},{12,8},{16,12},{20,16},{24,20},{28,24},{32,28}... | collective-permute-start | bytes 1179656 | tf_op jit(solution)/shard_map/ppermute | solution.py:34
  145.9 11.6 %copy-start.1 = (bf16[1024,768]{1,0:T(8,128)(2,1)S(1)}, bf16[1024,768]{1,0:T(8,128)(2,1)}, u32[]{:S(2)}) copy-start(bf16[1024,768]{1,0:T(8,128)(2,1)} %get-tuple-element.15.prev_ref) | copy-start | bytes 4718596
  150.7 16.3 %collective-permute-start.7 = (bf16[256,768]{1,0:T(8,128)(2,1)S(1)}, bf16[256,768]{1,0:T(8,128)(2,1)S(1)}, u32[]{:S(2)}, u32[]{:S(2)}) collective-permute-start(bf16[256,768]{1,0:T(8,128)(2,1)S(1)} %get-tuple-element.11), channel_id=1, source_target_pairs={{0,4},{4,8},{8,12},{12,16},{16,20},{20,24},{24,28},{28,32},{32,36}... | collective-permute-start | bytes 1179656 | tf_op jit(solution)/shard_map/ppermute | solution.py:33
  150.8 17.0 %collective-permute-start.8 = (bf16[256,768]{1,0:T(8,128)(2,1)S(1)}, bf16[256,768]{1,0:T(8,128)(2,1)S(1)}, u32[]{:S(2)}, u32[]{:S(2)}) collective-permute-start(bf16[256,768]{1,0:T(8,128)(2,1)S(1)} %get-tuple-element.10), channel_id=1, source_target_pairs={{0,124},{4,0},{8,4},{12,8},{16,12},{20,16},{24,20},{28,24},{32,28}... | collective-permute-start | bytes 1179656 | tf_op jit(solution)/shard_map/ppermute | solution.py:34
  163.7 38.5 %collective-permute-start.22 = (bf16[1024,768]{1,0:T(8,128)(2,1)S(1)}, bf16[1024,768]{1,0:T(8,128)(2,1)S(1)}, u32[]{:S(2)}, u32[]{:S(2)}) collective-permute-start(bf16[1024,768]{1,0:T(8,128)(2,1)S(1)} %shard_map.60), channel_id=1, source_target_pairs={{0,1},{1,2},{2,3},{3,0},{4,5},{5,6},{6,7},{7,4},{8,9},{9,10},{10,1... | collective-permute-start | bytes 4718600 | tf_op jit(solution)/shard_map/ppermute | solution.py:22
  163.8 38.6 %collective-permute-start.21 = (bf16[1024,768]{1,0:T(8,128)(2,1)S(1)}, bf16[1024,768]{1,0:T(8,128)(2,1)S(1)}, u32[]{:S(2)}, u32[]{:S(2)}) collective-permute-start(bf16[1024,768]{1,0:T(8,128)(2,1)S(1)} %shard_map.60), channel_id=1, source_target_pairs={{0,3},{1,0},{2,1},{3,2},{4,7},{5,4},{6,5},{7,6},{8,11},{9,8},{10,9... | collective-permute-start | bytes 4718600 | tf_op jit(solution)/shard_map/ppermute | solution.py:23
  174.9 61.1 %collective-permute-start.16 = (bf16[1024,768]{1,0:T(8,128)(2,1)S(1)}, bf16[1024,768]{1,0:T(8,128)(2,1)S(1)}, u32[]{:S(2)}, u32[]{:S(2)}) collective-permute-start(bf16[1024,768]{1,0:T(8,128)(2,1)S(1)} %shard_map.59), channel_id=1, source_target_pairs={{0,1},{1,2},{2,3},{3,0},{4,5},{5,6},{6,7},{7,4},{8,9},{9,10},{10,1... | collective-permute-start | bytes 4718600 | tf_op jit(solution)/shard_map/ppermute | solution.py:22
  175.0 61.1 %collective-permute-start.15 = (bf16[1024,768]{1,0:T(8,128)(2,1)S(1)}, bf16[1024,768]{1,0:T(8,128)(2,1)S(1)}, u32[]{:S(2)}, u32[]{:S(2)}) collective-permute-start(bf16[1024,768]{1,0:T(8,128)(2,1)S(1)} %shard_map.59), channel_id=1, source_target_pairs={{0,3},{1,0},{2,1},{3,2},{4,7},{5,4},{6,5},{7,6},{8,11},{9,8},{10,9... | collective-permute-start | bytes 4718600 | tf_op jit(solution)/shard_map/ppermute | solution.py:23
  202.3 50.5 %collective-permute-start.23 = (bf16[512,768]{1,0:T(8,128)(2,1)S(1)}, bf16[512,768]{1,0:T(8,128)(2,1)S(1)}, u32[]{:S(2)}, u32[]{:S(2)}) collective-permute-start(bf16[512,768]{1,0:T(8,128)(2,1)S(1)} %slice.108), channel_id=1, source_target_pairs={{0,1},{1,2},{2,3},{3,0},{4,5},{5,6},{6,7},{7,4},{8,9},{9,10},{10,1... | collective-permute-start | bytes 2359304 | tf_op jit(solution)/shard_map/ppermute | solution.py:24
  202.5 51.3 %collective-permute-start.24 = (bf16[512,768]{1,0:T(8,128)(2,1)S(1)}, bf16[512,768]{1,0:T(8,128)(2,1)S(1)}, u32[]{:S(2)}, u32[]{:S(2)}) collective-permute-start(bf16[512,768]{1,0:T(8,128)(2,1)S(1)} %slice.109), channel_id=1, source_target_pairs={{0,3},{1,0},{2,1},{3,2},{4,7},{5,4},{6,5},{7,6},{8,11},{9,8},{10,9... | collective-permute-start | bytes 2359304 | tf_op jit(solution)/shard_map/ppermute | solution.py:25
  207.2 32.3 %copy-start.7 = (bf16[1024,768]{1,0:T(8,128)(2,1)S(1)}, bf16[1024,768]{1,0:T(8,128)(2,1)}, u32[]{:S(2)}) copy-start(bf16[1024,768]{1,0:T(8,128)(2,1)} %copy-done.6) | copy-start | bytes 4718596
  236.0 29.2 %collective-permute-start.17 = (bf16[512,768]{1,0:T(8,128)(2,1)S(1)}, bf16[512,768]{1,0:T(8,128)(2,1)S(1)}, u32[]{:S(2)}, u32[]{:S(2)}) collective-permute-start(bf16[512,768]{1,0:T(8,128)(2,1)S(1)} %slice.106), channel_id=1, source_target_pairs={{0,1},{1,2},{2,3},{3,0},{4,5},{5,6},{6,7},{7,4},{8,9},{9,10},{10,1... | collective-permute-start | bytes 2359304 | tf_op jit(solution)/shard_map/ppermute | solution.py:24
  236.2 29.2 %collective-permute-start.18 = (bf16[512,768]{1,0:T(8,128)(2,1)S(1)}, bf16[512,768]{1,0:T(8,128)(2,1)S(1)}, u32[]{:S(2)}, u32[]{:S(2)}) collective-permute-start(bf16[512,768]{1,0:T(8,128)(2,1)S(1)} %slice.107), channel_id=1, source_target_pairs={{0,3},{1,0},{2,1},{3,2},{4,7},{5,4},{6,5},{7,6},{8,11},{9,8},{10,9... | collective-permute-start | bytes 2359304 | tf_op jit(solution)/shard_map/ppermute | solution.py:25
  239.5 15.4 %copy-start.5 = (bf16[1024,768]{1,0:T(8,128)(2,1)S(1)}, bf16[1024,768]{1,0:T(8,128)(2,1)}, u32[]{:S(2)}) copy-start(bf16[1024,768]{1,0:T(8,128)(2,1)} %copy-done.4) | copy-start | bytes 4718596
  257.4 16.1 %collective-permute-start.25 = (bf16[256,768]{1,0:T(8,128)(2,1)S(1)}, bf16[256,768]{1,0:T(8,128)(2,1)S(1)}, u32[]{:S(2)}, u32[]{:S(2)}) collective-permute-start(bf16[256,768]{1,0:T(8,128)(2,1)S(1)} %get-tuple-element.9), channel_id=1, source_target_pairs={{0,4},{4,8},{8,12},{12,16},{16,20},{20,24},{24,28},{28,32},{32,36}... | collective-permute-start | bytes 1179656 | tf_op jit(solution)/shard_map/ppermute | solution.py:33
  257.5 16.0 %collective-permute-start.26 = (bf16[256,768]{1,0:T(8,128)(2,1)S(1)}, bf16[256,768]{1,0:T(8,128)(2,1)S(1)}, u32[]{:S(2)}, u32[]{:S(2)}) collective-permute-start(bf16[256,768]{1,0:T(8,128)(2,1)S(1)} %get-tuple-element.8), channel_id=1, source_target_pairs={{0,124},{4,0},{8,4},{12,8},{16,12},{20,16},{24,20},{28,24},{32,28}... | collective-permute-start | bytes 1179656 | tf_op jit(solution)/shard_map/ppermute | solution.py:34
  266.5 16.2 %collective-permute-start.19 = (bf16[256,768]{1,0:T(8,128)(2,1)}, bf16[256,768]{1,0:T(8,128)(2,1)S(1)}, u32[]{:S(2)}, u32[]{:S(2)}) collective-permute-start(bf16[256,768]{1,0:T(8,128)(2,1)} %get-tuple-element.7), channel_id=1, source_target_pairs={{0,4},{4,8},{8,12},{12,16},{16,20},{20,24},{24,28},{28,32},{32,36}... | collective-permute-start | bytes 1179656 | tf_op jit(solution)/shard_map/ppermute | solution.py:33
  266.5 16.2 %collective-permute-start.20 = (bf16[256,768]{1,0:T(8,128)(2,1)S(1)}, bf16[256,768]{1,0:T(8,128)(2,1)S(1)}, u32[]{:S(2)}, u32[]{:S(2)}) collective-permute-start(bf16[256,768]{1,0:T(8,128)(2,1)S(1)} %get-tuple-element.6), channel_id=1, source_target_pairs={{0,124},{4,0},{8,4},{12,8},{16,12},{20,16},{24,20},{28,24},{32,28}... | collective-permute-start | bytes 1179656 | tf_op jit(solution)/shard_map/ppermute | solution.py:34
  (5 other events, 23.6 us)
